TPU v7x, 32 devices: a whole 2x2x4 slice. The times are simulated.
32 devices in a mesh: tile: 8 (over z, y), win: 4 (over x, core).
Axes of the slice: x: 2, y: 2, z: 4, core: 2. Of those that a mesh axis runs over, the one named last changes fastest.
Arguments:
- records: bfloat16 [16, 2048, 2048], P('win', 'tile'), may hold values from -6 to 6
- pair_first: int32 [2048], P('tile'), may hold values from 0 to 255
- pair_offset: int32 [2048], P('tile'), may hold values from 1 to 255
- owners: int32 [2048, 1], P('tile'), may hold values from 0 to 7; in each aligned block of 256 rows (0 to 255, 256 to 511, ...) at most 80 rows name the same one
Outputs:
- gathers: bfloat16 [8, 8, 80, 2048], P('tile', None, None, 'win')
Inputs may be any that keep to these rules, and one draw needn't show every extreme that they name: `owners`: among the 256 pairs of one tile no owner is named more than 80 times, and in every draw some tile names some owner exactly 80 times.
All inputs are finite; a program needn't handle non-finite values.
Results may differ from a plain program's by a relative error of at most 0.0066.
Values may be sent and summed in bfloat16 or wider, within the bound.
No kernel may reach another device: no remote copies, remote signals or barrier semaphores. Data moves between devices by JAX's collectives and lax.ppermute only.
A program may use at most 128 MiB of HBM per device.

v0:
```python
import math

import jax
import jax.numpy as jnp
from jax import lax
from jax.sharding import PartitionSpec as P

BAND = 64


power_floor = 1e-06


def passed_along(block, axis, distance):
    devices = range(lax.axis_size(axis))
    route = [((i - distance) % len(devices), i) for i in devices]
    return lax.ppermute(block, axis, route)


def forward_matrix(length):
    row_index = lax.broadcasted_iota(jnp.int32, (length // 2, length), 0)
    col_index = lax.broadcasted_iota(jnp.int32, (length // 2, length), 1)
    phases = row_index * col_index % length
    angles = phases.astype(jnp.float32) * (2.0 * math.pi / length)
    return jnp.concatenate([jnp.cos(angles), -jnp.sin(angles)], axis=0).astype(jnp.bfloat16)


def inverse_matrix(length, first_lag, lag_count, seg_total):
    half_bins = length // 2
    lag_index = lax.broadcasted_iota(jnp.int32, (lag_count, half_bins), 0) + first_lag
    bin_index = lax.broadcasted_iota(jnp.int32, (lag_count, half_bins), 1)
    phases = lag_index * bin_index % length
    angles = phases.astype(jnp.float32) * (2.0 * math.pi / length)
    weights = jnp.where(bin_index == 0, 1.0, 2.0).astype(jnp.float32) * (
        1.0 / math.sqrt(half_bins * seg_total)
    )
    return jnp.concatenate([weights * jnp.cos(angles), -weights * jnp.sin(angles)], axis=1)


def whiten(spectra, band_width):
    half_bins = spectra.shape[-2] // 2
    real_rows = spectra[..., :half_bins, :]
    imaginary = spectra[..., half_bins:, :]
    energy = real_rows * real_rows + imaginary * imaginary
    grouped = energy.shape[:-2] + (half_bins // band_width, band_width, energy.shape[-1])
    band_power = jnp.mean(energy.reshape(grouped), axis=-2, keepdims=True)
    inverse_rms = jnp.broadcast_to(lax.rsqrt(band_power + power_floor), grouped).reshape(
        energy.shape
    )
    return (spectra * jnp.concatenate([inverse_rms, inverse_rms], axis=-2)).astype(jnp.bfloat16)


def cross_terms(first_part, second_part):
    half_bins = first_part.shape[-2] // 2
    first_real = first_part[..., :half_bins, :].astype(jnp.float32)
    first_imag = first_part[..., half_bins:, :].astype(jnp.float32)
    second_real = second_part[..., :half_bins, :].astype(jnp.float32)
    second_imag = second_part[..., half_bins:, :].astype(jnp.float32)
    real_sum = first_real * second_real + first_imag * second_imag
    imag_sum = first_imag * second_real - first_real * second_imag
    return jnp.concatenate([real_sum, imag_sum], axis=-2)


def bucket_select(owner_ids, owner_count, capacity):
    onehot = (owner_ids[:, None] == jnp.arange(owner_count, dtype=jnp.int32)[None, :]).astype(
        jnp.int32
    )
    slot_rank = jnp.sum((jnp.cumsum(onehot, axis=0, dtype=jnp.int32) - 1) * onehot, axis=1)
    slot_id = owner_ids * capacity + slot_rank
    return (
        slot_id[None, :] == jnp.arange(owner_count * capacity, dtype=jnp.int32)[:, None]
    ).astype(jnp.bfloat16)


def per_device(records, pair_first, pair_offset, owners):
    tile_count = lax.axis_size("tile")
    win_count = lax.axis_size("win")
    length = records.shape[1] * tile_count
    seg_total = records.shape[0] * win_count
    forward = forward_matrix(length)
    spectra = jnp.einsum(
        "fn,snc->sfc",
        forward,
        lax.all_to_all(records, "tile", split_axis=2, concat_axis=1, tiled=True),
        preferred_element_type=jnp.float32,
    )
    whitened = whiten(spectra, BAND)
    following = passed_along(whitened, "tile", -1)
    joined = jnp.concatenate([whitened, following], axis=2)
    first_part = jnp.take(joined, pair_first, axis=2)
    second_part = jnp.take(joined, pair_first + pair_offset, axis=2)
    cross = jnp.sum(cross_terms(first_part, second_part), axis=0)
    lag_count = length // win_count
    stacked = lax.psum(cross, "win")
    inverse = inverse_matrix(length, lax.axis_index("win") * lag_count, lag_count, seg_total)
    correlation = jnp.dot(inverse, stacked, precision=lax.Precision.HIGHEST)
    capacity = 5 * pair_first.shape[0] // (2 * tile_count)
    chooser = bucket_select(owners[:, 0], tile_count, capacity)
    picked = lax.dot_general(
        chooser,
        correlation.astype(jnp.bfloat16),
        (((1,), (1,)), ((), ())),
        preferred_element_type=jnp.float32,
    )
    buckets = picked.astype(jnp.bfloat16).reshape(tile_count, capacity, lag_count)
    received = lax.all_to_all(buckets, "tile", split_axis=0, concat_axis=0, tiled=True)
    return received[None]


def solution(mesh):
    placed = (P("win", "tile", None), P("tile"), P("tile"), P("tile", None))
    return jax.shard_map(
        per_device,
        mesh=mesh,
        in_specs=placed,
        out_specs=P("tile", None, None, "win"),
        check_vma=False,
    )
```

profile of v0, /device:TPU:0, one launch (start us, length us, event | category | flops | bytes accessed | tf_op | source)
XLA Modules:
  0.0 394.4 jit_solution(4413621781152123788)
XLA Ops:
  6.5 7.5 %copy.9 = bf16[4,256,2048]{1,0,2:T(4,128)(2,1)} copy(bf16[4,256,2048]{2,1,0:T(8,128)(2,1)} %param.6) | data formatting | bytes 8388608 | tf_op args[0]
  14.0 7.3 %all-to-all-start = ((bf16[4,256,2048]{1,0,2:T(4,128)(2,1)}), bf16[4,256,2048]{1,0,2:T(4,128)(2,1)}, u32[]{:S(2)}, u32[]{:S(2)}) async-start(bf16[4,256,2048]{1,0,2:T(4,128)(2,1)} %copy.9), calls=%async_computation | async-start | bytes 8388608 | tf_op jit(solution)/shard_map/all_to_all | solution.py:84
  21.3 0.0 all-reduce.2.cloned.1.call-start
  21.3 34.8 %negate_convert_fusion = (bf16[1024,2048]{1,0:T(8,128)(2,1)}, bf16[1024,2048]{1,0:T(8,128)(2,1)}) fusion(), kind=kLoop, calls=%fused_computation.16 | loop fusion | flops 35651584 | bytes 8388608 | tf_op jit(solution)/shard_map/convert.1
  56.1 58.5 %all-to-all-done = bf16[4,256,2048]{1,0,2:T(4,128)(2,1)} async-done(((bf16[4,256,2048]{1,0,2:T(4,128)(2,1)}), bf16[4,256,2048]{1,0,2:T(4,128)(2,1)}, u32[]{:S(2)}, u32[]{:S(2)}) %all-to-all-start) | async-done | bytes 4194336 | tf_op jit(solution)/shard_map/all_to_all | solution.py:84
  114.6 7.5 %copy.10 = bf16[4,256,8,256]{3,1,2,0:T(8,128)(2,1)} copy(bf16[4,256,8,256]{1,0,3,2:T(4,128)(2,1)} %bitcast.5) | data formatting | bytes 8388608 | tf_op jit(solution)/shard_map/all_to_all | solution.py:84
  122.1 12.4 %fusion.10 = f32[4,2048,256]{2,1,0:T(8,128)S(1)} fusion(bf16[4,2048,256]{2,1,0:T(8,128)(2,1)} %bitcast.32, bf16[1024,2048]{1,0:T(8,128)(2,1)} %get-tuple-element.13, bf16[1024,2048]{1,0:T(8,128)(2,1)} %get-tuple-element.14), kind=kOutput, calls=%fused_computation.25 | convolution fusion | flops 8606711808 | bytes 20971520 | tf_op jit(solution)/shard_map/fn,snc->sfc/dot_general | solution.py:81
  134.5 1.2 bitcast_reduce_fusion
  135.8 0.3 broadcast_in_dim.31
  136.1 0.0 copy-start.3
  136.1 0.0 copy-start.4
  136.1 1.2 fusion.6
  137.3 0.0 copy-start.1
  137.4 1.9 copy-done.1
  139.3 2.4 collective-permute-start
  141.7 0.0 copy-done.3
  141.7 0.0 copy-done.4
  141.7 89.9 %collective-permute-done = bf16[4,2048,256]{2,1,0:T(8,128)(2,1)} collective-permute-done((bf16[4,2048,256]{2,1,0:T(8,128)(2,1)S(1)}, bf16[4,2048,256]{2,1,0:T(8,128)(2,1)}, u32[]{:S(2)}, u32[]{:S(2)}) %collective-permute-start) | collective-permute-done | bytes 4194336 | tf_op jit(solution)/shard_map/ppermute | solution.py:17
  231.7 7.3 %pad_maximum_fusion = bf16[4,2048,512]{2,1,0:T(8,128)(2,1)} fusion(bf16[4,2048,256]{2,1,0:T(8,128)(2,1)} %collective-permute-done, bf16[4,2048,256]{2,1,0:T(8,128)(2,1)} %copy-done.1), kind=kLoop, calls=%fused_computation.14 | loop fusion | flops 16777216 | bytes 16777216 | tf_op jit(solution)/shard_map/concatenate | solution.py:89
  239.0 14.9 %copy.11 = bf16[4,2048,512]{1,0,2:T(4,128)(2,1)} copy(bf16[4,2048,512]{2,1,0:T(8,128)(2,1)} %pad_maximum_fusion) | data formatting | bytes 16777216 | tf_op jit(solution)/shard_map/concatenate | solution.py:89
  253.9 13.3 %gather_fusion.1 = bf16[256,4,2048]{2,1,0:T(4,128)(2,1)} fusion(bf16[4,2048,512]{1,0,2:T(4,128)(2,1)} %copy.11, s32[1024]{0:T(1024)S(1)} %pad_clamp_fusion), kind=kCustom, calls=%fused_computation.1.clone | custom fusion | bytes 8389632 | tf_op jit(solution)/shard_map/jit(_take)/gather | solution.py:91
  267.1 13.3 %gather_fusion = bf16[256,4,2048]{2,1,0:T(4,128)(2,1)} fusion(bf16[4,2048,512]{1,0,2:T(4,128)(2,1)} %copy.11, s32[1024]{0:T(1024)S(1)} %pad_clamp_fusion.1), kind=kCustom, calls=%fused_computation.clone | custom fusion | bytes 8389632 | tf_op jit(solution)/shard_map/jit(_take)/gather | solution.py:90
  280.5 0.0 copy-start
  280.5 4.4 %select_bitcast_fusion = bf16[4,2048,256]{1,0,2:T(4,128)(2,1)S(1)} fusion(bf16[256,4,2048]{2,1,0:T(4,128)(2,1)} %gather_fusion.1, pred[256]{0:T(512)(128)(4,1)S(1)} %get-tuple-element.6), kind=kLoop, calls=%fused_computation.36 | loop fusion | flops 2097152 | bytes 8388864 | tf_op jit(solution)/shard_map/jit(_take)/select_n | solution.py:91
  284.9 0.0 copy-done
  284.9 1.9 select_bitcast_fusion.1
  286.8 6.4 %fusion.11 = (f32[4,1024,256]{1,0,2:T(4,128)}, f32[4,1024,256]{1,0,2:T(4,128)}) fusion(bf16[4,2048,256]{1,0,2:T(4,128)(2,1)S(1)} %select_bitcast_fusion, bf16[4,2048,256]{1,0,2:T(4,128)(2,1)S(1)} %select_bitcast_fusion.1), kind=kLoop, calls=%fused_computation.26 | loop fusion | flops 10485760 | bytes 16777216 | tf_op jit(solution)/shard_map/add | solution.py:59
  293.3 0.0 copy-start.2
  293.3 11.0 %maximum_reduce_fusion = f32[2048,256]{0,1:T(8,128)} fusion(f32[4,1024,256]{1,0,2:T(4,128)} %get-tuple-element.9, f32[4,1024,256]{1,0,2:T(4,128)} %get-tuple-element.8), kind=kLoop, calls=%fused_computation.15 | loop fusion | flops 3670016 | bytes 10485760 | tf_op jit(solution)/shard_map/reduce_sum | solution.py:92
  304.3 0.0 all-reduce.2.cloned.1.call-update
  304.3 0.0 copy-done.2
  304.3 0.6 reduce-window.6
  304.9 0.2 slice_reduce_fusion
  305.2 0.1 fusion.28
  305.3 9.8 %cosine_multiply_fusion = (f32[512,1024]{1,0:T(8,128)S(1)}, f32[512,1024]{1,0:T(8,128)}) fusion(s32[512]{0:T(512)S(1)} %iota_add_fusion, f32[1024]{0:T(1024)S(1)} %get-tuple-element.15, f32[1024]{0:T(1024)S(1)} %get-tuple-element.16), kind=kLoop, calls=%fused_computation.45 | loop fusion | flops 8388608 | bytes 4204544 | tf_op jit(solution)/shard_map/mul | solution.py:37
  315.1 42.7 %all-reduce.2.cloned.1.call-done = f32[2048,256]{0,1:T(8,128)} async-done(((f32[2048,256]{0,1:T(8,128)}), f32[2048,256]{0,1:T(8,128)}) %all-reduce.2.cloned.1.call-update) | async-done | bytes 2097168 | tf_op jit(solution)/shard_map/psum | solution.py:94
  357.8 5.7 %fusion.24 = bf16[512,256]{1,0:T(8,128)(2,1)S(1)} fusion(f32[2048,256]{0,1:T(8,128)} %all-reduce.2.cloned.1.call-done, f32[512,1024]{1,0:T(8,128)} %get-tuple-element.11, f32[512,1024]{1,0:T(8,128)S(1)} %get-tuple-element.10), kind=kOutput, calls=%fused_computation.50 | convolution fusion | flops 3222405120 | bytes 6553600 | tf_op jit(solution)/shard_map/dot_general | solution.py:96
  363.5 0.4 convolution_convert_fusion
  363.9 22.8 %all_to_all.23 = bf16[8,80,512]{2,1,0:T(8,128)(2,1)S(1)} all-to-all(bf16[8,80,512]{2,1,0:T(8,128)(2,1)S(1)} %bitcast.33), channel_id=1, replica_groups=mesh['tile'=8,'win'=4] {'tile'}, dimensions={0} | all-to-all | bytes 1310720 | tf_op jit(solution)/shard_map/all_to_all | solution.py:106
  386.7 0.8 copy.15
  (11 shorter events, 0.1 us)
Async XLA Ops:
  14.0 100.6 %all-to-all-start = ((bf16[4,256,2048]{1,0,2:T(4,128)(2,1)}), bf16[4,256,2048]{1,0,2:T(4,128)(2,1)}, u32[]{:S(2)}, u32[]{:S(2)}) async-start(bf16[4,256,2048]{1,0,2:T(4,128)(2,1)} %copy.9), calls=%async_computation | async-start | bytes 8388608 | tf_op jit(solution)/shard_map/all_to_all | solution.py:84
  21.3 336.5 %all-reduce.2.cloned.1.call-start = ((), (), s32[]{:S(2)}) async-start(), calls=%async_computation.2 | async-start | bytes 4194304 | tf_op jit(solution)/shard_map/psum | solution.py:94
  136.1 5.6 %copy-start.3 = (s32[256]{0:T(256)S(1)}, s32[256]{0:T(256)}, u32[]{:S(2)}) copy-start(s32[256]{0:T(256)} %param.7) | copy-start | bytes 3076
  136.1 5.6 %copy-start.4 = (s32[256]{0:T(256)S(1)}, s32[256]{0:T(256)}, u32[]{:S(2)}) copy-start(s32[256]{0:T(256)} %param.8) | copy-start | bytes 3076
  137.3 2.0 copy-start.1
  139.3 92.4 %collective-permute-start = (bf16[4,2048,256]{2,1,0:T(8,128)(2,1)S(1)}, bf16[4,2048,256]{2,1,0:T(8,128)(2,1)}, u32[]{:S(2)}, u32[]{:S(2)}) collective-permute-start(bf16[4,2048,256]{2,1,0:T(8,128)(2,1)S(1)} %fusion.6), channel_id=1, source_target_pairs={{4,0},{8,4},{12,8},{16,12},{20,16},{24,20},{28,24},{0,28},{5,1},{9... | collective-permute-start | bytes 12582920 | tf_op jit(solution)/shard_map/ppermute | solution.py:17
  280.5 4.4 %copy-start = (bf16[256,4,2048]{2,1,0:T(4,128)(2,1)S(1)}, bf16[256,4,2048]{2,1,0:T(4,128)(2,1)}, u32[]{:S(2)}) copy-start(bf16[256,4,2048]{2,1,0:T(4,128)(2,1)} %gather_fusion) | copy-start | bytes 12582916
  293.3 11.0 %copy-start.2 = (s32[256,1]{0,1:T(1,128)S(1)}, s32[256,1]{0,1:T(1,128)}, u32[]{:S(2)}) copy-start(s32[256,1]{0,1:T(1,128)} %param.9) | copy-start | bytes 3076
Sparse Core Ops, SparseCore 0:
  304.4 53.3 all-reduce.1
where the time goes:
time: 395 us; the launch traced here: 394 us
  waiting for transfers between devices  191 us (48%)
  other arithmetic  78.8 us (20%)
  local copies, waits for them, and re-layouts  59.8 us (15%)
  blocking collectives  22.8 us (6%)
  matrix products  18.5 us (5%)
  between operations  13.6 us (3%)
  starting transfers between devices  9.72 us (2%)
    ppermute x1, waiting for transfers between devices, passed_along(): return lax.ppermute(block, axis, route)  89.9 us
    all_to_all x1, waiting for transfers between devices, per_device(): lax.all_to_all(records, 'tile', split_axis=2, concat_axis=1, tiled=True)  58.5 us
    psum x1, waiting for transfers between devices, per_device(): stacked = lax.psum(cross, 'win')  42.7 us
    another operation x3, other arithmetic  35.4 us
    all_to_all x1, blocking collectives, per_device(): lax.all_to_all(buckets, 'tile', split_axis=0, concat_axis=0, tiled=True)  22.8 us
    concatenate x1, local copies, waits for them, and re-layouts, per_device(): joined = jnp.concatenate([whitened, following], axis=2)  14.9 us
    gather x1, local copies, waits for them, and re-layouts, per_device(): first_part = jnp.take(joined, pair_first, axis=2)  13.3 us
    gather x1, local copies, waits for them, and re-layouts, per_device(): second_part = jnp.take(joined, pair_first + pair_offset, axis=2)  13.3 us
  transfers between devices with their start and end apart: 3, of which 3 were waited for; matrix products, arithmetic and copies ran while one was open for 12% of the time, Pallas kernels for 0%

commit v1 on v0

--- a/solution.py
+++ b/solution.py
@@ -17,24 +17,35 @@
     return lax.ppermute(block, axis, route)
 
 
+def phase_table(rows, col_count, length):
+    split = 64 if col_count % 64 == 0 else 1
+    coarse = jnp.arange(col_count // split, dtype=jnp.int32) * split
+    fine = jnp.arange(split, dtype=jnp.int32)
+    scale = 2.0 * math.pi / length
+    coarse_angle = ((rows[:, None] * coarse[None, :]) % length).astype(jnp.float32) * scale
+    fine_angle = ((rows[:, None] * fine[None, :]) % length).astype(jnp.float32) * scale
+    c_hi, s_hi = jnp.cos(coarse_angle)[:, :, None], jnp.sin(coarse_angle)[:, :, None]
+    c_lo, s_lo = jnp.cos(fine_angle)[:, None, :], jnp.sin(fine_angle)[:, None, :]
+    shape = (rows.shape[0], col_count)
+    cosine = (c_hi * c_lo - s_hi * s_lo).reshape(shape)
+    sine = (s_hi * c_lo + c_hi * s_lo).reshape(shape)
+    return cosine, sine
+
+
 def forward_matrix(length):
-    row_index = lax.broadcasted_iota(jnp.int32, (length // 2, length), 0)
-    col_index = lax.broadcasted_iota(jnp.int32, (length // 2, length), 1)
-    phases = row_index * col_index % length
-    angles = phases.astype(jnp.float32) * (2.0 * math.pi / length)
-    return jnp.concatenate([jnp.cos(angles), -jnp.sin(angles)], axis=0).astype(jnp.bfloat16)
+    cosine, sine = phase_table(jnp.arange(length // 2, dtype=jnp.int32), length, length)
+    return jnp.concatenate([cosine, -sine], axis=0).astype(jnp.bfloat16)
 
 
 def inverse_matrix(length, first_lag, lag_count, seg_total):
     half_bins = length // 2
-    lag_index = lax.broadcasted_iota(jnp.int32, (lag_count, half_bins), 0) + first_lag
-    bin_index = lax.broadcasted_iota(jnp.int32, (lag_count, half_bins), 1)
-    phases = lag_index * bin_index % length
-    angles = phases.astype(jnp.float32) * (2.0 * math.pi / length)
+    lags = jnp.arange(lag_count, dtype=jnp.int32) + first_lag
+    cosine, sine = phase_table(lags, half_bins, length)
+    bin_index = jnp.arange(half_bins)[None, :]
     weights = jnp.where(bin_index == 0, 1.0, 2.0).astype(jnp.float32) * (
         1.0 / math.sqrt(half_bins * seg_total)
     )
-    return jnp.concatenate([weights * jnp.cos(angles), -weights * jnp.sin(angles)], axis=1)
+    return jnp.concatenate([weights * cosine, -weights * sine], axis=1)
 
 
 def whiten(spectra, band_width):
@@ -87,8 +98,11 @@
     whitened = whiten(spectra, BAND)
     following = passed_along(whitened, "tile", -1)
     joined = jnp.concatenate([whitened, following], axis=2)
-    first_part = jnp.take(joined, pair_first, axis=2)
-    second_part = jnp.take(joined, pair_first + pair_offset, axis=2)
+    channel_ids = jnp.arange(joined.shape[2], dtype=jnp.int32)[:, None]
+    pick_first = (channel_ids == pair_first[None, :]).astype(jnp.bfloat16)
+    pick_second = (channel_ids == (pair_first + pair_offset)[None, :]).astype(jnp.bfloat16)
+    first_part = jnp.einsum("sfc,cp->sfp", joined, pick_first, preferred_element_type=jnp.float32)
+    second_part = jnp.einsum("sfc,cp->sfp", joined, pick_second, preferred_element_type=jnp.float32)
     cross = jnp.sum(cross_terms(first_part, second_part), axis=0)
     lag_count = length // win_count
     stacked = lax.psum(cross, "win")

time: 395 us -> 345 us (0.87)
  other arithmetic: 78.8 us -> 20.2 us
  local copies, waits for them, and re-layouts: 59.8 us -> 29.3 us
  waiting for transfers between devices: 191 us -> 213 us
  matrix products: 18.5 us -> 35.7 us
    another operation x3, other arithmetic: 35.4 us -> 5.63 us
    gather x2 -> x0, local copies, waits for them, and re-layouts: 26.6 us -> none  [the longest x1 13.3 us: per_device(): first_part = jnp.take(joined, pair_first, axis=2)]
    all_to_all x1, waiting for transfers between devices: 58.5 us -> 73.6 us  [per_device(): lax.all_to_all(records, 'tile', split_axis=2, concat_axis=1, tiled=True)]
    concatenate x1 -> x0, local copies, waits for them, and re-layouts: 14.9 us -> none  [per_device(): joined = jnp.concatenate([whitened, following], axis=2)]
    dot_general x0 -> x2, matrix products: none -> 14 us  [the longest x1 9.09 us: per_device(): jnp.einsum('sfc,cp->sfp', joined, pick_second, preferred_element_type=jnp...]
    reduce_sum x1, other arithmetic: 11 us -> 1.95 us  [per_device(): cross = jnp.sum(cross_terms(first_part, second_part), axis=0)]
    mul x1 -> x3, other arithmetic: 9.78 us -> 1.66 us  [the longest x1 1.65 us: inverse_matrix(): return jnp.concatenate([weights * cosine, -weights * sine], axis=1)]
    psum x1, waiting for transfers between devices: 42.7 us -> 50.6 us  [per_device(): stacked = lax.psum(cross, 'win')]
  transfers between devices with their start and end apart: 3 -> 3, of which waited for: 3 -> 3; matrix products, arithmetic and copies ran while one was open for 12% -> 7% of each run, Pallas kernels for 0% -> 0%
where the time goes in v1:
time: 345 us
  waiting for transfers between devices  213 us (62%)
  matrix products  35.7 us (10%)
  local copies, waits for them, and re-layouts  29.3 us (8%)
  blocking collectives  22.8 us (7%)
  other arithmetic  20.2 us (6%)
  between operations  13.6 us (4%)
  starting transfers between devices  9.72 us (3%)
    ppermute x1, waiting for transfers between devices, passed_along(): return lax.ppermute(block, axis, route)  89.1 us
    all_to_all x1, waiting for transfers between devices, per_device(): lax.all_to_all(records, 'tile', split_axis=2, concat_axis=1, tiled=True)  73.6 us
    psum x1, waiting for transfers between devices, per_device(): stacked = lax.psum(cross, 'win')  50.6 us
    all_to_all x1, blocking collectives, per_device(): lax.all_to_all(buckets, 'tile', split_axis=0, concat_axis=0, tiled=True)  22.8 us
    dot_general x1, matrix products, per_device(): jnp.einsum('fn,snc->sfc', forward, lax.all_to_all(records, 'tile', split_...  12.4 us
    dot_general x1, matrix products, per_device(): jnp.einsum('sfc,cp->sfp', joined, pick_second, preferred_element_type=jnp...  9.09 us
    dot_general x1, matrix products, per_device(): correlation = jnp.dot(inverse, stacked, precision=lax.Precision.HIGHEST)  8.89 us
    unnamed x8, local copies, waits for them, and re-layouts  8.32 us
  transfers between devices with their start and end apart: 3, of which 3 were waited for; matrix products, arithmetic and copies ran while one was open for 7% of the time, Pallas kernels for 0%

profile of v1, /device:TPU:0, one launch (start us, length us, event | category | flops | bytes accessed | tf_op | source)
XLA Modules:
  0.0 344.6 jit_solution(2424194621263495125)
XLA Ops:
  6.5 7.5 %copy.11 = bf16[4,256,2048]{1,0,2:T(4,128)(2,1)} copy(bf16[4,256,2048]{2,1,0:T(8,128)(2,1)} %param.4) | data formatting | bytes 8388608 | tf_op args[0]
  14.0 7.3 %all-to-all-start = ((bf16[4,256,2048]{1,0,2:T(4,128)(2,1)}), bf16[4,256,2048]{1,0,2:T(4,128)(2,1)}, u32[]{:S(2)}, u32[]{:S(2)}) async-start(bf16[4,256,2048]{1,0,2:T(4,128)(2,1)} %copy.11), calls=%async_computation | async-start | bytes 8388608 | tf_op jit(solution)/shard_map/all_to_all | solution.py:95
  21.3 0.0 all-reduce.2.cloned.1.call-start
  21.4 1.0 fusion.34
  22.4 0.6 fusion.43
  23.0 5.0 %subtract_convert_fusion = (bf16[1024,32,64]{0,2,1:T(8,128)(2,1)}, bf16[1024,32,64]{0,2,1:T(8,128)(2,1)}) fusion(f32[1024,64]{0,1:T(8,128)S(1)} %get-tuple-element.17, f32[1024,32]{0,1:T(8,128)S(1)} %get-tuple-element.16, f32[1024,64]{0,1:T(8,128)S(1)} %get-tuple-element.18, f32[1024,32]{0,1:T(8,128)S(1)} %get-tuple-element.15), kind=kLoop, calls=%fused_computation.9 | loop fusion | flops 18874368 | bytes 9175040 | tf_op jit(solution)/shard_map/convert.3
  28.0 6.5 %copy.10 = bf16[1024,2048]{1,0:T(8,128)(2,1)} copy(bf16[1024,2048]{0,1:T(8,128)(2,1)} %bitcast.40) | data formatting | bytes 8388608 | tf_op jit(solution)/shard_map/neg | solution.py:37
  34.5 6.5 %copy.9 = bf16[1024,2048]{1,0:T(8,128)(2,1)} copy(bf16[1024,2048]{0,1:T(8,128)(2,1)} %bitcast.39) | data formatting | bytes 8388608 | tf_op jit(solution)/shard_map/sub | solution.py:30
  41.0 73.6 %all-to-all-done = bf16[4,256,2048]{1,0,2:T(4,128)(2,1)} async-done(((bf16[4,256,2048]{1,0,2:T(4,128)(2,1)}), bf16[4,256,2048]{1,0,2:T(4,128)(2,1)}, u32[]{:S(2)}, u32[]{:S(2)}) %all-to-all-start) | async-done | bytes 4194336 | tf_op jit(solution)/shard_map/all_to_all | solution.py:95
  114.6 7.5 %copy.12 = bf16[4,256,8,256]{3,1,2,0:T(8,128)(2,1)} copy(bf16[4,256,8,256]{1,0,3,2:T(4,128)(2,1)} %bitcast.9) | data formatting | bytes 8388608 | tf_op jit(solution)/shard_map/all_to_all | solution.py:95
  122.1 12.4 %fusion.6 = f32[4,2048,256]{2,1,0:T(8,128)S(1)} fusion(bf16[4,2048,256]{2,1,0:T(8,128)(2,1)} %bitcast.42, bf16[1024,2048]{1,0:T(8,128)(2,1)} %copy.10, bf16[1024,2048]{1,0:T(8,128)(2,1)} %copy.9), kind=kOutput, calls=%fused_computation.12 | convolution fusion | flops 8606711808 | bytes 20971520 | tf_op jit(solution)/shard_map/fn,snc->sfc/dot_general | solution.py:92
  134.5 1.2 bitcast_reduce_fusion
  135.8 0.3 broadcast_in_dim.12
  136.1 0.0 copy-start
  136.1 0.0 copy-start.1
  136.1 0.0 copy-start.2
  136.1 2.6 fusion.3
  138.8 2.4 collective-permute-start
  141.1 0.0 copy-done
  141.1 0.6 reduce-window.6
  141.7 0.2 slice_reduce_fusion
  142.0 0.0 copy-done.1
  142.0 0.0 copy-done.2
  142.0 0.1 fusion.51
  142.1 0.2 fusion.50
  142.3 89.1 %collective-permute-done = bf16[4,2048,256]{2,1,0:T(8,128)(2,1)} collective-permute-done((bf16[4,2048,256]{2,1,0:T(8,128)(2,1)}, bf16[4,2048,256]{2,1,0:T(8,128)(2,1)}, u32[]{:S(2)}, u32[]{:S(2)}) %collective-permute-start) | collective-permute-done | bytes 4194336 | tf_op jit(solution)/shard_map/ppermute | solution.py:17
  231.5 4.9 %fusion.5 = f32[4,2048,256]{2,1,0:T(8,128)S(1)} fusion(bf16[4,2048,256]{2,1,0:T(8,128)(2,1)} %collective-permute-done, bf16[4,2048,256]{2,1,0:T(8,128)(2,1)} %fusion.3, s32[256]{0:T(256)S(1)} %copy-done.2), kind=kOutput, calls=%fused_computation.11 | convolution fusion | flops 2164391936 | bytes 16778240 | tf_op jit(solution)/shard_map/sfc,cp->sfp/dot_general | solution.py:104
  236.3 9.1 %fusion.4 = f32[4,2048,256]{2,1,0:T(8,128)} fusion(bf16[4,2048,256]{2,1,0:T(8,128)(2,1)} %collective-permute-done, bf16[4,2048,256]{2,1,0:T(8,128)(2,1)} %fusion.3, s32[256]{0:T(256)S(1)} %add.123), kind=kOutput, calls=%fused_computation.10 | convolution fusion | flops 2164391936 | bytes 16778240 | tf_op jit(solution)/shard_map/sfc,cp->sfp/dot_general | solution.py:105
  245.4 4.0 %multiply_add_fusion = (f32[4,1024,256]{2,1,0:T(8,128)S(1)}, f32[4,1024,256]{2,1,0:T(8,128)S(1)}) fusion(f32[4,2048,256]{2,1,0:T(8,128)} %fusion.4, f32[4,2048,256]{2,1,0:T(8,128)S(1)} %fusion.5), kind=kLoop, calls=%fused_computation.22 | loop fusion | flops 6291456 | bytes 25165824 | tf_op jit(solution)/shard_map/add | solution.py:70
  249.5 2.0 maximum_reduce_fusion
  251.4 0.0 all-reduce.2.cloned.1.call-update
  251.5 0.5 fusion.45
  252.0 0.6 multiply_subtract_fusion.1
  252.6 1.7 bitcast_multiply_fusion
  254.2 50.6 %all-reduce.2.cloned.1.call-done = f32[2048,256]{1,0:T(8,128)} async-done(((f32[2048,256]{1,0:T(8,128)}), f32[2048,256]{1,0:T(8,128)}) %all-reduce.2.cloned.1.call-update) | async-done | bytes 2097168 | tf_op jit(solution)/shard_map/psum | solution.py:108
  304.9 8.9 %fusion.12 = bf16[512,256]{1,0:T(8,128)(2,1)S(1)} fusion(f32[2048,256]{1,0:T(8,128)} %all-reduce.2.cloned.1.call-done, f32[512,1024]{0,1:T(8,128)S(1)} %get-tuple-element.19, f32[512,1024]{0,1:T(8,128)} %get-tuple-element.20), kind=kOutput, calls=%fused_computation.28 | convolution fusion | flops 3222405120 | bytes 6553600 | tf_op jit(solution)/shard_map/dot_general | solution.py:110
  313.8 0.4 convolution_convert_fusion
  314.1 22.8 %all_to_all.23 = bf16[8,80,512]{2,1,0:T(8,128)(2,1)S(1)} all-to-all(bf16[8,80,512]{2,1,0:T(8,128)(2,1)S(1)} %bitcast.43), channel_id=1, replica_groups=mesh['tile'=8,'win'=4] {'tile'}, dimensions={0} | all-to-all | bytes 1310720 | tf_op jit(solution)/shard_map/all_to_all | solution.py:120
  336.9 0.8 copy.15
  (11 shorter events, 0.1 us)
Async XLA Ops:
  14.0 100.6 %all-to-all-start = ((bf16[4,256,2048]{1,0,2:T(4,128)(2,1)}), bf16[4,256,2048]{1,0,2:T(4,128)(2,1)}, u32[]{:S(2)}, u32[]{:S(2)}) async-start(bf16[4,256,2048]{1,0,2:T(4,128)(2,1)} %copy.11), calls=%async_computation | async-start | bytes 8388608 | tf_op jit(solution)/shard_map/all_to_all | solution.py:95
  21.3 283.6 %all-reduce.2.cloned.1.call-start = ((), (), s32[]{:S(2)}) async-start(), calls=%async_computation.2 | async-start | bytes 4194304 | tf_op jit(solution)/shard_map/psum | solution.py:108
  136.1 5.1 %copy-start = (s32[256,1]{0,1:T(1,128)S(1)}, s32[256,1]{0,1:T(1,128)}, u32[]{:S(2)}) copy-start(s32[256,1]{0,1:T(1,128)} %param.7) | copy-start | bytes 3076
  136.1 5.9 %copy-start.1 = (s32[256]{0:T(256)S(1)}, s32[256]{0:T(256)}, u32[]{:S(2)}) copy-start(s32[256]{0:T(256)} %param.6) | copy-start | bytes 3076
  136.1 5.9 %copy-start.2 = (s32[256]{0:T(256)S(1)}, s32[256]{0:T(256)}, u32[]{:S(2)}) copy-start(s32[256]{0:T(256)} %param.5) | copy-start | bytes 3076
  138.8 92.7 %collective-permute-start = (bf16[4,2048,256]{2,1,0:T(8,128)(2,1)}, bf16[4,2048,256]{2,1,0:T(8,128)(2,1)}, u32[]{:S(2)}, u32[]{:S(2)}) collective-permute-start(bf16[4,2048,256]{2,1,0:T(8,128)(2,1)} %fusion.3), channel_id=1, source_target_pairs={{4,0},{8,4},{12,8},{16,12},{20,16},{24,20},{28,24},{0,28},{5,1},{9... | collective-permute-start | bytes 12582920 | tf_op jit(solution)/shard_map/ppermute | solution.py:17
Sparse Core Ops, SparseCore 0:
  251.6 53.2 all-reduce.1

commit v2 on v1

--- a/solution.py
+++ b/solution.py
@@ -9,12 +9,6 @@
 
 
 power_floor = 1e-06
-
-
-def passed_along(block, axis, distance):
-    devices = range(lax.axis_size(axis))
-    route = [((i - distance) % len(devices), i) for i in devices]
-    return lax.ppermute(block, axis, route)
 
 
 def phase_table(rows, col_count, length):
@@ -83,48 +77,106 @@
     ).astype(jnp.bfloat16)
 
 
-def per_device(records, pair_first, pair_offset, owners):
-    tile_count = lax.axis_size("tile")
-    win_count = lax.axis_size("win")
-    length = records.shape[1] * tile_count
-    seg_total = records.shape[0] * win_count
-    forward = forward_matrix(length)
-    spectra = jnp.einsum(
-        "fn,snc->sfc",
-        forward,
-        lax.all_to_all(records, "tile", split_axis=2, concat_axis=1, tiled=True),
-        preferred_element_type=jnp.float32,
-    )
-    whitened = whiten(spectra, BAND)
-    following = passed_along(whitened, "tile", -1)
-    joined = jnp.concatenate([whitened, following], axis=2)
-    channel_ids = jnp.arange(joined.shape[2], dtype=jnp.int32)[:, None]
-    pick_first = (channel_ids == pair_first[None, :]).astype(jnp.bfloat16)
-    pick_second = (channel_ids == (pair_first + pair_offset)[None, :]).astype(jnp.bfloat16)
-    first_part = jnp.einsum("sfc,cp->sfp", joined, pick_first, preferred_element_type=jnp.float32)
-    second_part = jnp.einsum("sfc,cp->sfp", joined, pick_second, preferred_element_type=jnp.float32)
-    cross = jnp.sum(cross_terms(first_part, second_part), axis=0)
-    lag_count = length // win_count
-    stacked = lax.psum(cross, "win")
-    inverse = inverse_matrix(length, lax.axis_index("win") * lag_count, lag_count, seg_total)
-    correlation = jnp.dot(inverse, stacked, precision=lax.Precision.HIGHEST)
-    capacity = 5 * pair_first.shape[0] // (2 * tile_count)
-    chooser = bucket_select(owners[:, 0], tile_count, capacity)
-    picked = lax.dot_general(
-        chooser,
-        correlation.astype(jnp.bfloat16),
-        (((1,), (1,)), ((), ())),
-        preferred_element_type=jnp.float32,
-    )
-    buckets = picked.astype(jnp.bfloat16).reshape(tile_count, capacity, lag_count)
-    received = lax.all_to_all(buckets, "tile", split_axis=0, concat_axis=0, tiled=True)
-    return received[None]
+def tile_ring(mesh):
+    count = mesh.shape["tile"]
+    try:
+        column = mesh.devices.reshape(count, -1)[:, 0]
+        spots = [tuple(int(c) for c in d.coords) for d in column]
+    except (AttributeError, TypeError):
+        return list(range(count))
+    near = [
+        [j for j in range(count) if sum(abs(a - b) for a, b in zip(spots[i], spots[j])) == 1]
+        for i in range(count)
+    ]
+    path, seen, budget = [0], {0}, [20000]
+
+    def extend():
+        budget[0] -= 1
+        if budget[0] < 0:
+            return False
+        if len(path) == count:
+            return count < 3 or 0 in near[path[-1]]
+        options = [j for j in near[path[-1]] if j not in seen]
+        options.sort(key=lambda j: sum(1 for k in near[j] if k not in seen))
+        for j in options:
+            path.append(j)
+            seen.add(j)
+            if extend():
+                return True
+            path.pop()
+            seen.discard(j)
+        return False
+
+    return path if extend() else list(range(count))
+
+
+def make_per_device(ring):
+    count = len(ring)
+    block_of = [0] * count
+    for place, device in enumerate(ring):
+        block_of[device] = place
+    to_prev = [(ring[r], ring[(r - 1) % count]) for r in range(count)]
+    to_next = [(ring[r], ring[(r + 1) % count]) for r in range(count)]
+
+    def per_device(records, pair_first, pair_offset, owners):
+        tile_count = lax.axis_size("tile")
+        win_count = lax.axis_size("win")
+        length = records.shape[1] * tile_count
+        seg_total = records.shape[0] * win_count
+        block = records.shape[2] // tile_count
+        half = block // 2
+        my_block = jnp.asarray(block_of, dtype=jnp.int32)[lax.axis_index("tile")]
+        shifted = jnp.roll(records, -half, axis=2).reshape(
+            records.shape[0], records.shape[1], tile_count, block
+        )
+        outgoing = jnp.concatenate([shifted[:, :, b] for b in block_of], axis=2)
+        forward = forward_matrix(length)
+        spectra = jnp.einsum(
+            "fn,snc->sfc",
+            forward,
+            lax.all_to_all(outgoing, "tile", split_axis=2, concat_axis=1, tiled=True),
+            preferred_element_type=jnp.float32,
+        )
+        whitened = whiten(spectra, BAND)
+        from_prev = lax.ppermute(whitened[:, :, half:], "tile", to_next)
+        from_next = lax.ppermute(whitened[:, :, :half], "tile", to_prev)
+        joined = jnp.concatenate([from_prev, whitened, from_next], axis=2)
+        all_first = lax.all_gather(pair_first, "tile")
+        all_offset = lax.all_gather(pair_offset, "tile")
+        all_owners = lax.all_gather(owners[:, 0], "tile")
+        my_first = lax.dynamic_index_in_dim(all_first, my_block, 0, keepdims=False)
+        my_offset = lax.dynamic_index_in_dim(all_offset, my_block, 0, keepdims=False)
+        my_owners = lax.dynamic_index_in_dim(all_owners, my_block, 0, keepdims=False)
+        channel_ids = jnp.arange(joined.shape[2], dtype=jnp.int32)[:, None]
+        pick_first = (channel_ids == my_first[None, :]).astype(jnp.bfloat16)
+        pick_second = (channel_ids == (my_first + my_offset)[None, :]).astype(jnp.bfloat16)
+        first_part = jnp.einsum("sfc,cp->sfp", joined, pick_first, preferred_element_type=jnp.float32)
+        second_part = jnp.einsum("sfc,cp->sfp", joined, pick_second, preferred_element_type=jnp.float32)
+        cross = jnp.sum(cross_terms(first_part, second_part), axis=0)
+        lag_count = length // win_count
+        stacked = lax.psum(cross, "win")
+        inverse = inverse_matrix(length, lax.axis_index("win") * lag_count, lag_count, seg_total)
+        correlation = jnp.dot(inverse, stacked, precision=lax.Precision.HIGHEST)
+        capacity = 5 * pair_first.shape[0] // (2 * tile_count)
+        chooser = bucket_select(my_owners, tile_count, capacity)
+        picked = lax.dot_general(
+            chooser,
+            correlation.astype(jnp.bfloat16),
+            (((1,), (1,)), ((), ())),
+            preferred_element_type=jnp.float32,
+        )
+        buckets = picked.astype(jnp.bfloat16).reshape(tile_count, capacity, lag_count)
+        received = lax.all_to_all(buckets, "tile", split_axis=0, concat_axis=0, tiled=True)
+        ordered = jnp.stack([received[d] for d in ring], axis=0)
+        return ordered[None]
+
+    return per_device
 
 
 def solution(mesh):
     placed = (P("win", "tile", None), P("tile"), P("tile"), P("tile", None))
     return jax.shard_map(
-        per_device,
+        make_per_device(tile_ring(mesh)),
         mesh=mesh,
         in_specs=placed,
         out_specs=P("tile", None, None, "win"),

time: 345 us -> 393 us (1.14)
  waiting for transfers between devices: 213 us -> 119 us
  blocking collectives: 22.8 us -> 114 us
  local copies, waits for them, and re-layouts: 29.3 us -> 68.7 us
  other arithmetic: 20.2 us -> 32.3 us
    all_gather x0 -> x3, blocking collectives: none -> 91.4 us  [the longest x1 56.6 us: per_device(): all_owners = lax.all_gather(owners[:, 0], 'tile')]
    ppermute x1 -> x2, waiting for transfers between devices: 89.1 us -> 0.01 us  [the longest x1 0.01 us: per_device(): from_next = lax.ppermute(whitened[:, :, :half], 'tile', to_prev)]
    concatenate x0 -> x2, local copies, waits for them, and re-layouts: none -> 17.2 us  [per_device(): outgoing = jnp.concatenate([shifted[:, :, b] for b in block_of], axis=2)]
    slice x1 -> x4, local copies, waits for them, and re-layouts: 0.21 us -> 6.36 us  [the longest x3 4.27 us: per_device(): jnp.roll(records, -half, axis=2)]
    reshape x0 -> x1, local copies, waits for them, and re-layouts: none -> 5.4 us  [whiten(): jnp.broadcast_to(lax.rsqrt(band_power + power_floor), grouped)]
    add x0 -> x1, local copies, waits for them, and re-layouts: none -> 5.37 us  [whiten(): energy = real_rows * real_rows + imaginary * imaginary]
    psum x1, waiting for transfers between devices: 50.6 us -> 46 us  [per_device(): stacked = lax.psum(cross, 'win')]
    convert_element_type x1, other arithmetic: 2.64 us -> 6.96 us  [whiten(): (spectra * jnp.concatenate([inverse_rms, inverse_rms], axis=-2)).astype(j...]
  transfers between devices with their start and end apart: 3 -> 4, of which waited for: 3 -> 2; matrix products, arithmetic and copies ran while one was open for 7% -> 7% of each run, Pallas kernels for 0% -> 0%
where the time goes in v2:
time: 393 us; the launch traced here: 392 us
  waiting for transfers between devices  119 us (30%)
  blocking collectives  114 us (29%)
  local copies, waits for them, and re-layouts  68.7 us (17%)
  other arithmetic  32.3 us (8%)
  matrix products  32.3 us (8%)
  between operations  15.7 us (4%)
  starting transfers between devices  9.37 us (2%)
    all_to_all x1, waiting for transfers between devices, per_device(): lax.all_to_all(outgoing, 'tile', split_axis=2, concat_axis=1, tiled=True)  73.5 us
    all_gather x1, blocking collectives, per_device(): all_owners = lax.all_gather(owners[:, 0], 'tile')  56.6 us
    psum x1, waiting for transfers between devices, per_device(): stacked = lax.psum(cross, 'win')  46 us
    all_to_all x1, blocking collectives, per_device(): lax.all_to_all(buckets, 'tile', split_axis=0, concat_axis=0, tiled=True)  22.8 us
    all_gather x1, blocking collectives, per_device(): all_offset = lax.all_gather(pair_offset, 'tile')  18 us
    concatenate x2, local copies, waits for them, and re-layouts, per_device(): outgoing = jnp.concatenate([shifted[:, :, b] for b in block_of], axis=2)  17.2 us
    all_gather x1, blocking collectives, per_device(): all_first = lax.all_gather(pair_first, 'tile')  16.8 us
    unnamed x33, local copies, waits for them, and re-layouts  12.3 us
  transfers between devices with their start and end apart: 4, of which 2 were waited for; matrix products, arithmetic and copies ran while one was open for 7% of the time, Pallas kernels for 0%

profile of v2, /device:TPU:0, one launch (start us, length us, event | category | flops | bytes accessed | tf_op | source)
XLA Modules:
  0.0 392.1 jit_solution(10754620685707993327)
XLA Ops:
  6.5 4.3 %slice.87 = bf16[4,256,1920]{2,1,0:T(8,128)(2,1)} slice(bf16[4,256,2048]{2,1,0:T(8,128)(2,1)} %param.5), slice={[0:4], [0:256], [128:2048]} | slice | bytes 7864320 | tf_op jit(solution)/shard_map/jit(_roll_static)/slice | solution.py:129
  10.8 6.3 %copy.65 = bf16[4,256,1920]{1,2,0:T(8,128)(2,1)} copy(bf16[4,256,1920]{2,1,0:T(8,128)(2,1)} %slice.87) | data formatting | bytes 7864320
  17.1 0.0 slice-done
  17.1 0.1 copy.66
  17.3 2.4 pad_maximum_fusion.1
  20.0 17.2 %copy.52 = bf16[4,256,2048]{1,0,2:T(4,128)(2,1)} copy(bf16[4,256,2048]{1,2,0:T(8,128)(2,1)S(1)} %fusion.15) | data formatting | bytes 8388608 | tf_op jit(solution)/shard_map/concatenate | solution.py:132
  37.2 7.3 %all-to-all-start = ((bf16[4,256,2048]{1,0,2:T(4,128)(2,1)}), bf16[4,256,2048]{1,0,2:T(4,128)(2,1)}, u32[]{:S(2)}, u32[]{:S(2)}) async-start(bf16[4,256,2048]{1,0,2:T(4,128)(2,1)} %copy.52), calls=%async_computation | async-start | bytes 8388608 | tf_op jit(solution)/shard_map/all_to_all | solution.py:137
  44.5 0.0 all-reduce.2.cloned.1.call-start
  44.5 1.0 fusion.42
  45.6 0.6 fusion.51
  46.2 5.2 %subtract_convert_fusion = (bf16[1024,32,64]{0,2,1:T(8,128)(2,1)}, bf16[1024,32,64]{0,2,1:T(8,128)(2,1)}) fusion(f32[1024,64]{0,1:T(8,128)S(1)} %get-tuple-element.21, f32[1024,32]{0,1:T(8,128)S(1)} %get-tuple-element.20, f32[1024,64]{0,1:T(8,128)S(1)} %get-tuple-element.22, f32[1024,32]{0,1:T(8,128)S(1)} %get-tuple-element.19), kind=kLoop, calls=%fused_computation.9 | loop fusion | flops 18874368 | bytes 9175040 | tf_op jit(solution)/shard_map/convert.3
  51.4 6.5 %copy.55 = bf16[1024,2048]{1,0:T(8,128)(2,1)} copy(bf16[1024,2048]{0,1:T(8,128)(2,1)} %bitcast.102) | data formatting | bytes 8388608 | tf_op jit(solution)/shard_map/sub | solution.py:24
  57.8 6.5 %copy.56 = bf16[1024,2048]{1,0:T(8,128)(2,1)} copy(bf16[1024,2048]{0,1:T(8,128)(2,1)} %bitcast.101) | data formatting | bytes 8388608 | tf_op jit(solution)/shard_map/neg | solution.py:31
  64.3 73.5 %all-to-all-done = bf16[4,256,2048]{1,0,2:T(4,128)(2,1)} async-done(((bf16[4,256,2048]{1,0,2:T(4,128)(2,1)}), bf16[4,256,2048]{1,0,2:T(4,128)(2,1)}, u32[]{:S(2)}, u32[]{:S(2)}) %all-to-all-start) | async-done | bytes 4194336 | tf_op jit(solution)/shard_map/all_to_all | solution.py:137
  137.8 2.7 copy.53
  140.5 2.7 copy.73
  143.2 1.0 copy-done.3
  144.2 11.7 %fusion.4 = f32[4,2048,256]{1,2,0:T(8,128)S(1)} fusion(bf16[4,2048,256]{1,2,0:T(8,128)(2,1)} %bitcast.105, bf16[1024,2048]{1,0:T(8,128)(2,1)} %copy.56, bf16[1024,2048]{1,0:T(8,128)(2,1)S(1)} %copy-done.3), kind=kOutput, calls=%fused_computation.10 | convolution fusion | flops 8606711808 | bytes 20971520 | tf_op jit(solution)/shard_map/fn,snc->sfc/dot_general | solution.py:134
  156.0 3.2 copy-done
  159.2 2.9 fusion.5
  162.1 5.4 %copy.57 = f32[4,1024,256]{2,1,0:T(8,128)} copy(f32[4,1024,256]{1,2,0:T(8,128)} %fusion.5) | data formatting | bytes 8388608 | tf_op jit(solution)/shard_map/add | solution.py:49
  167.5 2.7 bitcast_reduce_fusion
  170.2 2.3 broadcast_in_dim.12
  172.5 5.4 %copy.58 = f32[4,1024,256]{1,2,0:T(8,128)} copy(f32[4,1024,256]{2,1,0:T(8,128)} %bitcast.104) | data formatting | bytes 8388608 | tf_op jit(solution)/shard_map/reshape | solution.py:52
  177.9 7.0 %fusion.3 = bf16[4,2048,256]{1,2,0:T(8,128)(2,1)S(1)} fusion(f32[4,2048,256]{1,2,0:T(8,128)} %copy-done, f32[4,1024,256]{1,2,0:T(8,128)} %copy.58), kind=kLoop, calls=%fused_computation.5 | loop fusion | flops 6291456 | bytes 16777216 | tf_op jit(solution)/shard_map/convert_element_type | solution.py:55
  184.9 0.0 copy-start.1
  184.9 0.0 copy-start.8
  184.9 0.0 copy-start.5
  184.9 0.0 copy-start.6
  184.9 0.0 copy-start.7
  184.9 2.1 fusion.66
  187.0 0.5 copy-done.1
  187.5 1.5 collective-permute-start
  189.0 0.6 collective-permute-start.1
  189.5 0.6 dynamic_slice.13
  191.4 0.0 copy-done.5
  191.4 56.6 %all-gather = s32[2048,1]{0,1:T(1,128)S(1)} all-gather(s32[256,1]{0,1:T(1,128)S(1)} %copy-done.5), channel_id=2, replica_groups=mesh['tile'=8,'win'=4] {'tile'}, dimensions={0}, use_global_device_ids=true | all-gather | bytes 9216 | tf_op jit(solution)/shard_map/all_gather | solution.py:146
  248.0 0.6 broadcast.396
  248.6 0.7 reduce.5
  250.0 0.6 reduce-window.6
  250.6 0.2 slice_reduce_fusion
  250.9 16.8 %all-gather.3 = s32[8,1,256]{2,1,0:T(1,128)S(1)} all-gather(s32[1,1,256]{2,1,0:T(1,128)S(1)} %bitcast.111), channel_id=3, replica_groups=mesh['tile'=8,'win'=4] {'tile'}, dimensions={0}, use_global_device_ids=true | all-gather | bytes 9216 | tf_op jit(solution)/shard_map/all_gather | solution.py:144
  267.7 0.0 copy-done.7
  267.7 18.0 %all-gather.4 = s32[8,1,256]{2,1,0:T(1,128)S(1)} all-gather(s32[1,1,256]{2,1,0:T(1,128)S(1)} %bitcast.112), channel_id=4, replica_groups=mesh['tile'=8,'win'=4] {'tile'}, dimensions={0}, use_global_device_ids=true | all-gather | bytes 9216 | tf_op jit(solution)/shard_map/all_gather | solution.py:145
  285.7 0.1 fusion.59
  285.8 0.2 fusion.58
  286.0 0.0 collective-permute-done
  286.0 0.0 collective-permute-done.1
  286.0 0.0 copy-start.2
  286.0 5.1 %fusion.11 = f32[4,2048,256]{2,1,0:T(8,128)S(1)} fusion(bf16[4,2048,128]{1,2,0:T(8,128)(2,1)} %collective-permute-done.1, bf16[4,2048,256]{1,2,0:T(8,128)(2,1)} %copy-done.1, bf16[4,2048,128]{1,2,0:T(8,128)(2,1)} %collective-permute-done, s32[256]{0:T(256)S(1)} %bitcast.114), kind=kOutput, calls=%fused_computation.23 | convolution fusion | flops 2172780544 | bytes 16778240 | tf_op jit(solution)/shard_map/sfc,cp->sfp/dot_general | solution.py:153
  291.1 0.0 copy-done.2
  291.2 6.2 %fusion.10 = f32[4,2048,256]{2,1,0:T(8,128)} fusion(bf16[4,2048,128]{1,2,0:T(8,128)(2,1)} %collective-permute-done.1, bf16[4,2048,256]{1,2,0:T(8,128)(2,1)S(1)} %copy-done.2, bf16[4,2048,128]{1,2,0:T(8,128)(2,1)} %collective-permute-done, s32[256]{0:T(256)S(1)} %bitcast.113), kind=kOutput, calls=%fused_computation.22 | convolution fusion | flops 2172780544 | bytes 16778240 | tf_op jit(solution)/shard_map/sfc,cp->sfp/dot_general | solution.py:154
  297.4 4.0 %multiply_add_fusion = (f32[4,1024,256]{2,1,0:T(8,128)S(1)}, f32[4,1024,256]{2,1,0:T(8,128)S(1)}) fusion(f32[4,2048,256]{2,1,0:T(8,128)} %fusion.10, f32[4,2048,256]{2,1,0:T(8,128)S(1)} %fusion.11), kind=kLoop, calls=%fused_computation.21 | loop fusion | flops 6291456 | bytes 25165824 | tf_op jit(solution)/shard_map/add | solution.py:64
  301.4 2.0 maximum_reduce_fusion
  303.4 0.0 all-reduce.2.cloned.1.call-update
  303.4 0.5 fusion.53
  304.0 0.6 multiply_subtract_fusion.1
  304.6 1.6 bitcast_multiply_fusion
  306.2 46.0 %all-reduce.2.cloned.1.call-done = f32[2048,256]{1,0:T(8,128)} async-done(((f32[2048,256]{1,0:T(8,128)}), f32[2048,256]{1,0:T(8,128)}) %all-reduce.2.cloned.1.call-update) | async-done | bytes 2097168 | tf_op jit(solution)/shard_map/psum | solution.py:157
  352.2 8.9 %fusion.12 = bf16[512,256]{1,0:T(8,128)(2,1)S(1)} fusion(f32[2048,256]{1,0:T(8,128)} %all-reduce.2.cloned.1.call-done, f32[512,1024]{0,1:T(8,128)S(1)} %get-tuple-element.23, f32[512,1024]{0,1:T(8,128)} %get-tuple-element.24), kind=kOutput, calls=%fused_computation.29 | convolution fusion | flops 3222405120 | bytes 6553600 | tf_op jit(solution)/shard_map/dot_general | solution.py:159
  361.1 0.4 convolution_convert_fusion
  361.5 22.8 %all_to_all.23 = bf16[8,80,512]{2,1,0:T(8,128)(2,1)S(1)} all-to-all(bf16[8,80,512]{2,1,0:T(8,128)(2,1)S(1)} %bitcast.106), channel_id=1, replica_groups=mesh['tile'=8,'win'=4] {'tile'}, dimensions={0} | all-to-all | bytes 1310720 | tf_op jit(solution)/shard_map/all_to_all | solution.py:169
  384.4 0.0 copy-start.4
  384.4 0.8 copy-done.4
  (33 shorter events, 0.5 us)
Async XLA Ops:
  10.8 6.3 %slice-start = ((bf16[4,256,2048]{2,1,0:T(8,128)(2,1)}), bf16[4,256,128]{2,1,0:T(8,128)(2,1)S(1)}, s32[]{:S(2)}) async-start(bf16[4,256,2048]{2,1,0:T(8,128)(2,1)} %param.5), calls=%async_computation.3 | async-start | bytes 524288 | tf_op jit(solution)/shard_map/jit(_roll_static)/slice | solution.py:129
  37.2 100.6 %all-to-all-start = ((bf16[4,256,2048]{1,0,2:T(4,128)(2,1)}), bf16[4,256,2048]{1,0,2:T(4,128)(2,1)}, u32[]{:S(2)}, u32[]{:S(2)}) async-start(bf16[4,256,2048]{1,0,2:T(4,128)(2,1)} %copy.52), calls=%async_computation | async-start | bytes 8388608 | tf_op jit(solution)/shard_map/all_to_all | solution.py:137
  44.5 307.7 %all-reduce.2.cloned.1.call-start = ((), (), s32[]{:S(2)}) async-start(), calls=%async_computation.2 | async-start | bytes 4194304 | tf_op jit(solution)/shard_map/psum | solution.py:157
  140.5 3.7 copy-start.3
  156.0 3.2 copy-start
  184.9 2.6 copy-start.1
  184.9 4.7 %copy-start.8 = (s32[8]{0:T(128)S(1)}, s32[8]{0:T(128)}, u32[]{:S(2)}) copy-start(s32[8]{0:T(128)} %constant.94.clone) | copy-start | bytes 100
  184.9 6.5 %copy-start.5 = (s32[256,1]{0,1:T(1,128)S(1)}, s32[256,1]{0,1:T(1,128)}, u32[]{:S(2)}) copy-start(s32[256,1]{0,1:T(1,128)} %param.8) | copy-start | bytes 3076
  184.9 66.0 %copy-start.6 = (s32[256]{0:T(256)S(1)}, s32[256]{0:T(256)}, u32[]{:S(2)}) copy-start(s32[256]{0:T(256)} %param.6) | copy-start | bytes 3076
  184.9 82.8 %copy-start.7 = (s32[256]{0:T(256)S(1)}, s32[256]{0:T(256)}, u32[]{:S(2)}) copy-start(s32[256]{0:T(256)} %param.7) | copy-start | bytes 3076
  187.5 98.5 %collective-permute-start = (bf16[4,2048,128]{1,2,0:T(8,128)(2,1)}, bf16[4,2048,128]{1,2,0:T(8,128)(2,1)}, u32[]{:S(2)}, u32[]{:S(2)}) collective-permute-start(bf16[4,2048,128]{1,2,0:T(8,128)(2,1)} %get-tuple-element.7), channel_id=1, source_target_pairs={{0,4},{4,12},{12,20},{20,28},{28,24},{24,16},{16,8},{8,0},{1,5},{5... | collective-permute-start | bytes 6291464 | tf_op jit(solution)/shard_map/ppermute | solution.py:141
  189.0 97.1 %collective-permute-start.1 = (bf16[4,2048,128]{1,2,0:T(8,128)(2,1)S(1)}, bf16[4,2048,128]{1,2,0:T(8,128)(2,1)}, u32[]{:S(2)}, u32[]{:S(2)}) collective-permute-start(bf16[4,2048,128]{1,2,0:T(8,128)(2,1)S(1)} %get-tuple-element.8), channel_id=1, source_target_pairs={{0,8},{4,0},{12,4},{20,12},{28,20},{24,28},{16,24},{8,16},{1,9},{5... | collective-permute-start | bytes 6291464 | tf_op jit(solution)/shard_map/ppermute | solution.py:142
  286.0 5.1 %copy-start.2 = (bf16[4,2048,256]{1,2,0:T(8,128)(2,1)S(1)}, bf16[4,2048,256]{1,2,0:T(8,128)(2,1)}, u32[]{:S(2)}) copy-start(bf16[4,2048,256]{1,2,0:T(8,128)(2,1)} %copy-done.1) | copy-start | bytes 12582916
  384.4 0.8 copy-start.4
Sparse Core Ops, SparseCore 0:
  303.6 48.6 all-reduce.1

commit v3 on v2

--- a/solution.py
+++ b/solution.py
@@ -117,36 +117,36 @@
         block_of[device] = place
     to_prev = [(ring[r], ring[(r - 1) % count]) for r in range(count)]
     to_next = [(ring[r], ring[(r + 1) % count]) for r in range(count)]
+    to_owner = [(b, ring[b]) for b in range(count)]
 
     def per_device(records, pair_first, pair_offset, owners):
+        pair_data = jnp.stack([pair_first, pair_offset, owners[:, 0]], axis=0)
         tile_count = lax.axis_size("tile")
         win_count = lax.axis_size("win")
         length = records.shape[1] * tile_count
         seg_total = records.shape[0] * win_count
         block = records.shape[2] // tile_count
         half = block // 2
-        my_block = jnp.asarray(block_of, dtype=jnp.int32)[lax.axis_index("tile")]
-        shifted = jnp.roll(records, -half, axis=2).reshape(
-            records.shape[0], records.shape[1], tile_count, block
-        )
-        outgoing = jnp.concatenate([shifted[:, :, b] for b in block_of], axis=2)
-        forward = forward_matrix(length)
-        spectra = jnp.einsum(
-            "fn,snc->sfc",
-            forward,
-            lax.all_to_all(outgoing, "tile", split_axis=2, concat_axis=1, tiled=True),
-            preferred_element_type=jnp.float32,
-        )
+        pieces = []
+        for b in block_of:
+            low = b * block + half
+            if low + block <= records.shape[2]:
+                pieces.append(records[:, :, low:low + block])
+            else:
+                pieces.append(
+                    jnp.concatenate(
+                        [records[:, :, low:], records[:, :, : low + block - records.shape[2]]], axis=2
+                    )
+                )
+        outgoing = jnp.stack(pieces, axis=0)
+        received = lax.all_to_all(outgoing, "tile", split_axis=0, concat_axis=0, tiled=True)
+        forward = forward_matrix(length).reshape(length, tile_count, records.shape[1])
+        spectra = jnp.einsum("fjm,jsmc->sfc", forward, received, preferred_element_type=jnp.float32)
         whitened = whiten(spectra, BAND)
         from_prev = lax.ppermute(whitened[:, :, half:], "tile", to_next)
         from_next = lax.ppermute(whitened[:, :, :half], "tile", to_prev)
         joined = jnp.concatenate([from_prev, whitened, from_next], axis=2)
-        all_first = lax.all_gather(pair_first, "tile")
-        all_offset = lax.all_gather(pair_offset, "tile")
-        all_owners = lax.all_gather(owners[:, 0], "tile")
-        my_first = lax.dynamic_index_in_dim(all_first, my_block, 0, keepdims=False)
-        my_offset = lax.dynamic_index_in_dim(all_offset, my_block, 0, keepdims=False)
-        my_owners = lax.dynamic_index_in_dim(all_owners, my_block, 0, keepdims=False)
+        my_first, my_offset, my_owners = lax.ppermute(pair_data, "tile", to_owner)
         channel_ids = jnp.arange(joined.shape[2], dtype=jnp.int32)[:, None]
         pick_first = (channel_ids == my_first[None, :]).astype(jnp.bfloat16)
         pick_second = (channel_ids == (my_first + my_offset)[None, :]).astype(jnp.bfloat16)

time: 393 us -> 332 us (0.84)
  blocking collectives: 114 us -> 22.8 us
  waiting for transfers between devices: 119 us -> 167 us
  local copies, waits for them, and re-layouts: 68.7 us -> 53.6 us
    all_gather x3 -> x0, blocking collectives: 91.4 us -> none  [the longest x1 56.6 us: per_device(): all_owners = lax.all_gather(owners[:, 0], 'tile')]
    ppermute x1, waiting for transfers between devices: 0.01 us -> 42.4 us  [per_device(): from_prev = lax.ppermute(whitened[:, :, half:], 'tile', to_next)]
    concatenate x2 -> x0, local copies, waits for them, and re-layouts: 17.2 us -> none  [per_device(): outgoing = jnp.concatenate([shifted[:, :, b] for b in block_of], axis=2)]
    unnamed x33 -> x37, local copies, waits for them, and re-layouts: 12.3 us -> 19.5 us
    all_to_all x2 -> x0, local copies, waits for them, and re-layouts: 5.45 us -> none  [per_device(): lax.all_to_all(outgoing, 'tile', split_axis=2, concat_axis=1, tiled=True)]
  transfers between devices with their start and end apart: 4 -> 5, of which waited for: 2 -> 4; matrix products, arithmetic and copies ran while one was open for 7% -> 7% of each run, Pallas kernels for 0% -> 0%
where the time goes in v3:
time: 332 us; the launch traced here: 331 us
  waiting for transfers between devices  167 us (50%)
  local copies, waits for them, and re-layouts  53.6 us (16%)
  matrix products  33.4 us (10%)
  other arithmetic  30.8 us (9%)
  blocking collectives  22.8 us (7%)
  between operations  13.7 us (4%)
  starting transfers between devices  10.4 us (3%)
    all_to_all x1, waiting for transfers between devices, per_device(): lax.all_to_all(outgoing, 'tile', split_axis=0, concat_axis=0, tiled=True)  73.5 us
    psum x1, waiting for transfers between devices, per_device(): stacked = lax.psum(cross, 'win')  49.4 us
    ppermute x1, waiting for transfers between devices, per_device(): from_prev = lax.ppermute(whitened[:, :, half:], 'tile', to_next)  42.4 us
    all_to_all x1, blocking collectives, per_device(): lax.all_to_all(buckets, 'tile', split_axis=0, concat_axis=0, tiled=True)  22.8 us
    unnamed x37, local copies, waits for them, and re-layouts  19.5 us
    dot_general x1, matrix products, per_device(): jnp.einsum('fjm,jsmc->sfc', forward, received, preferred_element_type=jnp...  12.8 us
    dot_general x1, matrix products, per_device(): correlation = jnp.dot(inverse, stacked, precision=lax.Precision.HIGHEST)  8.89 us
    all_to_all x1, starting transfers between devices, per_device(): lax.all_to_all(outgoing, 'tile', split_axis=0, concat_axis=0, tiled=True)  7.31 us
  transfers between devices with their start and end apart: 5, of which 4 were waited for; matrix products, arithmetic and copies ran while one was open for 7% of the time, Pallas kernels for 0%

profile of v3, /device:TPU:0, one launch (start us, length us, event | category | flops | bytes accessed | tf_op | source)
XLA Modules:
  0.0 331.4 jit_solution(11704587420913861093)
XLA Ops:
  6.5 3.1 fusion.60
  9.6 1.9 fusion.61
  11.5 2.0 copy.53
  13.5 1.9 bitcast_dynamic-update-slice_fusion.6
  15.4 1.0 copy.54
  16.4 1.1 copy.55
  17.6 1.8 copy.56
  19.4 1.0 copy.57
  20.3 0.2 copy.58
  20.6 0.2 copy.59
  20.8 0.2 copy.60
  21.0 0.2 copy.61
  21.2 0.8 bitcast_dynamic-update-slice_fusion.5
  22.0 1.8 fusion.15
  23.8 1.9 bitcast_dynamic-update-slice_fusion.4
  25.7 0.8 bitcast_dynamic-update-slice_fusion.3
  26.5 0.8 bitcast_dynamic-update-slice_fusion.2
  27.4 0.8 bitcast_dynamic-update-slice_fusion.1
  28.2 0.9 bitcast_dynamic-update-slice_fusion
  29.0 7.3 %all-to-all-start = ((bf16[8,4,256,256]{2,3,1,0:T(8,128)(2,1)}), bf16[8,4,256,256]{2,3,1,0:T(8,128)(2,1)}, u32[]{:S(2)}, u32[]{:S(2)}) async-start(bf16[8,4,256,256]{2,3,1,0:T(8,128)(2,1)} %bitcast_dynamic-update-slice_fusion), calls=%async_computation | async-start | bytes 8388608 | tf_op jit(solution)/shard_map/all_to_all | solution.py:142
  36.4 0.2 all-reduce.2.cloned.1.call-start
  36.6 1.0 fusion.35
  37.6 0.6 fusion.44
  38.2 5.0 %subtract_convert_fusion = (bf16[1024,32,64]{0,2,1:T(8,128)(2,1)}, bf16[1024,32,64]{0,2,1:T(8,128)(2,1)}) fusion(f32[1024,64]{0,1:T(8,128)S(1)} %get-tuple-element.31, f32[1024,32]{0,1:T(8,128)S(1)} %get-tuple-element.30, f32[1024,64]{0,1:T(8,128)S(1)} %get-tuple-element.32, f32[1024,32]{0,1:T(8,128)S(1)} %get-tuple-element.29), kind=kLoop, calls=%fused_computation.9 | loop fusion | flops 18874368 | bytes 9175040 | tf_op jit(solution)/shard_map/convert.3
  43.2 6.4 %copy.41 = bf16[1024,8,256]{2,0,1:T(8,128)(2,1)} copy(bf16[1024,8,256]{0,2,1:T(8,128)(2,1)} %bitcast.65) | data formatting | bytes 8388608 | tf_op jit(solution)/shard_map/sub | solution.py:24
  49.7 6.5 %copy.42 = bf16[1024,8,256]{2,0,1:T(8,128)(2,1)} copy(bf16[1024,8,256]{0,2,1:T(8,128)(2,1)} %bitcast.64) | data formatting | bytes 8388608 | tf_op jit(solution)/shard_map/neg | solution.py:31
  56.1 73.5 %all-to-all-done = bf16[8,4,256,256]{2,3,1,0:T(8,128)(2,1)} async-done(((bf16[8,4,256,256]{2,3,1,0:T(8,128)(2,1)}), bf16[8,4,256,256]{2,3,1,0:T(8,128)(2,1)}, u32[]{:S(2)}, u32[]{:S(2)}) %all-to-all-start) | async-done | bytes 4194336 | tf_op jit(solution)/shard_map/all_to_all | solution.py:142
  129.6 12.8 %fusion.4 = f32[4,2048,256]{1,2,0:T(8,128)S(1)} fusion(bf16[8,4,256,256]{2,3,1,0:T(8,128)(2,1)} %all-to-all-done, bf16[1024,8,256]{2,0,1:T(8,128)(2,1)} %copy.42, bf16[1024,8,256]{2,0,1:T(8,128)(2,1)} %copy.41), kind=kOutput, calls=%fused_computation.10 | convolution fusion | flops 8606711808 | bytes 20971520 | tf_op jit(solution)/shard_map/fjm,jsmc->sfc/dot_general | solution.py:144
  142.5 3.2 copy-done
  145.7 2.9 fusion.5
  148.6 5.4 %copy.44 = f32[4,1024,256]{2,1,0:T(8,128)} copy(f32[4,1024,256]{1,2,0:T(8,128)} %fusion.5) | data formatting | bytes 8388608 | tf_op jit(solution)/shard_map/add | solution.py:49
  154.0 2.7 bitcast_reduce_fusion
  156.8 2.3 broadcast_in_dim.12
  159.0 5.4 %copy.45 = f32[4,1024,256]{1,2,0:T(8,128)} copy(f32[4,1024,256]{2,1,0:T(8,128)} %bitcast.66) | data formatting | bytes 8388608 | tf_op jit(solution)/shard_map/reshape | solution.py:52
  164.4 7.0 %fusion.3 = bf16[4,2048,256]{1,2,0:T(8,128)(2,1)S(1)} fusion(f32[4,2048,256]{1,2,0:T(8,128)} %copy-done, f32[4,1024,256]{1,2,0:T(8,128)} %copy.45), kind=kLoop, calls=%fused_computation.5 | loop fusion | flops 6291456 | bytes 16777216 | tf_op jit(solution)/shard_map/convert_element_type | solution.py:55
  171.4 0.0 copy-start.5
  171.4 0.0 copy-start.6
  171.4 0.0 copy-start.7
  171.4 2.1 fusion.59
  173.5 0.5 copy-done.1
  174.0 1.5 collective-permute-start.1
  175.5 0.6 collective-permute-start.2
  176.1 0.9 collective-permute-start
  177.0 0.2 fusion.51
  177.2 0.0 collective-permute-done
  177.2 0.6 reduce-window.6
  177.8 0.2 slice_reduce_fusion
  178.1 0.1 fusion.52
  178.2 42.4 %collective-permute-done.1 = bf16[4,2048,128]{1,2,0:T(8,128)(2,1)} collective-permute-done((bf16[4,2048,128]{1,2,0:T(8,128)(2,1)}, bf16[4,2048,128]{1,2,0:T(8,128)(2,1)}, u32[]{:S(2)}, u32[]{:S(2)}) %collective-permute-start.1) | collective-permute-done | bytes 2097184 | tf_op jit(solution)/shard_map/ppermute | solution.py:146
  220.6 1.3 collective-permute-done.2
  222.0 5.1 %fusion.11 = f32[4,2048,256]{2,1,0:T(8,128)S(1)} fusion(bf16[4,2048,128]{1,2,0:T(8,128)(2,1)} %collective-permute-done.2, bf16[4,2048,256]{1,2,0:T(8,128)(2,1)} %copy-done.1, bf16[4,2048,128]{1,2,0:T(8,128)(2,1)} %collective-permute-done.1, s32[256]{0:T(256)S(1)} %bitcast.76), kind=kOutput, calls=%fused_computation.22 | convolution fusion | flops 2172780544 | bytes 16778240 | tf_op jit(solution)/shard_map/sfc,cp->sfp/dot_general | solution.py:153
  227.1 6.3 %fusion.10 = f32[4,2048,256]{2,1,0:T(8,128)} fusion(bf16[4,2048,128]{1,2,0:T(8,128)(2,1)} %collective-permute-done.2, bf16[4,2048,256]{1,2,0:T(8,128)(2,1)S(1)} %copy-done.2, bf16[4,2048,128]{1,2,0:T(8,128)(2,1)} %collective-permute-done.1, s32[256]{0:T(256)S(1)} %bitcast.75), kind=kOutput, calls=%fused_computation.21 | convolution fusion | flops 2172780544 | bytes 16778240 | tf_op jit(solution)/shard_map/sfc,cp->sfp/dot_general | solution.py:154
  233.4 4.0 %multiply_add_fusion = (f32[4,1024,256]{2,1,0:T(8,128)S(1)}, f32[4,1024,256]{2,1,0:T(8,128)S(1)}) fusion(f32[4,2048,256]{2,1,0:T(8,128)} %fusion.10, f32[4,2048,256]{2,1,0:T(8,128)S(1)} %fusion.11), kind=kLoop, calls=%fused_computation.20 | loop fusion | flops 6291456 | bytes 25165824 | tf_op jit(solution)/shard_map/add | solution.py:64
  237.4 2.0 maximum_reduce_fusion
  239.4 0.0 all-reduce.2.cloned.1.call-update
  239.4 0.5 fusion.46
  239.9 0.6 multiply_subtract_fusion.1
  240.5 1.7 bitcast_multiply_fusion
  242.2 49.4 %all-reduce.2.cloned.1.call-done = f32[2048,256]{1,0:T(8,128)} async-done(((f32[2048,256]{1,0:T(8,128)}), f32[2048,256]{1,0:T(8,128)}) %all-reduce.2.cloned.1.call-update) | async-done | bytes 2097168 | tf_op jit(solution)/shard_map/psum | solution.py:157
  291.6 8.9 %fusion.12 = bf16[512,256]{1,0:T(8,128)(2,1)S(1)} fusion(f32[2048,256]{1,0:T(8,128)} %all-reduce.2.cloned.1.call-done, f32[512,1024]{0,1:T(8,128)S(1)} %get-tuple-element.33, f32[512,1024]{0,1:T(8,128)} %get-tuple-element.34), kind=kOutput, calls=%fused_computation.28 | convolution fusion | flops 3222405120 | bytes 6553600 | tf_op jit(solution)/shard_map/dot_general | solution.py:159
  300.5 0.4 convolution_convert_fusion
  300.8 22.8 %all_to_all.10 = bf16[8,80,512]{2,1,0:T(8,128)(2,1)S(1)} all-to-all(bf16[8,80,512]{2,1,0:T(8,128)(2,1)S(1)} %bitcast.67), channel_id=1, replica_groups=mesh['tile'=8,'win'=4] {'tile'}, dimensions={0} | all-to-all | bytes 1310720 | tf_op jit(solution)/shard_map/all_to_all | solution.py:169
  323.7 0.0 copy-start.4
  323.8 0.8 copy-done.4
  (28 shorter events, 0.2 us)
Async XLA Ops:
  16.4 4.8 %copy-start.3 = (bf16[4,256,256]{1,2,0:T(8,128)(2,1)S(1)}, bf16[4,256,256]{1,2,0:T(8,128)(2,1)}, u32[]{:S(2)}) copy-start(bf16[4,256,256]{1,2,0:T(8,128)(2,1)} %copy.54) | copy-start | bytes 1572868
  29.0 100.6 %all-to-all-start = ((bf16[8,4,256,256]{2,3,1,0:T(8,128)(2,1)}), bf16[8,4,256,256]{2,3,1,0:T(8,128)(2,1)}, u32[]{:S(2)}, u32[]{:S(2)}) async-start(bf16[8,4,256,256]{2,3,1,0:T(8,128)(2,1)} %bitcast_dynamic-update-slice_fusion), calls=%async_computation | async-start | bytes 8388608 | tf_op jit(solution)/shard_map/all_to_all | solution.py:142
  36.4 255.2 %all-reduce.2.cloned.1.call-start = ((), (), s32[]{:S(2)}) async-start(), calls=%async_computation.2 | async-start | bytes 4194304 | tf_op jit(solution)/shard_map/psum | solution.py:157
  142.4 3.2 copy-start
  171.4 2.6 copy-start.1
  171.4 4.6 %copy-start.5 = (s32[256,1]{0,1:T(1,128)S(1)}, s32[256,1]{0,1:T(1,128)}, u32[]{:S(2)}) copy-start(s32[256,1]{0,1:T(1,128)} %param.7) | copy-start | bytes 3076
  171.4 4.6 %copy-start.6 = (s32[256]{0:T(256)S(1)}, s32[256]{0:T(256)}, u32[]{:S(2)}) copy-start(s32[256]{0:T(256)} %param.6) | copy-start | bytes 3076
  171.4 4.6 %copy-start.7 = (s32[256]{0:T(256)S(1)}, s32[256]{0:T(256)}, u32[]{:S(2)}) copy-start(s32[256]{0:T(256)} %param.5) | copy-start | bytes 3076
  174.0 46.6 %collective-permute-start.1 = (bf16[4,2048,128]{1,2,0:T(8,128)(2,1)}, bf16[4,2048,128]{1,2,0:T(8,128)(2,1)}, u32[]{:S(2)}, u32[]{:S(2)}) collective-permute-start(bf16[4,2048,128]{1,2,0:T(8,128)(2,1)} %get-tuple-element.7), channel_id=1, source_target_pairs={{0,4},{4,12},{12,20},{20,28},{28,24},{24,16},{16,8},{8,0},{1,5},{5... | collective-permute-start | bytes 6291464 | tf_op jit(solution)/shard_map/ppermute | solution.py:146
  175.5 46.5 %collective-permute-start.2 = (bf16[4,2048,128]{1,2,0:T(8,128)(2,1)S(1)}, bf16[4,2048,128]{1,2,0:T(8,128)(2,1)}, u32[]{:S(2)}, u32[]{:S(2)}) collective-permute-start(bf16[4,2048,128]{1,2,0:T(8,128)(2,1)S(1)} %get-tuple-element.8), channel_id=1, source_target_pairs={{0,8},{4,0},{12,4},{20,12},{28,20},{24,28},{16,24},{8,16},{1,9},{5... | collective-permute-start | bytes 6291464 | tf_op jit(solution)/shard_map/ppermute | solution.py:147
  176.1 1.1 collective-permute-start
  222.0 5.1 %copy-start.2 = (bf16[4,2048,256]{1,2,0:T(8,128)(2,1)S(1)}, bf16[4,2048,256]{1,2,0:T(8,128)(2,1)}, u32[]{:S(2)}) copy-start(bf16[4,2048,256]{1,2,0:T(8,128)(2,1)} %copy-done.1) | copy-start | bytes 12582916
  323.7 0.8 copy-start.4
Sparse Core Ops, SparseCore 0:
  239.5 52.0 all-reduce.1

commit v4 on v3

--- a/solution.py
+++ b/solution.py
@@ -127,32 +127,36 @@
         seg_total = records.shape[0] * win_count
         block = records.shape[2] // tile_count
         half = block // 2
-        pieces = []
-        for b in block_of:
-            low = b * block + half
-            if low + block <= records.shape[2]:
-                pieces.append(records[:, :, low:low + block])
-            else:
-                pieces.append(
-                    jnp.concatenate(
-                        [records[:, :, low:], records[:, :, : low + block - records.shape[2]]], axis=2
-                    )
-                )
-        outgoing = jnp.stack(pieces, axis=0)
-        received = lax.all_to_all(outgoing, "tile", split_axis=0, concat_axis=0, tiled=True)
         forward = forward_matrix(length).reshape(length, tile_count, records.shape[1])
-        spectra = jnp.einsum("fjm,jsmc->sfc", forward, received, preferred_element_type=jnp.float32)
-        whitened = whiten(spectra, BAND)
-        from_prev = lax.ppermute(whitened[:, :, half:], "tile", to_next)
-        from_next = lax.ppermute(whitened[:, :, :half], "tile", to_prev)
-        joined = jnp.concatenate([from_prev, whitened, from_next], axis=2)
         my_first, my_offset, my_owners = lax.ppermute(pair_data, "tile", to_owner)
-        channel_ids = jnp.arange(joined.shape[2], dtype=jnp.int32)[:, None]
+        channel_ids = jnp.arange(2 * block, dtype=jnp.int32)[:, None]
         pick_first = (channel_ids == my_first[None, :]).astype(jnp.bfloat16)
         pick_second = (channel_ids == (my_first + my_offset)[None, :]).astype(jnp.bfloat16)
-        first_part = jnp.einsum("sfc,cp->sfp", joined, pick_first, preferred_element_type=jnp.float32)
-        second_part = jnp.einsum("sfc,cp->sfp", joined, pick_second, preferred_element_type=jnp.float32)
-        cross = jnp.sum(cross_terms(first_part, second_part), axis=0)
+        cross = None
+        for segment in range(records.shape[0]):
+            pieces = []
+            for b in block_of:
+                low = b * block + half
+                if low + block <= records.shape[2]:
+                    pieces.append(records[segment, :, low:low + block])
+                else:
+                    pieces.append(
+                        jnp.concatenate(
+                            [records[segment, :, low:], records[segment, :, : low + block - records.shape[2]]],
+                            axis=1,
+                        )
+                    )
+            outgoing = jnp.stack(pieces, axis=0)
+            received = lax.all_to_all(outgoing, "tile", split_axis=0, concat_axis=0, tiled=True)
+            spectra = jnp.einsum("fjm,jmc->fc", forward, received, preferred_element_type=jnp.float32)
+            whitened = whiten(spectra, BAND)
+            from_prev = lax.ppermute(whitened[:, half:], "tile", to_next)
+            from_next = lax.ppermute(whitened[:, :half], "tile", to_prev)
+            joined = jnp.concatenate([from_prev, whitened, from_next], axis=1)
+            first_part = jnp.dot(joined, pick_first, preferred_element_type=jnp.float32)
+            second_part = jnp.dot(joined, pick_second, preferred_element_type=jnp.float32)
+            term = cross_terms(first_part, second_part)
+            cross = term if cross is None else cross + term
         lag_count = length // win_count
         stacked = lax.psum(cross, "win")
         inverse = inverse_matrix(length, lax.axis_index("win") * lag_count, lag_count, seg_total)

time: 332 us -> 276 us (0.83)
  waiting for transfers between devices: 167 us -> 118 us
  local copies, waits for them, and re-layouts: 53.6 us -> 29 us
  starting transfers between devices: 10.4 us -> 27.8 us
  other arithmetic: 30.8 us -> 16.9 us
  matrix products: 33.4 us -> 46.4 us
    ppermute x2 -> x8, waiting for transfers between devices: 43.8 us -> 7.76 us  [the longest x4 7.75 us: per_device(): from_next = lax.ppermute(whitened[:, :half], 'tile', to_prev)]
    dot_general x3 -> x12, matrix products: 24.2 us -> 37.1 us  [the longest x4 24.2 us: per_device(): jnp.einsum('fjm,jmc->fc', forward, received, preferred_element_type=jnp.f...]
    all_to_all x1 -> x4, waiting for transfers between devices: 73.5 us -> 61.1 us  [per_device(): lax.all_to_all(outgoing, 'tile', split_axis=0, concat_axis=0, tiled=True)]
    all_to_all x1 -> x4, starting transfers between devices: 7.31 us -> 18.9 us  [per_device(): lax.all_to_all(outgoing, 'tile', split_axis=0, concat_axis=0, tiled=True)]
    unnamed x37 -> x26, local copies, waits for them, and re-layouts: 19.5 us -> 10.3 us
    ppermute x2 -> x8, starting transfers between devices: 2.03 us -> 8.02 us  [the longest x4 7.61 us: per_device(): from_prev = lax.ppermute(whitened[:, half:], 'tile', to_next)]
    convert_element_type x1 -> x4, other arithmetic: 6.96 us -> 1.22 us  [whiten(): (spectra * jnp.concatenate([inverse_rms, inverse_rms], axis=-2)).astype(j...]
    add x1 -> x0, local copies, waits for them, and re-layouts: 5.39 us -> none  [whiten(): energy = real_rows * real_rows + imaginary * imaginary]
  transfers between devices with their start and end apart: 5 -> 14, of which waited for: 4 -> 7; matrix products, arithmetic and copies ran while one was open for 7% -> 24% of each run, Pallas kernels for 0% -> 0%
where the time goes in v4:
time: 276 us; the launch traced here: 275 us
  waiting for transfers between devices  118 us (43%)
  matrix products  46.4 us (17%)
  local copies, waits for them, and re-layouts  29 us (11%)
  starting transfers between devices  27.8 us (10%)
  blocking collectives  22.8 us (8%)
  other arithmetic  16.9 us (6%)
  between operations  13.9 us (5%)
    all_to_all x4, waiting for transfers between devices, per_device(): lax.all_to_all(outgoing, 'tile', split_axis=0, concat_axis=0, tiled=True)  61.1 us
    psum x1, waiting for transfers between devices, per_device(): stacked = lax.psum(cross, 'win')  49.1 us
    dot_general x4, matrix products, per_device(): jnp.einsum('fjm,jmc->fc', forward, received, preferred_element_type=jnp.f...  24.2 us
    all_to_all x1, blocking collectives, per_device(): lax.all_to_all(buckets, 'tile', split_axis=0, concat_axis=0, tiled=True)  22.8 us
    all_to_all x4, starting transfers between devices, per_device(): lax.all_to_all(outgoing, 'tile', split_axis=0, concat_axis=0, tiled=True)  18.9 us
    unnamed x26, local copies, waits for them, and re-layouts  10.3 us
    dot_general x1, matrix products, per_device(): correlation = jnp.dot(inverse, stacked, precision=lax.Precision.HIGHEST)  8.89 us
    ppermute x4, waiting for transfers between devices, per_device(): from_next = lax.ppermute(whitened[:, :half], 'tile', to_prev)  7.75 us
  transfers between devices with their start and end apart: 14, of which 7 were waited for; matrix products, arithmetic and copies ran while one was open for 24% of the time, Pallas kernels for 0%

profile of v4, /device:TPU:0, one launch (start us, length us, event | category | flops | bytes accessed | tf_op | source)
XLA Modules:
  0.0 274.7 jit_solution(15856081048291361738)
XLA Ops:
  6.5 2.1 slice_dynamic-update-slice_fusion.7
  8.6 1.1 slice_bitcast_fusion.1
  9.7 1.9 slice_dynamic-update-slice_fusion.6
  11.7 0.7 fusion.46
  12.4 0.7 fusion.48
  13.1 0.8 slice_dynamic-update-slice_fusion.5
  14.0 0.8 slice_dynamic-update-slice_fusion.4
  14.8 0.8 slice_dynamic-update-slice_fusion.3
  15.6 0.9 slice_dynamic-update-slice_fusion.2
  16.5 0.9 slice_dynamic-update-slice_fusion.1
  17.4 7.3 %all-to-all-start.3 = ((bf16[8,256,256]{2,1,0:T(8,128)(2,1)}), bf16[8,256,256]{2,1,0:T(8,128)(2,1)S(1)}, u32[]{:S(2)}, u32[]{:S(2)}) async-start(bf16[8,256,256]{2,1,0:T(8,128)(2,1)} %get-tuple-element.7), calls=%async_computation.3 | async-start | bytes 2097152 | tf_op jit(solution)/shard_map/all_to_all | solution.py:150
  24.7 0.7 collective-permute-start
  25.4 1.0 fusion.50
  26.7 0.6 fusion.59
  27.3 5.1 %subtract_convert_fusion = (bf16[1024,32,64]{0,2,1:T(8,128)(2,1)}, bf16[1024,32,64]{0,2,1:T(8,128)(2,1)}) fusion(f32[1024,64]{0,1:T(8,128)S(1)} %get-tuple-element.74, f32[1024,32]{0,1:T(8,128)S(1)} %get-tuple-element.69, f32[1024,64]{0,1:T(8,128)S(1)} %get-tuple-element.75, f32[1024,32]{0,1:T(8,128)S(1)} %get-tuple-element.68), kind=kLoop, calls=%fused_computation.2 | loop fusion | flops 18874368 | bytes 9175040 | tf_op jit(solution)/shard_map/convert.3
  32.3 6.4 %copy.5 = bf16[1024,8,256]{2,0,1:T(8,128)(2,1)} copy(bf16[1024,8,256]{0,2,1:T(8,128)(2,1)} %bitcast.82) | data formatting | bytes 8388608 | tf_op jit(solution)/shard_map/sub | solution.py:24
  38.8 6.5 %copy.6 = bf16[1024,8,256]{2,0,1:T(8,128)(2,1)} copy(bf16[1024,8,256]{0,2,1:T(8,128)(2,1)} %bitcast.81) | data formatting | bytes 8388608 | tf_op jit(solution)/shard_map/neg | solution.py:31
  45.3 0.6 reduce-window.6
  46.2 4.2 %all-to-all-done.3 = bf16[8,256,256]{2,1,0:T(8,128)(2,1)S(1)} async-done(((bf16[8,256,256]{2,1,0:T(8,128)(2,1)}), bf16[8,256,256]{2,1,0:T(8,128)(2,1)S(1)}, u32[]{:S(2)}, u32[]{:S(2)}) %all-to-all-start.3) | async-done | bytes 1048608 | tf_op jit(solution)/shard_map/all_to_all | solution.py:150
  50.4 3.8 %all-to-all-start.2 = ((bf16[8,256,256]{2,1,0:T(8,128)(2,1)}), bf16[8,256,256]{2,1,0:T(8,128)(2,1)S(1)}, u32[]{:S(2)}, u32[]{:S(2)}) async-start(bf16[8,256,256]{2,1,0:T(8,128)(2,1)} %get-tuple-element.8), calls=%async_computation.2 | async-start | bytes 2097152 | tf_op jit(solution)/shard_map/all_to_all | solution.py:150
  54.2 5.9 %convolution_bitcast_fusion = f32[2048,256]{1,0:T(8,128)S(1)} fusion(bf16[8,256,256]{2,1,0:T(8,128)(2,1)S(1)} %all-to-all-done.3, bf16[1024,8,256]{2,0,1:T(8,128)(2,1)} %copy.6, bf16[1024,8,256]{2,0,1:T(8,128)(2,1)} %copy.5), kind=kOutput, calls=%fused_computation.7 | convolution fusion | flops 2164260864 | bytes 11534336 | tf_op jit(solution)/shard_map/fjm,jmc->fc/dot_general | solution.py:151
  60.4 0.3 fusion.9
  60.8 1.1 fusion.79
  61.8 2.0 collective-permute-start.7
  63.8 17.6 %all-to-all-done.2 = bf16[8,256,256]{2,1,0:T(8,128)(2,1)S(1)} async-done(((bf16[8,256,256]{2,1,0:T(8,128)(2,1)}), bf16[8,256,256]{2,1,0:T(8,128)(2,1)S(1)}, u32[]{:S(2)}, u32[]{:S(2)}) %all-to-all-start.2) | async-done | bytes 1048608 | tf_op jit(solution)/shard_map/all_to_all | solution.py:150
  81.4 1.1 copy-done.1
  82.5 3.6 %all-to-all-start.1 = ((bf16[8,256,256]{2,1,0:T(8,128)(2,1)}), bf16[8,256,256]{2,1,0:T(8,128)(2,1)S(1)}, u32[]{:S(2)}, u32[]{:S(2)}) async-start(bf16[8,256,256]{2,1,0:T(8,128)(2,1)} %get-tuple-element.9), calls=%async_computation.1 | async-start | bytes 2097152 | tf_op jit(solution)/shard_map/all_to_all | solution.py:150
  86.0 6.1 %convolution_bitcast_fusion.1 = f32[2048,256]{1,0:T(8,128)S(1)} fusion(bf16[8,256,256]{2,1,0:T(8,128)(2,1)} %copy-done.1, bf16[1024,8,256]{2,0,1:T(8,128)(2,1)} %copy.6, bf16[1024,8,256]{2,0,1:T(8,128)(2,1)} %copy.5), kind=kOutput, calls=%fused_computation.8 | convolution fusion | flops 2164260864 | bytes 11534336 | tf_op jit(solution)/shard_map/fjm,jmc->fc/dot_general | solution.py:151
  92.5 0.3 fusion.8
  92.8 1.1 fusion.80
  93.9 1.9 collective-permute-start.5
  95.9 19.3 %all-to-all-done.1 = bf16[8,256,256]{2,1,0:T(8,128)(2,1)S(1)} async-done(((bf16[8,256,256]{2,1,0:T(8,128)(2,1)}), bf16[8,256,256]{2,1,0:T(8,128)(2,1)S(1)}, u32[]{:S(2)}, u32[]{:S(2)}) %all-to-all-start.1) | async-done | bytes 1048608 | tf_op jit(solution)/shard_map/all_to_all | solution.py:150
  115.1 4.2 %all-to-all-start = ((bf16[8,256,256]{2,1,0:T(8,128)(2,1)}), bf16[8,256,256]{2,1,0:T(8,128)(2,1)}, u32[]{:S(2)}, u32[]{:S(2)}) async-start(bf16[8,256,256]{2,1,0:T(8,128)(2,1)} %get-tuple-element.10), calls=%async_computation | async-start | bytes 2097152 | tf_op jit(solution)/shard_map/all_to_all | solution.py:150
  119.6 5.9 %convolution_bitcast_fusion.2 = f32[2048,256]{1,0:T(8,128)S(1)} fusion(bf16[8,256,256]{2,1,0:T(8,128)(2,1)S(1)} %all-to-all-done.1, bf16[1024,8,256]{2,0,1:T(8,128)(2,1)} %copy.6, bf16[1024,8,256]{2,0,1:T(8,128)(2,1)} %copy.5), kind=kOutput, calls=%fused_computation.9 | convolution fusion | flops 2164260864 | bytes 11534336 | tf_op jit(solution)/shard_map/fjm,jmc->fc/dot_general | solution.py:151
  125.9 0.3 fusion.7
  126.2 1.1 fusion.81
  127.2 1.7 collective-permute-start.3
  128.9 20.1 %all-to-all-done = bf16[8,256,256]{2,1,0:T(8,128)(2,1)} async-done(((bf16[8,256,256]{2,1,0:T(8,128)(2,1)}), bf16[8,256,256]{2,1,0:T(8,128)(2,1)}, u32[]{:S(2)}, u32[]{:S(2)}) %all-to-all-start) | async-done | bytes 1048608 | tf_op jit(solution)/shard_map/all_to_all | solution.py:150
  149.0 6.1 %convolution_bitcast_fusion.3 = f32[2048,256]{1,0:T(8,128)S(1)} fusion(bf16[8,256,256]{2,1,0:T(8,128)(2,1)} %all-to-all-done, bf16[1024,8,256]{2,0,1:T(8,128)(2,1)} %copy.6, bf16[1024,8,256]{2,0,1:T(8,128)(2,1)} %copy.5), kind=kOutput, calls=%fused_computation.10 | convolution fusion | flops 2164260864 | bytes 11534336 | tf_op jit(solution)/shard_map/fjm,jmc->fc/dot_general | solution.py:151
  155.4 0.3 fusion.4
  155.8 0.9 copy-done.2
  156.8 2.0 collective-permute-start.1
  158.8 2.0 fusion.18
  160.8 2.0 fusion.17
  162.8 0.3 multiply_add_fusion.1
  163.0 0.3 collective-permute-start.2
  163.3 2.0 fusion.20
  165.3 2.0 fusion.19
  167.3 0.3 multiply_add_fusion.2
  167.6 4.0 %collective-permute-done.4 = bf16[2048,128]{1,0:T(8,128)(2,1)S(1)} collective-permute-done((bf16[2048,128]{1,0:T(8,128)(2,1)S(1)}, bf16[2048,128]{1,0:T(8,128)(2,1)S(1)}, u32[]{:S(2)}, u32[]{:S(2)}) %collective-permute-start.4) | collective-permute-done | bytes 524320 | tf_op jit(solution)/shard_map/ppermute | solution.py:154
  171.6 1.8 fusion.22
  173.4 1.8 fusion.21
  175.5 3.7 %collective-permute-done.2 = bf16[2048,128]{1,0:T(8,128)(2,1)S(1)} collective-permute-done((bf16[2048,128]{1,0:T(8,128)(2,1)S(1)}, bf16[2048,128]{1,0:T(8,128)(2,1)S(1)}, u32[]{:S(2)}, u32[]{:S(2)}) %collective-permute-start.2) | collective-permute-done | bytes 524320 | tf_op jit(solution)/shard_map/ppermute | solution.py:154
  179.2 0.8 fusion.24
  180.0 0.8 fusion.23
  181.1 1.8 fusion.6
  182.9 0.5 fusion.61
  183.5 0.6 multiply_subtract_fusion
  184.1 1.7 bitcast_multiply_fusion
  185.8 49.1 %all-reduce.2.cloned.1.call-done = f32[2048,256]{1,0:T(8,128)} async-done(((f32[2048,256]{1,0:T(8,128)}), f32[2048,256]{1,0:T(8,128)}) %all-reduce.2.cloned.1.call-update) | async-done | bytes 2097168 | tf_op jit(solution)/shard_map/psum | solution.py:161
  234.8 8.9 %fusion.10 = bf16[512,256]{1,0:T(8,128)(2,1)S(1)} fusion(f32[2048,256]{1,0:T(8,128)} %all-reduce.2.cloned.1.call-done, f32[512,1024]{0,1:T(8,128)S(1)} %get-tuple-element.76, f32[512,1024]{0,1:T(8,128)} %get-tuple-element.77), kind=kOutput, calls=%fused_computation.31 | convolution fusion | flops 3222405120 | bytes 6553600 | tf_op jit(solution)/shard_map/dot_general | solution.py:163
  243.7 0.4 convolution_convert_fusion
  244.1 22.8 %all_to_all.25 = bf16[8,80,512]{2,1,0:T(8,128)(2,1)S(1)} all-to-all(bf16[8,80,512]{2,1,0:T(8,128)(2,1)S(1)} %bitcast.87), channel_id=1, replica_groups=mesh['tile'=8,'win'=4] {'tile'}, dimensions={0} | all-to-all | bytes 1310720 | tf_op jit(solution)/shard_map/all_to_all | solution.py:173
  267.0 0.8 copy-done.3
  (59 shorter events, 2.8 us)
Async XLA Ops:
  6.5 6.6 %copy-start = (bf16[4,256,2048]{2,1,0:T(8,128)(2,1)S(1)}, bf16[4,256,2048]{2,1,0:T(8,128)(2,1)}, u32[]{:S(2)}) copy-start(bf16[4,256,2048]{2,1,0:T(8,128)(2,1)} %param.4) | copy-start | bytes 12582916
  15.6 9.0 %copy-start.4 = (s32[256,1]{0,1:T(1,128)S(1)}, s32[256,1]{0,1:T(1,128)}, u32[]{:S(2)}) copy-start(s32[256,1]{0,1:T(1,128)} %param.7) | copy-start | bytes 3076
  15.6 9.0 %copy-start.5 = (s32[256]{0:T(256)S(1)}, s32[256]{0:T(256)}, u32[]{:S(2)}) copy-start(s32[256]{0:T(256)} %param.6) | copy-start | bytes 3076
  15.6 9.1 %copy-start.6 = (s32[256]{0:T(256)S(1)}, s32[256]{0:T(256)}, u32[]{:S(2)}) copy-start(s32[256]{0:T(256)} %param.5) | copy-start | bytes 3076
  17.4 33.1 %all-to-all-start.3 = ((bf16[8,256,256]{2,1,0:T(8,128)(2,1)}), bf16[8,256,256]{2,1,0:T(8,128)(2,1)S(1)}, u32[]{:S(2)}, u32[]{:S(2)}) async-start(bf16[8,256,256]{2,1,0:T(8,128)(2,1)} %get-tuple-element.7), calls=%async_computation.3 | async-start | bytes 2097152 | tf_op jit(solution)/shard_map/all_to_all | solution.py:150
  24.7 20.6 %collective-permute-start = (s32[3,256]{1,0:T(4,128)S(1)}, s32[3,256]{1,0:T(4,128)S(1)}, u32[]{:S(2)}, u32[]{:S(2)}) collective-permute-start(s32[3,256]{1,0:T(4,128)S(1)} %pad_add_fusion), channel_id=1, source_target_pairs={{0,0},{4,4},{8,12},{12,20},{16,28},{20,24},{24,16},{28,8},{1,1},{5... | collective-permute-start | bytes 9224 | tf_op jit(solution)/shard_map/ppermute | solution.py:131
  50.4 30.9 %all-to-all-start.2 = ((bf16[8,256,256]{2,1,0:T(8,128)(2,1)}), bf16[8,256,256]{2,1,0:T(8,128)(2,1)S(1)}, u32[]{:S(2)}, u32[]{:S(2)}) async-start(bf16[8,256,256]{2,1,0:T(8,128)(2,1)} %get-tuple-element.8), calls=%async_computation.2 | async-start | bytes 2097152 | tf_op jit(solution)/shard_map/all_to_all | solution.py:150
  61.8 94.0 %collective-permute-start.7 = (bf16[2048,128]{1,0:T(8,128)(2,1)}, bf16[2048,128]{1,0:T(8,128)(2,1)}, u32[]{:S(2)}, u32[]{:S(2)}) collective-permute-start(bf16[2048,128]{1,0:T(8,128)(2,1)} %get-tuple-element.49), channel_id=1, source_target_pairs={{0,4},{4,12},{12,20},{20,28},{28,24},{24,16},{16,8},{8,0},{1,5},{5... | collective-permute-start | bytes 1572872 | tf_op jit(solution)/shard_map/ppermute | solution.py:153
  63.8 93.0 %collective-permute-start.8 = (bf16[2048,128]{1,0:T(8,128)(2,1)}, bf16[2048,128]{1,0:T(8,128)(2,1)}, u32[]{:S(2)}, u32[]{:S(2)}) collective-permute-start(bf16[2048,128]{1,0:T(8,128)(2,1)} %get-tuple-element.50), channel_id=1, source_target_pairs={{0,8},{4,0},{12,4},{20,12},{28,20},{24,28},{16,24},{8,16},{1,9},{5... | collective-permute-start | bytes 1572872 | tf_op jit(solution)/shard_map/ppermute | solution.py:154
  81.4 1.1 copy-start.1
  82.5 32.7 %all-to-all-start.1 = ((bf16[8,256,256]{2,1,0:T(8,128)(2,1)}), bf16[8,256,256]{2,1,0:T(8,128)(2,1)S(1)}, u32[]{:S(2)}, u32[]{:S(2)}) async-start(bf16[8,256,256]{2,1,0:T(8,128)(2,1)} %get-tuple-element.9), calls=%async_computation.1 | async-start | bytes 2097152 | tf_op jit(solution)/shard_map/all_to_all | solution.py:150
  93.9 69.2 %collective-permute-start.5 = (bf16[2048,128]{1,0:T(8,128)(2,1)}, bf16[2048,128]{1,0:T(8,128)(2,1)}, u32[]{:S(2)}, u32[]{:S(2)}) collective-permute-start(bf16[2048,128]{1,0:T(8,128)(2,1)} %get-tuple-element.51), channel_id=1, source_target_pairs={{0,4},{4,12},{12,20},{20,28},{28,24},{24,16},{16,8},{8,0},{1,5},{5... | collective-permute-start | bytes 1572872 | tf_op jit(solution)/shard_map/ppermute | solution.py:153
  95.8 67.6 %collective-permute-start.6 = (bf16[2048,128]{1,0:T(8,128)(2,1)}, bf16[2048,128]{1,0:T(8,128)(2,1)}, u32[]{:S(2)}, u32[]{:S(2)}) collective-permute-start(bf16[2048,128]{1,0:T(8,128)(2,1)} %get-tuple-element.52), channel_id=1, source_target_pairs={{0,8},{4,0},{12,4},{20,12},{28,20},{24,28},{16,24},{8,16},{1,9},{5... | collective-permute-start | bytes 1572872 | tf_op jit(solution)/shard_map/ppermute | solution.py:154
  115.1 33.9 %all-to-all-start = ((bf16[8,256,256]{2,1,0:T(8,128)(2,1)}), bf16[8,256,256]{2,1,0:T(8,128)(2,1)}, u32[]{:S(2)}, u32[]{:S(2)}) async-start(bf16[8,256,256]{2,1,0:T(8,128)(2,1)} %get-tuple-element.10), calls=%async_computation | async-start | bytes 2097152 | tf_op jit(solution)/shard_map/all_to_all | solution.py:150
  119.4 115.4 %all-reduce.2.cloned.1.call-start = ((), (), s32[]{:S(2)}) async-start(), calls=%async_computation.5 | async-start | bytes 4194304 | tf_op jit(solution)/shard_map/psum | solution.py:161
  127.2 40.3 %collective-permute-start.3 = (bf16[2048,128]{1,0:T(8,128)(2,1)}, bf16[2048,128]{1,0:T(8,128)(2,1)}, u32[]{:S(2)}, u32[]{:S(2)}) collective-permute-start(bf16[2048,128]{1,0:T(8,128)(2,1)} %get-tuple-element.53), channel_id=1, source_target_pairs={{0,4},{4,12},{12,20},{20,28},{28,24},{24,16},{16,8},{8,0},{1,5},{5... | collective-permute-start | bytes 1572872 | tf_op jit(solution)/shard_map/ppermute | solution.py:153
  155.7 1.0 copy-start.2
  156.8 14.8 %collective-permute-start.4 = (bf16[2048,128]{1,0:T(8,128)(2,1)S(1)}, bf16[2048,128]{1,0:T(8,128)(2,1)S(1)}, u32[]{:S(2)}, u32[]{:S(2)}) collective-permute-start(bf16[2048,128]{1,0:T(8,128)(2,1)S(1)} %copy-done.2), channel_id=1, source_target_pairs={{0,8},{4,0},{12,4},{20,12},{28,20},{24,28},{16,24},{8,16},{1,9},{5... | collective-permute-start | bytes 1572872 | tf_op jit(solution)/shard_map/ppermute | solution.py:154
  156.8 18.7 %collective-permute-start.1 = (bf16[2048,128]{1,0:T(8,128)(2,1)S(1)}, bf16[2048,128]{1,0:T(8,128)(2,1)S(1)}, u32[]{:S(2)}, u32[]{:S(2)}) collective-permute-start(bf16[2048,128]{1,0:T(8,128)(2,1)S(1)} %get-tuple-element.55), channel_id=1, source_target_pairs={{0,4},{4,12},{12,20},{20,28},{28,24},{24,16},{16,8},{8,0},{1,5},{5... | collective-permute-start | bytes 1572872 | tf_op jit(solution)/shard_map/ppermute | solution.py:153
  163.0 16.2 %collective-permute-start.2 = (bf16[2048,128]{1,0:T(8,128)(2,1)S(1)}, bf16[2048,128]{1,0:T(8,128)(2,1)S(1)}, u32[]{:S(2)}, u32[]{:S(2)}) collective-permute-start(bf16[2048,128]{1,0:T(8,128)(2,1)S(1)} %get-tuple-element.56), channel_id=1, source_target_pairs={{0,8},{4,0},{12,4},{20,12},{28,20},{24,28},{16,24},{8,16},{1,9},{5... | collective-permute-start | bytes 1572872 | tf_op jit(solution)/shard_map/ppermute | solution.py:154
  267.0 0.8 copy-start.3
Sparse Core Ops, SparseCore 0:
  183.0 51.7 all-reduce.1

commit v5 on v4

--- a/solution.py
+++ b/solution.py
@@ -158,14 +158,15 @@
             term = cross_terms(first_part, second_part)
             cross = term if cross is None else cross + term
         lag_count = length // win_count
-        stacked = lax.psum(cross, "win")
-        inverse = inverse_matrix(length, lax.axis_index("win") * lag_count, lag_count, seg_total)
-        correlation = jnp.dot(inverse, stacked, precision=lax.Precision.HIGHEST)
+        stacked = lax.psum_scatter(cross, "win", scatter_dimension=1, tiled=True)
+        inverse = inverse_matrix(length, 0, length, seg_total)
+        own_pairs = jnp.dot(inverse, stacked, precision=lax.Precision.HIGHEST).astype(jnp.bfloat16)
+        correlation = lax.all_to_all(own_pairs, "win", split_axis=0, concat_axis=1, tiled=True)
         capacity = 5 * pair_first.shape[0] // (2 * tile_count)
         chooser = bucket_select(my_owners, tile_count, capacity)
         picked = lax.dot_general(
             chooser,
-            correlation.astype(jnp.bfloat16),
+            correlation,
             (((1,), (1,)), ((), ())),
             preferred_element_type=jnp.float32,
         )

time: 276 us -> 309 us (1.12)
  blocking collectives: 22.8 us -> 63.9 us
  waiting for transfers between devices: 118 us -> 100 us
  other arithmetic: 16.9 us -> 28.1 us
  local copies, waits for them, and re-layouts: 29 us -> 37.5 us
  starting transfers between devices: 27.8 us -> 19.9 us
  matrix products: 46.4 us -> 41.5 us
    psum x1 -> x0, waiting for transfers between devices: 49.1 us -> none  [per_device(): stacked = lax.psum(cross, 'win')]
    all_to_all x0 -> x2, blocking collectives: none -> 41.3 us  [the longest x1 32.9 us: per_device(): lax.all_to_all(outgoing, 'tile', split_axis=0, concat_axis=0, tiled=True)]
    ppermute x4, waiting for transfers between devices: 0.01 us -> 36.3 us  [per_device(): from_prev = lax.ppermute(whitened[:, half:], 'tile', to_next)]
    all_to_all x4 -> x3, waiting for transfers between devices: 61.1 us -> 35.6 us  [per_device(): lax.all_to_all(outgoing, 'tile', split_axis=0, concat_axis=0, tiled=True)]
    unnamed x1 -> x2, waiting for transfers between devices: 0.02 us -> 17.8 us
    unnamed x26 -> x37, local copies, waits for them, and re-layouts: 10.3 us -> 21.7 us
    all_to_all x4 -> x3, starting transfers between devices: 18.9 us -> 11.4 us  [per_device(): lax.all_to_all(outgoing, 'tile', split_axis=0, concat_axis=0, tiled=True)]
    mul x1, other arithmetic: 1.69 us -> 7.71 us  [inverse_matrix(): return jnp.concatenate([weights * cosine, -weights * sine], axis=1)]
  transfers between devices with their start and end apart: 14 -> 13, of which waited for: 7 -> 7; matrix products, arithmetic and copies ran while one was open for 24% -> 19% of each run, Pallas kernels for 0% -> 0%
where the time goes in v5:
time: 309 us; the launch traced here: 305 us
  waiting for transfers between devices  100 us (32%)
  blocking collectives  63.9 us (21%)
  matrix products  41.5 us (13%)
  local copies, waits for them, and re-layouts  37.5 us (12%)
  other arithmetic  28.1 us (9%)
  starting transfers between devices  19.9 us (6%)
  between operations  14.1 us (5%)
    ppermute x4, waiting for transfers between devices, per_device(): from_prev = lax.ppermute(whitened[:, half:], 'tile', to_next)  36.3 us
    all_to_all x3, waiting for transfers between devices, per_device(): lax.all_to_all(outgoing, 'tile', split_axis=0, concat_axis=0, tiled=True)  35.6 us
    all_to_all x1, blocking collectives, per_device(): lax.all_to_all(outgoing, 'tile', split_axis=0, concat_axis=0, tiled=True)  32.9 us
    all_to_all x1, blocking collectives, per_device(): lax.all_to_all(buckets, 'tile', split_axis=0, concat_axis=0, tiled=True)  22.7 us
    unnamed x37, local copies, waits for them, and re-layouts  21.7 us
    dot_general x4, matrix products, per_device(): jnp.einsum('fjm,jmc->fc', forward, received, preferred_element_type=jnp.f...  20.6 us
    unnamed x2, waiting for transfers between devices  17.8 us
    dot_general x1, matrix products, per_device(): jnp.dot(inverse, stacked, precision=lax.Precision.HIGHEST)  14.4 us
  transfers between devices with their start and end apart: 13, of which 7 were waited for; matrix products, arithmetic and copies ran while one was open for 19% of the time, Pallas kernels for 0%

profile of v5, /device:TPU:0, one launch (start us, length us, event | category | flops | bytes accessed | tf_op | source)
XLA Modules:
  0.0 305.4 jit_solution(12132941582493499267)
XLA Ops:
  6.5 1.3 slice_bitcast_fusion.1
  7.8 2.1 slice_dynamic-update-slice_fusion.7
  9.9 1.9 slice_dynamic-update-slice_fusion.6
  11.8 0.7 fusion.57
  12.5 0.8 fusion.55
  13.2 0.8 slice_dynamic-update-slice_fusion.5
  14.0 0.8 slice_dynamic-update-slice_fusion.4
  14.8 0.8 slice_dynamic-update-slice_fusion.3
  15.6 0.8 slice_dynamic-update-slice_fusion.2
  16.4 0.8 slice_dynamic-update-slice_fusion.1
  17.2 32.9 %all_to_all.44 = bf16[8,256,256]{2,1,0:T(8,128)(2,1)S(1)} all-to-all(bf16[8,256,256]{2,1,0:T(8,128)(2,1)S(1)} %get-tuple-element.8), channel_id=1, replica_groups=mesh['tile'=8,'win'=4] {'tile'}, dimensions={0} | all-to-all | bytes 2097152 | tf_op jit(solution)/shard_map/all_to_all | solution.py:150
  50.0 3.6 %all-to-all-start.1 = ((bf16[8,256,256]{2,1,0:T(8,128)(2,1)}), bf16[8,256,256]{2,1,0:T(8,128)(2,1)S(1)}, u32[]{:S(2)}, u32[]{:S(2)}) async-start(bf16[8,256,256]{2,1,0:T(8,128)(2,1)} %get-tuple-element.9), calls=%async_computation.1 | async-start | bytes 2097152 | tf_op jit(solution)/shard_map/all_to_all | solution.py:150
  53.7 0.7 collective-permute-start
  54.3 1.0 fusion.59
  55.4 0.6 fusion.68
  56.0 5.1 %subtract_convert_fusion = (bf16[1024,32,64]{0,2,1:T(8,128)(2,1)}, bf16[1024,32,64]{0,2,1:T(8,128)(2,1)}) fusion(f32[1024,64]{0,1:T(8,128)S(1)} %get-tuple-element.74, f32[1024,32]{0,1:T(8,128)S(1)} %get-tuple-element.65, f32[1024,64]{0,1:T(8,128)S(1)} %get-tuple-element.75, f32[1024,32]{0,1:T(8,128)S(1)} %get-tuple-element.64), kind=kLoop, calls=%fused_computation.8 | loop fusion | flops 18874368 | bytes 9175040 | tf_op jit(solution)/shard_map/convert.3
  61.0 6.4 %copy.8 = bf16[1024,8,256]{2,0,1:T(8,128)(2,1)} copy(bf16[1024,8,256]{0,2,1:T(8,128)(2,1)} %bitcast.92) | data formatting | bytes 8388608 | tf_op jit(solution)/shard_map/sub | solution.py:24
  67.5 6.5 %copy.9 = bf16[1024,8,256]{2,0,1:T(8,128)(2,1)} copy(bf16[1024,8,256]{0,2,1:T(8,128)(2,1)} %bitcast.91) | data formatting | bytes 8388608 | tf_op jit(solution)/shard_map/neg | solution.py:31
  74.0 0.6 reduce-window.6
  74.9 4.2 %all-to-all-done.1 = bf16[8,256,256]{2,1,0:T(8,128)(2,1)S(1)} async-done(((bf16[8,256,256]{2,1,0:T(8,128)(2,1)}), bf16[8,256,256]{2,1,0:T(8,128)(2,1)S(1)}, u32[]{:S(2)}, u32[]{:S(2)}) %all-to-all-start.1) | async-done | bytes 1048608 | tf_op jit(solution)/shard_map/all_to_all | solution.py:150
  79.2 3.6 %all-to-all-start = ((bf16[8,256,256]{2,1,0:T(8,128)(2,1)}), bf16[8,256,256]{2,1,0:T(8,128)(2,1)S(1)}, u32[]{:S(2)}, u32[]{:S(2)}) async-start(bf16[8,256,256]{2,1,0:T(8,128)(2,1)} %get-tuple-element.10), calls=%async_computation | async-start | bytes 2097152 | tf_op jit(solution)/shard_map/all_to_all | solution.py:150
  82.8 6.1 %convolution_bitcast_fusion.2 = f32[2048,256]{1,0:T(8,128)S(1)} fusion(bf16[8,256,256]{2,1,0:T(8,128)(2,1)S(1)} %all-to-all-done.1, bf16[1024,8,256]{2,0,1:T(8,128)(2,1)} %copy.9, bf16[1024,8,256]{2,0,1:T(8,128)(2,1)} %copy.8), kind=kOutput, calls=%fused_computation.13 | convolution fusion | flops 2164260864 | bytes 11534336 | tf_op jit(solution)/shard_map/fjm,jmc->fc/dot_general | solution.py:151
  88.9 1.3 copy-done.2
  90.4 2.5 convolution_bitcast_fusion.1
  93.0 1.4 copy-done
  94.5 14.1 %all-to-all-done = bf16[8,256,256]{2,1,0:T(8,128)(2,1)S(1)} async-done(((bf16[8,256,256]{2,1,0:T(8,128)(2,1)}), bf16[8,256,256]{2,1,0:T(8,128)(2,1)S(1)}, u32[]{:S(2)}, u32[]{:S(2)}) %all-to-all-start) | async-done | bytes 1048608 | tf_op jit(solution)/shard_map/all_to_all | solution.py:150
  108.6 4.3 %all-to-all-start.3 = ((bf16[8,256,256]{2,1,0:T(8,128)(2,1)}), bf16[8,256,256]{2,1,0:T(8,128)(2,1)}, u32[]{:S(2)}, u32[]{:S(2)}) async-start(bf16[8,256,256]{2,1,0:T(8,128)(2,1)} %get-tuple-element.7), calls=%async_computation.3 | async-start | bytes 2097152 | tf_op jit(solution)/shard_map/all_to_all | solution.py:150
  112.8 0.3 reduce-scatter.4.cloned.1.call-start
  113.2 5.9 %convolution_bitcast_fusion.3 = f32[2048,256]{1,0:T(8,128)S(1)} fusion(bf16[8,256,256]{2,1,0:T(8,128)(2,1)S(1)} %all-to-all-done, bf16[1024,8,256]{2,0,1:T(8,128)(2,1)} %copy.9, bf16[1024,8,256]{2,0,1:T(8,128)(2,1)} %copy.8), kind=kOutput, calls=%fused_computation.14 | convolution fusion | flops 2164260864 | bytes 11534336 | tf_op jit(solution)/shard_map/fjm,jmc->fc/dot_general | solution.py:151
  119.5 1.3 fusion.10
  121.1 17.3 %all-to-all-done.3 = bf16[8,256,256]{2,1,0:T(8,128)(2,1)} async-done(((bf16[8,256,256]{2,1,0:T(8,128)(2,1)}), bf16[8,256,256]{2,1,0:T(8,128)(2,1)}, u32[]{:S(2)}, u32[]{:S(2)}) %all-to-all-start.3) | async-done | bytes 1048608 | tf_op jit(solution)/shard_map/all_to_all | solution.py:150
  138.4 6.1 %convolution_bitcast_fusion = f32[2048,256]{1,0:T(8,128)S(1)} fusion(bf16[8,256,256]{2,1,0:T(8,128)(2,1)} %all-to-all-done.3, bf16[1024,8,256]{2,0,1:T(8,128)(2,1)} %copy.9, bf16[1024,8,256]{2,0,1:T(8,128)(2,1)} %copy.8), kind=kOutput, calls=%fused_computation.11 | convolution fusion | flops 2164260864 | bytes 11534336 | tf_op jit(solution)/shard_map/fjm,jmc->fc/dot_general | solution.py:151
  144.9 0.3 fusion.12
  145.6 1.3 collective-permute-start.1
  147.0 0.8 collective-permute-start.2
  147.8 1.3 collective-permute-start.3
  149.1 0.8 collective-permute-start.4
  150.0 1.3 collective-permute-start.7
  151.3 20.4 %collective-permute-done.3 = bf16[2048,128]{1,0:T(8,128)(2,1)S(1)} collective-permute-done((bf16[2048,128]{1,0:T(8,128)(2,1)S(1)}, bf16[2048,128]{1,0:T(8,128)(2,1)S(1)}, u32[]{:S(2)}, u32[]{:S(2)}) %collective-permute-start.3) | collective-permute-done | bytes 524320 | tf_op jit(solution)/shard_map/ppermute | solution.py:153
  171.7 1.3 collective-permute-start.5
  173.0 0.8 collective-permute-start.6
  173.8 0.8 fusion.21
  174.5 0.8 fusion.22
  175.6 15.9 %collective-permute-done.5 = bf16[2048,128]{1,0:T(8,128)(2,1)S(1)} collective-permute-done((bf16[2048,128]{1,0:T(8,128)(2,1)S(1)}, bf16[2048,128]{1,0:T(8,128)(2,1)S(1)}, u32[]{:S(2)}, u32[]{:S(2)}) %collective-permute-start.5) | collective-permute-done | bytes 524320 | tf_op jit(solution)/shard_map/ppermute | solution.py:153
  191.5 0.8 fusion.19
  192.3 0.8 fusion.20
  193.4 10.6 %collective-permute-done.8 = bf16[2048,128]{1,0:T(8,128)(2,1)S(1)} collective-permute-done((bf16[2048,128]{1,0:T(8,128)(2,1)S(1)}, bf16[2048,128]{1,0:T(8,128)(2,1)S(1)}, u32[]{:S(2)}, u32[]{:S(2)}) %collective-permute-start.8) | collective-permute-done | bytes 524320 | tf_op jit(solution)/shard_map/ppermute | solution.py:154
  203.9 0.8 fusion.17
  204.7 0.8 fusion.18
  205.8 0.8 fusion.24
  206.6 0.8 fusion.23
  207.6 0.5 fusion.9
  208.2 10.9 %copy.11 = f32[2048,256]{0,1:T(8,128)} copy(f32[2048,256]{1,0:T(8,128)S(1)} %fusion.9) | data formatting | bytes 4194304
  219.1 1.9 fusion.47
  221.0 1.9 fusion.46
  222.9 0.6 fusion.70
  223.5 2.5 multiply_subtract_fusion
  226.1 7.7 %bitcast_multiply_fusion = (f32[2048,1024]{0,1:T(8,128)}, f32[2048,1024]{0,1:T(8,128)}) fusion(f32[2048,16,64]{0,2,1:T(8,128)S(1)} %get-tuple-element.50, f32[1024]{0:T(1024)S(1)} %fusion.73, f32[2048,16,64]{0,2,1:T(8,128)S(1)} %get-tuple-element.49, f32[1024]{0:T(1024)S(1)} %select_multiply_fusion), kind=kLoop, calls=%fused_computation.5 | loop fusion | flops 4194304 | bytes 33562624 | tf_op jit(solution)/shard_map/mul | solution.py:42
  233.8 17.8 %reduce-scatter.4.cloned.1.call-done = f32[64,2048]{1,0:T(8,128)} async-done(((f32[256,2048]{1,0:T(8,128)}), f32[64,2048]{1,0:T(8,128)}) %reduce-scatter.4.cloned.1.call-update) | async-done | bytes 524304
  251.6 14.4 %fusion.4 = bf16[2048,64]{0,1:T(8,128)(2,1)S(1)} fusion(f32[2048,1024]{0,1:T(8,128)} %get-tuple-element.68, f32[2048,1024]{0,1:T(8,128)} %get-tuple-element.69, f32[64,2048]{1,0:T(8,128)} %reduce-scatter.4.cloned.1.call-done), kind=kOutput, calls=%fused_computation.15 | convolution fusion | flops 3225550848 | bytes 17563648 | tf_op jit(solution)/shard_map/dot_general | solution.py:163
  266.0 8.4 %all_to_all.45 = bf16[4,512,64]{1,2,0:T(8,128)(2,1)S(1)} all-to-all(bf16[4,512,64]{1,2,0:T(8,128)(2,1)S(1)} %bitcast.99), channel_id=1, replica_groups=mesh['tile'=8,'win'=4] {'win'}, dimensions={0} | all-to-all | bytes 524288 | tf_op jit(solution)/shard_map/all_to_all | solution.py:164
  274.4 0.3 convolution_convert_fusion
  274.7 22.7 %all_to_all.46 = bf16[8,80,512]{2,1,0:T(8,128)(2,1)S(1)} all-to-all(bf16[8,80,512]{2,1,0:T(8,128)(2,1)S(1)} %bitcast.98), channel_id=1, replica_groups=mesh['tile'=8,'win'=4] {'tile'}, dimensions={0} | all-to-all | bytes 1310720 | tf_op jit(solution)/shard_map/all_to_all | solution.py:174
  297.6 0.8 copy-done.8
  (71 shorter events, 3.6 us)
Async XLA Ops:
  6.5 6.7 %copy-start.4 = (bf16[4,256,2048]{2,1,0:T(8,128)(2,1)S(1)}, bf16[4,256,2048]{2,1,0:T(8,128)(2,1)}, u32[]{:S(2)}) copy-start(bf16[4,256,2048]{2,1,0:T(8,128)(2,1)} %param.4) | copy-start | bytes 12582916
  14.0 39.6 %copy-start.9 = (s32[256,1]{0,1:T(1,128)S(1)}, s32[256,1]{0,1:T(1,128)}, u32[]{:S(2)}) copy-start(s32[256,1]{0,1:T(1,128)} %param.7) | copy-start | bytes 3076
  14.0 39.6 %copy-start.10 = (s32[256]{0:T(256)S(1)}, s32[256]{0:T(256)}, u32[]{:S(2)}) copy-start(s32[256]{0:T(256)} %param.6) | copy-start | bytes 3076
  14.0 39.6 %copy-start.11 = (s32[256]{0:T(256)S(1)}, s32[256]{0:T(256)}, u32[]{:S(2)}) copy-start(s32[256]{0:T(256)} %param.5) | copy-start | bytes 3076
  50.0 29.2 %all-to-all-start.1 = ((bf16[8,256,256]{2,1,0:T(8,128)(2,1)}), bf16[8,256,256]{2,1,0:T(8,128)(2,1)S(1)}, u32[]{:S(2)}, u32[]{:S(2)}) async-start(bf16[8,256,256]{2,1,0:T(8,128)(2,1)} %get-tuple-element.9), calls=%async_computation.1 | async-start | bytes 2097152 | tf_op jit(solution)/shard_map/all_to_all | solution.py:150
  53.7 20.3 %collective-permute-start = (s32[3,256]{1,0:T(4,128)S(1)}, s32[3,256]{1,0:T(4,128)S(1)}, u32[]{:S(2)}, u32[]{:S(2)}) collective-permute-start(s32[3,256]{1,0:T(4,128)S(1)} %pad_add_fusion), channel_id=1, source_target_pairs={{0,0},{4,4},{8,12},{12,20},{16,28},{20,24},{24,16},{28,8},{1,1},{5... | collective-permute-start | bytes 9224 | tf_op jit(solution)/shard_map/ppermute | solution.py:131
  79.2 29.4 %all-to-all-start = ((bf16[8,256,256]{2,1,0:T(8,128)(2,1)}), bf16[8,256,256]{2,1,0:T(8,128)(2,1)S(1)}, u32[]{:S(2)}, u32[]{:S(2)}) async-start(bf16[8,256,256]{2,1,0:T(8,128)(2,1)} %get-tuple-element.10), calls=%async_computation | async-start | bytes 2097152 | tf_op jit(solution)/shard_map/all_to_all | solution.py:150
  82.8 7.6 %copy-start.5 = (bf16[1024,8,256]{2,0,1:T(8,128)(2,1)S(1)}, bf16[1024,8,256]{2,0,1:T(8,128)(2,1)}, u32[]{:S(2)}) copy-start(bf16[1024,8,256]{2,0,1:T(8,128)(2,1)} %copy.8) | copy-start | bytes 12582916
  82.8 7.6 %copy-start.6 = (bf16[1024,8,256]{2,0,1:T(8,128)(2,1)S(1)}, bf16[1024,8,256]{2,0,1:T(8,128)(2,1)}, u32[]{:S(2)}) copy-start(bf16[1024,8,256]{2,0,1:T(8,128)(2,1)} %copy.9) | copy-start | bytes 12582916
  88.9 1.3 copy-start.2
  92.9 1.4 copy-start
  108.6 29.9 %all-to-all-start.3 = ((bf16[8,256,256]{2,1,0:T(8,128)(2,1)}), bf16[8,256,256]{2,1,0:T(8,128)(2,1)}, u32[]{:S(2)}, u32[]{:S(2)}) async-start(bf16[8,256,256]{2,1,0:T(8,128)(2,1)} %get-tuple-element.7), calls=%async_computation.3 | async-start | bytes 2097152 | tf_op jit(solution)/shard_map/all_to_all | solution.py:150
  112.8 138.7 %reduce-scatter.4.cloned.1.call-start = ((), (), s32[]{:S(2)}) async-start(), calls=%async_computation.7 | async-start | bytes 2621440
  113.1 6.3 %copy-start.3 = (f32[2048,256]{1,0:T(8,128)S(1)}, f32[2048,256]{1,0:T(8,128)}, u32[]{:S(2)}) copy-start(f32[2048,256]{1,0:T(8,128)} %copy-done.2) | copy-start | bytes 6291460
  119.1 1.7 copy-start.1
  145.2 2.6 copy-start.7
  145.6 60.1 %collective-permute-start.1 = (bf16[2048,128]{1,0:T(8,128)(2,1)S(1)}, bf16[2048,128]{1,0:T(8,128)(2,1)S(1)}, u32[]{:S(2)}, u32[]{:S(2)}) collective-permute-start(bf16[2048,128]{1,0:T(8,128)(2,1)S(1)} %get-tuple-element.57), channel_id=1, source_target_pairs={{0,4},{4,12},{12,20},{20,28},{28,24},{24,16},{16,8},{8,0},{1,5},{5... | collective-permute-start | bytes 1572872 | tf_op jit(solution)/shard_map/ppermute | solution.py:153
  147.0 58.8 %collective-permute-start.2 = (bf16[2048,128]{1,0:T(8,128)(2,1)S(1)}, bf16[2048,128]{1,0:T(8,128)(2,1)S(1)}, u32[]{:S(2)}, u32[]{:S(2)}) collective-permute-start(bf16[2048,128]{1,0:T(8,128)(2,1)S(1)} %get-tuple-element.58), channel_id=1, source_target_pairs={{0,8},{4,0},{12,4},{20,12},{28,20},{24,28},{16,24},{8,16},{1,9},{5... | collective-permute-start | bytes 1572872 | tf_op jit(solution)/shard_map/ppermute | solution.py:154
  147.8 23.9 %collective-permute-start.3 = (bf16[2048,128]{1,0:T(8,128)(2,1)S(1)}, bf16[2048,128]{1,0:T(8,128)(2,1)S(1)}, u32[]{:S(2)}, u32[]{:S(2)}) collective-permute-start(bf16[2048,128]{1,0:T(8,128)(2,1)S(1)} %get-tuple-element.55), channel_id=1, source_target_pairs={{0,4},{4,12},{12,20},{20,28},{28,24},{24,16},{16,8},{8,0},{1,5},{5... | collective-permute-start | bytes 1572872 | tf_op jit(solution)/shard_map/ppermute | solution.py:153
  149.1 23.9 %collective-permute-start.4 = (bf16[2048,128]{1,0:T(8,128)(2,1)S(1)}, bf16[2048,128]{1,0:T(8,128)(2,1)S(1)}, u32[]{:S(2)}, u32[]{:S(2)}) collective-permute-start(bf16[2048,128]{1,0:T(8,128)(2,1)S(1)} %get-tuple-element.56), channel_id=1, source_target_pairs={{0,8},{4,0},{12,4},{20,12},{28,20},{24,28},{16,24},{8,16},{1,9},{5... | collective-permute-start | bytes 1572872 | tf_op jit(solution)/shard_map/ppermute | solution.py:154
  150.0 43.4 %collective-permute-start.7 = (bf16[2048,128]{1,0:T(8,128)(2,1)S(1)}, bf16[2048,128]{1,0:T(8,128)(2,1)S(1)}, u32[]{:S(2)}, u32[]{:S(2)}) collective-permute-start(bf16[2048,128]{1,0:T(8,128)(2,1)S(1)} %get-tuple-element.51), channel_id=1, source_target_pairs={{0,4},{4,12},{12,20},{20,28},{28,24},{24,16},{16,8},{8,0},{1,5},{5... | collective-permute-start | bytes 1572872 | tf_op jit(solution)/shard_map/ppermute | solution.py:153
  171.7 19.8 %collective-permute-start.5 = (bf16[2048,128]{1,0:T(8,128)(2,1)S(1)}, bf16[2048,128]{1,0:T(8,128)(2,1)S(1)}, u32[]{:S(2)}, u32[]{:S(2)}) collective-permute-start(bf16[2048,128]{1,0:T(8,128)(2,1)S(1)} %get-tuple-element.53), channel_id=1, source_target_pairs={{0,4},{4,12},{12,20},{20,28},{28,24},{24,16},{16,8},{8,0},{1,5},{5... | collective-permute-start | bytes 1572872 | tf_op jit(solution)/shard_map/ppermute | solution.py:153
  173.0 18.5 %collective-permute-start.6 = (bf16[2048,128]{1,0:T(8,128)(2,1)S(1)}, bf16[2048,128]{1,0:T(8,128)(2,1)S(1)}, u32[]{:S(2)}, u32[]{:S(2)}) collective-permute-start(bf16[2048,128]{1,0:T(8,128)(2,1)S(1)} %get-tuple-element.54), channel_id=1, source_target_pairs={{0,8},{4,0},{12,4},{20,12},{28,20},{24,28},{16,24},{8,16},{1,9},{5... | collective-permute-start | bytes 1572872 | tf_op jit(solution)/shard_map/ppermute | solution.py:154
  191.5 12.4 %collective-permute-start.8 = (bf16[2048,128]{1,0:T(8,128)(2,1)S(1)}, bf16[2048,128]{1,0:T(8,128)(2,1)S(1)}, u32[]{:S(2)}, u32[]{:S(2)}) collective-permute-start(bf16[2048,128]{1,0:T(8,128)(2,1)S(1)} %get-tuple-element.52), channel_id=1, source_target_pairs={{0,8},{4,0},{12,4},{20,12},{28,20},{24,28},{16,24},{8,16},{1,9},{5... | collective-permute-start | bytes 1572872 | tf_op jit(solution)/shard_map/ppermute | solution.py:154
  297.5 0.8 copy-start.8
Sparse Core Ops, SparseCore 0:
  219.2 32.2 reduce-scatter.3

commit v6 on v5

--- a/solution.py
+++ b/solution.py
@@ -133,6 +133,7 @@
         pick_first = (channel_ids == my_first[None, :]).astype(jnp.bfloat16)
         pick_second = (channel_ids == (my_first + my_offset)[None, :]).astype(jnp.bfloat16)
         cross = None
+        arrived = []
         for segment in range(records.shape[0]):
             pieces = []
             for b in block_of:
@@ -147,11 +148,14 @@
                         )
                     )
             outgoing = jnp.stack(pieces, axis=0)
+            if segment >= 2:
+                outgoing, _ = lax.optimization_barrier((outgoing, arrived[segment - 2]))
             received = lax.all_to_all(outgoing, "tile", split_axis=0, concat_axis=0, tiled=True)
             spectra = jnp.einsum("fjm,jmc->fc", forward, received, preferred_element_type=jnp.float32)
             whitened = whiten(spectra, BAND)
             from_prev = lax.ppermute(whitened[:, half:], "tile", to_next)
             from_next = lax.ppermute(whitened[:, :half], "tile", to_prev)
+            arrived.append((from_prev, from_next))
             joined = jnp.concatenate([from_prev, whitened, from_next], axis=1)
             first_part = jnp.dot(joined, pick_first, preferred_element_type=jnp.float32)
             second_part = jnp.dot(joined, pick_second, preferred_element_type=jnp.float32)
@@ -160,7 +164,7 @@
         lag_count = length // win_count
         stacked = lax.psum_scatter(cross, "win", scatter_dimension=1, tiled=True)
         inverse = inverse_matrix(length, 0, length, seg_total)
-        own_pairs = jnp.dot(inverse, stacked, precision=lax.Precision.HIGHEST).astype(jnp.bfloat16)
+        own_pairs = jnp.dot(inverse, stacked, precision=lax.Precision.HIGH).astype(jnp.bfloat16)
         correlation = lax.all_to_all(own_pairs, "win", split_axis=0, concat_axis=1, tiled=True)
         capacity = 5 * pair_first.shape[0] // (2 * tile_count)
         chooser = bucket_select(my_owners, tile_count, capacity)

time: 309 us -> 297 us (0.961)
  blocking collectives: 63.9 us -> 31 us
  starting transfers between devices: 19.9 us -> 34.7 us
  waiting for transfers between devices: 100 us -> 109 us
  local copies, waits for them, and re-layouts: 37.5 us -> 33.8 us
  matrix products: 41.5 us -> 44.6 us
    all_to_all x1 -> x0, blocking collectives: 32.9 us -> none  [per_device(): lax.all_to_all(outgoing, 'tile', split_axis=0, concat_axis=0, tiled=True)]
    all_to_all x3 -> x4, starting transfers between devices: 11.4 us -> 25.5 us  [per_device(): lax.all_to_all(outgoing, 'tile', split_axis=0, concat_axis=0, tiled=True)]
    ppermute x4, waiting for transfers between devices: 36.3 us -> 48.6 us  [per_device(): from_prev = lax.ppermute(whitened[:, half:], 'tile', to_next)]
    dot_general x1, matrix products: 14.4 us -> 8.55 us  [per_device(): jnp.dot(inverse, stacked, precision=lax.Precision.HIGH).astype(jnp.bfloat16)]
    ppermute x4, waiting for transfers between devices: 10.6 us -> 5.07 us  [per_device(): from_next = lax.ppermute(whitened[:, :half], 'tile', to_prev)]
    unnamed x37 -> x53, local copies, waits for them, and re-layouts: 21.7 us -> 16.8 us
    dot_general x4, matrix products: 3.06 us -> 7 us  [per_device(): first_part = jnp.dot(joined, pick_first, preferred_element_type=jnp.float32)]
    dot_general x4, matrix products: 3.06 us -> 6.9 us  [per_device(): jnp.dot(joined, pick_second, preferred_element_type=jnp.float32)]
  transfers between devices with their start and end apart: 13 -> 14, of which waited for: 7 -> 11; matrix products, arithmetic and copies ran while one was open for 19% -> 21% of each run, Pallas kernels for 0% -> 0%
where the time goes in v6:
time: 297 us; the launch traced here: 296 us
  waiting for transfers between devices  109 us (37%)
  matrix products  44.6 us (15%)
  starting transfers between devices  34.7 us (12%)
  local copies, waits for them, and re-layouts  33.8 us (11%)
  blocking collectives  31 us (10%)
  other arithmetic  29.6 us (10%)
  between operations  13.9 us (5%)
    ppermute x4, waiting for transfers between devices, per_device(): from_prev = lax.ppermute(whitened[:, half:], 'tile', to_next)  48.6 us
    all_to_all x4, waiting for transfers between devices, per_device(): lax.all_to_all(outgoing, 'tile', split_axis=0, concat_axis=0, tiled=True)  39.3 us
    all_to_all x4, starting transfers between devices, per_device(): lax.all_to_all(outgoing, 'tile', split_axis=0, concat_axis=0, tiled=True)  25.5 us
    all_to_all x1, blocking collectives, per_device(): lax.all_to_all(buckets, 'tile', split_axis=0, concat_axis=0, tiled=True)  22.6 us
    dot_general x4, matrix products, per_device(): jnp.einsum('fjm,jmc->fc', forward, received, preferred_element_type=jnp.f...  21.8 us
    unnamed x53, local copies, waits for them, and re-layouts  16.8 us
    unnamed x2, waiting for transfers between devices  15.9 us
    dot_general x1, matrix products, per_device(): jnp.dot(inverse, stacked, precision=lax.Precision.HIGH).astype(jnp.bfloat16)  8.55 us
  transfers between devices with their start and end apart: 14, of which 11 were waited for; matrix products, arithmetic and copies ran while one was open for 21% of the time, Pallas kernels for 0%

profile of v6, /device:TPU:0, one launch (start us, length us, event | category | flops | bytes accessed | tf_op | source)
XLA Modules:
  0.0 296.5 jit_solution(1192778265237952579)
XLA Ops:
  6.5 1.3 slice_bitcast_fusion.1
  7.8 2.1 slice_dynamic-update-slice_fusion.7
  9.9 1.8 slice_dynamic-update-slice_fusion.6
  11.8 0.8 fusion.55
  12.5 0.8 slice_dynamic-update-slice_fusion.5
  13.3 0.8 slice_dynamic-update-slice_fusion.4
  14.1 0.8 slice_dynamic-update-slice_fusion.3
  14.9 0.8 slice_dynamic-update-slice_fusion.2
  15.7 0.8 slice_dynamic-update-slice_fusion.1
  16.5 1.0 copy-done.10
  17.4 1.0 copy-done.11
  18.4 7.3 %all-to-all-start.1 = ((bf16[8,256,256]{2,1,0:T(8,128)(2,1)}), bf16[8,256,256]{2,1,0:T(8,128)(2,1)S(1)}, u32[]{:S(2)}, u32[]{:S(2)}) async-start(bf16[8,256,256]{2,1,0:T(8,128)(2,1)} %get-tuple-element.13), calls=%async_computation.1 | async-start | bytes 2097152 | tf_op jit(solution)/shard_map/all_to_all | solution.py:153
  26.4 1.0 fusion.59
  27.5 24.0 %all-to-all-done.1 = bf16[8,256,256]{2,1,0:T(8,128)(2,1)S(1)} async-done(((bf16[8,256,256]{2,1,0:T(8,128)(2,1)}), bf16[8,256,256]{2,1,0:T(8,128)(2,1)S(1)}, u32[]{:S(2)}, u32[]{:S(2)}) %all-to-all-start.1) | async-done | bytes 1048608 | tf_op jit(solution)/shard_map/all_to_all | solution.py:153
  51.5 4.3 %all-to-all-start = ((bf16[8,256,256]{2,1,0:T(8,128)(2,1)}), bf16[8,256,256]{2,1,0:T(8,128)(2,1)}, u32[]{:S(2)}, u32[]{:S(2)}) async-start(bf16[8,256,256]{2,1,0:T(8,128)(2,1)} %get-tuple-element.14), calls=%async_computation | async-start | bytes 2097152 | tf_op jit(solution)/shard_map/all_to_all | solution.py:153
  56.3 5.0 %subtract_convert_fusion = (bf16[1024,32,64]{0,2,1:T(8,128)(2,1)}, bf16[1024,32,64]{0,2,1:T(8,128)(2,1)}) fusion(f32[1024,64]{0,1:T(8,128)S(1)} %get-tuple-element.78, f32[1024,32]{0,1:T(8,128)S(1)} %get-tuple-element.69, f32[1024,64]{0,1:T(8,128)S(1)} %get-tuple-element.79, f32[1024,32]{0,1:T(8,128)S(1)} %get-tuple-element.68), kind=kLoop, calls=%fused_computation.8 | loop fusion | flops 18874368 | bytes 9175040 | tf_op jit(solution)/shard_map/convert.3
  61.3 6.5 %copy.8 = bf16[1024,8,256]{2,0,1:T(8,128)(2,1)} copy(bf16[1024,8,256]{0,2,1:T(8,128)(2,1)} %bitcast.92) | data formatting | bytes 8388608 | tf_op jit(solution)/shard_map/sub | solution.py:24
  67.8 6.5 %copy.9 = bf16[1024,8,256]{2,0,1:T(8,128)(2,1)} copy(bf16[1024,8,256]{0,2,1:T(8,128)(2,1)} %bitcast.91) | data formatting | bytes 8388608 | tf_op jit(solution)/shard_map/neg | solution.py:31
  74.2 5.8 %convolution_bitcast_fusion.2 = f32[2048,256]{1,0:T(8,128)S(1)} fusion(bf16[8,256,256]{2,1,0:T(8,128)(2,1)S(1)} %all-to-all-done.1, bf16[1024,8,256]{2,0,1:T(8,128)(2,1)} %copy.9, bf16[1024,8,256]{2,0,1:T(8,128)(2,1)} %copy.8), kind=kOutput, calls=%fused_computation.13 | convolution fusion | flops 2164260864 | bytes 11534336 | tf_op jit(solution)/shard_map/fjm,jmc->fc/dot_general | solution.py:154
  80.3 1.0 all-to-all-done
  81.3 6.1 %convolution_bitcast_fusion.3 = f32[2048,256]{1,0:T(8,128)S(1)} fusion(bf16[8,256,256]{2,1,0:T(8,128)(2,1)} %all-to-all-done, bf16[1024,8,256]{2,0,1:T(8,128)(2,1)} %copy.9, bf16[1024,8,256]{2,0,1:T(8,128)(2,1)} %copy.8), kind=kOutput, calls=%fused_computation.14 | convolution fusion | flops 2164260864 | bytes 11534336 | tf_op jit(solution)/shard_map/fjm,jmc->fc/dot_general | solution.py:154
  88.1 1.3 collective-permute-start.1
  89.4 0.8 collective-permute-start.2
  90.3 1.3 fusion.10
  91.6 8.7 %collective-permute-done.1 = bf16[2048,128]{1,0:T(8,128)(2,1)S(1)} collective-permute-done((bf16[2048,128]{1,0:T(8,128)(2,1)S(1)}, bf16[2048,128]{1,0:T(8,128)(2,1)S(1)}, u32[]{:S(2)}, u32[]{:S(2)}) %collective-permute-start.1) | collective-permute-done | bytes 524320 | tf_op jit(solution)/shard_map/ppermute | solution.py:156
  100.3 1.8 collective-permute-done.2
  102.1 0.8 copy-done.18
  102.9 4.5 %all-to-all-start.2 = ((bf16[8,256,256]{2,1,0:T(8,128)(2,1)}), bf16[8,256,256]{2,1,0:T(8,128)(2,1)}, u32[]{:S(2)}, u32[]{:S(2)}) async-start(bf16[8,256,256]{2,1,0:T(8,128)(2,1)} %copy-done.11), calls=%async_computation.2 | async-start | bytes 2097152 | tf_op jit(solution)/shard_map/all_to_all | solution.py:153
  107.4 1.3 fusion.85
  108.7 2.1 collective-permute-start.3
  111.9 24.2 %collective-permute-done.3 = bf16[2048,128]{1,0:T(8,128)(2,1)} collective-permute-done((bf16[2048,128]{1,0:T(8,128)(2,1)S(1)}, bf16[2048,128]{1,0:T(8,128)(2,1)}, u32[]{:S(2)}, u32[]{:S(2)}) %collective-permute-start.3) | collective-permute-done | bytes 524320 | tf_op jit(solution)/shard_map/ppermute | solution.py:156
  136.2 3.3 %fusion.22 = f32[2048,256]{1,0:T(8,128)} fusion(bf16[2048,128]{1,0:T(8,128)(2,1)} %collective-permute-done.4, bf16[2048,256]{1,0:T(8,128)(2,1)S(1)} %copy-done.6, bf16[2048,128]{1,0:T(8,128)(2,1)} %collective-permute-done.3, s32[256]{0:T(256)S(1)} %bitcast.109), kind=kOutput, calls=%fused_computation.61 | convolution fusion | flops 543293440 | bytes 4195328 | tf_op jit(solution)/shard_map/dot_general | solution.py:160
  139.5 2.2 fusion.24
  141.6 3.3 %fusion.21 = f32[2048,256]{1,0:T(8,128)} fusion(bf16[2048,128]{1,0:T(8,128)(2,1)} %collective-permute-done.4, bf16[2048,256]{1,0:T(8,128)(2,1)S(1)} %copy-done.6, bf16[2048,128]{1,0:T(8,128)(2,1)} %collective-permute-done.3, s32[256]{0:T(256)S(1)} %bitcast.113), kind=kOutput, calls=%fused_computation.60 | convolution fusion | flops 543293440 | bytes 4195328 | tf_op jit(solution)/shard_map/dot_general | solution.py:161
  144.9 9.4 %all-to-all-start.3 = ((bf16[8,256,256]{2,1,0:T(8,128)(2,1)}), bf16[8,256,256]{2,1,0:T(8,128)(2,1)}, u32[]{:S(2)}, u32[]{:S(2)}) async-start(bf16[8,256,256]{2,1,0:T(8,128)(2,1)} %copy-done.10), calls=%async_computation.3 | async-start | bytes 2097152 | tf_op jit(solution)/shard_map/all_to_all | solution.py:153
  154.4 2.1 fusion.23
  156.6 1.2 multiply_add_fusion.3
  157.8 0.7 copy-done.7
  158.5 1.7 multiply_add_fusion.4
  160.2 1.8 copy-done.1
  162.0 3.7 %convolution_bitcast_fusion.1 = f32[2048,256]{1,0:T(8,128)S(1)} fusion(bf16[8,256,256]{2,1,0:T(8,128)(2,1)} %all-to-all-done.2, bf16[1024,8,256]{2,0,1:T(8,128)(2,1)S(1)} %copy-done.2, bf16[1024,8,256]{2,0,1:T(8,128)(2,1)S(1)} %copy-done.1), kind=kOutput, calls=%fused_computation.12 | convolution fusion | flops 2164260864 | bytes 11534336 | tf_op jit(solution)/shard_map/fjm,jmc->fc/dot_general | solution.py:154
  165.9 14.3 %all-to-all-done.3 = bf16[8,256,256]{2,1,0:T(8,128)(2,1)} async-done(((bf16[8,256,256]{2,1,0:T(8,128)(2,1)}), bf16[8,256,256]{2,1,0:T(8,128)(2,1)}, u32[]{:S(2)}, u32[]{:S(2)}) %all-to-all-start.3) | async-done | bytes 1048608 | tf_op jit(solution)/shard_map/all_to_all | solution.py:153
  180.2 6.1 %convolution_bitcast_fusion = f32[2048,256]{1,0:T(8,128)S(1)} fusion(bf16[8,256,256]{2,1,0:T(8,128)(2,1)} %all-to-all-done.3, bf16[1024,8,256]{2,0,1:T(8,128)(2,1)} %copy.9, bf16[1024,8,256]{2,0,1:T(8,128)(2,1)} %copy.8), kind=kOutput, calls=%fused_computation.11 | convolution fusion | flops 2164260864 | bytes 11534336 | tf_op jit(solution)/shard_map/fjm,jmc->fc/dot_general | solution.py:154
  187.0 1.5 collective-permute-start.7
  189.5 1.5 collective-permute-start.5
  191.6 10.2 %collective-permute-done.7 = bf16[2048,128]{1,0:T(8,128)(2,1)S(1)} collective-permute-done((bf16[2048,128]{1,0:T(8,128)(2,1)S(1)}, bf16[2048,128]{1,0:T(8,128)(2,1)S(1)}, u32[]{:S(2)}, u32[]{:S(2)}) %collective-permute-start.7) | collective-permute-done | bytes 524320 | tf_op jit(solution)/shard_map/ppermute | solution.py:156
  201.8 1.4 collective-permute-done.8
  203.2 0.8 fusion.17
  204.0 0.8 fusion.18
  205.0 5.4 %collective-permute-done.5 = bf16[2048,128]{1,0:T(8,128)(2,1)S(1)} collective-permute-done((bf16[2048,128]{1,0:T(8,128)(2,1)S(1)}, bf16[2048,128]{1,0:T(8,128)(2,1)S(1)}, u32[]{:S(2)}, u32[]{:S(2)}) %collective-permute-start.5) | collective-permute-done | bytes 524320 | tf_op jit(solution)/shard_map/ppermute | solution.py:156
  210.5 1.9 collective-permute-done.6
  212.3 0.8 fusion.19
  213.1 0.8 fusion.20
  214.2 0.9 copy-done.3
  216.3 2.1 copy.11
  218.4 1.9 fusion.47
  220.3 1.9 fusion.46
  222.8 2.5 multiply_subtract_fusion
  225.3 7.6 %bitcast_multiply_fusion = (f32[2048,1024]{0,1:T(8,128)}, f32[2048,1024]{0,1:T(8,128)}) fusion(f32[2048,16,64]{0,2,1:T(8,128)S(1)} %get-tuple-element.54, f32[1024]{0:T(1024)S(1)} %fusion.73, f32[2048,16,64]{0,2,1:T(8,128)S(1)} %get-tuple-element.53, f32[1024]{0:T(1024)S(1)} %select_multiply_fusion), kind=kLoop, calls=%fused_computation.5 | loop fusion | flops 4194304 | bytes 33562624 | tf_op jit(solution)/shard_map/mul | solution.py:42
  232.9 15.8 %reduce-scatter.4.cloned.1.call-done = f32[64,2048]{1,0:T(8,128)} async-done(((f32[256,2048]{1,0:T(8,128)}), f32[64,2048]{1,0:T(8,128)}) %reduce-scatter.4.cloned.1.call-update) | async-done | bytes 524304
  248.7 8.6 %fusion.4 = bf16[2048,64]{0,1:T(8,128)(2,1)S(1)} fusion(f32[2048,1024]{0,1:T(8,128)} %get-tuple-element.72, f32[2048,1024]{0,1:T(8,128)} %get-tuple-element.73, f32[64,2048]{1,0:T(8,128)} %reduce-scatter.4.cloned.1.call-done), kind=kOutput, calls=%fused_computation.15 | convolution fusion | flops 1614938112 | bytes 17563648 | tf_op jit(solution)/shard_map/dot_general | solution.py:167
  257.3 8.4 %all_to_all.44 = bf16[4,512,64]{1,2,0:T(8,128)(2,1)S(1)} all-to-all(bf16[4,512,64]{1,2,0:T(8,128)(2,1)S(1)} %bitcast.99), channel_id=1, replica_groups=mesh['tile'=8,'win'=4] {'win'}, dimensions={0} | all-to-all | bytes 524288 | tf_op jit(solution)/shard_map/all_to_all | solution.py:168
  266.1 22.6 %all_to_all.45 = bf16[8,80,512]{2,1,0:T(8,128)(2,1)S(1)} all-to-all(bf16[8,80,512]{2,1,0:T(8,128)(2,1)S(1)} %bitcast.98), channel_id=1, replica_groups=mesh['tile'=8,'win'=4] {'tile'}, dimensions={0} | all-to-all | bytes 1310720 | tf_op jit(solution)/shard_map/all_to_all | solution.py:178
  288.8 0.8 copy-done.12
  (88 shorter events, 8.8 us)
Async XLA Ops:
  6.5 6.0 %copy-start = (bf16[4,256,2048]{2,1,0:T(8,128)(2,1)S(1)}, bf16[4,256,2048]{2,1,0:T(8,128)(2,1)}, u32[]{:S(2)}) copy-start(bf16[4,256,2048]{2,1,0:T(8,128)(2,1)} %param.4) | copy-start | bytes 12582916
  11.7 14.0 %copy-start.13 = (s32[256,1]{0,1:T(1,128)S(1)}, s32[256,1]{0,1:T(1,128)}, u32[]{:S(2)}) copy-start(s32[256,1]{0,1:T(1,128)} %param.7) | copy-start | bytes 3076
  11.7 14.0 %copy-start.14 = (s32[256]{0:T(256)S(1)}, s32[256]{0:T(256)}, u32[]{:S(2)}) copy-start(s32[256]{0:T(256)} %param.6) | copy-start | bytes 3076
  11.7 14.0 %copy-start.15 = (s32[256]{0:T(256)S(1)}, s32[256]{0:T(256)}, u32[]{:S(2)}) copy-start(s32[256]{0:T(256)} %param.5) | copy-start | bytes 3076
  16.5 1.0 copy-start.10
  17.4 1.0 copy-start.11
  18.4 33.1 %all-to-all-start.1 = ((bf16[8,256,256]{2,1,0:T(8,128)(2,1)}), bf16[8,256,256]{2,1,0:T(8,128)(2,1)S(1)}, u32[]{:S(2)}, u32[]{:S(2)}) async-start(bf16[8,256,256]{2,1,0:T(8,128)(2,1)} %get-tuple-element.13), calls=%async_computation.1 | async-start | bytes 2097152 | tf_op jit(solution)/shard_map/all_to_all | solution.py:153
  25.8 48.5 %collective-permute-start = (s32[3,256]{1,0:T(4,128)S(1)}, s32[3,256]{1,0:T(4,128)S(1)}, u32[]{:S(2)}, u32[]{:S(2)}) collective-permute-start(s32[3,256]{1,0:T(4,128)S(1)} %pad_add_fusion), channel_id=1, source_target_pairs={{0,0},{4,4},{8,12},{12,20},{16,28},{20,24},{24,16},{28,8},{1,1},{5... | collective-permute-start | bytes 9224 | tf_op jit(solution)/shard_map/ppermute | solution.py:131
  51.5 29.8 %all-to-all-start = ((bf16[8,256,256]{2,1,0:T(8,128)(2,1)}), bf16[8,256,256]{2,1,0:T(8,128)(2,1)}, u32[]{:S(2)}, u32[]{:S(2)}) async-start(bf16[8,256,256]{2,1,0:T(8,128)(2,1)} %get-tuple-element.14), calls=%async_computation | async-start | bytes 2097152 | tf_op jit(solution)/shard_map/all_to_all | solution.py:153
  88.1 12.1 %collective-permute-start.1 = (bf16[2048,128]{1,0:T(8,128)(2,1)S(1)}, bf16[2048,128]{1,0:T(8,128)(2,1)S(1)}, u32[]{:S(2)}, u32[]{:S(2)}) collective-permute-start(bf16[2048,128]{1,0:T(8,128)(2,1)S(1)} %get-tuple-element.61), channel_id=1, source_target_pairs={{0,4},{4,12},{12,20},{20,28},{28,24},{24,16},{16,8},{8,0},{1,5},{5... | collective-permute-start | bytes 1572872 | tf_op jit(solution)/shard_map/ppermute | solution.py:156
  89.4 12.7 %collective-permute-start.2 = (bf16[2048,128]{1,0:T(8,128)(2,1)S(1)}, bf16[2048,128]{1,0:T(8,128)(2,1)S(1)}, u32[]{:S(2)}, u32[]{:S(2)}) collective-permute-start(bf16[2048,128]{1,0:T(8,128)(2,1)S(1)} %get-tuple-element.62), channel_id=1, source_target_pairs={{0,8},{4,0},{12,4},{20,12},{28,20},{24,28},{16,24},{8,16},{1,9},{5... | collective-permute-start | bytes 1572872 | tf_op jit(solution)/shard_map/ppermute | solution.py:157
  91.6 44.6 %copy-start.6 = (bf16[2048,256]{1,0:T(8,128)(2,1)S(1)}, bf16[2048,256]{1,0:T(8,128)(2,1)}, u32[]{:S(2)}) copy-start(bf16[2048,256]{1,0:T(8,128)(2,1)} %fusion.10) | copy-start | bytes 3145732
  100.3 1.8 copy-start.16
  102.1 0.8 copy-start.18
  102.9 42.0 %all-to-all-start.2 = ((bf16[8,256,256]{2,1,0:T(8,128)(2,1)}), bf16[8,256,256]{2,1,0:T(8,128)(2,1)}, u32[]{:S(2)}, u32[]{:S(2)}) async-start(bf16[8,256,256]{2,1,0:T(8,128)(2,1)} %copy-done.11), calls=%async_computation.2 | async-start | bytes 2097152 | tf_op jit(solution)/shard_map/all_to_all | solution.py:153
  108.7 27.5 %collective-permute-start.3 = (bf16[2048,128]{1,0:T(8,128)(2,1)S(1)}, bf16[2048,128]{1,0:T(8,128)(2,1)}, u32[]{:S(2)}, u32[]{:S(2)}) collective-permute-start(bf16[2048,128]{1,0:T(8,128)(2,1)S(1)} %get-tuple-element.59), channel_id=1, source_target_pairs={{0,4},{4,12},{12,20},{20,28},{28,24},{24,16},{16,8},{8,0},{1,5},{5... | collective-permute-start | bytes 1572872 | tf_op jit(solution)/shard_map/ppermute | solution.py:156
  110.7 25.4 %collective-permute-start.4 = (bf16[2048,128]{1,0:T(8,128)(2,1)S(1)}, bf16[2048,128]{1,0:T(8,128)(2,1)}, u32[]{:S(2)}, u32[]{:S(2)}) collective-permute-start(bf16[2048,128]{1,0:T(8,128)(2,1)S(1)} %get-tuple-element.60), channel_id=1, source_target_pairs={{0,8},{4,0},{12,4},{20,12},{28,20},{24,28},{16,24},{8,16},{1,9},{5... | collective-permute-start | bytes 1572872 | tf_op jit(solution)/shard_map/ppermute | solution.py:157
  111.8 27.7 %copy-start.17 = (bf16[2048,128]{1,0:T(8,128)(2,1)S(1)}, bf16[2048,128]{1,0:T(8,128)(2,1)}, u32[]{:S(2)}) copy-start(bf16[2048,128]{1,0:T(8,128)(2,1)} %copy-done.16) | copy-start | bytes 1572868
  111.8 27.7 %copy-start.19 = (bf16[2048,128]{1,0:T(8,128)(2,1)S(1)}, bf16[2048,128]{1,0:T(8,128)(2,1)}, u32[]{:S(2)}) copy-start(bf16[2048,128]{1,0:T(8,128)(2,1)} %copy-done.18) | copy-start | bytes 1572868
  144.9 11.6 %copy-start.8 = (f32[2048,256]{1,0:T(8,128)S(1)}, f32[2048,256]{1,0:T(8,128)}, u32[]{:S(2)}) copy-start(f32[2048,256]{1,0:T(8,128)} %fusion.22) | copy-start | bytes 6291460
  144.9 35.2 %all-to-all-start.3 = ((bf16[8,256,256]{2,1,0:T(8,128)(2,1)}), bf16[8,256,256]{2,1,0:T(8,128)(2,1)}, u32[]{:S(2)}, u32[]{:S(2)}) async-start(bf16[8,256,256]{2,1,0:T(8,128)(2,1)} %copy-done.10), calls=%async_computation.3 | async-start | bytes 2097152 | tf_op jit(solution)/shard_map/all_to_all | solution.py:153
  154.4 94.4 %reduce-scatter.4.cloned.1.call-start = ((), (), s32[]{:S(2)}) async-start(), calls=%async_computation.7 | async-start | bytes 2621440
  154.4 2.1 copy-start.9
  156.5 2.0 copy-start.7
  156.6 3.6 %copy-start.2 = (bf16[1024,8,256]{2,0,1:T(8,128)(2,1)S(1)}, bf16[1024,8,256]{2,0,1:T(8,128)(2,1)}, u32[]{:S(2)}) copy-start(bf16[1024,8,256]{2,0,1:T(8,128)(2,1)} %copy.9) | copy-start | bytes 12582916
  158.5 3.4 %copy-start.1 = (bf16[1024,8,256]{2,0,1:T(8,128)(2,1)S(1)}, bf16[1024,8,256]{2,0,1:T(8,128)(2,1)}, u32[]{:S(2)}) copy-start(bf16[1024,8,256]{2,0,1:T(8,128)(2,1)} %copy.8) | copy-start | bytes 12582916
  187.0 14.8 %collective-permute-start.7 = (bf16[2048,128]{1,0:T(8,128)(2,1)S(1)}, bf16[2048,128]{1,0:T(8,128)(2,1)S(1)}, u32[]{:S(2)}, u32[]{:S(2)}) collective-permute-start(bf16[2048,128]{1,0:T(8,128)(2,1)S(1)} %get-tuple-element.55), channel_id=1, source_target_pairs={{0,4},{4,12},{12,20},{20,28},{28,24},{24,16},{16,8},{8,0},{1,5},{5... | collective-permute-start | bytes 1572872 | tf_op jit(solution)/shard_map/ppermute | solution.py:156
  188.4 14.8 %collective-permute-start.8 = (bf16[2048,128]{1,0:T(8,128)(2,1)S(1)}, bf16[2048,128]{1,0:T(8,128)(2,1)S(1)}, u32[]{:S(2)}, u32[]{:S(2)}) collective-permute-start(bf16[2048,128]{1,0:T(8,128)(2,1)S(1)} %get-tuple-element.56), channel_id=1, source_target_pairs={{0,8},{4,0},{12,4},{20,12},{28,20},{24,28},{16,24},{8,16},{1,9},{5... | collective-permute-start | bytes 1572872 | tf_op jit(solution)/shard_map/ppermute | solution.py:157
  189.5 20.9 %collective-permute-start.5 = (bf16[2048,128]{1,0:T(8,128)(2,1)S(1)}, bf16[2048,128]{1,0:T(8,128)(2,1)S(1)}, u32[]{:S(2)}, u32[]{:S(2)}) collective-permute-start(bf16[2048,128]{1,0:T(8,128)(2,1)S(1)} %get-tuple-element.57), channel_id=1, source_target_pairs={{0,4},{4,12},{12,20},{20,28},{28,24},{24,16},{16,8},{8,0},{1,5},{5... | collective-permute-start | bytes 1572872 | tf_op jit(solution)/shard_map/ppermute | solution.py:156
  191.0 21.4 %collective-permute-start.6 = (bf16[2048,128]{1,0:T(8,128)(2,1)S(1)}, bf16[2048,128]{1,0:T(8,128)(2,1)S(1)}, u32[]{:S(2)}, u32[]{:S(2)}) collective-permute-start(bf16[2048,128]{1,0:T(8,128)(2,1)S(1)} %get-tuple-element.58), channel_id=1, source_target_pairs={{0,8},{4,0},{12,4},{20,12},{28,20},{24,28},{16,24},{8,16},{1,9},{5... | collective-permute-start | bytes 1572872 | tf_op jit(solution)/shard_map/ppermute | solution.py:157
  213.9 1.2 copy-start.3
  213.9 1.5 copy-start.4
  213.9 1.8 copy-start.5
  288.8 0.8 copy-start.12
Sparse Core Ops, SparseCore 0:
  218.5 30.1 reduce-scatter.3

commit v7 on v4

--- a/solution.py
+++ b/solution.py
@@ -3,6 +3,8 @@
 import jax
 import jax.numpy as jnp
 from jax import lax
+from jax.experimental import pallas as pl
+from jax.experimental.pallas import tpu as pltpu
 from jax.sharding import PartitionSpec as P
 
 BAND = 64
@@ -110,6 +112,44 @@
     return path if extend() else list(range(count))
 
 
+def block_moves(block_of, block, half, width):
+    moves = []
+    for place, b in enumerate(block_of):
+        low = b * block + half
+        if low + block <= width:
+            moves.append((low, place, 0, block))
+        else:
+            moves.append((low, place, 0, width - low))
+            moves.append((0, place, width - low, low + block - width))
+    return moves
+
+
+def lay_out_blocks(records, block_of, block, half):
+    segs, rows, width = records.shape
+    moves = block_moves(block_of, block, half, width)
+
+    def kernel(src, dst, sems):
+        copies = []
+        for index, (col, place, at, size) in enumerate(moves):
+            copy = pltpu.make_async_copy(
+                src.at[:, :, pl.ds(col, size)],
+                dst.at[:, place, :, pl.ds(at, size)],
+                sems.at[index],
+            )
+            copy.start()
+            copies.append(copy)
+        for copy in copies:
+            copy.wait()
+
+    return pl.pallas_call(
+        kernel,
+        out_shape=jax.ShapeDtypeStruct((segs, len(block_of), rows, block), records.dtype),
+        in_specs=[pl.BlockSpec(memory_space=pl.ANY)],
+        out_specs=pl.BlockSpec(memory_space=pl.ANY),
+        scratch_shapes=[pltpu.SemaphoreType.DMA((len(moves),))],
+    )(records)
+
+
 def make_per_device(ring):
     count = len(ring)
     block_of = [0] * count
@@ -133,20 +173,9 @@
         pick_first = (channel_ids == my_first[None, :]).astype(jnp.bfloat16)
         pick_second = (channel_ids == (my_first + my_offset)[None, :]).astype(jnp.bfloat16)
         cross = None
+        laid_out = lay_out_blocks(records, block_of, block, half)
         for segment in range(records.shape[0]):
-            pieces = []
-            for b in block_of:
-                low = b * block + half
-                if low + block <= records.shape[2]:
-                    pieces.append(records[segment, :, low:low + block])
-                else:
-                    pieces.append(
-                        jnp.concatenate(
-                            [records[segment, :, low:], records[segment, :, : low + block - records.shape[2]]],
-                            axis=1,
-                        )
-                    )
-            outgoing = jnp.stack(pieces, axis=0)
+            outgoing = laid_out[segment]
             received = lax.all_to_all(outgoing, "tile", split_axis=0, concat_axis=0, tiled=True)
             spectra = jnp.einsum("fjm,jmc->fc", forward, received, preferred_element_type=jnp.float32)
             whitened = whiten(spectra, BAND)
@@ -160,7 +189,7 @@
         lag_count = length // win_count
         stacked = lax.psum(cross, "win")
         inverse = inverse_matrix(length, lax.axis_index("win") * lag_count, lag_count, seg_total)
-        correlation = jnp.dot(inverse, stacked, precision=lax.Precision.HIGHEST)
+        correlation = jnp.dot(inverse, stacked, precision=lax.Precision.HIGH)
         capacity = 5 * pair_first.shape[0] // (2 * tile_count)
         chooser = bucket_select(my_owners, tile_count, capacity)
         picked = lax.dot_general(

time: 276 us -> 394 us (1.43)
  Pallas kernels: 0 us -> 128 us
  local copies, waits for them, and re-layouts: 29 us -> 24 us
    pallas_call x0 -> x1, Pallas kernels: none -> 128 us  [lay_out_blocks(): pl.pallas_call(kernel, out_shape=jax.ShapeDtypeStruct((segs, len(block_of...]
    unnamed x26 -> x18, local copies, waits for them, and re-layouts: 10.3 us -> 2.9 us
  transfers between devices with their start and end apart: 14 -> 14, of which waited for: 7 -> 7; matrix products, arithmetic and copies ran while one was open for 24% -> 17% of each run, Pallas kernels for 0% -> 0%
where the time goes in v7:
time: 394 us; the launch traced here: 393 us
  Pallas kernels  128 us (32%)
  waiting for transfers between devices  118 us (30%)
  matrix products  43.2 us (11%)
  starting transfers between devices  27.9 us (7%)
  local copies, waits for them, and re-layouts  24 us (6%)
  blocking collectives  22.8 us (6%)
  other arithmetic  15.5 us (4%)
  between operations  13.9 us (4%)
    pallas_call x1, Pallas kernels, lay_out_blocks(): pl.pallas_call(kernel, out_shape=jax.ShapeDtypeStruct((segs, len(block_of...  128 us
    all_to_all x4, waiting for transfers between devices, per_device(): lax.all_to_all(outgoing, 'tile', split_axis=0, concat_axis=0, tiled=True)  61 us
    psum x1, waiting for transfers between devices, per_device(): stacked = lax.psum(cross, 'win')  49.1 us
    dot_general x4, matrix products, per_device(): jnp.einsum('fjm,jmc->fc', forward, received, preferred_element_type=jnp.f...  24.2 us
    all_to_all x1, blocking collectives, per_device(): lax.all_to_all(buckets, 'tile', split_axis=0, concat_axis=0, tiled=True)  22.8 us
    all_to_all x4, starting transfers between devices, per_device(): lax.all_to_all(outgoing, 'tile', split_axis=0, concat_axis=0, tiled=True)  19 us
  transfers between devices with their start and end apart: 14, of which 7 were waited for; matrix products, arithmetic and copies ran while one was open for 17% of the time, Pallas kernels for 0%

profile of v7, /device:TPU:0, one launch (start us, length us, event | category | flops | bytes accessed | tf_op | source)
XLA Modules:
  0.0 393.3 jit_solution(13741044656202685459)
XLA Ops:
  6.5 128.2 %shard_map.46 = bf16[4,8,256,256]{3,2,1,0:T(8,128)(2,1)} custom-call(bf16[4,256,2048]{2,1,0:T(8,128)(2,1)} %src.1), custom_call_target="tpu_custom_call" | custom-call | tf_op jit(solution)/shard_map/pallas_call | solution.py:144
  134.8 4.3 %slice_bitcast_fusion = (bf16[8,256,256]{2,1,0:T(8,128)(2,1)}, bf16[8,256,256]{2,1,0:T(8,128)(2,1)}, bf16[8,256,256]{2,1,0:T(8,128)(2,1)}, bf16[8,256,256]{2,1,0:T(8,128)(2,1)}) fusion(bf16[4,8,256,256]{3,2,1,0:T(8,128)(2,1)} %shard_map.46), kind=kLoop, calls=%fused_computation.35 | loop fusion | bytes 8388608 | tf_op jit(solution)/shard_map/squeeze | solution.py:178
  139.0 7.5 %all-to-all-start.3 = ((bf16[8,256,256]{2,1,0:T(8,128)(2,1)}), bf16[8,256,256]{2,1,0:T(8,128)(2,1)S(1)}, u32[]{:S(2)}, u32[]{:S(2)}) async-start(bf16[8,256,256]{2,1,0:T(8,128)(2,1)} %get-tuple-element.7), calls=%async_computation.3 | async-start | bytes 2097152 | tf_op jit(solution)/shard_map/all_to_all | solution.py:179
  146.5 0.7 collective-permute-start
  147.2 1.0 fusion.46
  148.3 0.2 fusion.62
  148.5 0.6 fusion.55
  149.1 5.1 %subtract_convert_fusion = (bf16[1024,32,64]{0,2,1:T(8,128)(2,1)}, bf16[1024,32,64]{0,2,1:T(8,128)(2,1)}) fusion(f32[1024,64]{0,1:T(8,128)S(1)} %get-tuple-element.38, f32[1024,32]{0,1:T(8,128)S(1)} %get-tuple-element.37, f32[1024,64]{0,1:T(8,128)S(1)} %get-tuple-element.39, f32[1024,32]{0,1:T(8,128)S(1)} %get-tuple-element.36), kind=kLoop, calls=%fused_computation.2 | loop fusion | flops 18874368 | bytes 9175040 | tf_op jit(solution)/shard_map/convert.3
  154.2 6.5 %copy.5 = bf16[1024,8,256]{2,0,1:T(8,128)(2,1)} copy(bf16[1024,8,256]{0,2,1:T(8,128)(2,1)} %bitcast.58) | data formatting | bytes 8388608 | tf_op jit(solution)/shard_map/sub | solution.py:26
  160.6 6.6 %copy.6 = bf16[1024,8,256]{2,0,1:T(8,128)(2,1)} copy(bf16[1024,8,256]{0,2,1:T(8,128)(2,1)} %bitcast.57) | data formatting | bytes 8388608 | tf_op jit(solution)/shard_map/neg | solution.py:33
  167.2 0.6 reduce-window.6
  167.8 0.2 slice_reduce_fusion
  168.2 4.1 %all-to-all-done.3 = bf16[8,256,256]{2,1,0:T(8,128)(2,1)S(1)} async-done(((bf16[8,256,256]{2,1,0:T(8,128)(2,1)}), bf16[8,256,256]{2,1,0:T(8,128)(2,1)S(1)}, u32[]{:S(2)}, u32[]{:S(2)}) %all-to-all-start.3) | async-done | bytes 1048608 | tf_op jit(solution)/shard_map/all_to_all | solution.py:179
  172.3 3.8 all-to-all-start.2
  176.0 5.9 %convolution_bitcast_fusion = f32[2048,256]{1,0:T(8,128)S(1)} fusion(bf16[8,256,256]{2,1,0:T(8,128)(2,1)S(1)} %all-to-all-done.3, bf16[1024,8,256]{2,0,1:T(8,128)(2,1)} %copy.6, bf16[1024,8,256]{2,0,1:T(8,128)(2,1)} %copy.5), kind=kOutput, calls=%fused_computation.7 | convolution fusion | flops 2164260864 | bytes 11534336 | tf_op jit(solution)/shard_map/fjm,jmc->fc/dot_general | solution.py:180
  182.0 0.2 bitcast_reduce_fusion
  182.3 0.3 fusion.9
  182.6 1.1 fusion.75
  183.6 2.0 collective-permute-start.7
  185.7 17.5 %all-to-all-done.2 = bf16[8,256,256]{2,1,0:T(8,128)(2,1)S(1)} async-done(((bf16[8,256,256]{2,1,0:T(8,128)(2,1)}), bf16[8,256,256]{2,1,0:T(8,128)(2,1)S(1)}, u32[]{:S(2)}, u32[]{:S(2)}) %all-to-all-start.2) | async-done | bytes 1048608 | tf_op jit(solution)/shard_map/all_to_all | solution.py:179
  203.2 1.1 copy-done
  204.3 3.6 all-to-all-start.1
  207.8 6.1 %convolution_bitcast_fusion.1 = f32[2048,256]{1,0:T(8,128)S(1)} fusion(bf16[8,256,256]{2,1,0:T(8,128)(2,1)} %copy-done, bf16[1024,8,256]{2,0,1:T(8,128)(2,1)} %copy.6, bf16[1024,8,256]{2,0,1:T(8,128)(2,1)} %copy.5), kind=kOutput, calls=%fused_computation.8 | convolution fusion | flops 2164260864 | bytes 11534336 | tf_op jit(solution)/shard_map/fjm,jmc->fc/dot_general | solution.py:180
  214.0 0.2 bitcast_reduce_fusion.1
  214.3 0.3 fusion.8
  214.6 1.1 fusion.76
  215.7 1.9 collective-permute-start.5
  217.7 19.3 %all-to-all-done.1 = bf16[8,256,256]{2,1,0:T(8,128)(2,1)S(1)} async-done(((bf16[8,256,256]{2,1,0:T(8,128)(2,1)}), bf16[8,256,256]{2,1,0:T(8,128)(2,1)S(1)}, u32[]{:S(2)}, u32[]{:S(2)}) %all-to-all-start.1) | async-done | bytes 1048608 | tf_op jit(solution)/shard_map/all_to_all | solution.py:179
  237.0 4.2 %all-to-all-start = ((bf16[8,256,256]{2,1,0:T(8,128)(2,1)}), bf16[8,256,256]{2,1,0:T(8,128)(2,1)}, u32[]{:S(2)}, u32[]{:S(2)}) async-start(bf16[8,256,256]{2,1,0:T(8,128)(2,1)} %get-tuple-element.10), calls=%async_computation | async-start | bytes 2097152 | tf_op jit(solution)/shard_map/all_to_all | solution.py:179
  241.2 0.2 all-reduce.2.cloned.1.call-start
  241.4 5.9 %convolution_bitcast_fusion.2 = f32[2048,256]{1,0:T(8,128)S(1)} fusion(bf16[8,256,256]{2,1,0:T(8,128)(2,1)S(1)} %all-to-all-done.1, bf16[1024,8,256]{2,0,1:T(8,128)(2,1)} %copy.6, bf16[1024,8,256]{2,0,1:T(8,128)(2,1)} %copy.5), kind=kOutput, calls=%fused_computation.9 | convolution fusion | flops 2164260864 | bytes 11534336 | tf_op jit(solution)/shard_map/fjm,jmc->fc/dot_general | solution.py:180
  247.4 0.2 bitcast_reduce_fusion.2
  247.7 0.3 fusion.7
  248.0 1.0 fusion.77
  249.0 1.7 collective-permute-start.3
  250.7 20.1 %all-to-all-done = bf16[8,256,256]{2,1,0:T(8,128)(2,1)} async-done(((bf16[8,256,256]{2,1,0:T(8,128)(2,1)}), bf16[8,256,256]{2,1,0:T(8,128)(2,1)}, u32[]{:S(2)}, u32[]{:S(2)}) %all-to-all-start) | async-done | bytes 1048608 | tf_op jit(solution)/shard_map/all_to_all | solution.py:179
  270.8 6.1 %convolution_bitcast_fusion.3 = f32[2048,256]{1,0:T(8,128)S(1)} fusion(bf16[8,256,256]{2,1,0:T(8,128)(2,1)} %all-to-all-done, bf16[1024,8,256]{2,0,1:T(8,128)(2,1)} %copy.6, bf16[1024,8,256]{2,0,1:T(8,128)(2,1)} %copy.5), kind=kOutput, calls=%fused_computation.10 | convolution fusion | flops 2164260864 | bytes 11534336 | tf_op jit(solution)/shard_map/fjm,jmc->fc/dot_general | solution.py:180
  277.3 0.3 fusion.4
  277.7 0.9 copy-done.1
  278.6 2.0 collective-permute-start.1
  280.6 2.0 fusion.18
  282.6 2.0 fusion.17
  284.6 0.3 multiply_add_fusion.1
  284.9 0.3 collective-permute-start.2
  285.2 2.0 fusion.20
  287.1 2.0 fusion.19
  289.1 0.3 multiply_add_fusion.2
  289.4 4.0 %collective-permute-done.4 = bf16[2048,128]{1,0:T(8,128)(2,1)S(1)} collective-permute-done((bf16[2048,128]{1,0:T(8,128)(2,1)S(1)}, bf16[2048,128]{1,0:T(8,128)(2,1)S(1)}, u32[]{:S(2)}, u32[]{:S(2)}) %collective-permute-start.4) | collective-permute-done | bytes 524320 | tf_op jit(solution)/shard_map/ppermute | solution.py:183
  293.4 1.8 fusion.22
  295.2 1.8 fusion.21
  297.0 0.3 multiply_add_fusion.3
  297.3 3.7 collective-permute-done.2
  301.1 0.8 fusion.24
  301.8 0.8 fusion.23
  302.6 0.3 multiply_add_fusion.4
  302.9 1.9 fusion.6
  304.8 0.5 fusion.57
  305.3 0.6 multiply_subtract_fusion
  305.9 1.7 bitcast_multiply_fusion
  307.6 49.1 %all-reduce.2.cloned.1.call-done = f32[2048,256]{1,0:T(8,128)} async-done(((f32[2048,256]{1,0:T(8,128)}), f32[2048,256]{1,0:T(8,128)}) %all-reduce.2.cloned.1.call-update) | async-done | bytes 2097168 | tf_op jit(solution)/shard_map/psum | solution.py:190
  356.7 5.6 %fusion.10 = bf16[512,256]{1,0:T(8,128)(2,1)S(1)} fusion(f32[2048,256]{1,0:T(8,128)} %all-reduce.2.cloned.1.call-done, f32[512,1024]{0,1:T(8,128)S(1)} %get-tuple-element.40, f32[512,1024]{0,1:T(8,128)} %get-tuple-element.41), kind=kOutput, calls=%fused_computation.31 | convolution fusion | flops 1611792384 | bytes 6553600 | tf_op jit(solution)/shard_map/dot_general | solution.py:192
  362.3 0.4 convolution_convert_fusion
  362.7 22.8 %all_to_all.25 = bf16[8,80,512]{2,1,0:T(8,128)(2,1)S(1)} all-to-all(bf16[8,80,512]{2,1,0:T(8,128)(2,1)S(1)} %bitcast.63), channel_id=1, replica_groups=mesh['tile'=8,'win'=4] {'tile'}, dimensions={0} | all-to-all | bytes 1310720 | tf_op jit(solution)/shard_map/all_to_all | solution.py:202
  385.6 0.8 copy-done.2
  (49 shorter events, 1.0 us)
Async XLA Ops:
  139.0 7.5 %copy-start.3 = (s32[256,1]{0,1:T(1,128)S(1)}, s32[256,1]{0,1:T(1,128)}, u32[]{:S(2)}) copy-start(s32[256,1]{0,1:T(1,128)} %param.7) | copy-start | bytes 3076
  139.0 7.5 %copy-start.4 = (s32[256]{0:T(256)S(1)}, s32[256]{0:T(256)}, u32[]{:S(2)}) copy-start(s32[256]{0:T(256)} %param.6) | copy-start | bytes 3076
  139.0 7.5 %copy-start.5 = (s32[256]{0:T(256)S(1)}, s32[256]{0:T(256)}, u32[]{:S(2)}) copy-start(s32[256]{0:T(256)} %param.5) | copy-start | bytes 3076
  139.0 33.2 %all-to-all-start.3 = ((bf16[8,256,256]{2,1,0:T(8,128)(2,1)}), bf16[8,256,256]{2,1,0:T(8,128)(2,1)S(1)}, u32[]{:S(2)}, u32[]{:S(2)}) async-start(bf16[8,256,256]{2,1,0:T(8,128)(2,1)} %get-tuple-element.7), calls=%async_computation.3 | async-start | bytes 2097152 | tf_op jit(solution)/shard_map/all_to_all | solution.py:179
  146.5 20.7 %collective-permute-start = (s32[3,256]{1,0:T(4,128)S(1)}, s32[3,256]{1,0:T(4,128)S(1)}, u32[]{:S(2)}, u32[]{:S(2)}) collective-permute-start(s32[3,256]{1,0:T(4,128)S(1)} %pad_add_fusion), channel_id=1, source_target_pairs={{0,0},{4,4},{8,12},{12,20},{16,28},{20,24},{24,16},{28,8},{1,1},{5... | collective-permute-start | bytes 9224 | tf_op jit(solution)/shard_map/ppermute | solution.py:171
  172.3 30.9 %all-to-all-start.2 = ((bf16[8,256,256]{2,1,0:T(8,128)(2,1)}), bf16[8,256,256]{2,1,0:T(8,128)(2,1)S(1)}, u32[]{:S(2)}, u32[]{:S(2)}) async-start(bf16[8,256,256]{2,1,0:T(8,128)(2,1)} %get-tuple-element.8), calls=%async_computation.2 | async-start | bytes 2097152 | tf_op jit(solution)/shard_map/all_to_all | solution.py:179
  183.6 94.0 %collective-permute-start.7 = (bf16[2048,128]{1,0:T(8,128)(2,1)}, bf16[2048,128]{1,0:T(8,128)(2,1)}, u32[]{:S(2)}, u32[]{:S(2)}) collective-permute-start(bf16[2048,128]{1,0:T(8,128)(2,1)} %get-tuple-element.17), channel_id=1, source_target_pairs={{0,4},{4,12},{12,20},{20,28},{28,24},{24,16},{16,8},{8,0},{1,5},{5... | collective-permute-start | bytes 1572872 | tf_op jit(solution)/shard_map/ppermute | solution.py:182
  185.7 93.0 %collective-permute-start.8 = (bf16[2048,128]{1,0:T(8,128)(2,1)}, bf16[2048,128]{1,0:T(8,128)(2,1)}, u32[]{:S(2)}, u32[]{:S(2)}) collective-permute-start(bf16[2048,128]{1,0:T(8,128)(2,1)} %get-tuple-element.18), channel_id=1, source_target_pairs={{0,8},{4,0},{12,4},{20,12},{28,20},{24,28},{16,24},{8,16},{1,9},{5... | collective-permute-start | bytes 1572872 | tf_op jit(solution)/shard_map/ppermute | solution.py:183
  203.2 1.1 copy-start
  204.3 32.7 %all-to-all-start.1 = ((bf16[8,256,256]{2,1,0:T(8,128)(2,1)}), bf16[8,256,256]{2,1,0:T(8,128)(2,1)S(1)}, u32[]{:S(2)}, u32[]{:S(2)}) async-start(bf16[8,256,256]{2,1,0:T(8,128)(2,1)} %get-tuple-element.9), calls=%async_computation.1 | async-start | bytes 2097152 | tf_op jit(solution)/shard_map/all_to_all | solution.py:179
  215.7 69.2 %collective-permute-start.5 = (bf16[2048,128]{1,0:T(8,128)(2,1)}, bf16[2048,128]{1,0:T(8,128)(2,1)}, u32[]{:S(2)}, u32[]{:S(2)}) collective-permute-start(bf16[2048,128]{1,0:T(8,128)(2,1)} %get-tuple-element.19), channel_id=1, source_target_pairs={{0,4},{4,12},{12,20},{20,28},{28,24},{24,16},{16,8},{8,0},{1,5},{5... | collective-permute-start | bytes 1572872 | tf_op jit(solution)/shard_map/ppermute | solution.py:182
  217.6 67.6 %collective-permute-start.6 = (bf16[2048,128]{1,0:T(8,128)(2,1)}, bf16[2048,128]{1,0:T(8,128)(2,1)}, u32[]{:S(2)}, u32[]{:S(2)}) collective-permute-start(bf16[2048,128]{1,0:T(8,128)(2,1)} %get-tuple-element.20), channel_id=1, source_target_pairs={{0,8},{4,0},{12,4},{20,12},{28,20},{24,28},{16,24},{8,16},{1,9},{5... | collective-permute-start | bytes 1572872 | tf_op jit(solution)/shard_map/ppermute | solution.py:183
  237.0 33.9 %all-to-all-start = ((bf16[8,256,256]{2,1,0:T(8,128)(2,1)}), bf16[8,256,256]{2,1,0:T(8,128)(2,1)}, u32[]{:S(2)}, u32[]{:S(2)}) async-start(bf16[8,256,256]{2,1,0:T(8,128)(2,1)} %get-tuple-element.10), calls=%async_computation | async-start | bytes 2097152 | tf_op jit(solution)/shard_map/all_to_all | solution.py:179
  241.2 115.5 %all-reduce.2.cloned.1.call-start = ((), (), s32[]{:S(2)}) async-start(), calls=%async_computation.5 | async-start | bytes 4194304 | tf_op jit(solution)/shard_map/psum | solution.py:190
  249.0 40.4 %collective-permute-start.3 = (bf16[2048,128]{1,0:T(8,128)(2,1)}, bf16[2048,128]{1,0:T(8,128)(2,1)}, u32[]{:S(2)}, u32[]{:S(2)}) collective-permute-start(bf16[2048,128]{1,0:T(8,128)(2,1)} %get-tuple-element.21), channel_id=1, source_target_pairs={{0,4},{4,12},{12,20},{20,28},{28,24},{24,16},{16,8},{8,0},{1,5},{5... | collective-permute-start | bytes 1572872 | tf_op jit(solution)/shard_map/ppermute | solution.py:182
  277.6 1.0 copy-start.1
  278.6 14.8 %collective-permute-start.4 = (bf16[2048,128]{1,0:T(8,128)(2,1)S(1)}, bf16[2048,128]{1,0:T(8,128)(2,1)S(1)}, u32[]{:S(2)}, u32[]{:S(2)}) collective-permute-start(bf16[2048,128]{1,0:T(8,128)(2,1)S(1)} %copy-done.1), channel_id=1, source_target_pairs={{0,8},{4,0},{12,4},{20,12},{28,20},{24,28},{16,24},{8,16},{1,9},{5... | collective-permute-start | bytes 1572872 | tf_op jit(solution)/shard_map/ppermute | solution.py:183
  278.6 18.7 %collective-permute-start.1 = (bf16[2048,128]{1,0:T(8,128)(2,1)S(1)}, bf16[2048,128]{1,0:T(8,128)(2,1)S(1)}, u32[]{:S(2)}, u32[]{:S(2)}) collective-permute-start(bf16[2048,128]{1,0:T(8,128)(2,1)S(1)} %get-tuple-element.23), channel_id=1, source_target_pairs={{0,4},{4,12},{12,20},{20,28},{28,24},{24,16},{16,8},{8,0},{1,5},{5... | collective-permute-start | bytes 1572872 | tf_op jit(solution)/shard_map/ppermute | solution.py:182
  284.9 16.2 %collective-permute-start.2 = (bf16[2048,128]{1,0:T(8,128)(2,1)S(1)}, bf16[2048,128]{1,0:T(8,128)(2,1)S(1)}, u32[]{:S(2)}, u32[]{:S(2)}) collective-permute-start(bf16[2048,128]{1,0:T(8,128)(2,1)S(1)} %get-tuple-element.24), channel_id=1, source_target_pairs={{0,8},{4,0},{12,4},{20,12},{28,20},{24,28},{16,24},{8,16},{1,9},{5... | collective-permute-start | bytes 1572872 | tf_op jit(solution)/shard_map/ppermute | solution.py:183
  385.6 0.8 copy-start.2
Sparse Core Ops, SparseCore 0:
  304.9 51.7 all-reduce.1

commit v8 on v4

--- a/solution.py
+++ b/solution.py
@@ -110,6 +110,16 @@
     return path if extend() else list(range(count))
 
 
+def hierarchical_sum(value, win_count):
+    if win_count % 2:
+        return lax.psum(value, "win")
+    near = [[2 * i, 2 * i + 1] for i in range(win_count // 2)]
+    far = [list(range(c, win_count, 2)) for c in range(2)]
+    part = lax.psum_scatter(value, "win", scatter_dimension=1, tiled=True, axis_index_groups=near)
+    part = lax.psum(part, "win", axis_index_groups=far)
+    return lax.all_gather(part, "win", axis=1, tiled=True, axis_index_groups=near)
+
+
 def make_per_device(ring):
     count = len(ring)
     block_of = [0] * count
@@ -158,9 +168,9 @@
             term = cross_terms(first_part, second_part)
             cross = term if cross is None else cross + term
         lag_count = length // win_count
-        stacked = lax.psum(cross, "win")
+        stacked = hierarchical_sum(cross, win_count)
         inverse = inverse_matrix(length, lax.axis_index("win") * lag_count, lag_count, seg_total)
-        correlation = jnp.dot(inverse, stacked, precision=lax.Precision.HIGHEST)
+        correlation = jnp.dot(inverse, stacked, precision=lax.Precision.HIGH)
         capacity = 5 * pair_first.shape[0] // (2 * tile_count)
         chooser = bucket_select(my_owners, tile_count, capacity)
         picked = lax.dot_general(

time: 276 us -> 287 us (1.040)
  waiting for transfers between devices: 118 us -> 133 us
  matrix products: 46.4 us -> 42.9 us
    reduce_scatter x0 -> x1, waiting for transfers between devices: none -> 10 us  [hierarchical_sum(): lax.psum_scatter(value, 'win', scatter_dimension=1, tiled=True, axis_inde...]
    all_gather x0 -> x1, waiting for transfers between devices: none -> 8.63 us  [hierarchical_sum(): lax.all_gather(part, 'win', axis=1, tiled=True, axis_index_groups=near)]
    psum x1, waiting for transfers between devices: 49.1 us -> 43.6 us  [hierarchical_sum(): part = lax.psum(part, 'win', axis_index_groups=far)]
    dot_general x1, matrix products: 8.89 us -> 5.65 us  [per_device(): correlation = jnp.dot(inverse, stacked, precision=lax.Precision.HIGH)]
    unnamed x26 -> x24, local copies, waits for them, and re-layouts: 10.3 us -> 9.19 us
  transfers between devices with their start and end apart: 14 -> 16, of which waited for: 7 -> 9; matrix products, arithmetic and copies ran while one was open for 24% -> 23% of each run, Pallas kernels for 0% -> 0%
where the time goes in v8:
time: 287 us; the launch traced here: 286 us
  waiting for transfers between devices  133 us (46%)
  matrix products  42.9 us (15%)
  starting transfers between devices  27.9 us (10%)
  local copies, waits for them, and re-layouts  27.8 us (10%)
  blocking collectives  23.7 us (8%)
  other arithmetic  16.8 us (6%)
  between operations  13.6 us (5%)
    all_to_all x4, waiting for transfers between devices, per_device(): lax.all_to_all(outgoing, 'tile', split_axis=0, concat_axis=0, tiled=True)  62.7 us
    psum x1, waiting for transfers between devices, hierarchical_sum(): part = lax.psum(part, 'win', axis_index_groups=far)  43.6 us
    dot_general x4, matrix products, per_device(): jnp.einsum('fjm,jmc->fc', forward, received, preferred_element_type=jnp.f...  23.9 us
    all_to_all x1, blocking collectives, per_device(): lax.all_to_all(buckets, 'tile', split_axis=0, concat_axis=0, tiled=True)  23.7 us
    all_to_all x4, starting transfers between devices, per_device(): lax.all_to_all(outgoing, 'tile', split_axis=0, concat_axis=0, tiled=True)  18.9 us
    reduce_scatter x1, waiting for transfers between devices, hierarchical_sum(): lax.psum_scatter(value, 'win', scatter_dimension=1, tiled=True, axis_inde...  10 us
    unnamed x24, local copies, waits for them, and re-layouts  9.19 us
    all_gather x1, waiting for transfers between devices, hierarchical_sum(): lax.all_gather(part, 'win', axis=1, tiled=True, axis_index_groups=near)  8.63 us
  transfers between devices with their start and end apart: 16, of which 9 were waited for; matrix products, arithmetic and copies ran while one was open for 23% of the time, Pallas kernels for 0%

profile of v8, /device:TPU:0, one launch (start us, length us, event | category | flops | bytes accessed | tf_op | source)
XLA Modules:
  0.0 285.6 jit_solution(2620884884012761832)
XLA Ops:
  6.5 2.1 slice_dynamic-update-slice_fusion.7
  8.6 1.1 slice_bitcast_fusion.1
  9.7 1.9 slice_dynamic-update-slice_fusion.6
  11.7 0.7 fusion.46
  12.4 0.7 fusion.48
  13.1 0.8 slice_dynamic-update-slice_fusion.5
  14.0 0.8 slice_dynamic-update-slice_fusion.4
  14.8 0.8 slice_dynamic-update-slice_fusion.3
  15.6 0.8 slice_dynamic-update-slice_fusion.2
  16.5 0.8 slice_dynamic-update-slice_fusion.1
  17.3 7.3 %all-to-all-start.3 = ((bf16[8,256,256]{2,1,0:T(8,128)(2,1)}), bf16[8,256,256]{2,1,0:T(8,128)(2,1)S(1)}, u32[]{:S(2)}, u32[]{:S(2)}) async-start(bf16[8,256,256]{2,1,0:T(8,128)(2,1)} %get-tuple-element.7), calls=%async_computation.3 | async-start | bytes 2097152 | tf_op jit(solution)/shard_map/all_to_all | solution.py:160
  24.7 0.7 collective-permute-start
  25.3 1.0 fusion.50
  26.4 0.6 fusion.59
  27.0 5.1 %subtract_convert_fusion = (bf16[1024,32,64]{0,2,1:T(8,128)(2,1)}, bf16[1024,32,64]{0,2,1:T(8,128)(2,1)}) fusion(f32[1024,64]{0,1:T(8,128)S(1)} %get-tuple-element.74, f32[1024,32]{0,1:T(8,128)S(1)} %get-tuple-element.69, f32[1024,64]{0,1:T(8,128)S(1)} %get-tuple-element.75, f32[1024,32]{0,1:T(8,128)S(1)} %get-tuple-element.68), kind=kLoop, calls=%fused_computation.2 | loop fusion | flops 18874368 | bytes 9175040 | tf_op jit(solution)/shard_map/convert.3
  32.0 6.4 %copy.5 = bf16[1024,8,256]{2,0,1:T(8,128)(2,1)} copy(bf16[1024,8,256]{0,2,1:T(8,128)(2,1)} %bitcast.82) | data formatting | bytes 8388608 | tf_op jit(solution)/shard_map/sub | solution.py:24
  38.5 6.5 %copy.6 = bf16[1024,8,256]{2,0,1:T(8,128)(2,1)} copy(bf16[1024,8,256]{0,2,1:T(8,128)(2,1)} %bitcast.81) | data formatting | bytes 8388608 | tf_op jit(solution)/shard_map/neg | solution.py:31
  45.0 0.6 reduce-window.6
  45.9 4.4 %all-to-all-done.3 = bf16[8,256,256]{2,1,0:T(8,128)(2,1)S(1)} async-done(((bf16[8,256,256]{2,1,0:T(8,128)(2,1)}), bf16[8,256,256]{2,1,0:T(8,128)(2,1)S(1)}, u32[]{:S(2)}, u32[]{:S(2)}) %all-to-all-start.3) | async-done | bytes 1048608 | tf_op jit(solution)/shard_map/all_to_all | solution.py:160
  50.4 3.8 %all-to-all-start.2 = ((bf16[8,256,256]{2,1,0:T(8,128)(2,1)}), bf16[8,256,256]{2,1,0:T(8,128)(2,1)S(1)}, u32[]{:S(2)}, u32[]{:S(2)}) async-start(bf16[8,256,256]{2,1,0:T(8,128)(2,1)} %get-tuple-element.8), calls=%async_computation.2 | async-start | bytes 2097152 | tf_op jit(solution)/shard_map/all_to_all | solution.py:160
  54.1 5.9 %convolution_bitcast_fusion = f32[2048,256]{1,0:T(8,128)S(1)} fusion(bf16[8,256,256]{2,1,0:T(8,128)(2,1)S(1)} %all-to-all-done.3, bf16[1024,8,256]{2,0,1:T(8,128)(2,1)} %copy.6, bf16[1024,8,256]{2,0,1:T(8,128)(2,1)} %copy.5), kind=kOutput, calls=%fused_computation.7 | convolution fusion | flops 2164260864 | bytes 11534336 | tf_op jit(solution)/shard_map/fjm,jmc->fc/dot_general | solution.py:161
  60.4 0.3 fusion.9
  60.7 1.1 fusion.79
  61.8 2.0 collective-permute-start.7
  63.8 17.5 %all-to-all-done.2 = bf16[8,256,256]{2,1,0:T(8,128)(2,1)S(1)} async-done(((bf16[8,256,256]{2,1,0:T(8,128)(2,1)}), bf16[8,256,256]{2,1,0:T(8,128)(2,1)S(1)}, u32[]{:S(2)}, u32[]{:S(2)}) %all-to-all-start.2) | async-done | bytes 1048608 | tf_op jit(solution)/shard_map/all_to_all | solution.py:160
  81.3 3.6 %all-to-all-start.1 = ((bf16[8,256,256]{2,1,0:T(8,128)(2,1)}), bf16[8,256,256]{2,1,0:T(8,128)(2,1)S(1)}, u32[]{:S(2)}, u32[]{:S(2)}) async-start(bf16[8,256,256]{2,1,0:T(8,128)(2,1)} %get-tuple-element.9), calls=%async_computation.1 | async-start | bytes 2097152 | tf_op jit(solution)/shard_map/all_to_all | solution.py:160
  84.9 5.9 %convolution_bitcast_fusion.1 = f32[2048,256]{1,0:T(8,128)S(1)} fusion(bf16[8,256,256]{2,1,0:T(8,128)(2,1)S(1)} %all-to-all-done.2, bf16[1024,8,256]{2,0,1:T(8,128)(2,1)} %copy.6, bf16[1024,8,256]{2,0,1:T(8,128)(2,1)} %copy.5), kind=kOutput, calls=%fused_computation.8 | convolution fusion | flops 2164260864 | bytes 11534336 | tf_op jit(solution)/shard_map/fjm,jmc->fc/dot_general | solution.py:161
  91.1 0.3 fusion.8
  91.4 1.0 fusion.80
  92.5 1.9 collective-permute-start.5
  94.5 20.6 %all-to-all-done.1 = bf16[8,256,256]{2,1,0:T(8,128)(2,1)S(1)} async-done(((bf16[8,256,256]{2,1,0:T(8,128)(2,1)}), bf16[8,256,256]{2,1,0:T(8,128)(2,1)S(1)}, u32[]{:S(2)}, u32[]{:S(2)}) %all-to-all-start.1) | async-done | bytes 1048608 | tf_op jit(solution)/shard_map/all_to_all | solution.py:160
  115.1 4.3 %all-to-all-start = ((bf16[8,256,256]{2,1,0:T(8,128)(2,1)}), bf16[8,256,256]{2,1,0:T(8,128)(2,1)}, u32[]{:S(2)}, u32[]{:S(2)}) async-start(bf16[8,256,256]{2,1,0:T(8,128)(2,1)} %get-tuple-element.10), calls=%async_computation | async-start | bytes 2097152 | tf_op jit(solution)/shard_map/all_to_all | solution.py:160
  119.6 5.9 %convolution_bitcast_fusion.2 = f32[2048,256]{1,0:T(8,128)S(1)} fusion(bf16[8,256,256]{2,1,0:T(8,128)(2,1)S(1)} %all-to-all-done.1, bf16[1024,8,256]{2,0,1:T(8,128)(2,1)} %copy.6, bf16[1024,8,256]{2,0,1:T(8,128)(2,1)} %copy.5), kind=kOutput, calls=%fused_computation.9 | convolution fusion | flops 2164260864 | bytes 11534336 | tf_op jit(solution)/shard_map/fjm,jmc->fc/dot_general | solution.py:161
  125.8 0.3 fusion.7
  126.1 1.1 fusion.81
  127.2 1.7 collective-permute-start.3
  128.8 20.1 %all-to-all-done = bf16[8,256,256]{2,1,0:T(8,128)(2,1)} async-done(((bf16[8,256,256]{2,1,0:T(8,128)(2,1)}), bf16[8,256,256]{2,1,0:T(8,128)(2,1)}, u32[]{:S(2)}, u32[]{:S(2)}) %all-to-all-start) | async-done | bytes 1048608 | tf_op jit(solution)/shard_map/all_to_all | solution.py:160
  148.9 6.1 %convolution_bitcast_fusion.3 = f32[2048,256]{1,0:T(8,128)S(1)} fusion(bf16[8,256,256]{2,1,0:T(8,128)(2,1)} %all-to-all-done, bf16[1024,8,256]{2,0,1:T(8,128)(2,1)} %copy.6, bf16[1024,8,256]{2,0,1:T(8,128)(2,1)} %copy.5), kind=kOutput, calls=%fused_computation.10 | convolution fusion | flops 2164260864 | bytes 11534336 | tf_op jit(solution)/shard_map/fjm,jmc->fc/dot_general | solution.py:161
  155.4 0.3 fusion.4
  155.8 0.9 copy-done.1
  156.7 2.0 collective-permute-start.1
  158.8 2.0 fusion.18
  160.7 2.0 fusion.17
  162.7 0.3 multiply_add_fusion.1
  163.0 0.3 collective-permute-start.2
  163.3 2.0 fusion.20
  165.3 2.0 fusion.19
  167.5 4.0 %collective-permute-done.4 = bf16[2048,128]{1,0:T(8,128)(2,1)S(1)} collective-permute-done((bf16[2048,128]{1,0:T(8,128)(2,1)S(1)}, bf16[2048,128]{1,0:T(8,128)(2,1)S(1)}, u32[]{:S(2)}, u32[]{:S(2)}) %collective-permute-start.4) | collective-permute-done | bytes 524320 | tf_op jit(solution)/shard_map/ppermute | solution.py:164
  171.5 1.8 fusion.22
  173.3 1.8 fusion.21
  175.4 3.7 %collective-permute-done.2 = bf16[2048,128]{1,0:T(8,128)(2,1)S(1)} collective-permute-done((bf16[2048,128]{1,0:T(8,128)(2,1)S(1)}, bf16[2048,128]{1,0:T(8,128)(2,1)S(1)}, u32[]{:S(2)}, u32[]{:S(2)}) %collective-permute-start.2) | collective-permute-done | bytes 524320 | tf_op jit(solution)/shard_map/ppermute | solution.py:164
  179.2 0.8 fusion.24
  179.9 0.8 fusion.23
  181.0 1.9 fusion.6
  183.0 10.0 %reduce-scatter.2.cloned.1.call-done = f32[2048,128]{1,0:T(8,128)} async-done(((f32[2048,256]{1,0:T(8,128)}), f32[2048,128]{1,0:T(8,128)}) %reduce-scatter.2.cloned.1.call-update) | async-done | bytes 1048592 | tf_op jit(solution)/shard_map/reduce_scatter | solution.py:118
  193.1 43.6 %all-reduce.2.cloned.1.call-done = f32[2048,128]{1,0:T(8,128)} async-done(((f32[2048,128]{1,0:T(8,128)}), f32[2048,128]{1,0:T(8,128)}) %all-reduce.2.cloned.1.call-update) | async-done | bytes 1048592 | tf_op jit(solution)/shard_map/psum | solution.py:119
  237.0 0.5 fusion.61
  237.5 0.6 multiply_subtract_fusion
  238.1 1.6 bitcast_multiply_fusion
  239.7 8.6 %all-gather.2.cloned.1.call-done = f32[2048,256]{1,0:T(8,128)} async-done(((f32[2048,128]{1,0:T(8,128)}), f32[2048,256]{1,0:T(8,128)}) %all-gather.2.cloned.1.call-update) | async-done | bytes 2097168 | tf_op jit(solution)/shard_map/all_gather | solution.py:120
  248.4 5.6 %fusion.10 = bf16[512,256]{1,0:T(8,128)(2,1)S(1)} fusion(f32[2048,256]{1,0:T(8,128)} %all-gather.2.cloned.1.call-done, f32[512,1024]{0,1:T(8,128)S(1)} %get-tuple-element.76, f32[512,1024]{0,1:T(8,128)} %get-tuple-element.77), kind=kOutput, calls=%fused_computation.31 | convolution fusion | flops 1611792384 | bytes 6553600 | tf_op jit(solution)/shard_map/dot_general | solution.py:173
  254.0 0.4 convolution_convert_fusion
  254.4 23.7 %all_to_all.25 = bf16[8,80,512]{2,1,0:T(8,128)(2,1)S(1)} all-to-all(bf16[8,80,512]{2,1,0:T(8,128)(2,1)S(1)} %bitcast.87), channel_id=1, replica_groups=mesh['tile'=8,'win'=4] {'tile'}, dimensions={0} | all-to-all | bytes 1310720 | tf_op jit(solution)/shard_map/all_to_all | solution.py:183
  278.2 0.8 copy-done.2
  (63 shorter events, 3.1 us)
Async XLA Ops:
  6.5 6.6 %copy-start = (bf16[4,256,2048]{2,1,0:T(8,128)(2,1)S(1)}, bf16[4,256,2048]{2,1,0:T(8,128)(2,1)}, u32[]{:S(2)}) copy-start(bf16[4,256,2048]{2,1,0:T(8,128)(2,1)} %param.4) | copy-start | bytes 12582916
  15.6 9.0 %copy-start.3 = (s32[256,1]{0,1:T(1,128)S(1)}, s32[256,1]{0,1:T(1,128)}, u32[]{:S(2)}) copy-start(s32[256,1]{0,1:T(1,128)} %param.7) | copy-start | bytes 3076
  15.6 9.0 %copy-start.4 = (s32[256]{0:T(256)S(1)}, s32[256]{0:T(256)}, u32[]{:S(2)}) copy-start(s32[256]{0:T(256)} %param.6) | copy-start | bytes 3076
  15.6 9.0 %copy-start.5 = (s32[256]{0:T(256)S(1)}, s32[256]{0:T(256)}, u32[]{:S(2)}) copy-start(s32[256]{0:T(256)} %param.5) | copy-start | bytes 3076
  17.3 33.1 %all-to-all-start.3 = ((bf16[8,256,256]{2,1,0:T(8,128)(2,1)}), bf16[8,256,256]{2,1,0:T(8,128)(2,1)S(1)}, u32[]{:S(2)}, u32[]{:S(2)}) async-start(bf16[8,256,256]{2,1,0:T(8,128)(2,1)} %get-tuple-element.7), calls=%async_computation.3 | async-start | bytes 2097152 | tf_op jit(solution)/shard_map/all_to_all | solution.py:160
  24.7 20.3 %collective-permute-start = (s32[3,256]{1,0:T(4,128)S(1)}, s32[3,256]{1,0:T(4,128)S(1)}, u32[]{:S(2)}, u32[]{:S(2)}) collective-permute-start(s32[3,256]{1,0:T(4,128)S(1)} %pad_add_fusion), channel_id=1, source_target_pairs={{0,0},{4,4},{8,12},{12,20},{16,28},{20,24},{24,16},{28,8},{1,1},{5... | collective-permute-start | bytes 9224 | tf_op jit(solution)/shard_map/ppermute | solution.py:141
  50.4 30.9 %all-to-all-start.2 = ((bf16[8,256,256]{2,1,0:T(8,128)(2,1)}), bf16[8,256,256]{2,1,0:T(8,128)(2,1)S(1)}, u32[]{:S(2)}, u32[]{:S(2)}) async-start(bf16[8,256,256]{2,1,0:T(8,128)(2,1)} %get-tuple-element.8), calls=%async_computation.2 | async-start | bytes 2097152 | tf_op jit(solution)/shard_map/all_to_all | solution.py:160
  61.8 94.0 %collective-permute-start.7 = (bf16[2048,128]{1,0:T(8,128)(2,1)}, bf16[2048,128]{1,0:T(8,128)(2,1)}, u32[]{:S(2)}, u32[]{:S(2)}) collective-permute-start(bf16[2048,128]{1,0:T(8,128)(2,1)} %get-tuple-element.49), channel_id=1, source_target_pairs={{0,4},{4,12},{12,20},{20,28},{28,24},{24,16},{16,8},{8,0},{1,5},{5... | collective-permute-start | bytes 1572872 | tf_op jit(solution)/shard_map/ppermute | solution.py:163
  63.8 93.0 %collective-permute-start.8 = (bf16[2048,128]{1,0:T(8,128)(2,1)}, bf16[2048,128]{1,0:T(8,128)(2,1)}, u32[]{:S(2)}, u32[]{:S(2)}) collective-permute-start(bf16[2048,128]{1,0:T(8,128)(2,1)} %get-tuple-element.50), channel_id=1, source_target_pairs={{0,8},{4,0},{12,4},{20,12},{28,20},{24,28},{16,24},{8,16},{1,9},{5... | collective-permute-start | bytes 1572872 | tf_op jit(solution)/shard_map/ppermute | solution.py:164
  81.3 33.7 %all-to-all-start.1 = ((bf16[8,256,256]{2,1,0:T(8,128)(2,1)}), bf16[8,256,256]{2,1,0:T(8,128)(2,1)S(1)}, u32[]{:S(2)}, u32[]{:S(2)}) async-start(bf16[8,256,256]{2,1,0:T(8,128)(2,1)} %get-tuple-element.9), calls=%async_computation.1 | async-start | bytes 2097152 | tf_op jit(solution)/shard_map/all_to_all | solution.py:160
  92.5 70.5 %collective-permute-start.5 = (bf16[2048,128]{1,0:T(8,128)(2,1)}, bf16[2048,128]{1,0:T(8,128)(2,1)}, u32[]{:S(2)}, u32[]{:S(2)}) collective-permute-start(bf16[2048,128]{1,0:T(8,128)(2,1)} %get-tuple-element.51), channel_id=1, source_target_pairs={{0,4},{4,12},{12,20},{20,28},{28,24},{24,16},{16,8},{8,0},{1,5},{5... | collective-permute-start | bytes 1572872 | tf_op jit(solution)/shard_map/ppermute | solution.py:163
  94.4 68.9 %collective-permute-start.6 = (bf16[2048,128]{1,0:T(8,128)(2,1)}, bf16[2048,128]{1,0:T(8,128)(2,1)}, u32[]{:S(2)}, u32[]{:S(2)}) collective-permute-start(bf16[2048,128]{1,0:T(8,128)(2,1)} %get-tuple-element.52), channel_id=1, source_target_pairs={{0,8},{4,0},{12,4},{20,12},{28,20},{24,28},{16,24},{8,16},{1,9},{5... | collective-permute-start | bytes 1572872 | tf_op jit(solution)/shard_map/ppermute | solution.py:164
  115.1 33.9 %all-to-all-start = ((bf16[8,256,256]{2,1,0:T(8,128)(2,1)}), bf16[8,256,256]{2,1,0:T(8,128)(2,1)}, u32[]{:S(2)}, u32[]{:S(2)}) async-start(bf16[8,256,256]{2,1,0:T(8,128)(2,1)} %get-tuple-element.10), calls=%async_computation | async-start | bytes 2097152 | tf_op jit(solution)/shard_map/all_to_all | solution.py:160
  119.3 73.6 %reduce-scatter.2.cloned.1.call-start = ((), (), s32[]{:S(2)}) async-start(), calls=%async_computation.6 | async-start | bytes 3145728 | tf_op jit(solution)/shard_map/reduce_scatter | solution.py:118
  127.2 40.3 %collective-permute-start.3 = (bf16[2048,128]{1,0:T(8,128)(2,1)}, bf16[2048,128]{1,0:T(8,128)(2,1)}, u32[]{:S(2)}, u32[]{:S(2)}) collective-permute-start(bf16[2048,128]{1,0:T(8,128)(2,1)} %get-tuple-element.53), channel_id=1, source_target_pairs={{0,4},{4,12},{12,20},{20,28},{28,24},{24,16},{16,8},{8,0},{1,5},{5... | collective-permute-start | bytes 1572872 | tf_op jit(solution)/shard_map/ppermute | solution.py:163
  155.7 1.0 copy-start.1
  156.7 14.8 %collective-permute-start.4 = (bf16[2048,128]{1,0:T(8,128)(2,1)S(1)}, bf16[2048,128]{1,0:T(8,128)(2,1)S(1)}, u32[]{:S(2)}, u32[]{:S(2)}) collective-permute-start(bf16[2048,128]{1,0:T(8,128)(2,1)S(1)} %copy-done.1), channel_id=1, source_target_pairs={{0,8},{4,0},{12,4},{20,12},{28,20},{24,28},{16,24},{8,16},{1,9},{5... | collective-permute-start | bytes 1572872 | tf_op jit(solution)/shard_map/ppermute | solution.py:164
  156.7 18.7 %collective-permute-start.1 = (bf16[2048,128]{1,0:T(8,128)(2,1)S(1)}, bf16[2048,128]{1,0:T(8,128)(2,1)S(1)}, u32[]{:S(2)}, u32[]{:S(2)}) collective-permute-start(bf16[2048,128]{1,0:T(8,128)(2,1)S(1)} %get-tuple-element.55), channel_id=1, source_target_pairs={{0,4},{4,12},{12,20},{20,28},{28,24},{24,16},{16,8},{8,0},{1,5},{5... | collective-permute-start | bytes 1572872 | tf_op jit(solution)/shard_map/ppermute | solution.py:163
  163.0 16.2 %collective-permute-start.2 = (bf16[2048,128]{1,0:T(8,128)(2,1)S(1)}, bf16[2048,128]{1,0:T(8,128)(2,1)S(1)}, u32[]{:S(2)}, u32[]{:S(2)}) collective-permute-start(bf16[2048,128]{1,0:T(8,128)(2,1)S(1)} %get-tuple-element.56), channel_id=1, source_target_pairs={{0,8},{4,0},{12,4},{20,12},{28,20},{24,28},{16,24},{8,16},{1,9},{5... | collective-permute-start | bytes 1572872 | tf_op jit(solution)/shard_map/ppermute | solution.py:164
  182.9 53.8 %all-reduce.2.cloned.1.call-start = ((), (), s32[]{:S(2)}) async-start(), calls=%async_computation.7 | async-start | bytes 2097152 | tf_op jit(solution)/shard_map/psum | solution.py:119
  193.0 55.4 %all-gather.2.cloned.1.call-start = ((), (), s32[]{:S(2)}) async-start(), calls=%async_computation.8 | async-start | bytes 3145728 | tf_op jit(solution)/shard_map/all_gather | solution.py:120
  278.2 0.8 copy-start.2
Sparse Core Ops, SparseCore 0:
  183.0 9.9 reduce-scatter.1
  195.3 41.3 all-reduce.1
  238.2 10.0 all-gather.1

commit v9 on v5

--- a/solution.py
+++ b/solution.py
@@ -108,6 +108,30 @@
         return False
 
     return path if extend() else list(range(count))
+
+
+def sum_and_invert(cross, length, lag_count, seg_total, win_count):
+    win = lax.axis_index("win")
+    if win_count % 2 or win_count & (win_count - 1):
+        stacked = lax.psum(cross, "win")
+        inverse = inverse_matrix(length, win * lag_count, lag_count, seg_total)
+        return jnp.dot(inverse, stacked, precision=lax.Precision.HIGH).astype(jnp.bfloat16)
+    core = win % 2
+    half = cross.shape[1] // 2
+    mine = lax.dynamic_slice_in_dim(cross, core * half, half, axis=1)
+    other = lax.dynamic_slice_in_dim(cross, (1 - core) * half, half, axis=1)
+    partner = [(w, w ^ 1) for w in range(win_count)]
+    total = mine + lax.ppermute(other, "win", partner)
+    step = 2
+    while step < win_count:
+        total = total + lax.ppermute(total, "win", [(w, w ^ step) for w in range(win_count)])
+        step *= 2
+    inverse = inverse_matrix(length, (win - core) * lag_count, 2 * lag_count, seg_total)
+    both = jnp.dot(inverse, total, precision=lax.Precision.HIGH).astype(jnp.bfloat16)
+    kept = lax.dynamic_slice_in_dim(both, core * lag_count, lag_count, axis=0)
+    given = lax.dynamic_slice_in_dim(both, (1 - core) * lag_count, lag_count, axis=0)
+    got = lax.ppermute(given, "win", partner)
+    return jnp.where(core == 0, jnp.concatenate([kept, got], axis=1), jnp.concatenate([got, kept], axis=1))
 
 
 def make_per_device(ring):
@@ -158,10 +182,7 @@
             term = cross_terms(first_part, second_part)
             cross = term if cross is None else cross + term
         lag_count = length // win_count
-        stacked = lax.psum_scatter(cross, "win", scatter_dimension=1, tiled=True)
-        inverse = inverse_matrix(length, 0, length, seg_total)
-        own_pairs = jnp.dot(inverse, stacked, precision=lax.Precision.HIGHEST).astype(jnp.bfloat16)
-        correlation = lax.all_to_all(own_pairs, "win", split_axis=0, concat_axis=1, tiled=True)
+        correlation = sum_and_invert(cross, length, lag_count, seg_total, win_count)
         capacity = 5 * pair_first.shape[0] // (2 * tile_count)
         chooser = bucket_select(my_owners, tile_count, capacity)
         picked = lax.dot_general(

time: 309 us -> 260 us (0.84); the launches traced: 305 us -> 260 us
  between operations: 14.1 us -> 0.63 us
  matrix products: 41.5 us -> 29.4 us
  local copies, waits for them, and re-layouts: 37.5 us -> 26.6 us
  other arithmetic: 28.1 us -> 18 us
  blocking collectives: 63.9 us -> 56.4 us
  waiting for transfers between devices: 100 us -> 107 us
    ppermute x0 -> x3, waiting for transfers between devices: none -> 24.6 us  [the longest x1 21.9 us: sum_and_invert(): lax.ppermute(total, 'win', [(w, w ^ step) for w in range(win_count)])]
    unnamed x2 -> x0, waiting for transfers between devices: 17.8 us -> none
    dot_general x1, matrix products: 14.4 us -> 2.29 us  [sum_and_invert(): jnp.dot(inverse, total, precision=lax.Precision.HIGH).astype(jnp.bfloat16)]
    unnamed x37 -> x36, local copies, waits for them, and re-layouts: 21.7 us -> 10.7 us
    all_to_all x1 -> x0, blocking collectives: 8.39 us -> none  [per_device(): lax.all_to_all(own_pairs, 'win', split_axis=0, concat_axis=1, tiled=True)]
    mul x1, other arithmetic: 7.71 us -> 0.61 us  [inverse_matrix(): return jnp.concatenate([weights * cosine, -weights * sine], axis=1)]
  transfers between devices with their start and end apart: 13 -> 15, of which waited for: 7 -> 9; matrix products, arithmetic and copies ran while one was open for 19% -> 18% of each run, Pallas kernels for 0% -> 0%
where the time goes in v9:
time: 260 us
  waiting for transfers between devices  107 us (41%)
  blocking collectives  56.4 us (22%)
  matrix products  29.4 us (11%)
  local copies, waits for them, and re-layouts  26.6 us (10%)
  starting transfers between devices  21.4 us (8%)
  other arithmetic  18 us (7%)
    ppermute x4, waiting for transfers between devices, per_device(): from_prev = lax.ppermute(whitened[:, half:], 'tile', to_next)  36.5 us
    all_to_all x3, waiting for transfers between devices, per_device(): lax.all_to_all(outgoing, 'tile', split_axis=0, concat_axis=0, tiled=True)  35.9 us
    all_to_all x1, blocking collectives, per_device(): lax.all_to_all(outgoing, 'tile', split_axis=0, concat_axis=0, tiled=True)  32.9 us
    all_to_all x1, blocking collectives, per_device(): lax.all_to_all(buckets, 'tile', split_axis=0, concat_axis=0, tiled=True)  23.5 us
    ppermute x1, waiting for transfers between devices, sum_and_invert(): lax.ppermute(total, 'win', [(w, w ^ step) for w in range(win_count)])  21.9 us
    dot_general x4, matrix products, per_device(): jnp.einsum('fjm,jmc->fc', forward, received, preferred_element_type=jnp.f...  20.6 us
    all_to_all x3, starting transfers between devices, per_device(): lax.all_to_all(outgoing, 'tile', split_axis=0, concat_axis=0, tiled=True)  11.6 us
    unnamed x36, local copies, waits for them, and re-layouts  10.7 us
  transfers between devices with their start and end apart: 15, of which 9 were waited for; matrix products, arithmetic and copies ran while one was open for 18% of the time, Pallas kernels for 0%

profile of v9, /device:TPU:0, one launch (start us, length us, event | category | flops | bytes accessed | tf_op | source)
XLA Modules:
  0.0 259.8 jit_solution(4885332967190172692)
XLA Ops:
  0.0 1.3 slice_bitcast_fusion.1
  1.3 2.1 slice_dynamic-update-slice_fusion.7
  3.4 1.9 slice_dynamic-update-slice_fusion.6
  5.2 0.7 fusion.58
  5.9 0.7 fusion.56
  6.7 0.8 slice_dynamic-update-slice_fusion.5
  7.4 0.8 slice_dynamic-update-slice_fusion.4
  8.2 0.8 slice_dynamic-update-slice_fusion.3
  9.0 0.8 slice_dynamic-update-slice_fusion.2
  9.8 0.8 slice_dynamic-update-slice_fusion.1
  10.6 32.9 %all_to_all.25 = bf16[8,256,256]{2,1,0:T(8,128)(2,1)S(1)} all-to-all(bf16[8,256,256]{2,1,0:T(8,128)(2,1)S(1)} %get-tuple-element.8), channel_id=1, replica_groups=mesh['tile'=8,'win'=4] {'tile'}, dimensions={0} | all-to-all | bytes 2097152 | tf_op jit(solution)/shard_map/all_to_all | solution.py:174
  43.4 3.6 %all-to-all-start.1 = ((bf16[8,256,256]{2,1,0:T(8,128)(2,1)}), bf16[8,256,256]{2,1,0:T(8,128)(2,1)S(1)}, u32[]{:S(2)}, u32[]{:S(2)}) async-start(bf16[8,256,256]{2,1,0:T(8,128)(2,1)} %get-tuple-element.9), calls=%async_computation.1 | async-start | bytes 2097152 | tf_op jit(solution)/shard_map/all_to_all | solution.py:174
  47.1 0.7 collective-permute-start
  47.8 1.0 fusion.62
  48.8 0.6 fusion.71
  49.4 5.1 %subtract_convert_fusion = (bf16[1024,32,64]{0,2,1:T(8,128)(2,1)}, bf16[1024,32,64]{0,2,1:T(8,128)(2,1)}) fusion(f32[1024,64]{0,1:T(8,128)S(1)} %get-tuple-element.78, f32[1024,32]{0,1:T(8,128)S(1)} %get-tuple-element.71, f32[1024,64]{0,1:T(8,128)S(1)} %get-tuple-element.79, f32[1024,32]{0,1:T(8,128)S(1)} %get-tuple-element.70), kind=kLoop, calls=%fused_computation.6 | loop fusion | flops 18874368 | bytes 9175040 | tf_op jit(solution)/shard_map/convert.3
  54.4 6.5 %copy.5 = bf16[1024,8,256]{2,0,1:T(8,128)(2,1)} copy(bf16[1024,8,256]{0,2,1:T(8,128)(2,1)} %bitcast.80) | data formatting | bytes 8388608 | tf_op jit(solution)/shard_map/sub | solution.py:24
  60.9 6.5 %copy.6 = bf16[1024,8,256]{2,0,1:T(8,128)(2,1)} copy(bf16[1024,8,256]{0,2,1:T(8,128)(2,1)} %bitcast.79) | data formatting | bytes 8388608 | tf_op jit(solution)/shard_map/neg | solution.py:31
  67.4 0.6 reduce-window.6
  68.3 4.3 %all-to-all-done.1 = bf16[8,256,256]{2,1,0:T(8,128)(2,1)S(1)} async-done(((bf16[8,256,256]{2,1,0:T(8,128)(2,1)}), bf16[8,256,256]{2,1,0:T(8,128)(2,1)S(1)}, u32[]{:S(2)}, u32[]{:S(2)}) %all-to-all-start.1) | async-done | bytes 1048608 | tf_op jit(solution)/shard_map/all_to_all | solution.py:174
  72.6 3.6 %all-to-all-start = ((bf16[8,256,256]{2,1,0:T(8,128)(2,1)}), bf16[8,256,256]{2,1,0:T(8,128)(2,1)S(1)}, u32[]{:S(2)}, u32[]{:S(2)}) async-start(bf16[8,256,256]{2,1,0:T(8,128)(2,1)} %get-tuple-element.10), calls=%async_computation | async-start | bytes 2097152 | tf_op jit(solution)/shard_map/all_to_all | solution.py:174
  76.2 6.1 %convolution_bitcast_fusion.2 = f32[2048,256]{1,0:T(8,128)S(1)} fusion(bf16[8,256,256]{2,1,0:T(8,128)(2,1)S(1)} %all-to-all-done.1, bf16[1024,8,256]{2,0,1:T(8,128)(2,1)} %copy.6, bf16[1024,8,256]{2,0,1:T(8,128)(2,1)} %copy.5), kind=kOutput, calls=%fused_computation.13 | convolution fusion | flops 2164260864 | bytes 11534336 | tf_op jit(solution)/shard_map/fjm,jmc->fc/dot_general | solution.py:175
  82.3 1.4 copy-done.2
  83.9 2.5 convolution_bitcast_fusion.1
  86.4 1.3 copy-done
  87.9 14.1 %all-to-all-done = bf16[8,256,256]{2,1,0:T(8,128)(2,1)S(1)} async-done(((bf16[8,256,256]{2,1,0:T(8,128)(2,1)}), bf16[8,256,256]{2,1,0:T(8,128)(2,1)S(1)}, u32[]{:S(2)}, u32[]{:S(2)}) %all-to-all-start) | async-done | bytes 1048608 | tf_op jit(solution)/shard_map/all_to_all | solution.py:174
  102.0 4.4 %all-to-all-start.3 = ((bf16[8,256,256]{2,1,0:T(8,128)(2,1)}), bf16[8,256,256]{2,1,0:T(8,128)(2,1)}, u32[]{:S(2)}, u32[]{:S(2)}) async-start(bf16[8,256,256]{2,1,0:T(8,128)(2,1)} %get-tuple-element.7), calls=%async_computation.3 | async-start | bytes 2097152 | tf_op jit(solution)/shard_map/all_to_all | solution.py:174
  106.4 5.9 %convolution_bitcast_fusion.3 = f32[2048,256]{1,0:T(8,128)S(1)} fusion(bf16[8,256,256]{2,1,0:T(8,128)(2,1)S(1)} %all-to-all-done, bf16[1024,8,256]{2,0,1:T(8,128)(2,1)} %copy.6, bf16[1024,8,256]{2,0,1:T(8,128)(2,1)} %copy.5), kind=kOutput, calls=%fused_computation.14 | convolution fusion | flops 2164260864 | bytes 11534336 | tf_op jit(solution)/shard_map/fjm,jmc->fc/dot_general | solution.py:175
  112.7 1.3 fusion.7
  114.4 17.5 %all-to-all-done.3 = bf16[8,256,256]{2,1,0:T(8,128)(2,1)} async-done(((bf16[8,256,256]{2,1,0:T(8,128)(2,1)}), bf16[8,256,256]{2,1,0:T(8,128)(2,1)}, u32[]{:S(2)}, u32[]{:S(2)}) %all-to-all-start.3) | async-done | bytes 1048608 | tf_op jit(solution)/shard_map/all_to_all | solution.py:174
  131.9 6.1 %convolution_bitcast_fusion = f32[2048,256]{1,0:T(8,128)S(1)} fusion(bf16[8,256,256]{2,1,0:T(8,128)(2,1)} %all-to-all-done.3, bf16[1024,8,256]{2,0,1:T(8,128)(2,1)} %copy.6, bf16[1024,8,256]{2,0,1:T(8,128)(2,1)} %copy.5), kind=kOutput, calls=%fused_computation.11 | convolution fusion | flops 2164260864 | bytes 11534336 | tf_op jit(solution)/shard_map/fjm,jmc->fc/dot_general | solution.py:175
  138.4 0.3 fusion.9
  139.1 1.3 collective-permute-start.1
  140.4 0.8 collective-permute-start.2
  141.3 1.3 collective-permute-start.3
  142.5 0.8 collective-permute-start.4
  143.4 1.3 collective-permute-start.7
  144.8 20.5 %collective-permute-done.3 = bf16[2048,128]{1,0:T(8,128)(2,1)S(1)} collective-permute-done((bf16[2048,128]{1,0:T(8,128)(2,1)S(1)}, bf16[2048,128]{1,0:T(8,128)(2,1)S(1)}, u32[]{:S(2)}, u32[]{:S(2)}) %collective-permute-start.3) | collective-permute-done | bytes 524320 | tf_op jit(solution)/shard_map/ppermute | solution.py:177
  165.2 1.2 collective-permute-start.5
  166.4 0.8 collective-permute-start.6
  167.2 0.8 fusion.22
  168.0 0.8 fusion.23
  169.1 16.0 %collective-permute-done.5 = bf16[2048,128]{1,0:T(8,128)(2,1)S(1)} collective-permute-done((bf16[2048,128]{1,0:T(8,128)(2,1)S(1)}, bf16[2048,128]{1,0:T(8,128)(2,1)S(1)}, u32[]{:S(2)}, u32[]{:S(2)}) %collective-permute-start.5) | collective-permute-done | bytes 524320 | tf_op jit(solution)/shard_map/ppermute | solution.py:177
  185.1 0.8 fusion.20
  185.8 0.8 fusion.21
  186.9 10.5 %collective-permute-done.8 = bf16[2048,128]{1,0:T(8,128)(2,1)S(1)} collective-permute-done((bf16[2048,128]{1,0:T(8,128)(2,1)S(1)}, bf16[2048,128]{1,0:T(8,128)(2,1)S(1)}, u32[]{:S(2)}, u32[]{:S(2)}) %collective-permute-start.8) | collective-permute-done | bytes 524320 | tf_op jit(solution)/shard_map/ppermute | solution.py:178
  197.4 0.8 fusion.18
  198.1 0.8 fusion.19
  199.2 0.8 fusion.25
  200.0 0.8 fusion.24
  201.0 0.5 fusion.6
  201.8 0.3 fusion.73
  202.2 1.0 fusion.65
  203.2 1.3 collective-permute-done.9
  204.5 1.3 dynamic-slice_add_fusion
  205.9 1.6 collective-permute-start.10
  207.4 1.2 multiply_subtract_fusion
  208.7 0.6 bitcast_multiply_fusion
  209.3 21.9 %collective-permute-done.10 = f32[2048,128]{1,0:T(8,128)S(1)} collective-permute-done((f32[2048,128]{1,0:T(8,128)S(1)}, f32[2048,128]{1,0:T(8,128)S(1)}, u32[]{:S(2)}, u32[]{:S(2)}) %collective-permute-start.10) | collective-permute-done | bytes 1048608 | tf_op jit(solution)/shard_map/ppermute | solution.py:127
  231.2 2.3 fusion.10
  233.6 1.3 collective-permute-done.11
  234.9 0.4 convolution_convert_fusion
  235.3 23.5 %all_to_all.26 = bf16[8,80,512]{2,1,0:T(8,128)(2,1)S(1)} all-to-all(bf16[8,80,512]{2,1,0:T(8,128)(2,1)S(1)} %bitcast.85), channel_id=1, replica_groups=mesh['tile'=8,'win'=4] {'tile'}, dimensions={0} | all-to-all | bytes 1310720 | tf_op jit(solution)/shard_map/all_to_all | solution.py:195
  258.9 0.8 copy-done.8
  (74 shorter events, 3.8 us)
Async XLA Ops:
  0.0 6.7 %copy-start.4 = (bf16[4,256,2048]{2,1,0:T(8,128)(2,1)S(1)}, bf16[4,256,2048]{2,1,0:T(8,128)(2,1)}, u32[]{:S(2)}) copy-start(bf16[4,256,2048]{2,1,0:T(8,128)(2,1)} %param.4) | copy-start | bytes 12582916
  7.4 39.6 %copy-start.9 = (s32[256,1]{0,1:T(1,128)S(1)}, s32[256,1]{0,1:T(1,128)}, u32[]{:S(2)}) copy-start(s32[256,1]{0,1:T(1,128)} %param.7) | copy-start | bytes 3076
  7.4 39.6 %copy-start.10 = (s32[256]{0:T(256)S(1)}, s32[256]{0:T(256)}, u32[]{:S(2)}) copy-start(s32[256]{0:T(256)} %param.6) | copy-start | bytes 3076
  7.4 39.6 %copy-start.11 = (s32[256]{0:T(256)S(1)}, s32[256]{0:T(256)}, u32[]{:S(2)}) copy-start(s32[256]{0:T(256)} %param.5) | copy-start | bytes 3076
  43.4 29.2 %all-to-all-start.1 = ((bf16[8,256,256]{2,1,0:T(8,128)(2,1)}), bf16[8,256,256]{2,1,0:T(8,128)(2,1)S(1)}, u32[]{:S(2)}, u32[]{:S(2)}) async-start(bf16[8,256,256]{2,1,0:T(8,128)(2,1)} %get-tuple-element.9), calls=%async_computation.1 | async-start | bytes 2097152 | tf_op jit(solution)/shard_map/all_to_all | solution.py:174
  47.1 20.3 %collective-permute-start = (s32[3,256]{1,0:T(4,128)S(1)}, s32[3,256]{1,0:T(4,128)S(1)}, u32[]{:S(2)}, u32[]{:S(2)}) collective-permute-start(s32[3,256]{1,0:T(4,128)S(1)} %pad_add_fusion), channel_id=1, source_target_pairs={{0,0},{4,4},{8,12},{12,20},{16,28},{20,24},{24,16},{28,8},{1,1},{5... | collective-permute-start | bytes 9224 | tf_op jit(solution)/shard_map/ppermute | solution.py:155
  72.6 29.4 %all-to-all-start = ((bf16[8,256,256]{2,1,0:T(8,128)(2,1)}), bf16[8,256,256]{2,1,0:T(8,128)(2,1)S(1)}, u32[]{:S(2)}, u32[]{:S(2)}) async-start(bf16[8,256,256]{2,1,0:T(8,128)(2,1)} %get-tuple-element.10), calls=%async_computation | async-start | bytes 2097152 | tf_op jit(solution)/shard_map/all_to_all | solution.py:174
  76.2 7.6 %copy-start.5 = (bf16[1024,8,256]{2,0,1:T(8,128)(2,1)S(1)}, bf16[1024,8,256]{2,0,1:T(8,128)(2,1)}, u32[]{:S(2)}) copy-start(bf16[1024,8,256]{2,0,1:T(8,128)(2,1)} %copy.5) | copy-start | bytes 12582916
  76.2 7.6 %copy-start.6 = (bf16[1024,8,256]{2,0,1:T(8,128)(2,1)S(1)}, bf16[1024,8,256]{2,0,1:T(8,128)(2,1)}, u32[]{:S(2)}) copy-start(bf16[1024,8,256]{2,0,1:T(8,128)(2,1)} %copy.6) | copy-start | bytes 12582916
  82.3 1.4 copy-start.2
  86.4 1.4 copy-start
  102.0 29.9 %all-to-all-start.3 = ((bf16[8,256,256]{2,1,0:T(8,128)(2,1)}), bf16[8,256,256]{2,1,0:T(8,128)(2,1)}, u32[]{:S(2)}, u32[]{:S(2)}) async-start(bf16[8,256,256]{2,1,0:T(8,128)(2,1)} %get-tuple-element.7), calls=%async_computation.3 | async-start | bytes 2097152 | tf_op jit(solution)/shard_map/all_to_all | solution.py:174
  106.4 6.3 %copy-start.3 = (f32[2048,256]{1,0:T(8,128)S(1)}, f32[2048,256]{1,0:T(8,128)}, u32[]{:S(2)}) copy-start(f32[2048,256]{1,0:T(8,128)} %copy-done.2) | copy-start | bytes 6291460
  112.4 1.7 copy-start.1
  138.7 2.6 copy-start.7
  139.1 60.1 %collective-permute-start.1 = (bf16[2048,128]{1,0:T(8,128)(2,1)S(1)}, bf16[2048,128]{1,0:T(8,128)(2,1)S(1)}, u32[]{:S(2)}, u32[]{:S(2)}) collective-permute-start(bf16[2048,128]{1,0:T(8,128)(2,1)S(1)} %get-tuple-element.55), channel_id=1, source_target_pairs={{0,4},{4,12},{12,20},{20,28},{28,24},{24,16},{16,8},{8,0},{1,5},{5... | collective-permute-start | bytes 1572872 | tf_op jit(solution)/shard_map/ppermute | solution.py:177
  140.4 58.8 %collective-permute-start.2 = (bf16[2048,128]{1,0:T(8,128)(2,1)S(1)}, bf16[2048,128]{1,0:T(8,128)(2,1)S(1)}, u32[]{:S(2)}, u32[]{:S(2)}) collective-permute-start(bf16[2048,128]{1,0:T(8,128)(2,1)S(1)} %get-tuple-element.56), channel_id=1, source_target_pairs={{0,8},{4,0},{12,4},{20,12},{28,20},{24,28},{16,24},{8,16},{1,9},{5... | collective-permute-start | bytes 1572872 | tf_op jit(solution)/shard_map/ppermute | solution.py:178
  141.3 23.9 %collective-permute-start.3 = (bf16[2048,128]{1,0:T(8,128)(2,1)S(1)}, bf16[2048,128]{1,0:T(8,128)(2,1)S(1)}, u32[]{:S(2)}, u32[]{:S(2)}) collective-permute-start(bf16[2048,128]{1,0:T(8,128)(2,1)S(1)} %get-tuple-element.53), channel_id=1, source_target_pairs={{0,4},{4,12},{12,20},{20,28},{28,24},{24,16},{16,8},{8,0},{1,5},{5... | collective-permute-start | bytes 1572872 | tf_op jit(solution)/shard_map/ppermute | solution.py:177
  142.5 23.9 %collective-permute-start.4 = (bf16[2048,128]{1,0:T(8,128)(2,1)S(1)}, bf16[2048,128]{1,0:T(8,128)(2,1)S(1)}, u32[]{:S(2)}, u32[]{:S(2)}) collective-permute-start(bf16[2048,128]{1,0:T(8,128)(2,1)S(1)} %get-tuple-element.54), channel_id=1, source_target_pairs={{0,8},{4,0},{12,4},{20,12},{28,20},{24,28},{16,24},{8,16},{1,9},{5... | collective-permute-start | bytes 1572872 | tf_op jit(solution)/shard_map/ppermute | solution.py:178
  143.4 43.5 %collective-permute-start.7 = (bf16[2048,128]{1,0:T(8,128)(2,1)S(1)}, bf16[2048,128]{1,0:T(8,128)(2,1)S(1)}, u32[]{:S(2)}, u32[]{:S(2)}) collective-permute-start(bf16[2048,128]{1,0:T(8,128)(2,1)S(1)} %get-tuple-element.49), channel_id=1, source_target_pairs={{0,4},{4,12},{12,20},{20,28},{28,24},{24,16},{16,8},{8,0},{1,5},{5... | collective-permute-start | bytes 1572872 | tf_op jit(solution)/shard_map/ppermute | solution.py:177
  165.2 19.9 %collective-permute-start.5 = (bf16[2048,128]{1,0:T(8,128)(2,1)S(1)}, bf16[2048,128]{1,0:T(8,128)(2,1)S(1)}, u32[]{:S(2)}, u32[]{:S(2)}) collective-permute-start(bf16[2048,128]{1,0:T(8,128)(2,1)S(1)} %get-tuple-element.51), channel_id=1, source_target_pairs={{0,4},{4,12},{12,20},{20,28},{28,24},{24,16},{16,8},{8,0},{1,5},{5... | collective-permute-start | bytes 1572872 | tf_op jit(solution)/shard_map/ppermute | solution.py:177
  166.4 18.7 %collective-permute-start.6 = (bf16[2048,128]{1,0:T(8,128)(2,1)S(1)}, bf16[2048,128]{1,0:T(8,128)(2,1)S(1)}, u32[]{:S(2)}, u32[]{:S(2)}) collective-permute-start(bf16[2048,128]{1,0:T(8,128)(2,1)S(1)} %get-tuple-element.52), channel_id=1, source_target_pairs={{0,8},{4,0},{12,4},{20,12},{28,20},{24,28},{16,24},{8,16},{1,9},{5... | collective-permute-start | bytes 1572872 | tf_op jit(solution)/shard_map/ppermute | solution.py:178
  185.1 12.3 %collective-permute-start.8 = (bf16[2048,128]{1,0:T(8,128)(2,1)S(1)}, bf16[2048,128]{1,0:T(8,128)(2,1)S(1)}, u32[]{:S(2)}, u32[]{:S(2)}) collective-permute-start(bf16[2048,128]{1,0:T(8,128)(2,1)S(1)} %get-tuple-element.50), channel_id=1, source_target_pairs={{0,8},{4,0},{12,4},{20,12},{28,20},{24,28},{16,24},{8,16},{1,9},{5... | collective-permute-start | bytes 1572872 | tf_op jit(solution)/shard_map/ppermute | solution.py:178
  201.7 2.9 %collective-permute-start.9 = (f32[2048,128]{1,0:T(8,128)S(1)}, f32[2048,128]{1,0:T(8,128)}, u32[]{:S(2)}, u32[]{:S(2)}) collective-permute-start(f32[2048,128]{1,0:T(8,128)S(1)} %constant_dynamic-slice_fusion.2), channel_id=1, source_target_pairs={{0,1},{1,0},{2,3},{3,2},{4,5},{5,4},{6,7},{7,6},{8,9},{9,8},{10,11... | collective-permute-start | bytes 3145736 | tf_op jit(solution)/shard_map/ppermute | solution.py:124
  205.9 25.3 %collective-permute-start.10 = (f32[2048,128]{1,0:T(8,128)S(1)}, f32[2048,128]{1,0:T(8,128)S(1)}, u32[]{:S(2)}, u32[]{:S(2)}) collective-permute-start(f32[2048,128]{1,0:T(8,128)S(1)} %dynamic-slice_add_fusion), channel_id=1, source_target_pairs={{0,2},{1,3},{2,0},{3,1},{4,6},{5,7},{6,4},{7,5},{8,10},{9,11},{10,... | collective-permute-start | bytes 3145736 | tf_op jit(solution)/shard_map/ppermute | solution.py:127
  233.5 1.4 collective-permute-start.11
  258.9 0.8 copy-start.8

commit v10 on v9

--- a/solution.py
+++ b/solution.py
@@ -157,6 +157,7 @@
         pick_first = (channel_ids == my_first[None, :]).astype(jnp.bfloat16)
         pick_second = (channel_ids == (my_first + my_offset)[None, :]).astype(jnp.bfloat16)
         cross = None
+        arrived = []
         for segment in range(records.shape[0]):
             pieces = []
             for b in block_of:
@@ -172,10 +173,13 @@
                     )
             outgoing = jnp.stack(pieces, axis=0)
             received = lax.all_to_all(outgoing, "tile", split_axis=0, concat_axis=0, tiled=True)
+            if arrived:
+                received, _ = lax.optimization_barrier((received, arrived[-1]))
             spectra = jnp.einsum("fjm,jmc->fc", forward, received, preferred_element_type=jnp.float32)
             whitened = whiten(spectra, BAND)
             from_prev = lax.ppermute(whitened[:, half:], "tile", to_next)
             from_next = lax.ppermute(whitened[:, :half], "tile", to_prev)
+            arrived.append((from_prev, from_next))
             joined = jnp.concatenate([from_prev, whitened, from_next], axis=1)
             first_part = jnp.dot(joined, pick_first, preferred_element_type=jnp.float32)
             second_part = jnp.dot(joined, pick_second, preferred_element_type=jnp.float32)

time: 260 us -> 233 us (0.90)
  waiting for transfers between devices: 107 us -> 72.4 us
  blocking collectives: 56.4 us -> 21.9 us
  starting transfers between devices: 21.4 us -> 50.5 us
  matrix products: 29.4 us -> 40.1 us
    all_to_all x1 -> x0, blocking collectives: 32.9 us -> none  [per_device(): lax.all_to_all(outgoing, 'tile', split_axis=0, concat_axis=0, tiled=True)]
    ppermute x4, waiting for transfers between devices: 36.5 us -> 11.8 us  [per_device(): from_prev = lax.ppermute(whitened[:, half:], 'tile', to_next)]
    ppermute x4, starting transfers between devices: 2.48 us -> 16.1 us  [per_device(): from_next = lax.ppermute(whitened[:, :half], 'tile', to_prev)]
    ppermute x4, waiting for transfers between devices: 10.5 us -> 1.23 us  [per_device(): from_next = lax.ppermute(whitened[:, :half], 'tile', to_prev)]
    all_to_all x3 -> x4, starting transfers between devices: 11.6 us -> 19.4 us  [per_device(): lax.all_to_all(outgoing, 'tile', split_axis=0, concat_axis=0, tiled=True)]
    ppermute x4, starting transfers between devices: 4.95 us -> 12.6 us  [per_device(): from_prev = lax.ppermute(whitened[:, half:], 'tile', to_next)]
    dot_general x4, matrix products: 3.06 us -> 6.65 us  [per_device(): jnp.dot(joined, pick_second, preferred_element_type=jnp.float32)]
    dot_general x4, matrix products: 3.06 us -> 6.63 us  [per_device(): first_part = jnp.dot(joined, pick_first, preferred_element_type=jnp.float32)]
  transfers between devices with their start and end apart: 15 -> 16, of which waited for: 9 -> 11; matrix products, arithmetic and copies ran while one was open for 18% -> 26% of each run, Pallas kernels for 0% -> 0%
where the time goes in v10:
time: 233 us; the launch traced here: 232 us
  waiting for transfers between devices  72.4 us (31%)
  starting transfers between devices  50.5 us (22%)
  matrix products  40.1 us (17%)
  local copies, waits for them, and re-layouts  27.5 us (12%)
  blocking collectives  21.9 us (9%)
  other arithmetic  19.4 us (8%)
    all_to_all x4, waiting for transfers between devices, per_device(): lax.all_to_all(outgoing, 'tile', split_axis=0, concat_axis=0, tiled=True)  34.8 us
    dot_general x4, matrix products, per_device(): jnp.einsum('fjm,jmc->fc', forward, received, preferred_element_type=jnp.f...  24.2 us
    all_to_all x1, blocking collectives, per_device(): lax.all_to_all(buckets, 'tile', split_axis=0, concat_axis=0, tiled=True)  21.9 us
    ppermute x1, waiting for transfers between devices, sum_and_invert(): lax.ppermute(total, 'win', [(w, w ^ step) for w in range(win_count)])  21.9 us
    all_to_all x4, starting transfers between devices, per_device(): lax.all_to_all(outgoing, 'tile', split_axis=0, concat_axis=0, tiled=True)  19.4 us
    ppermute x4, starting transfers between devices, per_device(): from_next = lax.ppermute(whitened[:, :half], 'tile', to_prev)  16.1 us
    ppermute x4, starting transfers between devices, per_device(): from_prev = lax.ppermute(whitened[:, half:], 'tile', to_next)  12.6 us
    ppermute x4, waiting for transfers between devices, per_device(): from_prev = lax.ppermute(whitened[:, half:], 'tile', to_next)  11.8 us
  transfers between devices with their start and end apart: 16, of which 11 were waited for; matrix products, arithmetic and copies ran while one was open for 26% of the time, Pallas kernels for 0%

profile of v10, /device:TPU:0, one launch (start us, length us, event | category | flops | bytes accessed | tf_op | source)
XLA Modules:
  0.0 232.4 jit_solution(9112509929613954011)
XLA Ops:
  0.0 2.0 slice_dynamic-update-slice_fusion.7
  2.0 1.1 slice_bitcast_fusion.1
  3.2 1.9 slice_dynamic-update-slice_fusion.6
  5.1 0.7 fusion.56
  5.8 0.7 fusion.58
  6.5 0.9 slice_dynamic-update-slice_fusion.5
  7.4 0.8 slice_dynamic-update-slice_fusion.4
  8.2 0.9 slice_dynamic-update-slice_fusion.3
  9.1 0.8 slice_dynamic-update-slice_fusion.2
  9.9 0.8 slice_dynamic-update-slice_fusion.1
  10.7 7.3 %all-to-all-start = ((bf16[8,256,256]{2,1,0:T(8,128)(2,1)}), bf16[8,256,256]{2,1,0:T(8,128)(2,1)S(1)}, u32[]{:S(2)}, u32[]{:S(2)}) async-start(bf16[8,256,256]{2,1,0:T(8,128)(2,1)} %get-tuple-element.16), calls=%async_computation | async-start | bytes 2097152 | tf_op jit(solution)/shard_map/all_to_all | solution.py:175
  18.1 0.7 collective-permute-start
  18.7 1.0 fusion.62
  19.8 0.6 fusion.71
  20.4 5.1 %subtract_convert_fusion = (bf16[1024,32,64]{0,2,1:T(8,128)(2,1)}, bf16[1024,32,64]{0,2,1:T(8,128)(2,1)}) fusion(f32[1024,64]{0,1:T(8,128)S(1)} %get-tuple-element.84, f32[1024,32]{0,1:T(8,128)S(1)} %get-tuple-element.77, f32[1024,64]{0,1:T(8,128)S(1)} %get-tuple-element.85, f32[1024,32]{0,1:T(8,128)S(1)} %get-tuple-element.76), kind=kLoop, calls=%fused_computation.6 | loop fusion | flops 18874368 | bytes 9175040 | tf_op jit(solution)/shard_map/convert.3
  25.4 6.4 %copy.5 = bf16[1024,8,256]{2,0,1:T(8,128)(2,1)} copy(bf16[1024,8,256]{0,2,1:T(8,128)(2,1)} %bitcast.80) | data formatting | bytes 8388608 | tf_op jit(solution)/shard_map/sub | solution.py:24
  31.9 6.5 %copy.6 = bf16[1024,8,256]{2,0,1:T(8,128)(2,1)} copy(bf16[1024,8,256]{0,2,1:T(8,128)(2,1)} %bitcast.79) | data formatting | bytes 8388608 | tf_op jit(solution)/shard_map/neg | solution.py:31
  38.3 5.4 %all-to-all-done = bf16[8,256,256]{2,1,0:T(8,128)(2,1)S(1)} async-done(((bf16[8,256,256]{2,1,0:T(8,128)(2,1)}), bf16[8,256,256]{2,1,0:T(8,128)(2,1)S(1)}, u32[]{:S(2)}, u32[]{:S(2)}) %all-to-all-start) | async-done | bytes 1048608 | tf_op jit(solution)/shard_map/all_to_all | solution.py:175
  43.8 3.6 %all-to-all-start.1 = ((bf16[8,256,256]{2,1,0:T(8,128)(2,1)}), bf16[8,256,256]{2,1,0:T(8,128)(2,1)S(1)}, u32[]{:S(2)}, u32[]{:S(2)}) async-start(bf16[8,256,256]{2,1,0:T(8,128)(2,1)} %get-tuple-element.15), calls=%async_computation.1 | async-start | bytes 2097152 | tf_op jit(solution)/shard_map/all_to_all | solution.py:175
  47.4 5.9 %convolution_bitcast_fusion.3 = f32[2048,256]{1,0:T(8,128)S(1)} fusion(bf16[8,256,256]{2,1,0:T(8,128)(2,1)S(1)} %all-to-all-done, bf16[1024,8,256]{2,0,1:T(8,128)(2,1)} %copy.6, bf16[1024,8,256]{2,0,1:T(8,128)(2,1)} %copy.5), kind=kOutput, calls=%fused_computation.14 | convolution fusion | flops 2164260864 | bytes 11534336 | tf_op jit(solution)/shard_map/fjm,jmc->fc/dot_general | solution.py:178
  54.0 2.1 collective-permute-start.1
  56.2 0.6 reduce-window.6
  57.1 17.5 %all-to-all-done.1 = bf16[8,256,256]{2,1,0:T(8,128)(2,1)S(1)} async-done(((bf16[8,256,256]{2,1,0:T(8,128)(2,1)}), bf16[8,256,256]{2,1,0:T(8,128)(2,1)S(1)}, u32[]{:S(2)}, u32[]{:S(2)}) %all-to-all-start.1) | async-done | bytes 1048608 | tf_op jit(solution)/shard_map/all_to_all | solution.py:175
  74.6 4.3 %all-to-all-start.2 = ((bf16[8,256,256]{2,1,0:T(8,128)(2,1)}), bf16[8,256,256]{2,1,0:T(8,128)(2,1)}, u32[]{:S(2)}, u32[]{:S(2)}) async-start(bf16[8,256,256]{2,1,0:T(8,128)(2,1)} %get-tuple-element.14), calls=%async_computation.2 | async-start | bytes 2097152 | tf_op jit(solution)/shard_map/all_to_all | solution.py:175
  78.9 5.9 %convolution_bitcast_fusion.2 = f32[2048,256]{1,0:T(8,128)S(1)} fusion(bf16[8,256,256]{2,1,0:T(8,128)(2,1)S(1)} %all-to-all-done.1, bf16[1024,8,256]{2,0,1:T(8,128)(2,1)} %copy.6, bf16[1024,8,256]{2,0,1:T(8,128)(2,1)} %copy.5), kind=kOutput, calls=%fused_computation.13 | convolution fusion | flops 2164260864 | bytes 11534336 | tf_op jit(solution)/shard_map/fjm,jmc->fc/dot_general | solution.py:178
  85.4 1.1 fusion.89
  86.5 1.9 collective-permute-start.3
  88.4 10.1 %collective-permute-start.4 = (bf16[2048,128]{1,0:T(8,128)(2,1)}, bf16[2048,128]{1,0:T(8,128)(2,1)}, u32[]{:S(2)}, u32[]{:S(2)}) collective-permute-start(bf16[2048,128]{1,0:T(8,128)(2,1)} %get-tuple-element.60), channel_id=1, source_target_pairs={{0,8},{4,0},{12,4},{20,12},{28,20},{24,28},{16,24},{8,16},{1,9},{5... | collective-permute-start | bytes 1572872 | tf_op jit(solution)/shard_map/ppermute | solution.py:181
  98.5 2.0 fusion.25
  100.4 2.0 fusion.24
  102.4 1.3 multiply_add_fusion.4
  103.7 4.8 %all-to-all-done.2 = bf16[8,256,256]{2,1,0:T(8,128)(2,1)} async-done(((bf16[8,256,256]{2,1,0:T(8,128)(2,1)}), bf16[8,256,256]{2,1,0:T(8,128)(2,1)}, u32[]{:S(2)}, u32[]{:S(2)}) %all-to-all-start.2) | async-done | bytes 1048608 | tf_op jit(solution)/shard_map/all_to_all | solution.py:175
  108.5 4.2 %all-to-all-start.3 = ((bf16[8,256,256]{2,1,0:T(8,128)(2,1)}), bf16[8,256,256]{2,1,0:T(8,128)(2,1)}, u32[]{:S(2)}, u32[]{:S(2)}) async-start(bf16[8,256,256]{2,1,0:T(8,128)(2,1)} %get-tuple-element.13), calls=%async_computation.3 | async-start | bytes 2097152 | tf_op jit(solution)/shard_map/all_to_all | solution.py:175
  113.1 6.1 %convolution_bitcast_fusion.1 = f32[2048,256]{1,0:T(8,128)S(1)} fusion(bf16[8,256,256]{2,1,0:T(8,128)(2,1)} %all-to-all-done.2, bf16[1024,8,256]{2,0,1:T(8,128)(2,1)} %copy.6, bf16[1024,8,256]{2,0,1:T(8,128)(2,1)} %copy.5), kind=kOutput, calls=%fused_computation.12 | convolution fusion | flops 2164260864 | bytes 11534336 | tf_op jit(solution)/shard_map/fjm,jmc->fc/dot_general | solution.py:178
  119.8 1.1 fusion.88
  120.9 4.9 %collective-permute-start.5 = (bf16[2048,128]{1,0:T(8,128)(2,1)}, bf16[2048,128]{1,0:T(8,128)(2,1)}, u32[]{:S(2)}, u32[]{:S(2)}) collective-permute-start(bf16[2048,128]{1,0:T(8,128)(2,1)} %get-tuple-element.57), channel_id=1, source_target_pairs={{0,4},{4,12},{12,20},{20,28},{28,24},{24,16},{16,8},{8,0},{1,5},{5... | collective-permute-start | bytes 1572872 | tf_op jit(solution)/shard_map/ppermute | solution.py:180
  125.8 3.7 %collective-permute-start.6 = (bf16[2048,128]{1,0:T(8,128)(2,1)}, bf16[2048,128]{1,0:T(8,128)(2,1)}, u32[]{:S(2)}, u32[]{:S(2)}) collective-permute-start(bf16[2048,128]{1,0:T(8,128)(2,1)} %get-tuple-element.58), channel_id=1, source_target_pairs={{0,8},{4,0},{12,4},{20,12},{28,20},{24,28},{16,24},{8,16},{1,9},{5... | collective-permute-start | bytes 1572872 | tf_op jit(solution)/shard_map/ppermute | solution.py:181
  129.5 2.0 fusion.23
  131.5 2.0 fusion.22
  133.5 1.6 multiply_add_fusion.3
  135.1 7.1 %all-to-all-done.3 = bf16[8,256,256]{2,1,0:T(8,128)(2,1)} async-done(((bf16[8,256,256]{2,1,0:T(8,128)(2,1)}), bf16[8,256,256]{2,1,0:T(8,128)(2,1)}, u32[]{:S(2)}, u32[]{:S(2)}) %all-to-all-start.3) | async-done | bytes 1048608 | tf_op jit(solution)/shard_map/all_to_all | solution.py:175
  142.2 4.9 %collective-permute-done.5 = bf16[2048,128]{1,0:T(8,128)(2,1)} collective-permute-done((bf16[2048,128]{1,0:T(8,128)(2,1)}, bf16[2048,128]{1,0:T(8,128)(2,1)}, u32[]{:S(2)}, u32[]{:S(2)}) %collective-permute-start.5) | collective-permute-done | bytes 524320 | tf_op jit(solution)/shard_map/ppermute | solution.py:180
  147.2 6.1 %convolution_bitcast_fusion = f32[2048,256]{1,0:T(8,128)S(1)} fusion(bf16[8,256,256]{2,1,0:T(8,128)(2,1)} %all-to-all-done.3, bf16[1024,8,256]{2,0,1:T(8,128)(2,1)} %copy.6, bf16[1024,8,256]{2,0,1:T(8,128)(2,1)} %copy.5), kind=kOutput, calls=%fused_computation.11 | convolution fusion | flops 2164260864 | bytes 11534336 | tf_op jit(solution)/shard_map/fjm,jmc->fc/dot_general | solution.py:178
  154.0 3.8 %collective-permute-start.7 = (bf16[2048,128]{1,0:T(8,128)(2,1)S(1)}, bf16[2048,128]{1,0:T(8,128)(2,1)S(1)}, u32[]{:S(2)}, u32[]{:S(2)}) collective-permute-start(bf16[2048,128]{1,0:T(8,128)(2,1)S(1)} %get-tuple-element.55), channel_id=1, source_target_pairs={{0,4},{4,12},{12,20},{20,28},{28,24},{24,16},{16,8},{8,0},{1,5},{5... | collective-permute-start | bytes 1572872 | tf_op jit(solution)/shard_map/ppermute | solution.py:180
  157.8 2.2 collective-permute-start.8
  160.0 2.0 fusion.21
  161.9 2.0 fusion.20
  164.2 6.5 %collective-permute-done.7 = bf16[2048,128]{1,0:T(8,128)(2,1)S(1)} collective-permute-done((bf16[2048,128]{1,0:T(8,128)(2,1)S(1)}, bf16[2048,128]{1,0:T(8,128)(2,1)S(1)}, u32[]{:S(2)}, u32[]{:S(2)}) %collective-permute-start.7) | collective-permute-done | bytes 524320 | tf_op jit(solution)/shard_map/ppermute | solution.py:180
  170.6 1.2 collective-permute-done.8
  171.9 0.8 fusion.19
  172.6 0.8 fusion.18
  173.7 0.9 copy-done.1
  175.3 0.5 fusion.6
  176.4 1.0 fusion.65
  177.4 1.3 collective-permute-done.9
  178.8 1.3 dynamic-slice_add_fusion
  180.1 1.6 collective-permute-start.10
  181.6 1.2 multiply_subtract_fusion
  182.9 0.6 bitcast_multiply_fusion
  183.5 21.9 %collective-permute-done.10 = f32[2048,128]{1,0:T(8,128)S(1)} collective-permute-done((f32[2048,128]{1,0:T(8,128)S(1)}, f32[2048,128]{1,0:T(8,128)S(1)}, u32[]{:S(2)}, u32[]{:S(2)}) %collective-permute-start.10) | collective-permute-done | bytes 1048608 | tf_op jit(solution)/shard_map/ppermute | solution.py:127
  205.4 2.3 fusion.10
  207.8 1.3 collective-permute-done.11
  209.5 21.9 %all_to_all.25 = bf16[8,80,512]{2,1,0:T(8,128)(2,1)S(1)} all-to-all(bf16[8,80,512]{2,1,0:T(8,128)(2,1)S(1)} %bitcast.85), channel_id=1, replica_groups=mesh['tile'=8,'win'=4] {'tile'}, dimensions={0} | all-to-all | bytes 1310720 | tf_op jit(solution)/shard_map/all_to_all | solution.py:199
  231.6 0.8 copy-done.4
  (67 shorter events, 5.5 us)
Async XLA Ops:
  0.0 6.5 %copy-start = (bf16[4,256,2048]{2,1,0:T(8,128)(2,1)S(1)}, bf16[4,256,2048]{2,1,0:T(8,128)(2,1)}, u32[]{:S(2)}) copy-start(bf16[4,256,2048]{2,1,0:T(8,128)(2,1)} %param.4) | copy-start | bytes 12582916
  5.1 13.0 %copy-start.5 = (s32[256,1]{0,1:T(1,128)S(1)}, s32[256,1]{0,1:T(1,128)}, u32[]{:S(2)}) copy-start(s32[256,1]{0,1:T(1,128)} %param.7) | copy-start | bytes 3076
  5.1 13.0 %copy-start.6 = (s32[256]{0:T(256)S(1)}, s32[256]{0:T(256)}, u32[]{:S(2)}) copy-start(s32[256]{0:T(256)} %param.6) | copy-start | bytes 3076
  5.1 13.0 %copy-start.7 = (s32[256]{0:T(256)S(1)}, s32[256]{0:T(256)}, u32[]{:S(2)}) copy-start(s32[256]{0:T(256)} %param.5) | copy-start | bytes 3076
  10.7 33.1 %all-to-all-start = ((bf16[8,256,256]{2,1,0:T(8,128)(2,1)}), bf16[8,256,256]{2,1,0:T(8,128)(2,1)S(1)}, u32[]{:S(2)}, u32[]{:S(2)}) async-start(bf16[8,256,256]{2,1,0:T(8,128)(2,1)} %get-tuple-element.16), calls=%async_computation | async-start | bytes 2097152 | tf_op jit(solution)/shard_map/all_to_all | solution.py:175
  18.1 20.3 %collective-permute-start = (s32[3,256]{1,0:T(4,128)S(1)}, s32[3,256]{1,0:T(4,128)S(1)}, u32[]{:S(2)}, u32[]{:S(2)}) collective-permute-start(s32[3,256]{1,0:T(4,128)S(1)} %pad_add_fusion), channel_id=1, source_target_pairs={{0,0},{4,4},{8,12},{12,20},{16,28},{20,24},{24,16},{28,8},{1,1},{5... | collective-permute-start | bytes 9224 | tf_op jit(solution)/shard_map/ppermute | solution.py:155
  43.8 30.8 %all-to-all-start.1 = ((bf16[8,256,256]{2,1,0:T(8,128)(2,1)}), bf16[8,256,256]{2,1,0:T(8,128)(2,1)S(1)}, u32[]{:S(2)}, u32[]{:S(2)}) async-start(bf16[8,256,256]{2,1,0:T(8,128)(2,1)} %get-tuple-element.15), calls=%async_computation.1 | async-start | bytes 2097152 | tf_op jit(solution)/shard_map/all_to_all | solution.py:175
  54.0 24.8 %collective-permute-start.1 = (bf16[2048,128]{1,0:T(8,128)(2,1)S(1)}, bf16[2048,128]{1,0:T(8,128)(2,1)}, u32[]{:S(2)}, u32[]{:S(2)}) collective-permute-start(bf16[2048,128]{1,0:T(8,128)(2,1)S(1)} %get-tuple-element.61), channel_id=1, source_target_pairs={{0,4},{4,12},{12,20},{20,28},{28,24},{24,16},{16,8},{8,0},{1,5},{5... | collective-permute-start | bytes 1572872 | tf_op jit(solution)/shard_map/ppermute | solution.py:180
  56.1 22.8 %collective-permute-start.2 = (bf16[2048,128]{1,0:T(8,128)(2,1)S(1)}, bf16[2048,128]{1,0:T(8,128)(2,1)}, u32[]{:S(2)}, u32[]{:S(2)}) collective-permute-start(bf16[2048,128]{1,0:T(8,128)(2,1)S(1)} %get-tuple-element.62), channel_id=1, source_target_pairs={{0,8},{4,0},{12,4},{20,12},{28,20},{24,28},{16,24},{8,16},{1,9},{5... | collective-permute-start | bytes 1572872 | tf_op jit(solution)/shard_map/ppermute | solution.py:181
  74.6 33.9 %all-to-all-start.2 = ((bf16[8,256,256]{2,1,0:T(8,128)(2,1)}), bf16[8,256,256]{2,1,0:T(8,128)(2,1)}, u32[]{:S(2)}, u32[]{:S(2)}) async-start(bf16[8,256,256]{2,1,0:T(8,128)(2,1)} %get-tuple-element.14), calls=%async_computation.2 | async-start | bytes 2097152 | tf_op jit(solution)/shard_map/all_to_all | solution.py:175
  86.5 26.6 %collective-permute-start.3 = (bf16[2048,128]{1,0:T(8,128)(2,1)}, bf16[2048,128]{1,0:T(8,128)(2,1)}, u32[]{:S(2)}, u32[]{:S(2)}) collective-permute-start(bf16[2048,128]{1,0:T(8,128)(2,1)} %get-tuple-element.59), channel_id=1, source_target_pairs={{0,4},{4,12},{12,20},{20,28},{28,24},{24,16},{16,8},{8,0},{1,5},{5... | collective-permute-start | bytes 1572872 | tf_op jit(solution)/shard_map/ppermute | solution.py:180
  88.4 24.7 %collective-permute-start.4 = (bf16[2048,128]{1,0:T(8,128)(2,1)}, bf16[2048,128]{1,0:T(8,128)(2,1)}, u32[]{:S(2)}, u32[]{:S(2)}) collective-permute-start(bf16[2048,128]{1,0:T(8,128)(2,1)} %get-tuple-element.60), channel_id=1, source_target_pairs={{0,8},{4,0},{12,4},{20,12},{28,20},{24,28},{16,24},{8,16},{1,9},{5... | collective-permute-start | bytes 1572872 | tf_op jit(solution)/shard_map/ppermute | solution.py:181
  108.5 33.7 %all-to-all-start.3 = ((bf16[8,256,256]{2,1,0:T(8,128)(2,1)}), bf16[8,256,256]{2,1,0:T(8,128)(2,1)}, u32[]{:S(2)}, u32[]{:S(2)}) async-start(bf16[8,256,256]{2,1,0:T(8,128)(2,1)} %get-tuple-element.13), calls=%async_computation.3 | async-start | bytes 2097152 | tf_op jit(solution)/shard_map/all_to_all | solution.py:175
  120.9 26.3 %collective-permute-start.5 = (bf16[2048,128]{1,0:T(8,128)(2,1)}, bf16[2048,128]{1,0:T(8,128)(2,1)}, u32[]{:S(2)}, u32[]{:S(2)}) collective-permute-start(bf16[2048,128]{1,0:T(8,128)(2,1)} %get-tuple-element.57), channel_id=1, source_target_pairs={{0,4},{4,12},{12,20},{20,28},{28,24},{24,16},{16,8},{8,0},{1,5},{5... | collective-permute-start | bytes 1572872 | tf_op jit(solution)/shard_map/ppermute | solution.py:180
  125.8 21.4 %collective-permute-start.6 = (bf16[2048,128]{1,0:T(8,128)(2,1)}, bf16[2048,128]{1,0:T(8,128)(2,1)}, u32[]{:S(2)}, u32[]{:S(2)}) collective-permute-start(bf16[2048,128]{1,0:T(8,128)(2,1)} %get-tuple-element.58), channel_id=1, source_target_pairs={{0,8},{4,0},{12,4},{20,12},{28,20},{24,28},{16,24},{8,16},{1,9},{5... | collective-permute-start | bytes 1572872 | tf_op jit(solution)/shard_map/ppermute | solution.py:181
  154.0 16.6 %collective-permute-start.7 = (bf16[2048,128]{1,0:T(8,128)(2,1)S(1)}, bf16[2048,128]{1,0:T(8,128)(2,1)S(1)}, u32[]{:S(2)}, u32[]{:S(2)}) collective-permute-start(bf16[2048,128]{1,0:T(8,128)(2,1)S(1)} %get-tuple-element.55), channel_id=1, source_target_pairs={{0,4},{4,12},{12,20},{20,28},{28,24},{24,16},{16,8},{8,0},{1,5},{5... | collective-permute-start | bytes 1572872 | tf_op jit(solution)/shard_map/ppermute | solution.py:180
  157.8 14.1 %collective-permute-start.8 = (bf16[2048,128]{1,0:T(8,128)(2,1)S(1)}, bf16[2048,128]{1,0:T(8,128)(2,1)S(1)}, u32[]{:S(2)}, u32[]{:S(2)}) collective-permute-start(bf16[2048,128]{1,0:T(8,128)(2,1)S(1)} %get-tuple-element.56), channel_id=1, source_target_pairs={{0,8},{4,0},{12,4},{20,12},{28,20},{24,28},{16,24},{8,16},{1,9},{5... | collective-permute-start | bytes 1572872 | tf_op jit(solution)/shard_map/ppermute | solution.py:181
  173.4 1.2 copy-start.1
  173.4 1.5 copy-start.2
  173.4 1.8 copy-start.3
  175.9 2.9 %collective-permute-start.9 = (f32[2048,128]{1,0:T(8,128)S(1)}, f32[2048,128]{1,0:T(8,128)}, u32[]{:S(2)}, u32[]{:S(2)}) collective-permute-start(f32[2048,128]{1,0:T(8,128)S(1)} %constant_dynamic-slice_fusion.2), channel_id=1, source_target_pairs={{0,1},{1,0},{2,3},{3,2},{4,5},{5,4},{6,7},{7,6},{8,9},{9,8},{10,11... | collective-permute-start | bytes 3145736 | tf_op jit(solution)/shard_map/ppermute | solution.py:124
  180.1 25.3 %collective-permute-start.10 = (f32[2048,128]{1,0:T(8,128)S(1)}, f32[2048,128]{1,0:T(8,128)S(1)}, u32[]{:S(2)}, u32[]{:S(2)}) collective-permute-start(f32[2048,128]{1,0:T(8,128)S(1)} %dynamic-slice_add_fusion), channel_id=1, source_target_pairs={{0,2},{1,3},{2,0},{3,1},{4,6},{5,7},{6,4},{7,5},{8,10},{9,11},{10,... | collective-permute-start | bytes 3145736 | tf_op jit(solution)/shard_map/ppermute | solution.py:127
  207.7 1.4 collective-permute-start.11
  231.6 0.8 copy-start.4

commit v11 on v10

--- a/solution.py
+++ b/solution.py
@@ -117,17 +117,23 @@
         inverse = inverse_matrix(length, win * lag_count, lag_count, seg_total)
         return jnp.dot(inverse, stacked, precision=lax.Precision.HIGH).astype(jnp.bfloat16)
     core = win % 2
+    chip = win // 2
     half = cross.shape[1] // 2
     mine = lax.dynamic_slice_in_dim(cross, core * half, half, axis=1)
     other = lax.dynamic_slice_in_dim(cross, (1 - core) * half, half, axis=1)
     partner = [(w, w ^ 1) for w in range(win_count)]
     total = mine + lax.ppermute(other, "win", partner)
-    step = 2
-    while step < win_count:
-        total = total + lax.ppermute(total, "win", [(w, w ^ step) for w in range(win_count)])
-        step *= 2
-    inverse = inverse_matrix(length, (win - core) * lag_count, 2 * lag_count, seg_total)
-    both = jnp.dot(inverse, total, precision=lax.Precision.HIGH).astype(jnp.bfloat16)
+    inverse = inverse_matrix(length, 0, length, seg_total)
+    lags = jnp.dot(inverse, total, precision=lax.Precision.HIGH)
+    bit = win_count // 4
+    while bit >= 1:
+        rows = lags.shape[0] // 2
+        upper = (chip // bit) % 2
+        keep = lax.dynamic_slice_in_dim(lags, upper * rows, rows, axis=0)
+        send = lax.dynamic_slice_in_dim(lags, (1 - upper) * rows, rows, axis=0)
+        lags = keep + lax.ppermute(send, "win", [(w, w ^ (2 * bit)) for w in range(win_count)])
+        bit //= 2
+    both = lags.astype(jnp.bfloat16)
     kept = lax.dynamic_slice_in_dim(both, core * lag_count, lag_count, axis=0)
     given = lax.dynamic_slice_in_dim(both, (1 - core) * lag_count, lag_count, axis=0)
     got = lax.ppermute(given, "win", partner)

time: 233 us -> 244 us (1.047)
  waiting for transfers between devices: 72.4 us -> 46.9 us
  other arithmetic: 19.4 us -> 36.3 us
  starting transfers between devices: 50.5 us -> 62.5 us
  matrix products: 40.1 us -> 46.1 us
    ppermute x1, waiting for transfers between devices: 21.9 us -> 10.6 us  [sum_and_invert(): lax.ppermute(send, 'win', [(w, w ^ 2 * bit) for w in range(win_count)])]
    all_to_all x4, waiting for transfers between devices: 34.8 us -> 23.8 us  [per_device(): lax.all_to_all(outgoing, 'tile', split_axis=0, concat_axis=0, tiled=True)]
    mul x1, other arithmetic: 0.61 us -> 7.56 us  [inverse_matrix(): return jnp.concatenate([weights * cosine, -weights * sine], axis=1)]
    ppermute x4, starting transfers between devices: 16.1 us -> 22.3 us  [per_device(): from_next = lax.ppermute(whitened[:, :half], 'tile', to_prev)]
    dot_general x1, matrix products: 2.29 us -> 8.24 us  [sum_and_invert(): lags = jnp.dot(inverse, total, precision=lax.Precision.HIGH)]
    sub x1, other arithmetic: 1.22 us -> 7.04 us  [phase_table(): cosine = (c_hi * c_lo - s_hi * s_lo).reshape(shape)]
    all_to_all x4, starting transfers between devices: 19.4 us -> 23.6 us  [per_device(): lax.all_to_all(outgoing, 'tile', split_axis=0, concat_axis=0, tiled=True)]
    unnamed x28 -> x32, local copies, waits for them, and re-layouts: 9.75 us -> 11 us
  transfers between devices with their start and end apart: 16 -> 16, of which waited for: 11 -> 8; matrix products, arithmetic and copies ran while one was open for 26% -> 35% of each run, Pallas kernels for 0% -> 0%
where the time goes in v11:
time: 244 us
  starting transfers between devices  62.5 us (26%)
  waiting for transfers between devices  46.9 us (19%)
  matrix products  46.1 us (19%)
  other arithmetic  36.3 us (15%)
  local copies, waits for them, and re-layouts  28.8 us (12%)
  blocking collectives  22.5 us (9%)
    dot_general x4, matrix products, per_device(): jnp.einsum('fjm,jmc->fc', forward, received, preferred_element_type=jnp.f...  24.2 us
    all_to_all x4, waiting for transfers between devices, per_device(): lax.all_to_all(outgoing, 'tile', split_axis=0, concat_axis=0, tiled=True)  23.8 us
    all_to_all x4, starting transfers between devices, per_device(): lax.all_to_all(outgoing, 'tile', split_axis=0, concat_axis=0, tiled=True)  23.6 us
    all_to_all x1, blocking collectives, per_device(): lax.all_to_all(buckets, 'tile', split_axis=0, concat_axis=0, tiled=True)  22.5 us
    ppermute x4, starting transfers between devices, per_device(): from_next = lax.ppermute(whitened[:, :half], 'tile', to_prev)  22.3 us
    ppermute x4, starting transfers between devices, per_device(): from_prev = lax.ppermute(whitened[:, half:], 'tile', to_next)  14.1 us
    unnamed x32, local copies, waits for them, and re-layouts  11 us
    ppermute x1, waiting for transfers between devices, sum_and_invert(): lax.ppermute(send, 'win', [(w, w ^ 2 * bit) for w in range(win_count)])  10.6 us
  transfers between devices with their start and end apart: 16, of which 8 were waited for; matrix products, arithmetic and copies ran while one was open for 35% of the time, Pallas kernels for 0%

profile of v11, /device:TPU:0, one launch (start us, length us, event | category | flops | bytes accessed | tf_op | source)
XLA Modules:
  0.0 243.7 jit_solution(8512624168528419125)
XLA Ops:
  0.0 0.9 pad_add_fusion
  0.9 0.8 collective-permute-start
  1.7 1.1 slice_bitcast_fusion.1
  2.8 1.9 slice_dynamic-update-slice_fusion.7
  4.7 1.9 slice_dynamic-update-slice_fusion.6
  6.6 0.7 fusion.61
  7.3 0.7 fusion.59
  8.0 0.8 slice_dynamic-update-slice_fusion.5
  8.8 0.8 slice_dynamic-update-slice_fusion.4
  9.6 0.8 slice_dynamic-update-slice_fusion.3
  10.3 0.8 slice_dynamic-update-slice_fusion.2
  11.1 0.8 slice_dynamic-update-slice_fusion.1
  11.9 1.0 copy-done.4
  12.9 9.1 %all-to-all-start = ((bf16[8,256,256]{2,1,0:T(8,128)(2,1)}), bf16[8,256,256]{2,1,0:T(8,128)(2,1)S(1)}, u32[]{:S(2)}, u32[]{:S(2)}) async-start(bf16[8,256,256]{2,1,0:T(8,128)(2,1)} %get-tuple-element.16), calls=%async_computation | async-start | bytes 2097152 | tf_op jit(solution)/shard_map/all_to_all | solution.py:181
  22.1 1.9 fusion.50
  24.0 1.9 fusion.49
  25.9 1.0 fusion.63
  27.5 0.6 fusion.74
  28.1 5.0 %subtract_convert_fusion = (bf16[1024,32,64]{0,2,1:T(8,128)(2,1)}, bf16[1024,32,64]{0,2,1:T(8,128)(2,1)}) fusion(f32[1024,64]{0,1:T(8,128)S(1)} %get-tuple-element.82, f32[1024,32]{0,1:T(8,128)S(1)} %get-tuple-element.73, f32[1024,64]{0,1:T(8,128)S(1)} %get-tuple-element.83, f32[1024,32]{0,1:T(8,128)S(1)} %get-tuple-element.72), kind=kLoop, calls=%fused_computation.8 | loop fusion | flops 18874368 | bytes 9175040 | tf_op jit(solution)/shard_map/convert.3
  33.1 7.0 %multiply_subtract_fusion = (f32[2048,16,64]{0,2,1:T(8,128)}, f32[2048,16,64]{0,2,1:T(8,128)}) fusion(f32[2048,64]{0,1:T(8,128)S(1)} %fusion.49, f32[2048,16]{0,1:T(8,128)S(1)} %get-tuple-element.75, f32[2048,64]{0,1:T(8,128)S(1)} %fusion.50, f32[2048,16]{0,1:T(8,128)S(1)} %get-tuple-element.74), kind=kLoop, calls=%fused_computation.10 | loop fusion | flops 12582912 | bytes 18087936 | tf_op jit(solution)/shard_map/sub | solution.py:24
  40.1 6.4 %copy.5 = bf16[1024,8,256]{2,0,1:T(8,128)(2,1)} copy(bf16[1024,8,256]{0,2,1:T(8,128)(2,1)} %bitcast.84) | data formatting | bytes 8388608 | tf_op jit(solution)/shard_map/sub | solution.py:24
  46.6 6.5 %copy.6 = bf16[1024,8,256]{2,0,1:T(8,128)(2,1)} copy(bf16[1024,8,256]{0,2,1:T(8,128)(2,1)} %bitcast.83) | data formatting | bytes 8388608 | tf_op jit(solution)/shard_map/neg | solution.py:31
  53.1 6.0 %all-to-all-start.1 = ((bf16[8,256,256]{2,1,0:T(8,128)(2,1)}), bf16[8,256,256]{2,1,0:T(8,128)(2,1)S(1)}, u32[]{:S(2)}, u32[]{:S(2)}) async-start(bf16[8,256,256]{2,1,0:T(8,128)(2,1)} %get-tuple-element.15), calls=%async_computation.1 | async-start | bytes 2097152 | tf_op jit(solution)/shard_map/all_to_all | solution.py:181
  59.1 5.9 %convolution_bitcast_fusion.3 = f32[2048,256]{1,0:T(8,128)S(1)} fusion(bf16[8,256,256]{2,1,0:T(8,128)(2,1)S(1)} %all-to-all-done, bf16[1024,8,256]{2,0,1:T(8,128)(2,1)} %copy.6, bf16[1024,8,256]{2,0,1:T(8,128)(2,1)} %copy.5), kind=kOutput, calls=%fused_computation.14 | convolution fusion | flops 2164260864 | bytes 11534336 | tf_op jit(solution)/shard_map/fjm,jmc->fc/dot_general | solution.py:184
  65.7 2.1 collective-permute-start.1
  68.8 17.4 %all-to-all-done.1 = bf16[8,256,256]{2,1,0:T(8,128)(2,1)S(1)} async-done(((bf16[8,256,256]{2,1,0:T(8,128)(2,1)}), bf16[8,256,256]{2,1,0:T(8,128)(2,1)S(1)}, u32[]{:S(2)}, u32[]{:S(2)}) %all-to-all-start.1) | async-done | bytes 1048608 | tf_op jit(solution)/shard_map/all_to_all | solution.py:181
  86.2 4.2 %all-to-all-start.2 = ((bf16[8,256,256]{2,1,0:T(8,128)(2,1)}), bf16[8,256,256]{2,1,0:T(8,128)(2,1)}, u32[]{:S(2)}, u32[]{:S(2)}) async-start(bf16[8,256,256]{2,1,0:T(8,128)(2,1)} %get-tuple-element.14), calls=%async_computation.2 | async-start | bytes 2097152 | tf_op jit(solution)/shard_map/all_to_all | solution.py:181
  90.5 5.9 %convolution_bitcast_fusion.2 = f32[2048,256]{1,0:T(8,128)S(1)} fusion(bf16[8,256,256]{2,1,0:T(8,128)(2,1)S(1)} %all-to-all-done.1, bf16[1024,8,256]{2,0,1:T(8,128)(2,1)} %copy.6, bf16[1024,8,256]{2,0,1:T(8,128)(2,1)} %copy.5), kind=kOutput, calls=%fused_computation.13 | convolution fusion | flops 2164260864 | bytes 11534336 | tf_op jit(solution)/shard_map/fjm,jmc->fc/dot_general | solution.py:184
  97.1 1.0 fusion.91
  98.1 1.9 collective-permute-start.3
  100.0 12.1 %collective-permute-start.4 = (bf16[2048,128]{1,0:T(8,128)(2,1)}, bf16[2048,128]{1,0:T(8,128)(2,1)}, u32[]{:S(2)}, u32[]{:S(2)}) collective-permute-start(bf16[2048,128]{1,0:T(8,128)(2,1)} %get-tuple-element.62), channel_id=1, source_target_pairs={{0,8},{4,0},{12,4},{20,12},{28,20},{24,28},{16,24},{8,16},{1,9},{5... | collective-permute-start | bytes 1572872 | tf_op jit(solution)/shard_map/ppermute | solution.py:187
  112.1 2.0 fusion.23
  114.1 2.0 fusion.22
  116.3 3.7 %all-to-all-done.2 = bf16[8,256,256]{2,1,0:T(8,128)(2,1)} async-done(((bf16[8,256,256]{2,1,0:T(8,128)(2,1)}), bf16[8,256,256]{2,1,0:T(8,128)(2,1)}, u32[]{:S(2)}, u32[]{:S(2)}) %all-to-all-start.2) | async-done | bytes 1048608 | tf_op jit(solution)/shard_map/all_to_all | solution.py:181
  120.1 4.2 %all-to-all-start.3 = ((bf16[8,256,256]{2,1,0:T(8,128)(2,1)}), bf16[8,256,256]{2,1,0:T(8,128)(2,1)}, u32[]{:S(2)}, u32[]{:S(2)}) async-start(bf16[8,256,256]{2,1,0:T(8,128)(2,1)} %copy-done.4), calls=%async_computation.3 | async-start | bytes 2097152 | tf_op jit(solution)/shard_map/all_to_all | solution.py:181
  124.4 6.1 %convolution_bitcast_fusion.1 = f32[2048,256]{1,0:T(8,128)S(1)} fusion(bf16[8,256,256]{2,1,0:T(8,128)(2,1)} %all-to-all-done.2, bf16[1024,8,256]{2,0,1:T(8,128)(2,1)} %copy.6, bf16[1024,8,256]{2,0,1:T(8,128)(2,1)} %copy.5), kind=kOutput, calls=%fused_computation.12 | convolution fusion | flops 2164260864 | bytes 11534336 | tf_op jit(solution)/shard_map/fjm,jmc->fc/dot_general | solution.py:184
  131.1 1.1 fusion.90
  132.2 5.1 %collective-permute-start.5 = (bf16[2048,128]{1,0:T(8,128)(2,1)}, bf16[2048,128]{1,0:T(8,128)(2,1)}, u32[]{:S(2)}, u32[]{:S(2)}) collective-permute-start(bf16[2048,128]{1,0:T(8,128)(2,1)} %get-tuple-element.59), channel_id=1, source_target_pairs={{0,4},{4,12},{12,20},{20,28},{28,24},{24,16},{16,8},{8,0},{1,5},{5... | collective-permute-start | bytes 1572872 | tf_op jit(solution)/shard_map/ppermute | solution.py:186
  137.4 8.7 %collective-permute-start.6 = (bf16[2048,128]{1,0:T(8,128)(2,1)}, bf16[2048,128]{1,0:T(8,128)(2,1)}, u32[]{:S(2)}, u32[]{:S(2)}) collective-permute-start(bf16[2048,128]{1,0:T(8,128)(2,1)} %get-tuple-element.60), channel_id=1, source_target_pairs={{0,8},{4,0},{12,4},{20,12},{28,20},{24,28},{16,24},{8,16},{1,9},{5... | collective-permute-start | bytes 1572872 | tf_op jit(solution)/shard_map/ppermute | solution.py:187
  146.0 2.0 fusion.20
  148.0 2.0 fusion.21
  150.0 1.3 multiply_add_fusion.3
  151.2 2.6 %all-to-all-done.3 = bf16[8,256,256]{2,1,0:T(8,128)(2,1)} async-done(((bf16[8,256,256]{2,1,0:T(8,128)(2,1)}), bf16[8,256,256]{2,1,0:T(8,128)(2,1)}, u32[]{:S(2)}, u32[]{:S(2)}) %all-to-all-start.3) | async-done | bytes 1048608 | tf_op jit(solution)/shard_map/all_to_all | solution.py:181
  153.8 3.4 %collective-permute-done.5 = bf16[2048,128]{1,0:T(8,128)(2,1)} collective-permute-done((bf16[2048,128]{1,0:T(8,128)(2,1)}, bf16[2048,128]{1,0:T(8,128)(2,1)}, u32[]{:S(2)}, u32[]{:S(2)}) %collective-permute-start.5) | collective-permute-done | bytes 524320 | tf_op jit(solution)/shard_map/ppermute | solution.py:186
  157.3 6.1 %convolution_bitcast_fusion = f32[2048,256]{1,0:T(8,128)S(1)} fusion(bf16[8,256,256]{2,1,0:T(8,128)(2,1)} %all-to-all-done.3, bf16[1024,8,256]{2,0,1:T(8,128)(2,1)} %copy.6, bf16[1024,8,256]{2,0,1:T(8,128)(2,1)} %copy.5), kind=kOutput, calls=%fused_computation.11 | convolution fusion | flops 2164260864 | bytes 11534336 | tf_op jit(solution)/shard_map/fjm,jmc->fc/dot_general | solution.py:184
  164.1 5.0 %collective-permute-start.7 = (bf16[2048,128]{1,0:T(8,128)(2,1)S(1)}, bf16[2048,128]{1,0:T(8,128)(2,1)S(1)}, u32[]{:S(2)}, u32[]{:S(2)}) collective-permute-start(bf16[2048,128]{1,0:T(8,128)(2,1)S(1)} %get-tuple-element.57), channel_id=1, source_target_pairs={{0,4},{4,12},{12,20},{20,28},{28,24},{24,16},{16,8},{8,0},{1,5},{5... | collective-permute-start | bytes 1572872 | tf_op jit(solution)/shard_map/ppermute | solution.py:186
  169.1 1.5 collective-permute-start.8
  170.6 2.0 fusion.18
  172.6 2.0 fusion.19
  174.8 5.9 %collective-permute-done.7 = bf16[2048,128]{1,0:T(8,128)(2,1)S(1)} collective-permute-done((bf16[2048,128]{1,0:T(8,128)(2,1)S(1)}, bf16[2048,128]{1,0:T(8,128)(2,1)S(1)}, u32[]{:S(2)}, u32[]{:S(2)}) %collective-permute-start.7) | collective-permute-done | bytes 524320 | tf_op jit(solution)/shard_map/ppermute | solution.py:186
  180.7 1.8 collective-permute-done.8
  182.5 0.8 fusion.16
  183.3 0.8 fusion.17
  184.1 1.3 multiply_add_fusion.1
  185.4 2.6 %fusion.6 = f32[2048,256]{1,0:T(8,128)S(1)} fusion(f32[1024,256]{1,0:T(8,128)S(1)} %get-tuple-element.54, f32[1024,256]{1,0:T(8,128)S(1)} %get-tuple-element.53, f32[1024,256]{1,0:T(8,128)S(1)} %copy-done.1, f32[1024,256]{1,0:T(8,128)S(1)} %get-tuple-element.51, f32[1024,256]{1,0:T(8,128)S(1)} %get-tuple-element.50, f32[1024,256]{1,0:T(8,128)S(1)} %get-tuple-element.49, ...), kind=kLoop, calls=%fused_computation.20 | loop fusion | flops 3670016 | bytes 10485760 | tf_op jit(solution)/shard_map/add | solution.py:193
  188.1 1.0 slice-done.3
  189.1 1.2 slice-done.1
  190.3 7.6 %bitcast_multiply_fusion = (f32[2048,1024]{0,1:T(8,128)}, f32[2048,1024]{0,1:T(8,128)}) fusion(f32[2048,16,64]{0,2,1:T(8,128)S(1)} %bitcast.82, f32[1024]{0:T(1024)S(1)} %fusion.77, f32[2048,16,64]{0,2,1:T(8,128)S(1)} %bitcast.80, f32[1024]{0:T(1024)S(1)} %select_multiply_fusion), kind=kLoop, calls=%fused_computation.5 | loop fusion | flops 4194304 | bytes 33562624 | tf_op jit(solution)/shard_map/mul | solution.py:42
  197.9 8.2 %fusion = f32[2048,128]{0,1:T(8,128)S(1)} fusion(f32[2048,1024]{0,1:T(8,128)} %get-tuple-element.76, f32[2048,1024]{0,1:T(8,128)} %get-tuple-element.77, f32[2048,128]{1,0:T(8,128)S(1)} %collective-permute-done.9, f32[2048,256]{1,0:T(8,128)S(1)} %fusion.6, s32[]{:T(128)S(6)} %select_n.123), kind=kOutput, calls=%fused_computation | convolution fusion | flops 3225681920 | bytes 19922948 | tf_op jit(solution)/shard_map/dot_general | solution.py:127
  206.2 1.6 collective-permute-start.10
  207.8 10.6 %collective-permute-done.10 = f32[1024,128]{0,1:T(8,128)S(1)} collective-permute-done((f32[1024,128]{0,1:T(8,128)S(1)}, f32[1024,128]{0,1:T(8,128)S(1)}, u32[]{:S(2)}, u32[]{:S(2)}) %collective-permute-start.10) | collective-permute-done | bytes 524320 | tf_op jit(solution)/shard_map/ppermute | solution.py:134
  218.5 1.3 collective-permute-done.11
  220.2 22.5 %all_to_all.25 = bf16[8,80,512]{2,1,0:T(8,128)(2,1)S(1)} all-to-all(bf16[8,80,512]{2,1,0:T(8,128)(2,1)S(1)} %bitcast.89), channel_id=1, replica_groups=mesh['tile'=8,'win'=4] {'tile'}, dimensions={0} | all-to-all | bytes 1310720 | tf_op jit(solution)/shard_map/all_to_all | solution.py:205
  242.8 0.8 copy-done.5
  (74 shorter events, 5.4 us)
Async XLA Ops:
  0.0 8.0 %copy-start = (bf16[4,256,2048]{2,1,0:T(8,128)(2,1)S(1)}, bf16[4,256,2048]{2,1,0:T(8,128)(2,1)}, u32[]{:S(2)}) copy-start(bf16[4,256,2048]{2,1,0:T(8,128)(2,1)} %param.4) | copy-start | bytes 12582916
  0.9 52.2 %collective-permute-start = (s32[3,256]{1,0:T(4,128)S(1)}, s32[3,256]{1,0:T(4,128)S(1)}, u32[]{:S(2)}, u32[]{:S(2)}) collective-permute-start(s32[3,256]{1,0:T(4,128)S(1)} %pad_add_fusion), channel_id=1, source_target_pairs={{0,0},{4,4},{8,12},{12,20},{16,28},{20,24},{24,16},{28,8},{1,1},{5... | collective-permute-start | bytes 9224 | tf_op jit(solution)/shard_map/ppermute | solution.py:161
  11.9 1.0 copy-start.4
  12.9 40.2 %all-to-all-start = ((bf16[8,256,256]{2,1,0:T(8,128)(2,1)}), bf16[8,256,256]{2,1,0:T(8,128)(2,1)S(1)}, u32[]{:S(2)}, u32[]{:S(2)}) async-start(bf16[8,256,256]{2,1,0:T(8,128)(2,1)} %get-tuple-element.16), calls=%async_computation | async-start | bytes 2097152 | tf_op jit(solution)/shard_map/all_to_all | solution.py:181
  53.1 33.1 %all-to-all-start.1 = ((bf16[8,256,256]{2,1,0:T(8,128)(2,1)}), bf16[8,256,256]{2,1,0:T(8,128)(2,1)S(1)}, u32[]{:S(2)}, u32[]{:S(2)}) async-start(bf16[8,256,256]{2,1,0:T(8,128)(2,1)} %get-tuple-element.15), calls=%async_computation.1 | async-start | bytes 2097152 | tf_op jit(solution)/shard_map/all_to_all | solution.py:181
  65.7 24.8 %collective-permute-start.1 = (bf16[2048,128]{1,0:T(8,128)(2,1)S(1)}, bf16[2048,128]{1,0:T(8,128)(2,1)}, u32[]{:S(2)}, u32[]{:S(2)}) collective-permute-start(bf16[2048,128]{1,0:T(8,128)(2,1)S(1)} %get-tuple-element.63), channel_id=1, source_target_pairs={{0,4},{4,12},{12,20},{20,28},{28,24},{24,16},{16,8},{8,0},{1,5},{5... | collective-permute-start | bytes 1572872 | tf_op jit(solution)/shard_map/ppermute | solution.py:186
  67.8 22.7 %collective-permute-start.2 = (bf16[2048,128]{1,0:T(8,128)(2,1)S(1)}, bf16[2048,128]{1,0:T(8,128)(2,1)}, u32[]{:S(2)}, u32[]{:S(2)}) collective-permute-start(bf16[2048,128]{1,0:T(8,128)(2,1)S(1)} %get-tuple-element.64), channel_id=1, source_target_pairs={{0,8},{4,0},{12,4},{20,12},{28,20},{24,28},{16,24},{8,16},{1,9},{5... | collective-permute-start | bytes 1572872 | tf_op jit(solution)/shard_map/ppermute | solution.py:187
  86.2 33.9 %all-to-all-start.2 = ((bf16[8,256,256]{2,1,0:T(8,128)(2,1)}), bf16[8,256,256]{2,1,0:T(8,128)(2,1)}, u32[]{:S(2)}, u32[]{:S(2)}) async-start(bf16[8,256,256]{2,1,0:T(8,128)(2,1)} %get-tuple-element.14), calls=%async_computation.2 | async-start | bytes 2097152 | tf_op jit(solution)/shard_map/all_to_all | solution.py:181
  98.1 26.2 %collective-permute-start.3 = (bf16[2048,128]{1,0:T(8,128)(2,1)}, bf16[2048,128]{1,0:T(8,128)(2,1)}, u32[]{:S(2)}, u32[]{:S(2)}) collective-permute-start(bf16[2048,128]{1,0:T(8,128)(2,1)} %get-tuple-element.61), channel_id=1, source_target_pairs={{0,4},{4,12},{12,20},{20,28},{28,24},{24,16},{16,8},{8,0},{1,5},{5... | collective-permute-start | bytes 1572872 | tf_op jit(solution)/shard_map/ppermute | solution.py:186
  100.0 24.4 %collective-permute-start.4 = (bf16[2048,128]{1,0:T(8,128)(2,1)}, bf16[2048,128]{1,0:T(8,128)(2,1)}, u32[]{:S(2)}, u32[]{:S(2)}) collective-permute-start(bf16[2048,128]{1,0:T(8,128)(2,1)} %get-tuple-element.62), channel_id=1, source_target_pairs={{0,8},{4,0},{12,4},{20,12},{28,20},{24,28},{16,24},{8,16},{1,9},{5... | collective-permute-start | bytes 1572872 | tf_op jit(solution)/shard_map/ppermute | solution.py:187
  120.1 33.7 %all-to-all-start.3 = ((bf16[8,256,256]{2,1,0:T(8,128)(2,1)}), bf16[8,256,256]{2,1,0:T(8,128)(2,1)}, u32[]{:S(2)}, u32[]{:S(2)}) async-start(bf16[8,256,256]{2,1,0:T(8,128)(2,1)} %copy-done.4), calls=%async_computation.3 | async-start | bytes 2097152 | tf_op jit(solution)/shard_map/all_to_all | solution.py:181
  131.1 16.9 %copy-start.2 = (bf16[2048,256]{1,0:T(8,128)(2,1)}, bf16[2048,256]{1,0:T(8,128)(2,1)S(1)}, u32[]{:S(2)}) copy-start(bf16[2048,256]{1,0:T(8,128)(2,1)S(1)} %fusion.8) | copy-start | bytes 3145732
  132.2 25.0 %collective-permute-start.5 = (bf16[2048,128]{1,0:T(8,128)(2,1)}, bf16[2048,128]{1,0:T(8,128)(2,1)}, u32[]{:S(2)}, u32[]{:S(2)}) collective-permute-start(bf16[2048,128]{1,0:T(8,128)(2,1)} %get-tuple-element.59), channel_id=1, source_target_pairs={{0,4},{4,12},{12,20},{20,28},{28,24},{24,16},{16,8},{8,0},{1,5},{5... | collective-permute-start | bytes 1572872 | tf_op jit(solution)/shard_map/ppermute | solution.py:186
  137.4 19.9 %collective-permute-start.6 = (bf16[2048,128]{1,0:T(8,128)(2,1)}, bf16[2048,128]{1,0:T(8,128)(2,1)}, u32[]{:S(2)}, u32[]{:S(2)}) collective-permute-start(bf16[2048,128]{1,0:T(8,128)(2,1)} %get-tuple-element.60), channel_id=1, source_target_pairs={{0,8},{4,0},{12,4},{20,12},{28,20},{24,28},{16,24},{8,16},{1,9},{5... | collective-permute-start | bytes 1572872 | tf_op jit(solution)/shard_map/ppermute | solution.py:187
  163.6 7.0 %copy-start.3 = (bf16[2048,256]{1,0:T(8,128)(2,1)S(1)}, bf16[2048,256]{1,0:T(8,128)(2,1)}, u32[]{:S(2)}) copy-start(bf16[2048,256]{1,0:T(8,128)(2,1)} %copy-done.2) | copy-start | bytes 3145732
  164.1 16.6 %collective-permute-start.7 = (bf16[2048,128]{1,0:T(8,128)(2,1)S(1)}, bf16[2048,128]{1,0:T(8,128)(2,1)S(1)}, u32[]{:S(2)}, u32[]{:S(2)}) collective-permute-start(bf16[2048,128]{1,0:T(8,128)(2,1)S(1)} %get-tuple-element.57), channel_id=1, source_target_pairs={{0,4},{4,12},{12,20},{20,28},{28,24},{24,16},{16,8},{8,0},{1,5},{5... | collective-permute-start | bytes 1572872 | tf_op jit(solution)/shard_map/ppermute | solution.py:186
  169.1 13.4 %collective-permute-start.8 = (bf16[2048,128]{1,0:T(8,128)(2,1)S(1)}, bf16[2048,128]{1,0:T(8,128)(2,1)S(1)}, u32[]{:S(2)}, u32[]{:S(2)}) collective-permute-start(bf16[2048,128]{1,0:T(8,128)(2,1)S(1)} %get-tuple-element.58), channel_id=1, source_target_pairs={{0,8},{4,0},{12,4},{20,12},{28,20},{24,28},{16,24},{8,16},{1,9},{5... | collective-permute-start | bytes 1572872 | tf_op jit(solution)/shard_map/ppermute | solution.py:187
  183.3 2.1 copy-start.1
  183.3 4.8 %slice-start.2 = ((s8[8388608]{0:T(1024)(128)(4,1)}), s8[4194304]{0:T(1024)(128)(4,1)S(1)}, s32[]{:S(2)}) async-start(s8[8388608]{0:T(1024)(128)(4,1)} %bitcast.81), calls=%async_computation.7 | async-start | bytes 8388608
  184.1 4.0 %slice-start = ((s8[8388608]{0:T(1024)(128)(4,1)}), s8[4194304]{0:T(1024)(128)(4,1)S(1)}, s32[]{:S(2)}) async-start(s8[8388608]{0:T(1024)(128)(4,1)} %bitcast.79), calls=%async_computation.5 | async-start | bytes 8388608
  184.1 5.0 %slice-start.3 = ((s8[8388608]{0:T(1024)(128)(4,1)}), s8[4194304]{0:T(1024)(128)(4,1)S(1)}, s32[]{:S(2)}) async-start(s8[8388608]{0:T(1024)(128)(4,1)} %bitcast.81), calls=%async_computation.8 | async-start | bytes 8388608
  185.4 5.0 %slice-start.1 = ((s8[8388608]{0:T(1024)(128)(4,1)}), s8[4194304]{0:T(1024)(128)(4,1)S(1)}, s32[]{:S(2)}) async-start(s8[8388608]{0:T(1024)(128)(4,1)} %bitcast.79), calls=%async_computation.6 | async-start | bytes 8388608
  188.0 9.9 %collective-permute-start.9 = (f32[2048,128]{1,0:T(8,128)S(1)}, f32[2048,128]{1,0:T(8,128)S(1)}, u32[]{:S(2)}, u32[]{:S(2)}) collective-permute-start(f32[2048,128]{1,0:T(8,128)S(1)} %constant_dynamic-slice_fusion.3), channel_id=1, source_target_pairs={{0,1},{1,0},{2,3},{3,2},{4,5},{5,4},{6,7},{7,6},{8,9},{9,8},{10,11... | collective-permute-start | bytes 3145736 | tf_op jit(solution)/shard_map/ppermute | solution.py:125
  206.2 12.1 %collective-permute-start.10 = (f32[1024,128]{0,1:T(8,128)S(1)}, f32[1024,128]{0,1:T(8,128)S(1)}, u32[]{:S(2)}, u32[]{:S(2)}) collective-permute-start(f32[1024,128]{0,1:T(8,128)S(1)} %constant_dynamic-slice_fusion.2), channel_id=1, source_target_pairs={{0,2},{1,3},{2,0},{3,1},{4,6},{5,7},{6,4},{7,5},{8,10},{9,11},{10,... | collective-permute-start | bytes 1572872 | tf_op jit(solution)/shard_map/ppermute | solution.py:134
  218.4 1.4 collective-permute-start.11
  242.8 0.8 copy-start.5

commit v12 on v11

--- a/solution.py
+++ b/solution.py
@@ -110,7 +110,7 @@
     return path if extend() else list(range(count))
 
 
-def sum_and_invert(cross, length, lag_count, seg_total, win_count):
+def sum_and_invert(cross, length, lag_count, seg_total, win_count, lag_start):
     win = lax.axis_index("win")
     if win_count % 2 or win_count & (win_count - 1):
         stacked = lax.psum(cross, "win")
@@ -123,7 +123,7 @@
     other = lax.dynamic_slice_in_dim(cross, (1 - core) * half, half, axis=1)
     partner = [(w, w ^ 1) for w in range(win_count)]
     total = mine + lax.ppermute(other, "win", partner)
-    inverse = inverse_matrix(length, 0, length, seg_total)
+    inverse = inverse_matrix(length, lag_start, length, seg_total)
     lags = jnp.dot(inverse, total, precision=lax.Precision.HIGH)
     bit = win_count // 4
     while bit >= 1:
@@ -185,6 +185,8 @@
             whitened = whiten(spectra, BAND)
             from_prev = lax.ppermute(whitened[:, half:], "tile", to_next)
             from_next = lax.ppermute(whitened[:, :half], "tile", to_prev)
+            if segment == 0:
+                lag_start, _ = lax.optimization_barrier((jnp.int32(0), whitened))
             arrived.append((from_prev, from_next))
             joined = jnp.concatenate([from_prev, whitened, from_next], axis=1)
             first_part = jnp.dot(joined, pick_first, preferred_element_type=jnp.float32)
@@ -192,7 +194,7 @@
             term = cross_terms(first_part, second_part)
             cross = term if cross is None else cross + term
         lag_count = length // win_count
-        correlation = sum_and_invert(cross, length, lag_count, seg_total, win_count)
+        correlation = sum_and_invert(cross, length, lag_count, seg_total, win_count, lag_start)
         capacity = 5 * pair_first.shape[0] // (2 * tile_count)
         chooser = bucket_select(my_owners, tile_count, capacity)
         picked = lax.dot_general(

time: 244 us -> 233 us (0.955)
  starting transfers between devices: 62.5 us -> 54.5 us
  other arithmetic: 36.3 us -> 31.2 us
    all_to_all x4, starting transfers between devices: 23.6 us -> 19.7 us  [per_device(): lax.all_to_all(outgoing, 'tile', split_axis=0, concat_axis=0, tiled=True)]
    ppermute x4, starting transfers between devices: 22.3 us -> 19.4 us  [per_device(): from_next = lax.ppermute(whitened[:, :half], 'tile', to_prev)]
    mul x1 -> x2, other arithmetic: 7.56 us -> 8.05 us  [inverse_matrix(): return jnp.concatenate([weights * cosine, -weights * sine], axis=1)]
    unnamed x32 -> x38, local copies, waits for them, and re-layouts: 11 us -> 11 us
  transfers between devices with their start and end apart: 16 -> 16, of which waited for: 8 -> 9; matrix products, arithmetic and copies ran while one was open for 35% -> 32% of each run, Pallas kernels for 0% -> 0%
where the time goes in v12:
time: 233 us; the launch traced here: 232 us
  starting transfers between devices  54.5 us (23%)
  waiting for transfers between devices  48.8 us (21%)
  matrix products  46.1 us (20%)
  other arithmetic  31.2 us (13%)
  local copies, waits for them, and re-layouts  28.8 us (12%)
  blocking collectives  21.8 us (9%)
    dot_general x4, matrix products, per_device(): jnp.einsum('fjm,jmc->fc', forward, received, preferred_element_type=jnp.f...  24.2 us
    all_to_all x4, waiting for transfers between devices, per_device(): lax.all_to_all(outgoing, 'tile', split_axis=0, concat_axis=0, tiled=True)  23.1 us
    all_to_all x1, blocking collectives, per_device(): lax.all_to_all(buckets, 'tile', split_axis=0, concat_axis=0, tiled=True)  21.8 us
    all_to_all x4, starting transfers between devices, per_device(): lax.all_to_all(outgoing, 'tile', split_axis=0, concat_axis=0, tiled=True)  19.7 us
    ppermute x4, starting transfers between devices, per_device(): from_next = lax.ppermute(whitened[:, :half], 'tile', to_prev)  19.4 us
    ppermute x4, starting transfers between devices, per_device(): from_prev = lax.ppermute(whitened[:, half:], 'tile', to_next)  13 us
    ppermute x1, waiting for transfers between devices, sum_and_invert(): lax.ppermute(send, 'win', [(w, w ^ 2 * bit) for w in range(win_count)])  12 us
    unnamed x38, local copies, waits for them, and re-layouts  11 us
  transfers between devices with their start and end apart: 16, of which 9 were waited for; matrix products, arithmetic and copies ran while one was open for 32% of the time, Pallas kernels for 0%

profile of v12, /device:TPU:0, one launch (start us, length us, event | category | flops | bytes accessed | tf_op | source)
XLA Modules:
  0.0 231.8 jit_solution(3087666648187214863)
XLA Ops:
  0.0 2.0 slice_dynamic-update-slice_fusion.7
  2.0 1.1 slice_bitcast_fusion.1
  3.1 1.9 slice_dynamic-update-slice_fusion.6
  5.0 0.8 fusion.59
  5.8 0.7 fusion.61
  6.5 0.8 slice_dynamic-update-slice_fusion.5
  7.2 0.8 slice_dynamic-update-slice_fusion.4
  8.0 0.8 slice_dynamic-update-slice_fusion.3
  8.8 0.8 slice_dynamic-update-slice_fusion.2
  9.6 0.8 slice_dynamic-update-slice_fusion.1
  10.4 1.0 copy-done.4
  11.4 7.3 %all-to-all-start = ((bf16[8,256,256]{2,1,0:T(8,128)(2,1)}), bf16[8,256,256]{2,1,0:T(8,128)(2,1)S(1)}, u32[]{:S(2)}, u32[]{:S(2)}) async-start(bf16[8,256,256]{2,1,0:T(8,128)(2,1)} %get-tuple-element.18), calls=%async_computation | async-start | bytes 2097152 | tf_op jit(solution)/shard_map/all_to_all | solution.py:181
  18.7 0.7 collective-permute-start
  19.4 1.0 fusion.63
  20.5 0.6 fusion.71
  21.1 5.1 %subtract_convert_fusion = (bf16[1024,32,64]{0,2,1:T(8,128)(2,1)}, bf16[1024,32,64]{0,2,1:T(8,128)(2,1)}) fusion(f32[1024,64]{0,1:T(8,128)S(1)} %get-tuple-element.84, f32[1024,32]{0,1:T(8,128)S(1)} %get-tuple-element.79, f32[1024,64]{0,1:T(8,128)S(1)} %get-tuple-element.85, f32[1024,32]{0,1:T(8,128)S(1)} %get-tuple-element.78), kind=kLoop, calls=%fused_computation.10 | loop fusion | flops 18874368 | bytes 9175040 | tf_op jit(solution)/shard_map/convert.3
  26.1 6.4 %copy.5 = bf16[1024,8,256]{2,0,1:T(8,128)(2,1)} copy(bf16[1024,8,256]{0,2,1:T(8,128)(2,1)} %bitcast.84) | data formatting | bytes 8388608 | tf_op jit(solution)/shard_map/sub | solution.py:24
  32.6 6.5 %copy.6 = bf16[1024,8,256]{2,0,1:T(8,128)(2,1)} copy(bf16[1024,8,256]{0,2,1:T(8,128)(2,1)} %bitcast.83) | data formatting | bytes 8388608 | tf_op jit(solution)/shard_map/neg | solution.py:31
  39.0 0.6 reduce-window.6
  40.0 4.4 %all-to-all-done = bf16[8,256,256]{2,1,0:T(8,128)(2,1)S(1)} async-done(((bf16[8,256,256]{2,1,0:T(8,128)(2,1)}), bf16[8,256,256]{2,1,0:T(8,128)(2,1)S(1)}, u32[]{:S(2)}, u32[]{:S(2)}) %all-to-all-start) | async-done | bytes 1048608 | tf_op jit(solution)/shard_map/all_to_all | solution.py:181
  44.4 3.8 %all-to-all-start.1 = ((bf16[8,256,256]{2,1,0:T(8,128)(2,1)}), bf16[8,256,256]{2,1,0:T(8,128)(2,1)S(1)}, u32[]{:S(2)}, u32[]{:S(2)}) async-start(bf16[8,256,256]{2,1,0:T(8,128)(2,1)} %get-tuple-element.17), calls=%async_computation.1 | async-start | bytes 2097152 | tf_op jit(solution)/shard_map/all_to_all | solution.py:181
  48.2 5.9 %convolution_bitcast_fusion.3 = f32[2048,256]{1,0:T(8,128)S(1)} fusion(bf16[8,256,256]{2,1,0:T(8,128)(2,1)S(1)} %all-to-all-done, bf16[1024,8,256]{2,0,1:T(8,128)(2,1)} %copy.6, bf16[1024,8,256]{2,0,1:T(8,128)(2,1)} %copy.5), kind=kOutput, calls=%fused_computation.14 | convolution fusion | flops 2164260864 | bytes 11534336 | tf_op jit(solution)/shard_map/fjm,jmc->fc/dot_general | solution.py:184
  54.8 2.1 collective-permute-start.1
  57.0 0.6 fusion.69
  57.6 2.0 fusion.48
  59.6 6.9 %multiply_subtract_fusion = (f32[2048,16,64]{0,2,1:T(8,128)}, f32[2048,16,64]{0,2,1:T(8,128)}) fusion(f32[2048,64]{0,1:T(8,128)S(1)} %get-tuple-element.74, f32[2048,16]{0,1:T(8,128)S(1)} %get-tuple-element.72, f32[2048,64]{0,1:T(8,128)S(1)} %get-tuple-element.73, f32[2048,16]{0,1:T(8,128)S(1)} %get-tuple-element.71), kind=kLoop, calls=%fused_computation.8 | loop fusion | flops 12582912 | bytes 18087936 | tf_op jit(solution)/shard_map/sub | solution.py:24
  66.5 8.9 %all-to-all-done.1 = bf16[8,256,256]{2,1,0:T(8,128)(2,1)S(1)} async-done(((bf16[8,256,256]{2,1,0:T(8,128)(2,1)}), bf16[8,256,256]{2,1,0:T(8,128)(2,1)S(1)}, u32[]{:S(2)}, u32[]{:S(2)}) %all-to-all-start.1) | async-done | bytes 1048608 | tf_op jit(solution)/shard_map/all_to_all | solution.py:181
  75.4 4.4 %all-to-all-start.2 = ((bf16[8,256,256]{2,1,0:T(8,128)(2,1)}), bf16[8,256,256]{2,1,0:T(8,128)(2,1)}, u32[]{:S(2)}, u32[]{:S(2)}) async-start(bf16[8,256,256]{2,1,0:T(8,128)(2,1)} %get-tuple-element.16), calls=%async_computation.2 | async-start | bytes 2097152 | tf_op jit(solution)/shard_map/all_to_all | solution.py:181
  79.8 5.9 %convolution_bitcast_fusion.2 = f32[2048,256]{1,0:T(8,128)S(1)} fusion(bf16[8,256,256]{2,1,0:T(8,128)(2,1)S(1)} %all-to-all-done.1, bf16[1024,8,256]{2,0,1:T(8,128)(2,1)} %copy.6, bf16[1024,8,256]{2,0,1:T(8,128)(2,1)} %copy.5), kind=kOutput, calls=%fused_computation.13 | convolution fusion | flops 2164260864 | bytes 11534336 | tf_op jit(solution)/shard_map/fjm,jmc->fc/dot_general | solution.py:184
  86.4 1.0 fusion.88
  87.4 1.7 collective-permute-start.3
  89.1 10.4 %collective-permute-start.4 = (bf16[2048,128]{1,0:T(8,128)(2,1)}, bf16[2048,128]{1,0:T(8,128)(2,1)}, u32[]{:S(2)}, u32[]{:S(2)}) collective-permute-start(bf16[2048,128]{1,0:T(8,128)(2,1)} %get-tuple-element.64), channel_id=1, source_target_pairs={{0,8},{4,0},{12,4},{20,12},{28,20},{24,28},{16,24},{8,16},{1,9},{5... | collective-permute-start | bytes 1572872 | tf_op jit(solution)/shard_map/ppermute | solution.py:187
  99.5 2.0 fusion.23
  101.4 2.0 fusion.22
  103.7 5.5 %all-to-all-done.2 = bf16[8,256,256]{2,1,0:T(8,128)(2,1)} async-done(((bf16[8,256,256]{2,1,0:T(8,128)(2,1)}), bf16[8,256,256]{2,1,0:T(8,128)(2,1)}, u32[]{:S(2)}, u32[]{:S(2)}) %all-to-all-start.2) | async-done | bytes 1048608 | tf_op jit(solution)/shard_map/all_to_all | solution.py:181
  109.2 4.2 %all-to-all-start.3 = ((bf16[8,256,256]{2,1,0:T(8,128)(2,1)}), bf16[8,256,256]{2,1,0:T(8,128)(2,1)}, u32[]{:S(2)}, u32[]{:S(2)}) async-start(bf16[8,256,256]{2,1,0:T(8,128)(2,1)} %copy-done.4), calls=%async_computation.3 | async-start | bytes 2097152 | tf_op jit(solution)/shard_map/all_to_all | solution.py:181
  113.5 6.1 %convolution_bitcast_fusion.1 = f32[2048,256]{1,0:T(8,128)S(1)} fusion(bf16[8,256,256]{2,1,0:T(8,128)(2,1)} %all-to-all-done.2, bf16[1024,8,256]{2,0,1:T(8,128)(2,1)} %copy.6, bf16[1024,8,256]{2,0,1:T(8,128)(2,1)} %copy.5), kind=kOutput, calls=%fused_computation.12 | convolution fusion | flops 2164260864 | bytes 11534336 | tf_op jit(solution)/shard_map/fjm,jmc->fc/dot_general | solution.py:184
  120.3 1.1 fusion.87
  121.4 5.2 %collective-permute-start.5 = (bf16[2048,128]{1,0:T(8,128)(2,1)}, bf16[2048,128]{1,0:T(8,128)(2,1)}, u32[]{:S(2)}, u32[]{:S(2)}) collective-permute-start(bf16[2048,128]{1,0:T(8,128)(2,1)} %get-tuple-element.61), channel_id=1, source_target_pairs={{0,4},{4,12},{12,20},{20,28},{28,24},{24,16},{16,8},{8,0},{1,5},{5... | collective-permute-start | bytes 1572872 | tf_op jit(solution)/shard_map/ppermute | solution.py:186
  126.6 6.9 %collective-permute-start.6 = (bf16[2048,128]{1,0:T(8,128)(2,1)}, bf16[2048,128]{1,0:T(8,128)(2,1)}, u32[]{:S(2)}, u32[]{:S(2)}) collective-permute-start(bf16[2048,128]{1,0:T(8,128)(2,1)} %get-tuple-element.62), channel_id=1, source_target_pairs={{0,8},{4,0},{12,4},{20,12},{28,20},{24,28},{16,24},{8,16},{1,9},{5... | collective-permute-start | bytes 1572872 | tf_op jit(solution)/shard_map/ppermute | solution.py:187
  133.5 2.0 fusion.21
  135.4 2.0 fusion.20
  137.4 1.3 multiply_add_fusion.3
  138.7 4.3 %all-to-all-done.3 = bf16[8,256,256]{2,1,0:T(8,128)(2,1)} async-done(((bf16[8,256,256]{2,1,0:T(8,128)(2,1)}), bf16[8,256,256]{2,1,0:T(8,128)(2,1)}, u32[]{:S(2)}, u32[]{:S(2)}) %all-to-all-start.3) | async-done | bytes 1048608 | tf_op jit(solution)/shard_map/all_to_all | solution.py:181
  143.0 4.6 %collective-permute-done.5 = bf16[2048,128]{1,0:T(8,128)(2,1)} collective-permute-done((bf16[2048,128]{1,0:T(8,128)(2,1)}, bf16[2048,128]{1,0:T(8,128)(2,1)}, u32[]{:S(2)}, u32[]{:S(2)}) %collective-permute-start.5) | collective-permute-done | bytes 524320 | tf_op jit(solution)/shard_map/ppermute | solution.py:186
  147.6 6.1 %convolution_bitcast_fusion = f32[2048,256]{1,0:T(8,128)S(1)} fusion(bf16[8,256,256]{2,1,0:T(8,128)(2,1)} %all-to-all-done.3, bf16[1024,8,256]{2,0,1:T(8,128)(2,1)} %copy.6, bf16[1024,8,256]{2,0,1:T(8,128)(2,1)} %copy.5), kind=kOutput, calls=%fused_computation.11 | convolution fusion | flops 2164260864 | bytes 11534336 | tf_op jit(solution)/shard_map/fjm,jmc->fc/dot_general | solution.py:184
  154.5 4.0 %collective-permute-start.7 = (bf16[2048,128]{1,0:T(8,128)(2,1)S(1)}, bf16[2048,128]{1,0:T(8,128)(2,1)S(1)}, u32[]{:S(2)}, u32[]{:S(2)}) collective-permute-start(bf16[2048,128]{1,0:T(8,128)(2,1)S(1)} %get-tuple-element.59), channel_id=1, source_target_pairs={{0,4},{4,12},{12,20},{20,28},{28,24},{24,16},{16,8},{8,0},{1,5},{5... | collective-permute-start | bytes 1572872 | tf_op jit(solution)/shard_map/ppermute | solution.py:186
  158.5 2.1 collective-permute-start.8
  160.6 2.0 fusion.19
  162.6 2.0 fusion.18
  164.8 6.3 %collective-permute-done.7 = bf16[2048,128]{1,0:T(8,128)(2,1)S(1)} collective-permute-done((bf16[2048,128]{1,0:T(8,128)(2,1)S(1)}, bf16[2048,128]{1,0:T(8,128)(2,1)S(1)}, u32[]{:S(2)}, u32[]{:S(2)}) %collective-permute-start.7) | collective-permute-done | bytes 524320 | tf_op jit(solution)/shard_map/ppermute | solution.py:186
  171.2 1.4 collective-permute-done.8
  172.5 0.8 fusion.17
  173.3 0.8 fusion.16
  174.4 1.3 copy-done.1
  176.4 0.8 slice-done.3
  177.2 4.2 %bitcast_multiply_fusion = f32[2048,1024]{0,1:T(8,128)} fusion(f32[2048,16,64]{0,2,1:T(8,128)S(1)} %bitcast.82, f32[1024]{0:T(1024)S(1)} %fusion.74), kind=kLoop, calls=%fused_computation.5 | loop fusion | flops 2097152 | bytes 16781312 | tf_op jit(solution)/shard_map/mul | solution.py:42
  181.4 3.9 %bitcast_multiply_fusion.1 = f32[2048,1024]{0,1:T(8,128)} fusion(f32[2048,16,64]{0,2,1:T(8,128)S(1)} %bitcast.80, f32[1024]{0:T(1024)S(1)} %select_multiply_fusion), kind=kLoop, calls=%fused_computation.6 | loop fusion | flops 2097152 | bytes 16781312 | tf_op jit(solution)/shard_map/mul | solution.py:42
  185.3 8.2 %fusion = f32[2048,128]{0,1:T(8,128)S(1)} fusion(f32[2048,1024]{0,1:T(8,128)} %bitcast_multiply_fusion, f32[2048,1024]{0,1:T(8,128)} %bitcast_multiply_fusion.1, f32[2048,128]{1,0:T(8,128)S(1)} %collective-permute-done.9, f32[2048,256]{1,0:T(8,128)S(1)} %fusion.6, s32[]{:T(128)S(6)} %select_n.119), kind=kOutput, calls=%fused_computation | convolution fusion | flops 3225681920 | bytes 19922948 | tf_op jit(solution)/shard_map/dot_general | solution.py:127
  193.6 1.6 collective-permute-start.10
  195.1 12.0 %collective-permute-done.10 = f32[1024,128]{0,1:T(8,128)S(1)} collective-permute-done((f32[1024,128]{0,1:T(8,128)S(1)}, f32[1024,128]{0,1:T(8,128)S(1)}, u32[]{:S(2)}, u32[]{:S(2)}) %collective-permute-start.10) | collective-permute-done | bytes 524320 | tf_op jit(solution)/shard_map/ppermute | solution.py:134
  207.3 1.3 collective-permute-done.11
  209.0 21.8 %all_to_all.25 = bf16[8,80,512]{2,1,0:T(8,128)(2,1)S(1)} all-to-all(bf16[8,80,512]{2,1,0:T(8,128)(2,1)S(1)} %bitcast.89), channel_id=1, replica_groups=mesh['tile'=8,'win'=4] {'tile'}, dimensions={0} | all-to-all | bytes 1310720 | tf_op jit(solution)/shard_map/all_to_all | solution.py:207
  231.0 0.8 copy-done.5
  (81 shorter events, 5.1 us)
Async XLA Ops:
  0.0 6.5 %copy-start = (bf16[4,256,2048]{2,1,0:T(8,128)(2,1)S(1)}, bf16[4,256,2048]{2,1,0:T(8,128)(2,1)}, u32[]{:S(2)}) copy-start(bf16[4,256,2048]{2,1,0:T(8,128)(2,1)} %param.4) | copy-start | bytes 12582916
  5.0 13.7 %copy-start.6 = (s32[256,1]{0,1:T(1,128)S(1)}, s32[256,1]{0,1:T(1,128)}, u32[]{:S(2)}) copy-start(s32[256,1]{0,1:T(1,128)} %param.7) | copy-start | bytes 3076
  5.0 13.7 %copy-start.7 = (s32[256]{0:T(256)S(1)}, s32[256]{0:T(256)}, u32[]{:S(2)}) copy-start(s32[256]{0:T(256)} %param.6) | copy-start | bytes 3076
  5.0 13.7 %copy-start.8 = (s32[256]{0:T(256)S(1)}, s32[256]{0:T(256)}, u32[]{:S(2)}) copy-start(s32[256]{0:T(256)} %param.5) | copy-start | bytes 3076
  10.4 1.0 copy-start.4
  11.4 33.1 %all-to-all-start = ((bf16[8,256,256]{2,1,0:T(8,128)(2,1)}), bf16[8,256,256]{2,1,0:T(8,128)(2,1)S(1)}, u32[]{:S(2)}, u32[]{:S(2)}) async-start(bf16[8,256,256]{2,1,0:T(8,128)(2,1)} %get-tuple-element.18), calls=%async_computation | async-start | bytes 2097152 | tf_op jit(solution)/shard_map/all_to_all | solution.py:181
  18.7 20.3 %collective-permute-start = (s32[3,256]{1,0:T(4,128)S(1)}, s32[3,256]{1,0:T(4,128)S(1)}, u32[]{:S(2)}, u32[]{:S(2)}) collective-permute-start(s32[3,256]{1,0:T(4,128)S(1)} %pad_add_fusion), channel_id=1, source_target_pairs={{0,0},{4,4},{8,12},{12,20},{16,28},{20,24},{24,16},{28,8},{1,1},{5... | collective-permute-start | bytes 9224 | tf_op jit(solution)/shard_map/ppermute | solution.py:161
  44.4 30.9 %all-to-all-start.1 = ((bf16[8,256,256]{2,1,0:T(8,128)(2,1)}), bf16[8,256,256]{2,1,0:T(8,128)(2,1)S(1)}, u32[]{:S(2)}, u32[]{:S(2)}) async-start(bf16[8,256,256]{2,1,0:T(8,128)(2,1)} %get-tuple-element.17), calls=%async_computation.1 | async-start | bytes 2097152 | tf_op jit(solution)/shard_map/all_to_all | solution.py:181
  54.8 25.0 %collective-permute-start.1 = (bf16[2048,128]{1,0:T(8,128)(2,1)S(1)}, bf16[2048,128]{1,0:T(8,128)(2,1)}, u32[]{:S(2)}, u32[]{:S(2)}) collective-permute-start(bf16[2048,128]{1,0:T(8,128)(2,1)S(1)} %get-tuple-element.65), channel_id=1, source_target_pairs={{0,4},{4,12},{12,20},{20,28},{28,24},{24,16},{16,8},{8,0},{1,5},{5... | collective-permute-start | bytes 1572872 | tf_op jit(solution)/shard_map/ppermute | solution.py:186
  56.9 22.9 %collective-permute-start.2 = (bf16[2048,128]{1,0:T(8,128)(2,1)S(1)}, bf16[2048,128]{1,0:T(8,128)(2,1)}, u32[]{:S(2)}, u32[]{:S(2)}) collective-permute-start(bf16[2048,128]{1,0:T(8,128)(2,1)S(1)} %get-tuple-element.66), channel_id=1, source_target_pairs={{0,8},{4,0},{12,4},{20,12},{28,20},{24,28},{16,24},{8,16},{1,9},{5... | collective-permute-start | bytes 1572872 | tf_op jit(solution)/shard_map/ppermute | solution.py:187
  75.4 33.9 %all-to-all-start.2 = ((bf16[8,256,256]{2,1,0:T(8,128)(2,1)}), bf16[8,256,256]{2,1,0:T(8,128)(2,1)}, u32[]{:S(2)}, u32[]{:S(2)}) async-start(bf16[8,256,256]{2,1,0:T(8,128)(2,1)} %get-tuple-element.16), calls=%async_computation.2 | async-start | bytes 2097152 | tf_op jit(solution)/shard_map/all_to_all | solution.py:181
  87.4 26.1 %collective-permute-start.3 = (bf16[2048,128]{1,0:T(8,128)(2,1)}, bf16[2048,128]{1,0:T(8,128)(2,1)}, u32[]{:S(2)}, u32[]{:S(2)}) collective-permute-start(bf16[2048,128]{1,0:T(8,128)(2,1)} %get-tuple-element.63), channel_id=1, source_target_pairs={{0,4},{4,12},{12,20},{20,28},{28,24},{24,16},{16,8},{8,0},{1,5},{5... | collective-permute-start | bytes 1572872 | tf_op jit(solution)/shard_map/ppermute | solution.py:186
  89.1 24.4 %collective-permute-start.4 = (bf16[2048,128]{1,0:T(8,128)(2,1)}, bf16[2048,128]{1,0:T(8,128)(2,1)}, u32[]{:S(2)}, u32[]{:S(2)}) collective-permute-start(bf16[2048,128]{1,0:T(8,128)(2,1)} %get-tuple-element.64), channel_id=1, source_target_pairs={{0,8},{4,0},{12,4},{20,12},{28,20},{24,28},{16,24},{8,16},{1,9},{5... | collective-permute-start | bytes 1572872 | tf_op jit(solution)/shard_map/ppermute | solution.py:187
  109.2 33.8 %all-to-all-start.3 = ((bf16[8,256,256]{2,1,0:T(8,128)(2,1)}), bf16[8,256,256]{2,1,0:T(8,128)(2,1)}, u32[]{:S(2)}, u32[]{:S(2)}) async-start(bf16[8,256,256]{2,1,0:T(8,128)(2,1)} %copy-done.4), calls=%async_computation.3 | async-start | bytes 2097152 | tf_op jit(solution)/shard_map/all_to_all | solution.py:181
  120.3 15.2 %copy-start.2 = (bf16[2048,256]{1,0:T(8,128)(2,1)}, bf16[2048,256]{1,0:T(8,128)(2,1)S(1)}, u32[]{:S(2)}) copy-start(bf16[2048,256]{1,0:T(8,128)(2,1)S(1)} %fusion.8) | copy-start | bytes 3145732
  121.4 26.2 %collective-permute-start.5 = (bf16[2048,128]{1,0:T(8,128)(2,1)}, bf16[2048,128]{1,0:T(8,128)(2,1)}, u32[]{:S(2)}, u32[]{:S(2)}) collective-permute-start(bf16[2048,128]{1,0:T(8,128)(2,1)} %get-tuple-element.61), channel_id=1, source_target_pairs={{0,4},{4,12},{12,20},{20,28},{28,24},{24,16},{16,8},{8,0},{1,5},{5... | collective-permute-start | bytes 1572872 | tf_op jit(solution)/shard_map/ppermute | solution.py:186
  126.6 21.1 %collective-permute-start.6 = (bf16[2048,128]{1,0:T(8,128)(2,1)}, bf16[2048,128]{1,0:T(8,128)(2,1)}, u32[]{:S(2)}, u32[]{:S(2)}) collective-permute-start(bf16[2048,128]{1,0:T(8,128)(2,1)} %get-tuple-element.62), channel_id=1, source_target_pairs={{0,8},{4,0},{12,4},{20,12},{28,20},{24,28},{16,24},{8,16},{1,9},{5... | collective-permute-start | bytes 1572872 | tf_op jit(solution)/shard_map/ppermute | solution.py:187
  154.0 6.6 %copy-start.3 = (bf16[2048,256]{1,0:T(8,128)(2,1)S(1)}, bf16[2048,256]{1,0:T(8,128)(2,1)}, u32[]{:S(2)}) copy-start(bf16[2048,256]{1,0:T(8,128)(2,1)} %copy-done.2) | copy-start | bytes 3145732
  154.5 16.7 %collective-permute-start.7 = (bf16[2048,128]{1,0:T(8,128)(2,1)S(1)}, bf16[2048,128]{1,0:T(8,128)(2,1)S(1)}, u32[]{:S(2)}, u32[]{:S(2)}) collective-permute-start(bf16[2048,128]{1,0:T(8,128)(2,1)S(1)} %get-tuple-element.59), channel_id=1, source_target_pairs={{0,4},{4,12},{12,20},{20,28},{28,24},{24,16},{16,8},{8,0},{1,5},{5... | collective-permute-start | bytes 1572872 | tf_op jit(solution)/shard_map/ppermute | solution.py:186
  158.5 14.0 %collective-permute-start.8 = (bf16[2048,128]{1,0:T(8,128)(2,1)S(1)}, bf16[2048,128]{1,0:T(8,128)(2,1)S(1)}, u32[]{:S(2)}, u32[]{:S(2)}) collective-permute-start(bf16[2048,128]{1,0:T(8,128)(2,1)S(1)} %get-tuple-element.60), channel_id=1, source_target_pairs={{0,8},{4,0},{12,4},{20,12},{28,20},{24,28},{16,24},{8,16},{1,9},{5... | collective-permute-start | bytes 1572872 | tf_op jit(solution)/shard_map/ppermute | solution.py:187
  173.3 3.1 %slice-start.2 = ((s8[8388608]{0:T(1024)(128)(4,1)}), s8[4194304]{0:T(1024)(128)(4,1)S(1)}, s32[]{:S(2)}) async-start(s8[8388608]{0:T(1024)(128)(4,1)} %bitcast.81), calls=%async_computation.7 | async-start | bytes 8388608
  174.1 1.6 copy-start.1
  174.1 3.1 %slice-start.3 = ((s8[8388608]{0:T(1024)(128)(4,1)}), s8[4194304]{0:T(1024)(128)(4,1)S(1)}, s32[]{:S(2)}) async-start(s8[8388608]{0:T(1024)(128)(4,1)} %bitcast.81), calls=%async_computation.8 | async-start | bytes 8388608
  175.7 5.7 %slice-start = ((s8[8388608]{0:T(1024)(128)(4,1)}), s8[4194304]{0:T(1024)(128)(4,1)S(1)}, s32[]{:S(2)}) async-start(s8[8388608]{0:T(1024)(128)(4,1)} %bitcast.79), calls=%async_computation.5 | async-start | bytes 8388608
  176.3 8.9 %collective-permute-start.9 = (f32[2048,128]{1,0:T(8,128)S(1)}, f32[2048,128]{1,0:T(8,128)S(1)}, u32[]{:S(2)}, u32[]{:S(2)}) collective-permute-start(f32[2048,128]{1,0:T(8,128)S(1)} %constant_dynamic-slice_fusion.3), channel_id=1, source_target_pairs={{0,1},{1,0},{2,3},{3,2},{4,5},{5,4},{6,7},{7,6},{8,9},{9,8},{10,11... | collective-permute-start | bytes 3145736 | tf_op jit(solution)/shard_map/ppermute | solution.py:125
  177.2 4.2 %slice-start.1 = ((s8[8388608]{0:T(1024)(128)(4,1)}), s8[4194304]{0:T(1024)(128)(4,1)S(1)}, s32[]{:S(2)}) async-start(s8[8388608]{0:T(1024)(128)(4,1)} %bitcast.79), calls=%async_computation.6 | async-start | bytes 8388608
  193.6 13.5 %collective-permute-start.10 = (f32[1024,128]{0,1:T(8,128)S(1)}, f32[1024,128]{0,1:T(8,128)S(1)}, u32[]{:S(2)}, u32[]{:S(2)}) collective-permute-start(f32[1024,128]{0,1:T(8,128)S(1)} %constant_dynamic-slice_fusion.2), channel_id=1, source_target_pairs={{0,2},{1,3},{2,0},{3,1},{4,6},{5,7},{6,4},{7,5},{8,10},{9,11},{10,... | collective-permute-start | bytes 1572872 | tf_op jit(solution)/shard_map/ppermute | solution.py:134
  207.2 1.4 collective-permute-start.11
  230.9 0.8 copy-start.5

commit v13 on v12

--- a/solution.py
+++ b/solution.py
@@ -3,6 +3,7 @@
 import jax
 import jax.numpy as jnp
 from jax import lax
+from jax.experimental import pallas as pl
 from jax.sharding import PartitionSpec as P
 
 BAND = 64
@@ -140,6 +141,28 @@
     return jnp.where(core == 0, jnp.concatenate([kept, got], axis=1), jnp.concatenate([got, kept], axis=1))
 
 
+def lay_out_blocks(records, block_of, block, half):
+    segs, rows, width = records.shape
+    parts = len(block_of)
+
+    def kernel(src, dst):
+        for place, b in enumerate(block_of):
+            low = b * block + half
+            if low + block <= width:
+                dst[0, place] = src[0, :, low:low + block]
+            else:
+                dst[0, place, :, : width - low] = src[0, :, low:]
+                dst[0, place, :, width - low:] = src[0, :, : low + block - width]
+
+    return pl.pallas_call(
+        kernel,
+        out_shape=jax.ShapeDtypeStruct((segs, parts, rows, block), records.dtype),
+        grid=(segs,),
+        in_specs=[pl.BlockSpec((1, rows, width), lambda s: (s, 0, 0))],
+        out_specs=pl.BlockSpec((1, parts, rows, block), lambda s: (s, 0, 0, 0)),
+    )(records)
+
+
 def make_per_device(ring):
     count = len(ring)
     block_of = [0] * count
@@ -164,20 +187,9 @@
         pick_second = (channel_ids == (my_first + my_offset)[None, :]).astype(jnp.bfloat16)
         cross = None
         arrived = []
+        laid_out = lay_out_blocks(records, block_of, block, half)
         for segment in range(records.shape[0]):
-            pieces = []
-            for b in block_of:
-                low = b * block + half
-                if low + block <= records.shape[2]:
-                    pieces.append(records[segment, :, low:low + block])
-                else:
-                    pieces.append(
-                        jnp.concatenate(
-                            [records[segment, :, low:], records[segment, :, : low + block - records.shape[2]]],
-                            axis=1,
-                        )
-                    )
-            outgoing = jnp.stack(pieces, axis=0)
+            outgoing = laid_out[segment]
             received = lax.all_to_all(outgoing, "tile", split_axis=0, concat_axis=0, tiled=True)
             if arrived:
                 received, _ = lax.optimization_barrier((received, arrived[-1]))

time: 233 us -> 231 us (level)
  local copies, waits for them, and re-layouts: 28.8 us -> 23.4 us
  Pallas kernels: 0 us -> 4.76 us
    unnamed x38 -> x28, local copies, waits for them, and re-layouts: 11 us -> 3.01 us
    pallas_call x0 -> x1, Pallas kernels: none -> 4.76 us  [lay_out_blocks(): pl.pallas_call(kernel, out_shape=jax.ShapeDtypeStruct((segs, parts, rows,...]
    squeeze x1, local copies, waits for them, and re-layouts: 1.11 us -> 4.45 us  [per_device(): outgoing = laid_out[segment]]
where the time goes in v13:
time: 231 us; the launch traced here: 230 us
  starting transfers between devices  54.5 us (24%)
  waiting for transfers between devices  48.6 us (21%)
  matrix products  46.1 us (20%)
  other arithmetic  29.9 us (13%)
  local copies, waits for them, and re-layouts  23.4 us (10%)
  blocking collectives  21.9 us (9%)
  Pallas kernels  4.76 us (2%)
    dot_general x4, matrix products, per_device(): jnp.einsum('fjm,jmc->fc', forward, received, preferred_element_type=jnp.f...  24.2 us
    all_to_all x4, waiting for transfers between devices, per_device(): lax.all_to_all(outgoing, 'tile', split_axis=0, concat_axis=0, tiled=True)  22.9 us
    all_to_all x1, blocking collectives, per_device(): lax.all_to_all(buckets, 'tile', split_axis=0, concat_axis=0, tiled=True)  21.9 us
    all_to_all x4, starting transfers between devices, per_device(): lax.all_to_all(outgoing, 'tile', split_axis=0, concat_axis=0, tiled=True)  19.7 us
    ppermute x4, starting transfers between devices, per_device(): from_next = lax.ppermute(whitened[:, :half], 'tile', to_prev)  19.4 us
    ppermute x4, starting transfers between devices, per_device(): from_prev = lax.ppermute(whitened[:, half:], 'tile', to_next)  13 us
    ppermute x1, waiting for transfers between devices, sum_and_invert(): lax.ppermute(send, 'win', [(w, w ^ 2 * bit) for w in range(win_count)])  12 us
    ppermute x4, waiting for transfers between devices, per_device(): from_prev = lax.ppermute(whitened[:, half:], 'tile', to_next)  11 us
  transfers between devices with their start and end apart: 16, of which 9 were waited for; matrix products, arithmetic and copies ran while one was open for 32% of the time, Pallas kernels for 0%

profile of v13, /device:TPU:0, one launch (start us, length us, event | category | flops | bytes accessed | tf_op | source)
XLA Modules:
  0.0 229.7 jit_solution(5853495835382037424)
XLA Ops:
  0.0 4.8 %shard_map.46 = bf16[4,8,256,256]{3,2,1,0:T(8,128)(2,1)} custom-call(bf16[4,256,2048]{2,1,0:T(8,128)(2,1)} %src.1), custom_call_target="tpu_custom_call" | custom-call | tf_op jit(solution)/shard_map/pallas_call | solution.py:157
  4.8 4.5 %slice_bitcast_fusion = (bf16[8,256,256]{2,1,0:T(8,128)(2,1)}, bf16[8,256,256]{2,1,0:T(8,128)(2,1)}, bf16[8,256,256]{2,1,0:T(8,128)(2,1)}, bf16[8,256,256]{2,1,0:T(8,128)(2,1)}) fusion(bf16[4,8,256,256]{3,2,1,0:T(8,128)(2,1)} %shard_map.46), kind=kLoop, calls=%fused_computation.34 | loop fusion | bytes 8388608 | tf_op jit(solution)/shard_map/squeeze | solution.py:192
  9.2 7.3 %all-to-all-start = ((bf16[8,256,256]{2,1,0:T(8,128)(2,1)}), bf16[8,256,256]{2,1,0:T(8,128)(2,1)S(1)}, u32[]{:S(2)}, u32[]{:S(2)}) async-start(bf16[8,256,256]{2,1,0:T(8,128)(2,1)} %get-tuple-element.18), calls=%async_computation | async-start | bytes 2097152 | tf_op jit(solution)/shard_map/all_to_all | solution.py:193
  16.6 0.7 collective-permute-start
  17.3 1.0 fusion.59
  18.3 0.6 fusion.67
  18.9 5.1 %subtract_convert_fusion = (bf16[1024,32,64]{0,2,1:T(8,128)(2,1)}, bf16[1024,32,64]{0,2,1:T(8,128)(2,1)}) fusion(f32[1024,64]{0,1:T(8,128)S(1)} %get-tuple-element.48, f32[1024,32]{0,1:T(8,128)S(1)} %get-tuple-element.47, f32[1024,64]{0,1:T(8,128)S(1)} %get-tuple-element.49, f32[1024,32]{0,1:T(8,128)S(1)} %get-tuple-element.46), kind=kLoop, calls=%fused_computation.10 | loop fusion | flops 18874368 | bytes 9175040 | tf_op jit(solution)/shard_map/convert.3
  24.0 6.5 %copy.5 = bf16[1024,8,256]{2,0,1:T(8,128)(2,1)} copy(bf16[1024,8,256]{0,2,1:T(8,128)(2,1)} %bitcast.60) | data formatting | bytes 8388608 | tf_op jit(solution)/shard_map/sub | solution.py:25
  30.5 6.5 %copy.6 = bf16[1024,8,256]{2,0,1:T(8,128)(2,1)} copy(bf16[1024,8,256]{0,2,1:T(8,128)(2,1)} %bitcast.59) | data formatting | bytes 8388608 | tf_op jit(solution)/shard_map/neg | solution.py:32
  37.0 0.6 reduce-window.6
  37.9 4.4 %all-to-all-done = bf16[8,256,256]{2,1,0:T(8,128)(2,1)S(1)} async-done(((bf16[8,256,256]{2,1,0:T(8,128)(2,1)}), bf16[8,256,256]{2,1,0:T(8,128)(2,1)S(1)}, u32[]{:S(2)}, u32[]{:S(2)}) %all-to-all-start) | async-done | bytes 1048608 | tf_op jit(solution)/shard_map/all_to_all | solution.py:193
  42.3 3.8 %all-to-all-start.1 = ((bf16[8,256,256]{2,1,0:T(8,128)(2,1)}), bf16[8,256,256]{2,1,0:T(8,128)(2,1)S(1)}, u32[]{:S(2)}, u32[]{:S(2)}) async-start(bf16[8,256,256]{2,1,0:T(8,128)(2,1)} %get-tuple-element.17), calls=%async_computation.1 | async-start | bytes 2097152 | tf_op jit(solution)/shard_map/all_to_all | solution.py:193
  46.1 5.9 %convolution_bitcast_fusion.3 = f32[2048,256]{1,0:T(8,128)S(1)} fusion(bf16[8,256,256]{2,1,0:T(8,128)(2,1)S(1)} %all-to-all-done, bf16[1024,8,256]{2,0,1:T(8,128)(2,1)} %copy.6, bf16[1024,8,256]{2,0,1:T(8,128)(2,1)} %copy.5), kind=kOutput, calls=%fused_computation.14 | convolution fusion | flops 2164260864 | bytes 11534336 | tf_op jit(solution)/shard_map/fjm,jmc->fc/dot_general | solution.py:196
  52.3 0.3 fusion.4
  52.7 2.1 collective-permute-start.1
  54.8 0.6 fusion.65
  55.4 2.0 fusion.48
  57.5 7.1 %multiply_subtract_fusion = (f32[2048,16,64]{0,2,1:T(8,128)}, f32[2048,16,64]{0,2,1:T(8,128)}) fusion(f32[2048,64]{0,1:T(8,128)S(1)} %get-tuple-element.42, f32[2048,16]{0,1:T(8,128)S(1)} %get-tuple-element.40, f32[2048,64]{0,1:T(8,128)S(1)} %get-tuple-element.41, f32[2048,16]{0,1:T(8,128)S(1)} %get-tuple-element.39), kind=kLoop, calls=%fused_computation.8 | loop fusion | flops 12582912 | bytes 18087936 | tf_op jit(solution)/shard_map/sub | solution.py:25
  64.5 8.7 %all-to-all-done.1 = bf16[8,256,256]{2,1,0:T(8,128)(2,1)S(1)} async-done(((bf16[8,256,256]{2,1,0:T(8,128)(2,1)}), bf16[8,256,256]{2,1,0:T(8,128)(2,1)S(1)}, u32[]{:S(2)}, u32[]{:S(2)}) %all-to-all-start.1) | async-done | bytes 1048608 | tf_op jit(solution)/shard_map/all_to_all | solution.py:193
  73.2 4.4 %all-to-all-start.2 = ((bf16[8,256,256]{2,1,0:T(8,128)(2,1)}), bf16[8,256,256]{2,1,0:T(8,128)(2,1)}, u32[]{:S(2)}, u32[]{:S(2)}) async-start(bf16[8,256,256]{2,1,0:T(8,128)(2,1)} %get-tuple-element.16), calls=%async_computation.2 | async-start | bytes 2097152 | tf_op jit(solution)/shard_map/all_to_all | solution.py:193
  77.7 5.9 %convolution_bitcast_fusion.2 = f32[2048,256]{1,0:T(8,128)S(1)} fusion(bf16[8,256,256]{2,1,0:T(8,128)(2,1)S(1)} %all-to-all-done.1, bf16[1024,8,256]{2,0,1:T(8,128)(2,1)} %copy.6, bf16[1024,8,256]{2,0,1:T(8,128)(2,1)} %copy.5), kind=kOutput, calls=%fused_computation.13 | convolution fusion | flops 2164260864 | bytes 11534336 | tf_op jit(solution)/shard_map/fjm,jmc->fc/dot_general | solution.py:196
  83.9 0.3 fusion.7
  84.3 1.0 fusion.84
  85.3 1.7 collective-permute-start.3
  87.0 10.4 %collective-permute-start.4 = (bf16[2048,128]{1,0:T(8,128)(2,1)}, bf16[2048,128]{1,0:T(8,128)(2,1)}, u32[]{:S(2)}, u32[]{:S(2)}) collective-permute-start(bf16[2048,128]{1,0:T(8,128)(2,1)} %get-tuple-element.32), channel_id=1, source_target_pairs={{0,8},{4,0},{12,4},{20,12},{28,20},{24,28},{16,24},{8,16},{1,9},{5... | collective-permute-start | bytes 1572872 | tf_op jit(solution)/shard_map/ppermute | solution.py:199
  97.4 2.0 fusion.23
  99.3 2.0 fusion.22
  101.3 0.3 multiply_add_fusion.4
  101.6 5.5 %all-to-all-done.2 = bf16[8,256,256]{2,1,0:T(8,128)(2,1)} async-done(((bf16[8,256,256]{2,1,0:T(8,128)(2,1)}), bf16[8,256,256]{2,1,0:T(8,128)(2,1)}, u32[]{:S(2)}, u32[]{:S(2)}) %all-to-all-start.2) | async-done | bytes 1048608 | tf_op jit(solution)/shard_map/all_to_all | solution.py:193
  107.1 4.3 %all-to-all-start.3 = ((bf16[8,256,256]{2,1,0:T(8,128)(2,1)}), bf16[8,256,256]{2,1,0:T(8,128)(2,1)}, u32[]{:S(2)}, u32[]{:S(2)}) async-start(bf16[8,256,256]{2,1,0:T(8,128)(2,1)} %get-tuple-element.15), calls=%async_computation.3 | async-start | bytes 2097152 | tf_op jit(solution)/shard_map/all_to_all | solution.py:193
  111.4 6.1 %convolution_bitcast_fusion.1 = f32[2048,256]{1,0:T(8,128)S(1)} fusion(bf16[8,256,256]{2,1,0:T(8,128)(2,1)} %all-to-all-done.2, bf16[1024,8,256]{2,0,1:T(8,128)(2,1)} %copy.6, bf16[1024,8,256]{2,0,1:T(8,128)(2,1)} %copy.5), kind=kOutput, calls=%fused_computation.12 | convolution fusion | flops 2164260864 | bytes 11534336 | tf_op jit(solution)/shard_map/fjm,jmc->fc/dot_general | solution.py:196
  117.8 0.3 fusion.8
  118.2 1.2 fusion.83
  119.3 5.2 %collective-permute-start.5 = (bf16[2048,128]{1,0:T(8,128)(2,1)}, bf16[2048,128]{1,0:T(8,128)(2,1)}, u32[]{:S(2)}, u32[]{:S(2)}) collective-permute-start(bf16[2048,128]{1,0:T(8,128)(2,1)} %get-tuple-element.29), channel_id=1, source_target_pairs={{0,4},{4,12},{12,20},{20,28},{28,24},{24,16},{16,8},{8,0},{1,5},{5... | collective-permute-start | bytes 1572872 | tf_op jit(solution)/shard_map/ppermute | solution.py:198
  124.5 6.8 %collective-permute-start.6 = (bf16[2048,128]{1,0:T(8,128)(2,1)}, bf16[2048,128]{1,0:T(8,128)(2,1)}, u32[]{:S(2)}, u32[]{:S(2)}) collective-permute-start(bf16[2048,128]{1,0:T(8,128)(2,1)} %get-tuple-element.30), channel_id=1, source_target_pairs={{0,8},{4,0},{12,4},{20,12},{28,20},{24,28},{16,24},{8,16},{1,9},{5... | collective-permute-start | bytes 1572872 | tf_op jit(solution)/shard_map/ppermute | solution.py:199
  131.3 2.0 fusion.21
  133.3 2.0 fusion.20
  135.3 1.3 multiply_add_fusion.3
  136.6 4.3 %all-to-all-done.3 = bf16[8,256,256]{2,1,0:T(8,128)(2,1)} async-done(((bf16[8,256,256]{2,1,0:T(8,128)(2,1)}), bf16[8,256,256]{2,1,0:T(8,128)(2,1)}, u32[]{:S(2)}, u32[]{:S(2)}) %all-to-all-start.3) | async-done | bytes 1048608 | tf_op jit(solution)/shard_map/all_to_all | solution.py:193
  140.9 4.7 %collective-permute-done.5 = bf16[2048,128]{1,0:T(8,128)(2,1)} collective-permute-done((bf16[2048,128]{1,0:T(8,128)(2,1)}, bf16[2048,128]{1,0:T(8,128)(2,1)}, u32[]{:S(2)}, u32[]{:S(2)}) %collective-permute-start.5) | collective-permute-done | bytes 524320 | tf_op jit(solution)/shard_map/ppermute | solution.py:198
  145.5 6.1 %convolution_bitcast_fusion = f32[2048,256]{1,0:T(8,128)S(1)} fusion(bf16[8,256,256]{2,1,0:T(8,128)(2,1)} %all-to-all-done.3, bf16[1024,8,256]{2,0,1:T(8,128)(2,1)} %copy.6, bf16[1024,8,256]{2,0,1:T(8,128)(2,1)} %copy.5), kind=kOutput, calls=%fused_computation.11 | convolution fusion | flops 2164260864 | bytes 11534336 | tf_op jit(solution)/shard_map/fjm,jmc->fc/dot_general | solution.py:196
  152.0 0.3 fusion.9
  152.4 4.0 %collective-permute-start.7 = (bf16[2048,128]{1,0:T(8,128)(2,1)S(1)}, bf16[2048,128]{1,0:T(8,128)(2,1)S(1)}, u32[]{:S(2)}, u32[]{:S(2)}) collective-permute-start(bf16[2048,128]{1,0:T(8,128)(2,1)S(1)} %get-tuple-element.27), channel_id=1, source_target_pairs={{0,4},{4,12},{12,20},{20,28},{28,24},{24,16},{16,8},{8,0},{1,5},{5... | collective-permute-start | bytes 1572872 | tf_op jit(solution)/shard_map/ppermute | solution.py:198
  156.4 2.1 collective-permute-start.8
  158.5 2.0 fusion.19
  160.5 2.0 fusion.18
  162.4 0.3 multiply_add_fusion.2
  162.7 6.3 %collective-permute-done.7 = bf16[2048,128]{1,0:T(8,128)(2,1)S(1)} collective-permute-done((bf16[2048,128]{1,0:T(8,128)(2,1)S(1)}, bf16[2048,128]{1,0:T(8,128)(2,1)S(1)}, u32[]{:S(2)}, u32[]{:S(2)}) %collective-permute-start.7) | collective-permute-done | bytes 524320 | tf_op jit(solution)/shard_map/ppermute | solution.py:198
  169.0 1.4 collective-permute-done.8
  170.4 0.8 fusion.17
  171.2 0.8 fusion.16
  172.0 0.3 multiply_add_fusion.1
  172.2 1.3 copy-done
  173.6 0.5 fusion.6
  174.3 0.8 slice-done.3
  175.1 4.2 %bitcast_multiply_fusion = f32[2048,1024]{0,1:T(8,128)} fusion(f32[2048,16,64]{0,2,1:T(8,128)S(1)} %bitcast.58, f32[1024]{0:T(1024)S(1)} %fusion.70), kind=kLoop, calls=%fused_computation.5 | loop fusion | flops 2097152 | bytes 16781312 | tf_op jit(solution)/shard_map/mul | solution.py:43
  179.2 3.9 %bitcast_multiply_fusion.1 = f32[2048,1024]{0,1:T(8,128)} fusion(f32[2048,16,64]{0,2,1:T(8,128)S(1)} %bitcast.56, f32[1024]{0:T(1024)S(1)} %select_multiply_fusion), kind=kLoop, calls=%fused_computation.6 | loop fusion | flops 2097152 | bytes 16781312 | tf_op jit(solution)/shard_map/mul | solution.py:43
  183.1 8.2 %fusion = f32[2048,128]{0,1:T(8,128)S(1)} fusion(f32[2048,1024]{0,1:T(8,128)} %bitcast_multiply_fusion, f32[2048,1024]{0,1:T(8,128)} %bitcast_multiply_fusion.1, f32[2048,128]{1,0:T(8,128)S(1)} %collective-permute-done.9, f32[2048,256]{1,0:T(8,128)S(1)} %fusion.6, s32[]{:T(128)S(6)} %select_n.119), kind=kOutput, calls=%fused_computation | convolution fusion | flops 3225681920 | bytes 19922948 | tf_op jit(solution)/shard_map/dot_general | solution.py:128
  191.4 1.6 collective-permute-start.10
  193.0 12.0 %collective-permute-done.10 = f32[1024,128]{0,1:T(8,128)S(1)} collective-permute-done((f32[1024,128]{0,1:T(8,128)S(1)}, f32[1024,128]{0,1:T(8,128)S(1)}, u32[]{:S(2)}, u32[]{:S(2)}) %collective-permute-start.10) | collective-permute-done | bytes 524320 | tf_op jit(solution)/shard_map/ppermute | solution.py:135
  205.1 1.3 collective-permute-done.11
  206.5 0.4 convolution_convert_fusion
  206.9 21.9 %all_to_all.25 = bf16[8,80,512]{2,1,0:T(8,128)(2,1)S(1)} all-to-all(bf16[8,80,512]{2,1,0:T(8,128)(2,1)S(1)} %bitcast.65), channel_id=1, replica_groups=mesh['tile'=8,'win'=4] {'tile'}, dimensions={0} | all-to-all | bytes 1310720 | tf_op jit(solution)/shard_map/all_to_all | solution.py:219
  228.8 0.8 copy-done.3
  (69 shorter events, 2.2 us)
Async XLA Ops:
  4.8 11.8 %copy-start.4 = (s32[256,1]{0,1:T(1,128)S(1)}, s32[256,1]{0,1:T(1,128)}, u32[]{:S(2)}) copy-start(s32[256,1]{0,1:T(1,128)} %param.7) | copy-start | bytes 3076
  4.8 11.8 %copy-start.5 = (s32[256]{0:T(256)S(1)}, s32[256]{0:T(256)}, u32[]{:S(2)}) copy-start(s32[256]{0:T(256)} %param.6) | copy-start | bytes 3076
  4.8 11.8 %copy-start.6 = (s32[256]{0:T(256)S(1)}, s32[256]{0:T(256)}, u32[]{:S(2)}) copy-start(s32[256]{0:T(256)} %param.5) | copy-start | bytes 3076
  9.2 33.1 %all-to-all-start = ((bf16[8,256,256]{2,1,0:T(8,128)(2,1)}), bf16[8,256,256]{2,1,0:T(8,128)(2,1)S(1)}, u32[]{:S(2)}, u32[]{:S(2)}) async-start(bf16[8,256,256]{2,1,0:T(8,128)(2,1)} %get-tuple-element.18), calls=%async_computation | async-start | bytes 2097152 | tf_op jit(solution)/shard_map/all_to_all | solution.py:193
  16.6 20.4 %collective-permute-start = (s32[3,256]{1,0:T(4,128)S(1)}, s32[3,256]{1,0:T(4,128)S(1)}, u32[]{:S(2)}, u32[]{:S(2)}) collective-permute-start(s32[3,256]{1,0:T(4,128)S(1)} %pad_add_fusion), channel_id=1, source_target_pairs={{0,0},{4,4},{8,12},{12,20},{16,28},{20,24},{24,16},{28,8},{1,1},{5... | collective-permute-start | bytes 9224 | tf_op jit(solution)/shard_map/ppermute | solution.py:184
  42.3 30.9 %all-to-all-start.1 = ((bf16[8,256,256]{2,1,0:T(8,128)(2,1)}), bf16[8,256,256]{2,1,0:T(8,128)(2,1)S(1)}, u32[]{:S(2)}, u32[]{:S(2)}) async-start(bf16[8,256,256]{2,1,0:T(8,128)(2,1)} %get-tuple-element.17), calls=%async_computation.1 | async-start | bytes 2097152 | tf_op jit(solution)/shard_map/all_to_all | solution.py:193
  52.7 25.0 %collective-permute-start.1 = (bf16[2048,128]{1,0:T(8,128)(2,1)S(1)}, bf16[2048,128]{1,0:T(8,128)(2,1)}, u32[]{:S(2)}, u32[]{:S(2)}) collective-permute-start(bf16[2048,128]{1,0:T(8,128)(2,1)S(1)} %get-tuple-element.33), channel_id=1, source_target_pairs={{0,4},{4,12},{12,20},{20,28},{28,24},{24,16},{16,8},{8,0},{1,5},{5... | collective-permute-start | bytes 1572872 | tf_op jit(solution)/shard_map/ppermute | solution.py:198
  54.8 22.9 %collective-permute-start.2 = (bf16[2048,128]{1,0:T(8,128)(2,1)S(1)}, bf16[2048,128]{1,0:T(8,128)(2,1)}, u32[]{:S(2)}, u32[]{:S(2)}) collective-permute-start(bf16[2048,128]{1,0:T(8,128)(2,1)S(1)} %get-tuple-element.34), channel_id=1, source_target_pairs={{0,8},{4,0},{12,4},{20,12},{28,20},{24,28},{16,24},{8,16},{1,9},{5... | collective-permute-start | bytes 1572872 | tf_op jit(solution)/shard_map/ppermute | solution.py:199
  73.2 33.9 %all-to-all-start.2 = ((bf16[8,256,256]{2,1,0:T(8,128)(2,1)}), bf16[8,256,256]{2,1,0:T(8,128)(2,1)}, u32[]{:S(2)}, u32[]{:S(2)}) async-start(bf16[8,256,256]{2,1,0:T(8,128)(2,1)} %get-tuple-element.16), calls=%async_computation.2 | async-start | bytes 2097152 | tf_op jit(solution)/shard_map/all_to_all | solution.py:193
  85.3 26.1 %collective-permute-start.3 = (bf16[2048,128]{1,0:T(8,128)(2,1)}, bf16[2048,128]{1,0:T(8,128)(2,1)}, u32[]{:S(2)}, u32[]{:S(2)}) collective-permute-start(bf16[2048,128]{1,0:T(8,128)(2,1)} %get-tuple-element.31), channel_id=1, source_target_pairs={{0,4},{4,12},{12,20},{20,28},{28,24},{24,16},{16,8},{8,0},{1,5},{5... | collective-permute-start | bytes 1572872 | tf_op jit(solution)/shard_map/ppermute | solution.py:198
  87.0 24.4 %collective-permute-start.4 = (bf16[2048,128]{1,0:T(8,128)(2,1)}, bf16[2048,128]{1,0:T(8,128)(2,1)}, u32[]{:S(2)}, u32[]{:S(2)}) collective-permute-start(bf16[2048,128]{1,0:T(8,128)(2,1)} %get-tuple-element.32), channel_id=1, source_target_pairs={{0,8},{4,0},{12,4},{20,12},{28,20},{24,28},{16,24},{8,16},{1,9},{5... | collective-permute-start | bytes 1572872 | tf_op jit(solution)/shard_map/ppermute | solution.py:199
  107.1 33.8 %all-to-all-start.3 = ((bf16[8,256,256]{2,1,0:T(8,128)(2,1)}), bf16[8,256,256]{2,1,0:T(8,128)(2,1)}, u32[]{:S(2)}, u32[]{:S(2)}) async-start(bf16[8,256,256]{2,1,0:T(8,128)(2,1)} %get-tuple-element.15), calls=%async_computation.3 | async-start | bytes 2097152 | tf_op jit(solution)/shard_map/all_to_all | solution.py:193
  118.1 15.2 %copy-start.1 = (bf16[2048,256]{1,0:T(8,128)(2,1)}, bf16[2048,256]{1,0:T(8,128)(2,1)S(1)}, u32[]{:S(2)}) copy-start(bf16[2048,256]{1,0:T(8,128)(2,1)S(1)} %fusion.8) | copy-start | bytes 3145732
  119.3 26.2 %collective-permute-start.5 = (bf16[2048,128]{1,0:T(8,128)(2,1)}, bf16[2048,128]{1,0:T(8,128)(2,1)}, u32[]{:S(2)}, u32[]{:S(2)}) collective-permute-start(bf16[2048,128]{1,0:T(8,128)(2,1)} %get-tuple-element.29), channel_id=1, source_target_pairs={{0,4},{4,12},{12,20},{20,28},{28,24},{24,16},{16,8},{8,0},{1,5},{5... | collective-permute-start | bytes 1572872 | tf_op jit(solution)/shard_map/ppermute | solution.py:198
  124.5 21.0 %collective-permute-start.6 = (bf16[2048,128]{1,0:T(8,128)(2,1)}, bf16[2048,128]{1,0:T(8,128)(2,1)}, u32[]{:S(2)}, u32[]{:S(2)}) collective-permute-start(bf16[2048,128]{1,0:T(8,128)(2,1)} %get-tuple-element.30), channel_id=1, source_target_pairs={{0,8},{4,0},{12,4},{20,12},{28,20},{24,28},{16,24},{8,16},{1,9},{5... | collective-permute-start | bytes 1572872 | tf_op jit(solution)/shard_map/ppermute | solution.py:199
  151.9 6.6 %copy-start.2 = (bf16[2048,256]{1,0:T(8,128)(2,1)S(1)}, bf16[2048,256]{1,0:T(8,128)(2,1)}, u32[]{:S(2)}) copy-start(bf16[2048,256]{1,0:T(8,128)(2,1)} %copy-done.1) | copy-start | bytes 3145732
  152.4 16.7 %collective-permute-start.7 = (bf16[2048,128]{1,0:T(8,128)(2,1)S(1)}, bf16[2048,128]{1,0:T(8,128)(2,1)S(1)}, u32[]{:S(2)}, u32[]{:S(2)}) collective-permute-start(bf16[2048,128]{1,0:T(8,128)(2,1)S(1)} %get-tuple-element.27), channel_id=1, source_target_pairs={{0,4},{4,12},{12,20},{20,28},{28,24},{24,16},{16,8},{8,0},{1,5},{5... | collective-permute-start | bytes 1572872 | tf_op jit(solution)/shard_map/ppermute | solution.py:198
  156.4 14.0 %collective-permute-start.8 = (bf16[2048,128]{1,0:T(8,128)(2,1)S(1)}, bf16[2048,128]{1,0:T(8,128)(2,1)S(1)}, u32[]{:S(2)}, u32[]{:S(2)}) collective-permute-start(bf16[2048,128]{1,0:T(8,128)(2,1)S(1)} %get-tuple-element.28), channel_id=1, source_target_pairs={{0,8},{4,0},{12,4},{20,12},{28,20},{24,28},{16,24},{8,16},{1,9},{5... | collective-permute-start | bytes 1572872 | tf_op jit(solution)/shard_map/ppermute | solution.py:199
  171.2 3.1 %slice-start.2 = ((s8[8388608]{0:T(1024)(128)(4,1)}), s8[4194304]{0:T(1024)(128)(4,1)S(1)}, s32[]{:S(2)}) async-start(s8[8388608]{0:T(1024)(128)(4,1)} %bitcast.57), calls=%async_computation.7 | async-start | bytes 8388608
  171.9 1.6 copy-start
  172.0 3.1 %slice-start.3 = ((s8[8388608]{0:T(1024)(128)(4,1)}), s8[4194304]{0:T(1024)(128)(4,1)S(1)}, s32[]{:S(2)}) async-start(s8[8388608]{0:T(1024)(128)(4,1)} %bitcast.57), calls=%async_computation.8 | async-start | bytes 8388608
  173.6 5.7 %slice-start = ((s8[8388608]{0:T(1024)(128)(4,1)}), s8[4194304]{0:T(1024)(128)(4,1)S(1)}, s32[]{:S(2)}) async-start(s8[8388608]{0:T(1024)(128)(4,1)} %bitcast.55), calls=%async_computation.5 | async-start | bytes 8388608
  174.2 8.9 %collective-permute-start.9 = (f32[2048,128]{1,0:T(8,128)S(1)}, f32[2048,128]{1,0:T(8,128)S(1)}, u32[]{:S(2)}, u32[]{:S(2)}) collective-permute-start(f32[2048,128]{1,0:T(8,128)S(1)} %constant_dynamic-slice_fusion.3), channel_id=1, source_target_pairs={{0,1},{1,0},{2,3},{3,2},{4,5},{5,4},{6,7},{7,6},{8,9},{9,8},{10,11... | collective-permute-start | bytes 3145736 | tf_op jit(solution)/shard_map/ppermute | solution.py:126
  175.1 4.2 %slice-start.1 = ((s8[8388608]{0:T(1024)(128)(4,1)}), s8[4194304]{0:T(1024)(128)(4,1)S(1)}, s32[]{:S(2)}) async-start(s8[8388608]{0:T(1024)(128)(4,1)} %bitcast.55), calls=%async_computation.6 | async-start | bytes 8388608
  191.4 13.5 %collective-permute-start.10 = (f32[1024,128]{0,1:T(8,128)S(1)}, f32[1024,128]{0,1:T(8,128)S(1)}, u32[]{:S(2)}, u32[]{:S(2)}) collective-permute-start(f32[1024,128]{0,1:T(8,128)S(1)} %constant_dynamic-slice_fusion.2), channel_id=1, source_target_pairs={{0,2},{1,3},{2,0},{3,1},{4,6},{5,7},{6,4},{7,5},{8,10},{9,11},{10,... | collective-permute-start | bytes 1572872 | tf_op jit(solution)/shard_map/ppermute | solution.py:135
  205.1 1.4 collective-permute-start.11
  228.8 0.8 copy-start.3

commit v14 on v13

--- a/solution.py
+++ b/solution.py
@@ -141,7 +141,7 @@
     return jnp.where(core == 0, jnp.concatenate([kept, got], axis=1), jnp.concatenate([got, kept], axis=1))
 
 
-def lay_out_blocks(records, block_of, block, half):
+def lay_out_blocks(records, segment, block_of, block, half):
     segs, rows, width = records.shape
     parts = len(block_of)
 
@@ -149,17 +149,17 @@
         for place, b in enumerate(block_of):
             low = b * block + half
             if low + block <= width:
-                dst[0, place] = src[0, :, low:low + block]
+                dst[place] = src[0, :, low:low + block]
             else:
-                dst[0, place, :, : width - low] = src[0, :, low:]
-                dst[0, place, :, width - low:] = src[0, :, : low + block - width]
+                dst[place, :, : width - low] = src[0, :, low:]
+                dst[place, :, width - low:] = src[0, :, : low + block - width]
 
     return pl.pallas_call(
         kernel,
-        out_shape=jax.ShapeDtypeStruct((segs, parts, rows, block), records.dtype),
-        grid=(segs,),
-        in_specs=[pl.BlockSpec((1, rows, width), lambda s: (s, 0, 0))],
-        out_specs=pl.BlockSpec((1, parts, rows, block), lambda s: (s, 0, 0, 0)),
+        out_shape=jax.ShapeDtypeStruct((parts, rows, block), records.dtype),
+        grid=(1,),
+        in_specs=[pl.BlockSpec((1, rows, width), lambda i: (segment, 0, 0))],
+        out_specs=pl.BlockSpec((parts, rows, block), lambda i: (0, 0, 0)),
     )(records)
 
 
@@ -187,9 +187,8 @@
         pick_second = (channel_ids == (my_first + my_offset)[None, :]).astype(jnp.bfloat16)
         cross = None
         arrived = []
-        laid_out = lay_out_blocks(records, block_of, block, half)
         for segment in range(records.shape[0]):
-            outgoing = laid_out[segment]
+            outgoing = lay_out_blocks(records, segment, block_of, block, half)
             received = lax.all_to_all(outgoing, "tile", split_axis=0, concat_axis=0, tiled=True)
             if arrived:
                 received, _ = lax.optimization_barrier((received, arrived[-1]))

time: 231 us -> 229 us (level)
  waiting for transfers between devices: 48.6 us -> 39.4 us
  starting transfers between devices: 54.5 us -> 62.6 us
  Pallas kernels: 4.76 us -> 9.43 us
  local copies, waits for them, and re-layouts: 23.4 us -> 19 us
    all_to_all x4, waiting for transfers between devices: 22.9 us -> 15.1 us  [per_device(): lax.all_to_all(outgoing, 'tile', split_axis=0, concat_axis=0, tiled=True)]
    pallas_call x1 -> x4, Pallas kernels: 4.76 us -> 9.43 us  [lay_out_blocks(): pl.pallas_call(kernel, out_shape=jax.ShapeDtypeStruct((parts, rows, block...]
    squeeze x1 -> x0, local copies, waits for them, and re-layouts: 4.45 us -> none  [per_device(): outgoing = laid_out[segment]]
    all_to_all x4, starting transfers between devices: 19.7 us -> 23.8 us  [per_device(): lax.all_to_all(outgoing, 'tile', split_axis=0, concat_axis=0, tiled=True)]
    ppermute x4, starting transfers between devices: 19.4 us -> 22.5 us  [per_device(): from_next = lax.ppermute(whitened[:, :half], 'tile', to_prev)]
  transfers between devices with their start and end apart: 16 -> 16, of which waited for: 9 -> 8; matrix products, arithmetic and copies ran while one was open for 32% -> 32% of each run, Pallas kernels for 0% -> 3%
where the time goes in v14:
time: 229 us
  starting transfers between devices  62.6 us (27%)
  matrix products  46.1 us (20%)
  waiting for transfers between devices  39.4 us (17%)
  other arithmetic  29.8 us (13%)
  blocking collectives  21.8 us (10%)
  local copies, waits for them, and re-layouts  19 us (8%)
  Pallas kernels  9.43 us (4%)
    dot_general x4, matrix products, per_device(): jnp.einsum('fjm,jmc->fc', forward, received, preferred_element_type=jnp.f...  24.2 us
    all_to_all x4, starting transfers between devices, per_device(): lax.all_to_all(outgoing, 'tile', split_axis=0, concat_axis=0, tiled=True)  23.8 us
    ppermute x4, starting transfers between devices, per_device(): from_next = lax.ppermute(whitened[:, :half], 'tile', to_prev)  22.5 us
    all_to_all x1, blocking collectives, per_device(): lax.all_to_all(buckets, 'tile', split_axis=0, concat_axis=0, tiled=True)  21.8 us
    all_to_all x4, waiting for transfers between devices, per_device(): lax.all_to_all(outgoing, 'tile', split_axis=0, concat_axis=0, tiled=True)  15.1 us
    ppermute x4, starting transfers between devices, per_device(): from_prev = lax.ppermute(whitened[:, half:], 'tile', to_next)  14 us
    ppermute x1, waiting for transfers between devices, sum_and_invert(): lax.ppermute(send, 'win', [(w, w ^ 2 * bit) for w in range(win_count)])  12 us
    pallas_call x4, Pallas kernels, lay_out_blocks(): pl.pallas_call(kernel, out_shape=jax.ShapeDtypeStruct((parts, rows, block...  9.43 us
  transfers between devices with their start and end apart: 16, of which 8 were waited for; matrix products, arithmetic and copies ran while one was open for 32% of the time, Pallas kernels for 3%

profile of v14, /device:TPU:0, one launch (start us, length us, event | category | flops | bytes accessed | tf_op | source)
XLA Modules:
  0.0 228.5 jit_solution(3551664789059020342)
XLA Ops:
  0.0 2.4 %shard_map.46 = bf16[8,256,256]{2,1,0:T(8,128)(2,1)} custom-call(bf16[4,256,2048]{2,1,0:T(8,128)(2,1)} %src.7), custom_call_target="tpu_custom_call" | custom-call | tf_op jit(solution)/shard_map/pallas_call | solution.py:157
  2.4 7.3 %all-to-all-start = ((bf16[8,256,256]{2,1,0:T(8,128)(2,1)}), bf16[8,256,256]{2,1,0:T(8,128)(2,1)S(1)}, u32[]{:S(2)}, u32[]{:S(2)}) async-start(bf16[8,256,256]{2,1,0:T(8,128)(2,1)} %shard_map.46), calls=%async_computation | async-start | bytes 2097152 | tf_op jit(solution)/shard_map/all_to_all | solution.py:192
  9.8 0.7 collective-permute-start
  10.5 2.3 %shard_map.47 = bf16[8,256,256]{2,1,0:T(8,128)(2,1)} custom-call(bf16[4,256,2048]{2,1,0:T(8,128)(2,1)} %src.7), custom_call_target="tpu_custom_call" | custom-call | tf_op jit(solution)/shard_map/pallas_call | solution.py:157
  12.8 2.3 %shard_map.48 = bf16[8,256,256]{2,1,0:T(8,128)(2,1)} custom-call(bf16[4,256,2048]{2,1,0:T(8,128)(2,1)} %src.7), custom_call_target="tpu_custom_call" | custom-call | tf_op jit(solution)/shard_map/pallas_call | solution.py:157
  15.1 2.4 %shard_map.49 = bf16[8,256,256]{2,1,0:T(8,128)(2,1)} custom-call(bf16[4,256,2048]{2,1,0:T(8,128)(2,1)} %src.7), custom_call_target="tpu_custom_call" | custom-call | tf_op jit(solution)/shard_map/pallas_call | solution.py:157
  17.5 1.0 fusion.59
  18.5 0.6 fusion.67
  19.1 5.1 %subtract_convert_fusion = (bf16[1024,32,64]{0,2,1:T(8,128)(2,1)}, bf16[1024,32,64]{0,2,1:T(8,128)(2,1)}) fusion(f32[1024,64]{0,1:T(8,128)S(1)} %get-tuple-element.44, f32[1024,32]{0,1:T(8,128)S(1)} %get-tuple-element.43, f32[1024,64]{0,1:T(8,128)S(1)} %get-tuple-element.45, f32[1024,32]{0,1:T(8,128)S(1)} %get-tuple-element.42), kind=kLoop, calls=%fused_computation.10 | loop fusion | flops 18874368 | bytes 9175040 | tf_op jit(solution)/shard_map/convert.3
  24.2 6.4 %copy.5 = bf16[1024,8,256]{2,0,1:T(8,128)(2,1)} copy(bf16[1024,8,256]{0,2,1:T(8,128)(2,1)} %bitcast.52) | data formatting | bytes 8388608 | tf_op jit(solution)/shard_map/sub | solution.py:25
  30.6 6.5 %copy.6 = bf16[1024,8,256]{2,0,1:T(8,128)(2,1)} copy(bf16[1024,8,256]{0,2,1:T(8,128)(2,1)} %bitcast.51) | data formatting | bytes 8388608 | tf_op jit(solution)/shard_map/neg | solution.py:32
  37.1 0.6 reduce-window.6
  38.1 7.8 %all-to-all-start.1 = ((bf16[8,256,256]{2,1,0:T(8,128)(2,1)}), bf16[8,256,256]{2,1,0:T(8,128)(2,1)S(1)}, u32[]{:S(2)}, u32[]{:S(2)}) async-start(bf16[8,256,256]{2,1,0:T(8,128)(2,1)} %shard_map.47), calls=%async_computation.1 | async-start | bytes 2097152 | tf_op jit(solution)/shard_map/all_to_all | solution.py:192
  45.9 5.9 %convolution_bitcast_fusion.3 = f32[2048,256]{1,0:T(8,128)S(1)} fusion(bf16[8,256,256]{2,1,0:T(8,128)(2,1)S(1)} %all-to-all-done, bf16[1024,8,256]{2,0,1:T(8,128)(2,1)} %copy.6, bf16[1024,8,256]{2,0,1:T(8,128)(2,1)} %copy.5), kind=kOutput, calls=%fused_computation.14 | convolution fusion | flops 2164260864 | bytes 11534336 | tf_op jit(solution)/shard_map/fjm,jmc->fc/dot_general | solution.py:195
  52.1 0.3 fusion.4
  52.5 2.1 collective-permute-start.1
  54.7 0.6 fusion.65
  55.3 2.0 fusion.48
  57.3 6.9 %multiply_subtract_fusion = (f32[2048,16,64]{0,2,1:T(8,128)}, f32[2048,16,64]{0,2,1:T(8,128)}) fusion(f32[2048,64]{0,1:T(8,128)S(1)} %get-tuple-element.38, f32[2048,16]{0,1:T(8,128)S(1)} %get-tuple-element.36, f32[2048,64]{0,1:T(8,128)S(1)} %get-tuple-element.37, f32[2048,16]{0,1:T(8,128)S(1)} %get-tuple-element.35), kind=kLoop, calls=%fused_computation.8 | loop fusion | flops 12582912 | bytes 18087936 | tf_op jit(solution)/shard_map/sub | solution.py:25
  64.3 8.8 %all-to-all-done.1 = bf16[8,256,256]{2,1,0:T(8,128)(2,1)S(1)} async-done(((bf16[8,256,256]{2,1,0:T(8,128)(2,1)}), bf16[8,256,256]{2,1,0:T(8,128)(2,1)S(1)}, u32[]{:S(2)}, u32[]{:S(2)}) %all-to-all-start.1) | async-done | bytes 1048608 | tf_op jit(solution)/shard_map/all_to_all | solution.py:192
  73.0 4.4 %all-to-all-start.2 = ((bf16[8,256,256]{2,1,0:T(8,128)(2,1)}), bf16[8,256,256]{2,1,0:T(8,128)(2,1)}, u32[]{:S(2)}, u32[]{:S(2)}) async-start(bf16[8,256,256]{2,1,0:T(8,128)(2,1)} %shard_map.48), calls=%async_computation.2 | async-start | bytes 2097152 | tf_op jit(solution)/shard_map/all_to_all | solution.py:192
  77.5 5.9 %convolution_bitcast_fusion.2 = f32[2048,256]{1,0:T(8,128)S(1)} fusion(bf16[8,256,256]{2,1,0:T(8,128)(2,1)S(1)} %all-to-all-done.1, bf16[1024,8,256]{2,0,1:T(8,128)(2,1)} %copy.6, bf16[1024,8,256]{2,0,1:T(8,128)(2,1)} %copy.5), kind=kOutput, calls=%fused_computation.13 | convolution fusion | flops 2164260864 | bytes 11534336 | tf_op jit(solution)/shard_map/fjm,jmc->fc/dot_general | solution.py:195
  83.7 0.3 fusion.7
  84.1 1.0 fusion.84
  85.1 1.7 collective-permute-start.3
  86.8 12.1 %collective-permute-start.4 = (bf16[2048,128]{1,0:T(8,128)(2,1)}, bf16[2048,128]{1,0:T(8,128)(2,1)}, u32[]{:S(2)}, u32[]{:S(2)}) collective-permute-start(bf16[2048,128]{1,0:T(8,128)(2,1)} %get-tuple-element.28), channel_id=1, source_target_pairs={{0,8},{4,0},{12,4},{20,12},{28,20},{24,28},{16,24},{8,16},{1,9},{5... | collective-permute-start | bytes 1572872 | tf_op jit(solution)/shard_map/ppermute | solution.py:198
  98.9 2.0 fusion.23
  100.9 2.0 fusion.22
  103.1 3.8 %all-to-all-done.2 = bf16[8,256,256]{2,1,0:T(8,128)(2,1)} async-done(((bf16[8,256,256]{2,1,0:T(8,128)(2,1)}), bf16[8,256,256]{2,1,0:T(8,128)(2,1)}, u32[]{:S(2)}, u32[]{:S(2)}) %all-to-all-start.2) | async-done | bytes 1048608 | tf_op jit(solution)/shard_map/all_to_all | solution.py:192
  106.9 4.2 %all-to-all-start.3 = ((bf16[8,256,256]{2,1,0:T(8,128)(2,1)}), bf16[8,256,256]{2,1,0:T(8,128)(2,1)}, u32[]{:S(2)}, u32[]{:S(2)}) async-start(bf16[8,256,256]{2,1,0:T(8,128)(2,1)} %shard_map.49), calls=%async_computation.3 | async-start | bytes 2097152 | tf_op jit(solution)/shard_map/all_to_all | solution.py:192
  111.2 6.1 %convolution_bitcast_fusion.1 = f32[2048,256]{1,0:T(8,128)S(1)} fusion(bf16[8,256,256]{2,1,0:T(8,128)(2,1)} %all-to-all-done.2, bf16[1024,8,256]{2,0,1:T(8,128)(2,1)} %copy.6, bf16[1024,8,256]{2,0,1:T(8,128)(2,1)} %copy.5), kind=kOutput, calls=%fused_computation.12 | convolution fusion | flops 2164260864 | bytes 11534336 | tf_op jit(solution)/shard_map/fjm,jmc->fc/dot_general | solution.py:195
  117.6 0.3 fusion.8
  117.9 1.2 fusion.83
  119.1 5.1 %collective-permute-start.5 = (bf16[2048,128]{1,0:T(8,128)(2,1)}, bf16[2048,128]{1,0:T(8,128)(2,1)}, u32[]{:S(2)}, u32[]{:S(2)}) collective-permute-start(bf16[2048,128]{1,0:T(8,128)(2,1)} %get-tuple-element.25), channel_id=1, source_target_pairs={{0,4},{4,12},{12,20},{20,28},{28,24},{24,16},{16,8},{8,0},{1,5},{5... | collective-permute-start | bytes 1572872 | tf_op jit(solution)/shard_map/ppermute | solution.py:197
  124.2 8.7 %collective-permute-start.6 = (bf16[2048,128]{1,0:T(8,128)(2,1)}, bf16[2048,128]{1,0:T(8,128)(2,1)}, u32[]{:S(2)}, u32[]{:S(2)}) collective-permute-start(bf16[2048,128]{1,0:T(8,128)(2,1)} %get-tuple-element.26), channel_id=1, source_target_pairs={{0,8},{4,0},{12,4},{20,12},{28,20},{24,28},{16,24},{8,16},{1,9},{5... | collective-permute-start | bytes 1572872 | tf_op jit(solution)/shard_map/ppermute | solution.py:198
  132.9 2.0 fusion.21
  134.9 2.0 fusion.20
  136.9 1.3 multiply_add_fusion.3
  138.1 2.5 %all-to-all-done.3 = bf16[8,256,256]{2,1,0:T(8,128)(2,1)} async-done(((bf16[8,256,256]{2,1,0:T(8,128)(2,1)}), bf16[8,256,256]{2,1,0:T(8,128)(2,1)}, u32[]{:S(2)}, u32[]{:S(2)}) %all-to-all-start.3) | async-done | bytes 1048608 | tf_op jit(solution)/shard_map/all_to_all | solution.py:192
  140.7 3.5 %collective-permute-done.5 = bf16[2048,128]{1,0:T(8,128)(2,1)} collective-permute-done((bf16[2048,128]{1,0:T(8,128)(2,1)}, bf16[2048,128]{1,0:T(8,128)(2,1)}, u32[]{:S(2)}, u32[]{:S(2)}) %collective-permute-start.5) | collective-permute-done | bytes 524320 | tf_op jit(solution)/shard_map/ppermute | solution.py:197
  144.1 6.1 %convolution_bitcast_fusion = f32[2048,256]{1,0:T(8,128)S(1)} fusion(bf16[8,256,256]{2,1,0:T(8,128)(2,1)} %all-to-all-done.3, bf16[1024,8,256]{2,0,1:T(8,128)(2,1)} %copy.6, bf16[1024,8,256]{2,0,1:T(8,128)(2,1)} %copy.5), kind=kOutput, calls=%fused_computation.11 | convolution fusion | flops 2164260864 | bytes 11534336 | tf_op jit(solution)/shard_map/fjm,jmc->fc/dot_general | solution.py:195
  150.6 0.3 fusion.9
  151.0 5.1 %collective-permute-start.7 = (bf16[2048,128]{1,0:T(8,128)(2,1)S(1)}, bf16[2048,128]{1,0:T(8,128)(2,1)S(1)}, u32[]{:S(2)}, u32[]{:S(2)}) collective-permute-start(bf16[2048,128]{1,0:T(8,128)(2,1)S(1)} %get-tuple-element.23), channel_id=1, source_target_pairs={{0,4},{4,12},{12,20},{20,28},{28,24},{24,16},{16,8},{8,0},{1,5},{5... | collective-permute-start | bytes 1572872 | tf_op jit(solution)/shard_map/ppermute | solution.py:197
  156.0 1.6 collective-permute-start.8
  157.6 2.0 fusion.19
  159.6 2.0 fusion.18
  161.6 0.3 multiply_add_fusion.2
  161.9 5.7 %collective-permute-done.7 = bf16[2048,128]{1,0:T(8,128)(2,1)S(1)} collective-permute-done((bf16[2048,128]{1,0:T(8,128)(2,1)S(1)}, bf16[2048,128]{1,0:T(8,128)(2,1)S(1)}, u32[]{:S(2)}, u32[]{:S(2)}) %collective-permute-start.7) | collective-permute-done | bytes 524320 | tf_op jit(solution)/shard_map/ppermute | solution.py:197
  167.6 1.8 collective-permute-done.8
  169.4 0.8 fusion.17
  170.2 0.8 fusion.16
  171.0 0.3 multiply_add_fusion.1
  171.2 1.3 copy-done
  172.6 0.5 fusion.6
  173.3 0.8 slice-done.3
  174.1 4.2 %bitcast_multiply_fusion = f32[2048,1024]{0,1:T(8,128)} fusion(f32[2048,16,64]{0,2,1:T(8,128)S(1)} %bitcast.50, f32[1024]{0:T(1024)S(1)} %fusion.70), kind=kLoop, calls=%fused_computation.5 | loop fusion | flops 2097152 | bytes 16781312 | tf_op jit(solution)/shard_map/mul | solution.py:43
  178.2 3.9 %bitcast_multiply_fusion.1 = f32[2048,1024]{0,1:T(8,128)} fusion(f32[2048,16,64]{0,2,1:T(8,128)S(1)} %bitcast.48, f32[1024]{0:T(1024)S(1)} %select_multiply_fusion), kind=kLoop, calls=%fused_computation.6 | loop fusion | flops 2097152 | bytes 16781312 | tf_op jit(solution)/shard_map/mul | solution.py:43
  182.1 8.2 %fusion = f32[2048,128]{0,1:T(8,128)S(1)} fusion(f32[2048,1024]{0,1:T(8,128)} %bitcast_multiply_fusion, f32[2048,1024]{0,1:T(8,128)} %bitcast_multiply_fusion.1, f32[2048,128]{1,0:T(8,128)S(1)} %collective-permute-done.9, f32[2048,256]{1,0:T(8,128)S(1)} %fusion.6, s32[]{:T(128)S(6)} %select_n.119), kind=kOutput, calls=%fused_computation | convolution fusion | flops 3225681920 | bytes 19922948 | tf_op jit(solution)/shard_map/dot_general | solution.py:128
  190.4 1.6 collective-permute-start.10
  192.0 12.0 %collective-permute-done.10 = f32[1024,128]{0,1:T(8,128)S(1)} collective-permute-done((f32[1024,128]{0,1:T(8,128)S(1)}, f32[1024,128]{0,1:T(8,128)S(1)}, u32[]{:S(2)}, u32[]{:S(2)}) %collective-permute-start.10) | collective-permute-done | bytes 524320 | tf_op jit(solution)/shard_map/ppermute | solution.py:135
  204.1 1.3 collective-permute-done.11
  205.5 0.4 convolution_convert_fusion
  205.8 21.8 %all_to_all.25 = bf16[8,80,512]{2,1,0:T(8,128)(2,1)S(1)} all-to-all(bf16[8,80,512]{2,1,0:T(8,128)(2,1)S(1)} %bitcast.57), channel_id=1, replica_groups=mesh['tile'=8,'win'=4] {'tile'}, dimensions={0} | all-to-all | bytes 1310720 | tf_op jit(solution)/shard_map/all_to_all | solution.py:218
  227.7 0.8 copy-done.3
  (71 shorter events, 2.4 us)
Async XLA Ops:
  0.0 9.7 %copy-start.6 = (s32[256]{0:T(256)S(1)}, s32[256]{0:T(256)}, u32[]{:S(2)}) copy-start(s32[256]{0:T(256)} %param.5) | copy-start | bytes 3076
  0.0 9.8 %copy-start.5 = (s32[256]{0:T(256)S(1)}, s32[256]{0:T(256)}, u32[]{:S(2)}) copy-start(s32[256]{0:T(256)} %param.6) | copy-start | bytes 3076
  0.0 9.8 %copy-start.4 = (s32[256,1]{0,1:T(1,128)S(1)}, s32[256,1]{0,1:T(1,128)}, u32[]{:S(2)}) copy-start(s32[256,1]{0,1:T(1,128)} %param.7) | copy-start | bytes 3076
  2.4 35.7 %all-to-all-start = ((bf16[8,256,256]{2,1,0:T(8,128)(2,1)}), bf16[8,256,256]{2,1,0:T(8,128)(2,1)S(1)}, u32[]{:S(2)}, u32[]{:S(2)}) async-start(bf16[8,256,256]{2,1,0:T(8,128)(2,1)} %shard_map.46), calls=%async_computation | async-start | bytes 2097152 | tf_op jit(solution)/shard_map/all_to_all | solution.py:192
  9.8 27.3 %collective-permute-start = (s32[3,256]{1,0:T(4,128)S(1)}, s32[3,256]{1,0:T(4,128)S(1)}, u32[]{:S(2)}, u32[]{:S(2)}) collective-permute-start(s32[3,256]{1,0:T(4,128)S(1)} %pad_add_fusion), channel_id=1, source_target_pairs={{0,0},{4,4},{8,12},{12,20},{16,28},{20,24},{24,16},{28,8},{1,1},{5... | collective-permute-start | bytes 9224 | tf_op jit(solution)/shard_map/ppermute | solution.py:184
  38.1 34.9 %all-to-all-start.1 = ((bf16[8,256,256]{2,1,0:T(8,128)(2,1)}), bf16[8,256,256]{2,1,0:T(8,128)(2,1)S(1)}, u32[]{:S(2)}, u32[]{:S(2)}) async-start(bf16[8,256,256]{2,1,0:T(8,128)(2,1)} %shard_map.47), calls=%async_computation.1 | async-start | bytes 2097152 | tf_op jit(solution)/shard_map/all_to_all | solution.py:192
  52.5 24.9 %collective-permute-start.1 = (bf16[2048,128]{1,0:T(8,128)(2,1)S(1)}, bf16[2048,128]{1,0:T(8,128)(2,1)}, u32[]{:S(2)}, u32[]{:S(2)}) collective-permute-start(bf16[2048,128]{1,0:T(8,128)(2,1)S(1)} %get-tuple-element.29), channel_id=1, source_target_pairs={{0,4},{4,12},{12,20},{20,28},{28,24},{24,16},{16,8},{8,0},{1,5},{5... | collective-permute-start | bytes 1572872 | tf_op jit(solution)/shard_map/ppermute | solution.py:197
  54.6 22.9 %collective-permute-start.2 = (bf16[2048,128]{1,0:T(8,128)(2,1)S(1)}, bf16[2048,128]{1,0:T(8,128)(2,1)}, u32[]{:S(2)}, u32[]{:S(2)}) collective-permute-start(bf16[2048,128]{1,0:T(8,128)(2,1)S(1)} %get-tuple-element.30), channel_id=1, source_target_pairs={{0,8},{4,0},{12,4},{20,12},{28,20},{24,28},{16,24},{8,16},{1,9},{5... | collective-permute-start | bytes 1572872 | tf_op jit(solution)/shard_map/ppermute | solution.py:198
  73.0 33.9 %all-to-all-start.2 = ((bf16[8,256,256]{2,1,0:T(8,128)(2,1)}), bf16[8,256,256]{2,1,0:T(8,128)(2,1)}, u32[]{:S(2)}, u32[]{:S(2)}) async-start(bf16[8,256,256]{2,1,0:T(8,128)(2,1)} %shard_map.48), calls=%async_computation.2 | async-start | bytes 2097152 | tf_op jit(solution)/shard_map/all_to_all | solution.py:192
  85.1 26.1 %collective-permute-start.3 = (bf16[2048,128]{1,0:T(8,128)(2,1)}, bf16[2048,128]{1,0:T(8,128)(2,1)}, u32[]{:S(2)}, u32[]{:S(2)}) collective-permute-start(bf16[2048,128]{1,0:T(8,128)(2,1)} %get-tuple-element.27), channel_id=1, source_target_pairs={{0,4},{4,12},{12,20},{20,28},{28,24},{24,16},{16,8},{8,0},{1,5},{5... | collective-permute-start | bytes 1572872 | tf_op jit(solution)/shard_map/ppermute | solution.py:197
  86.8 24.4 %collective-permute-start.4 = (bf16[2048,128]{1,0:T(8,128)(2,1)}, bf16[2048,128]{1,0:T(8,128)(2,1)}, u32[]{:S(2)}, u32[]{:S(2)}) collective-permute-start(bf16[2048,128]{1,0:T(8,128)(2,1)} %get-tuple-element.28), channel_id=1, source_target_pairs={{0,8},{4,0},{12,4},{20,12},{28,20},{24,28},{16,24},{8,16},{1,9},{5... | collective-permute-start | bytes 1572872 | tf_op jit(solution)/shard_map/ppermute | solution.py:198
  106.9 33.7 %all-to-all-start.3 = ((bf16[8,256,256]{2,1,0:T(8,128)(2,1)}), bf16[8,256,256]{2,1,0:T(8,128)(2,1)}, u32[]{:S(2)}, u32[]{:S(2)}) async-start(bf16[8,256,256]{2,1,0:T(8,128)(2,1)} %shard_map.49), calls=%async_computation.3 | async-start | bytes 2097152 | tf_op jit(solution)/shard_map/all_to_all | solution.py:192
  117.9 16.9 %copy-start.1 = (bf16[2048,256]{1,0:T(8,128)(2,1)}, bf16[2048,256]{1,0:T(8,128)(2,1)S(1)}, u32[]{:S(2)}) copy-start(bf16[2048,256]{1,0:T(8,128)(2,1)S(1)} %fusion.8) | copy-start | bytes 3145732
  119.1 25.0 %collective-permute-start.5 = (bf16[2048,128]{1,0:T(8,128)(2,1)}, bf16[2048,128]{1,0:T(8,128)(2,1)}, u32[]{:S(2)}, u32[]{:S(2)}) collective-permute-start(bf16[2048,128]{1,0:T(8,128)(2,1)} %get-tuple-element.25), channel_id=1, source_target_pairs={{0,4},{4,12},{12,20},{20,28},{28,24},{24,16},{16,8},{8,0},{1,5},{5... | collective-permute-start | bytes 1572872 | tf_op jit(solution)/shard_map/ppermute | solution.py:197
  124.2 19.9 %collective-permute-start.6 = (bf16[2048,128]{1,0:T(8,128)(2,1)}, bf16[2048,128]{1,0:T(8,128)(2,1)}, u32[]{:S(2)}, u32[]{:S(2)}) collective-permute-start(bf16[2048,128]{1,0:T(8,128)(2,1)} %get-tuple-element.26), channel_id=1, source_target_pairs={{0,8},{4,0},{12,4},{20,12},{28,20},{24,28},{16,24},{8,16},{1,9},{5... | collective-permute-start | bytes 1572872 | tf_op jit(solution)/shard_map/ppermute | solution.py:198
  150.5 7.2 %copy-start.2 = (bf16[2048,256]{1,0:T(8,128)(2,1)S(1)}, bf16[2048,256]{1,0:T(8,128)(2,1)}, u32[]{:S(2)}) copy-start(bf16[2048,256]{1,0:T(8,128)(2,1)} %copy-done.1) | copy-start | bytes 3145732
  151.0 16.6 %collective-permute-start.7 = (bf16[2048,128]{1,0:T(8,128)(2,1)S(1)}, bf16[2048,128]{1,0:T(8,128)(2,1)S(1)}, u32[]{:S(2)}, u32[]{:S(2)}) collective-permute-start(bf16[2048,128]{1,0:T(8,128)(2,1)S(1)} %get-tuple-element.23), channel_id=1, source_target_pairs={{0,4},{4,12},{12,20},{20,28},{28,24},{24,16},{16,8},{8,0},{1,5},{5... | collective-permute-start | bytes 1572872 | tf_op jit(solution)/shard_map/ppermute | solution.py:197
  156.0 13.4 %collective-permute-start.8 = (bf16[2048,128]{1,0:T(8,128)(2,1)S(1)}, bf16[2048,128]{1,0:T(8,128)(2,1)S(1)}, u32[]{:S(2)}, u32[]{:S(2)}) collective-permute-start(bf16[2048,128]{1,0:T(8,128)(2,1)S(1)} %get-tuple-element.24), channel_id=1, source_target_pairs={{0,8},{4,0},{12,4},{20,12},{28,20},{24,28},{16,24},{8,16},{1,9},{5... | collective-permute-start | bytes 1572872 | tf_op jit(solution)/shard_map/ppermute | solution.py:198
  170.2 3.1 %slice-start.2 = ((s8[8388608]{0:T(1024)(128)(4,1)}), s8[4194304]{0:T(1024)(128)(4,1)S(1)}, s32[]{:S(2)}) async-start(s8[8388608]{0:T(1024)(128)(4,1)} %bitcast.49), calls=%async_computation.7 | async-start | bytes 8388608
  170.9 1.6 copy-start
  170.9 3.1 %slice-start.3 = ((s8[8388608]{0:T(1024)(128)(4,1)}), s8[4194304]{0:T(1024)(128)(4,1)S(1)}, s32[]{:S(2)}) async-start(s8[8388608]{0:T(1024)(128)(4,1)} %bitcast.49), calls=%async_computation.8 | async-start | bytes 8388608
  172.5 5.7 %slice-start = ((s8[8388608]{0:T(1024)(128)(4,1)}), s8[4194304]{0:T(1024)(128)(4,1)S(1)}, s32[]{:S(2)}) async-start(s8[8388608]{0:T(1024)(128)(4,1)} %bitcast.47), calls=%async_computation.5 | async-start | bytes 8388608
  173.2 8.9 %collective-permute-start.9 = (f32[2048,128]{1,0:T(8,128)S(1)}, f32[2048,128]{1,0:T(8,128)S(1)}, u32[]{:S(2)}, u32[]{:S(2)}) collective-permute-start(f32[2048,128]{1,0:T(8,128)S(1)} %constant_dynamic-slice_fusion.3), channel_id=1, source_target_pairs={{0,1},{1,0},{2,3},{3,2},{4,5},{5,4},{6,7},{7,6},{8,9},{9,8},{10,11... | collective-permute-start | bytes 3145736 | tf_op jit(solution)/shard_map/ppermute | solution.py:126
  174.1 4.2 %slice-start.1 = ((s8[8388608]{0:T(1024)(128)(4,1)}), s8[4194304]{0:T(1024)(128)(4,1)S(1)}, s32[]{:S(2)}) async-start(s8[8388608]{0:T(1024)(128)(4,1)} %bitcast.47), calls=%async_computation.6 | async-start | bytes 8388608
  190.4 13.5 %collective-permute-start.10 = (f32[1024,128]{0,1:T(8,128)S(1)}, f32[1024,128]{0,1:T(8,128)S(1)}, u32[]{:S(2)}, u32[]{:S(2)}) collective-permute-start(f32[1024,128]{0,1:T(8,128)S(1)} %constant_dynamic-slice_fusion.2), channel_id=1, source_target_pairs={{0,2},{1,3},{2,0},{3,1},{4,6},{5,7},{6,4},{7,5},{8,10},{9,11},{10,... | collective-permute-start | bytes 1572872 | tf_op jit(solution)/shard_map/ppermute | solution.py:135
  204.0 1.4 collective-permute-start.11
  227.7 0.8 copy-start.3

commit v15 on v14

--- a/solution.py
+++ b/solution.py
@@ -111,7 +111,12 @@
     return path if extend() else list(range(count))
 
 
-def sum_and_invert(cross, length, lag_count, seg_total, win_count, lag_start):
+def inverse_table(length, lag_start):
+    cosine, sine = phase_table(jnp.arange(length, dtype=jnp.int32) + lag_start, length // 2, length)
+    return jnp.concatenate([cosine, -sine], axis=1)
+
+
+def sum_and_invert(cross, length, lag_count, seg_total, win_count, table):
     win = lax.axis_index("win")
     if win_count % 2 or win_count & (win_count - 1):
         stacked = lax.psum(cross, "win")
@@ -124,8 +129,12 @@
     other = lax.dynamic_slice_in_dim(cross, (1 - core) * half, half, axis=1)
     partner = [(w, w ^ 1) for w in range(win_count)]
     total = mine + lax.ppermute(other, "win", partner)
-    inverse = inverse_matrix(length, lag_start, length, seg_total)
-    lags = jnp.dot(inverse, total, precision=lax.Precision.HIGH)
+    half_bins = length // 2
+    weights = jnp.where(jnp.arange(half_bins) == 0, 1.0, 2.0).astype(jnp.float32) * (
+        1.0 / math.sqrt(half_bins * seg_total)
+    )
+    scaled = total * jnp.concatenate([weights, weights])[:, None]
+    lags = jnp.dot(table, scaled, precision=lax.Precision.HIGH)
     bit = win_count // 4
     while bit >= 1:
         rows = lags.shape[0] // 2
@@ -192,6 +201,8 @@
             received = lax.all_to_all(outgoing, "tile", split_axis=0, concat_axis=0, tiled=True)
             if arrived:
                 received, _ = lax.optimization_barrier((received, arrived[-1]))
+            if segment == min(2, records.shape[0] - 1):
+                received, table = lax.optimization_barrier((received, inverse_table(length, lag_start)))
             spectra = jnp.einsum("fjm,jmc->fc", forward, received, preferred_element_type=jnp.float32)
             whitened = whiten(spectra, BAND)
             from_prev = lax.ppermute(whitened[:, half:], "tile", to_next)
@@ -205,7 +216,7 @@
             term = cross_terms(first_part, second_part)
             cross = term if cross is None else cross + term
         lag_count = length // win_count
-        correlation = sum_and_invert(cross, length, lag_count, seg_total, win_count, lag_start)
+        correlation = sum_and_invert(cross, length, lag_count, seg_total, win_count, table)
         capacity = 5 * pair_first.shape[0] // (2 * tile_count)
         chooser = bucket_select(my_owners, tile_count, capacity)
         picked = lax.dot_general(

time: 229 us -> 225 us (0.983)
  other arithmetic: 29.8 us -> 24.8 us
    mul x3 -> x1, other arithmetic: 8.04 us -> 0.01 us  [sum_and_invert(): jnp.where(jnp.arange(half_bins) == 0, 1.0, 2.0).astype(jnp.float32)]
    concatenate x0 -> x2, other arithmetic: none -> 6.3 us  [the longest x1 6.3 us: inverse_table(): return jnp.concatenate([cosine, -sine], axis=1)]
    sub x1, other arithmetic: 6.93 us -> 2.38 us  [phase_table(): cosine = (c_hi * c_lo - s_hi * s_lo).reshape(shape)]
    all_to_all x4, waiting for transfers between devices: 15.1 us -> 11.9 us  [per_device(): lax.all_to_all(outgoing, 'tile', split_axis=0, concat_axis=0, tiled=True)]
    ppermute x1, waiting for transfers between devices: 0.01 us -> 2.71 us  [sum_and_invert(): total = mine + lax.ppermute(other, 'win', partner)]
  transfers between devices with their start and end apart: 16 -> 16, of which waited for: 8 -> 9; matrix products, arithmetic and copies ran while one was open for 32% -> 31% of each run, Pallas kernels for 3% -> 3%
where the time goes in v15:
time: 225 us; the launch traced here: 224 us
  starting transfers between devices  62.6 us (28%)
  matrix products  46.6 us (21%)
  waiting for transfers between devices  39.6 us (18%)
  other arithmetic  24.8 us (11%)
  blocking collectives  21.8 us (10%)
  local copies, waits for them, and re-layouts  18.4 us (8%)
  Pallas kernels  9.39 us (4%)
    dot_general x4, matrix products, per_device(): jnp.einsum('fjm,jmc->fc', forward, received, preferred_element_type=jnp.f...  24.2 us
    all_to_all x4, starting transfers between devices, per_device(): lax.all_to_all(outgoing, 'tile', split_axis=0, concat_axis=0, tiled=True)  23.6 us
    ppermute x4, starting transfers between devices, per_device(): from_next = lax.ppermute(whitened[:, :half], 'tile', to_prev)  22.7 us
    all_to_all x1, blocking collectives, per_device(): lax.all_to_all(buckets, 'tile', split_axis=0, concat_axis=0, tiled=True)  21.8 us
    ppermute x4, starting transfers between devices, per_device(): from_prev = lax.ppermute(whitened[:, half:], 'tile', to_next)  14 us
    ppermute x1, waiting for transfers between devices, sum_and_invert(): lax.ppermute(send, 'win', [(w, w ^ 2 * bit) for w in range(win_count)])  12.6 us
    all_to_all x4, waiting for transfers between devices, per_device(): lax.all_to_all(outgoing, 'tile', split_axis=0, concat_axis=0, tiled=True)  11.9 us
    pallas_call x4, Pallas kernels, lay_out_blocks(): pl.pallas_call(kernel, out_shape=jax.ShapeDtypeStruct((parts, rows, block...  9.39 us
  transfers between devices with their start and end apart: 16, of which 9 were waited for; matrix products, arithmetic and copies ran while one was open for 31% of the time, Pallas kernels for 3%

profile of v15, /device:TPU:0, one launch (start us, length us, event | category | flops | bytes accessed | tf_op | source)
XLA Modules:
  0.0 223.9 jit_solution(8510117950756054198)
XLA Ops:
  0.0 2.4 %shard_map.48 = bf16[8,256,256]{2,1,0:T(8,128)(2,1)} custom-call(bf16[4,256,2048]{2,1,0:T(8,128)(2,1)} %src.7), custom_call_target="tpu_custom_call" | custom-call | tf_op jit(solution)/shard_map/pallas_call | solution.py:166
  2.4 7.3 %all-to-all-start.2 = ((bf16[8,256,256]{2,1,0:T(8,128)(2,1)}), bf16[8,256,256]{2,1,0:T(8,128)(2,1)S(1)}, u32[]{:S(2)}, u32[]{:S(2)}) async-start(bf16[8,256,256]{2,1,0:T(8,128)(2,1)} %shard_map.48), calls=%async_computation.2 | async-start | bytes 2097152 | tf_op jit(solution)/shard_map/all_to_all | solution.py:201
  9.8 0.7 collective-permute-start
  10.5 1.0 fusion.58
  11.5 0.6 fusion.66
  12.1 5.0 %subtract_convert_fusion = (bf16[1024,32,64]{0,2,1:T(8,128)(2,1)}, bf16[1024,32,64]{0,2,1:T(8,128)(2,1)}) fusion(f32[1024,64]{0,1:T(8,128)S(1)} %get-tuple-element.48, f32[1024,32]{0,1:T(8,128)S(1)} %get-tuple-element.47, f32[1024,64]{0,1:T(8,128)S(1)} %get-tuple-element.49, f32[1024,32]{0,1:T(8,128)S(1)} %get-tuple-element.46), kind=kLoop, calls=%fused_computation.5 | loop fusion | flops 18874368 | bytes 9175040 | tf_op jit(solution)/shard_map/convert.3
  17.1 2.3 %shard_map.47 = bf16[8,256,256]{2,1,0:T(8,128)(2,1)} custom-call(bf16[4,256,2048]{2,1,0:T(8,128)(2,1)} %src.7), custom_call_target="tpu_custom_call" | custom-call | tf_op jit(solution)/shard_map/pallas_call | solution.py:166
  19.4 2.3 %shard_map.46 = bf16[8,256,256]{2,1,0:T(8,128)(2,1)} custom-call(bf16[4,256,2048]{2,1,0:T(8,128)(2,1)} %src.7), custom_call_target="tpu_custom_call" | custom-call | tf_op jit(solution)/shard_map/pallas_call | solution.py:166
  21.7 2.4 %shard_map.49 = bf16[8,256,256]{2,1,0:T(8,128)(2,1)} custom-call(bf16[4,256,2048]{2,1,0:T(8,128)(2,1)} %src.7), custom_call_target="tpu_custom_call" | custom-call | tf_op jit(solution)/shard_map/pallas_call | solution.py:166
  24.1 6.5 %copy.5 = bf16[1024,8,256]{2,0,1:T(8,128)(2,1)} copy(bf16[1024,8,256]{0,2,1:T(8,128)(2,1)} %bitcast.49) | data formatting | bytes 8388608 | tf_op jit(solution)/shard_map/sub | solution.py:25
  30.5 6.6 %copy.6 = bf16[1024,8,256]{2,0,1:T(8,128)(2,1)} copy(bf16[1024,8,256]{0,2,1:T(8,128)(2,1)} %bitcast.48) | data formatting | bytes 8388608 | tf_op jit(solution)/shard_map/neg | solution.py:32
  37.1 0.6 reduce-window.6
  38.1 7.8 %all-to-all-start.1 = ((bf16[8,256,256]{2,1,0:T(8,128)(2,1)}), bf16[8,256,256]{2,1,0:T(8,128)(2,1)S(1)}, u32[]{:S(2)}, u32[]{:S(2)}) async-start(bf16[8,256,256]{2,1,0:T(8,128)(2,1)} %shard_map.47), calls=%async_computation.1 | async-start | bytes 2097152 | tf_op jit(solution)/shard_map/all_to_all | solution.py:201
  45.9 5.9 %convolution_bitcast_fusion.3 = f32[2048,256]{1,0:T(8,128)S(1)} fusion(bf16[8,256,256]{2,1,0:T(8,128)(2,1)S(1)} %all-to-all-done.2, bf16[1024,8,256]{2,0,1:T(8,128)(2,1)} %copy.6, bf16[1024,8,256]{2,0,1:T(8,128)(2,1)} %copy.5), kind=kOutput, calls=%fused_computation.9 | convolution fusion | flops 2164260864 | bytes 11534336 | tf_op jit(solution)/shard_map/fjm,jmc->fc/dot_general | solution.py:206
  52.2 0.3 fusion
  52.5 2.0 fusion.47
  54.6 0.6 fusion.64
  55.2 2.1 collective-permute-start.1
  57.5 2.4 %multiply_subtract_fusion = (f32[2048,16,64]{0,2,1:T(8,128)S(1)}, f32[2048,16,64]{0,2,1:T(8,128)S(1)}) fusion(f32[2048,64]{0,1:T(8,128)S(1)} %get-tuple-element.42, f32[2048,16]{0,1:T(8,128)S(1)} %get-tuple-element.40, f32[2048,64]{0,1:T(8,128)S(1)} %get-tuple-element.41, f32[2048,16]{0,1:T(8,128)S(1)} %get-tuple-element.39), kind=kLoop, calls=%fused_computation.3 | loop fusion | flops 14680064 | bytes 18087936 | tf_op jit(solution)/shard_map/sub | solution.py:25
  59.9 6.3 %pad_maximum_fusion = f32[2048,2048]{0,1:T(8,128)} fusion(f32[2048,1024]{0,1:T(8,128)S(1)} %bitcast.47, f32[2048,1024]{0,1:T(8,128)S(1)} %bitcast.46), kind=kLoop, calls=%fused_computation | loop fusion | flops 4194304 | bytes 33554432 | tf_op jit(solution)/shard_map/concatenate | solution.py:116
  66.2 6.9 %all-to-all-done.1 = bf16[8,256,256]{2,1,0:T(8,128)(2,1)S(1)} async-done(((bf16[8,256,256]{2,1,0:T(8,128)(2,1)}), bf16[8,256,256]{2,1,0:T(8,128)(2,1)S(1)}, u32[]{:S(2)}, u32[]{:S(2)}) %all-to-all-start.1) | async-done | bytes 1048608 | tf_op jit(solution)/shard_map/all_to_all | solution.py:201
  73.1 4.2 %all-to-all-start = ((bf16[8,256,256]{2,1,0:T(8,128)(2,1)}), bf16[8,256,256]{2,1,0:T(8,128)(2,1)}, u32[]{:S(2)}, u32[]{:S(2)}) async-start(bf16[8,256,256]{2,1,0:T(8,128)(2,1)} %shard_map.46), calls=%async_computation | async-start | bytes 2097152 | tf_op jit(solution)/shard_map/all_to_all | solution.py:201
  77.3 5.9 %convolution_bitcast_fusion.2 = f32[2048,256]{1,0:T(8,128)S(1)} fusion(bf16[8,256,256]{2,1,0:T(8,128)(2,1)S(1)} %all-to-all-done.1, bf16[1024,8,256]{2,0,1:T(8,128)(2,1)} %copy.6, bf16[1024,8,256]{2,0,1:T(8,128)(2,1)} %copy.5), kind=kOutput, calls=%fused_computation.8 | convolution fusion | flops 2164260864 | bytes 11534336 | tf_op jit(solution)/shard_map/fjm,jmc->fc/dot_general | solution.py:206
  83.6 0.3 fusion.1
  83.9 1.0 fusion.81
  84.9 1.9 collective-permute-start.3
  86.8 12.1 %collective-permute-start.4 = (bf16[2048,128]{1,0:T(8,128)(2,1)}, bf16[2048,128]{1,0:T(8,128)(2,1)}, u32[]{:S(2)}, u32[]{:S(2)}) collective-permute-start(bf16[2048,128]{1,0:T(8,128)(2,1)} %get-tuple-element.31), channel_id=1, source_target_pairs={{0,8},{4,0},{12,4},{20,12},{28,20},{24,28},{16,24},{8,16},{1,9},{5... | collective-permute-start | bytes 1572872 | tf_op jit(solution)/shard_map/ppermute | solution.py:209
  98.9 2.0 fusion.21
  100.9 2.0 fusion.20
  102.9 1.3 multiply_add_fusion.3
  104.1 2.8 %all-to-all-done = bf16[8,256,256]{2,1,0:T(8,128)(2,1)} async-done(((bf16[8,256,256]{2,1,0:T(8,128)(2,1)}), bf16[8,256,256]{2,1,0:T(8,128)(2,1)}, u32[]{:S(2)}, u32[]{:S(2)}) %all-to-all-start) | async-done | bytes 1048608 | tf_op jit(solution)/shard_map/all_to_all | solution.py:201
  106.9 4.2 %all-to-all-start.3 = ((bf16[8,256,256]{2,1,0:T(8,128)(2,1)}), bf16[8,256,256]{2,1,0:T(8,128)(2,1)}, u32[]{:S(2)}, u32[]{:S(2)}) async-start(bf16[8,256,256]{2,1,0:T(8,128)(2,1)} %shard_map.49), calls=%async_computation.3 | async-start | bytes 2097152 | tf_op jit(solution)/shard_map/all_to_all | solution.py:201
  111.2 6.1 %convolution_bitcast_fusion.1 = f32[2048,256]{1,0:T(8,128)S(1)} fusion(bf16[8,256,256]{2,1,0:T(8,128)(2,1)} %all-to-all-done, bf16[1024,8,256]{2,0,1:T(8,128)(2,1)} %copy.6, bf16[1024,8,256]{2,0,1:T(8,128)(2,1)} %copy.5), kind=kOutput, calls=%fused_computation.7 | convolution fusion | flops 2164260864 | bytes 11534336 | tf_op jit(solution)/shard_map/fjm,jmc->fc/dot_general | solution.py:206
  117.6 0.3 fusion.4
  117.9 1.0 fusion.80
  119.0 5.1 %collective-permute-start.5 = (bf16[2048,128]{1,0:T(8,128)(2,1)}, bf16[2048,128]{1,0:T(8,128)(2,1)}, u32[]{:S(2)}, u32[]{:S(2)}) collective-permute-start(bf16[2048,128]{1,0:T(8,128)(2,1)} %get-tuple-element.29), channel_id=1, source_target_pairs={{0,4},{4,12},{12,20},{20,28},{28,24},{24,16},{16,8},{8,0},{1,5},{5... | collective-permute-start | bytes 1572872 | tf_op jit(solution)/shard_map/ppermute | solution.py:208
  124.1 8.7 %collective-permute-start.6 = (bf16[2048,128]{1,0:T(8,128)(2,1)}, bf16[2048,128]{1,0:T(8,128)(2,1)}, u32[]{:S(2)}, u32[]{:S(2)}) collective-permute-start(bf16[2048,128]{1,0:T(8,128)(2,1)} %get-tuple-element.30), channel_id=1, source_target_pairs={{0,8},{4,0},{12,4},{20,12},{28,20},{24,28},{16,24},{8,16},{1,9},{5... | collective-permute-start | bytes 1572872 | tf_op jit(solution)/shard_map/ppermute | solution.py:209
  132.8 2.0 fusion.19
  134.7 2.0 fusion.18
  136.7 1.7 multiply_add_fusion.2
  138.4 2.2 all-to-all-done.3
  140.7 3.4 %collective-permute-done.5 = bf16[2048,128]{1,0:T(8,128)(2,1)} collective-permute-done((bf16[2048,128]{1,0:T(8,128)(2,1)}, bf16[2048,128]{1,0:T(8,128)(2,1)}, u32[]{:S(2)}, u32[]{:S(2)}) %collective-permute-start.5) | collective-permute-done | bytes 524320 | tf_op jit(solution)/shard_map/ppermute | solution.py:208
  144.1 6.1 %convolution_bitcast_fusion = f32[2048,256]{1,0:T(8,128)S(1)} fusion(bf16[8,256,256]{2,1,0:T(8,128)(2,1)} %all-to-all-done.3, bf16[1024,8,256]{2,0,1:T(8,128)(2,1)} %copy.6, bf16[1024,8,256]{2,0,1:T(8,128)(2,1)} %copy.5), kind=kOutput, calls=%fused_computation.6 | convolution fusion | flops 2164260864 | bytes 11534336 | tf_op jit(solution)/shard_map/fjm,jmc->fc/dot_general | solution.py:206
  150.5 0.3 fusion.5
  150.9 4.9 %collective-permute-start.7 = (bf16[2048,128]{1,0:T(8,128)(2,1)S(1)}, bf16[2048,128]{1,0:T(8,128)(2,1)S(1)}, u32[]{:S(2)}, u32[]{:S(2)}) collective-permute-start(bf16[2048,128]{1,0:T(8,128)(2,1)S(1)} %get-tuple-element.27), channel_id=1, source_target_pairs={{0,4},{4,12},{12,20},{20,28},{28,24},{24,16},{16,8},{8,0},{1,5},{5... | collective-permute-start | bytes 1572872 | tf_op jit(solution)/shard_map/ppermute | solution.py:208
  155.8 1.6 collective-permute-start.8
  157.4 2.0 fusion.17
  159.4 2.0 fusion.16
  161.6 5.9 %collective-permute-done.7 = bf16[2048,128]{1,0:T(8,128)(2,1)S(1)} collective-permute-done((bf16[2048,128]{1,0:T(8,128)(2,1)S(1)}, bf16[2048,128]{1,0:T(8,128)(2,1)S(1)}, u32[]{:S(2)}, u32[]{:S(2)}) %collective-permute-start.7) | collective-permute-done | bytes 524320 | tf_op jit(solution)/shard_map/ppermute | solution.py:208
  167.6 1.8 collective-permute-done.8
  169.4 0.8 fusion.15
  170.1 0.8 fusion.14
  171.2 0.9 copy-done
  172.1 0.3 copy-done.1
  172.5 0.3 copy-done.2
  172.8 0.5 fusion.3
  173.6 2.7 %collective-permute-done.9 = f32[2048,128]{1,0:T(8,128)} collective-permute-done((f32[2048,128]{1,0:T(8,128)S(1)}, f32[2048,128]{1,0:T(8,128)}, u32[]{:S(2)}, u32[]{:S(2)}) %collective-permute-start.9) | collective-permute-done | bytes 1048608 | tf_op jit(solution)/shard_map/ppermute | solution.py:131
  176.3 8.8 %fusion.10 = f32[2048,128]{0,1:T(8,128)S(1)} fusion(f32[2048,2048]{0,1:T(8,128)} %pad_maximum_fusion, f32[2048,128]{1,0:T(8,128)} %collective-permute-done.9, f32[2048,256]{1,0:T(8,128)S(1)} %fusion.3, s32[]{:T(128)S(6)} %select_n.110, f32[2048]{0:T(1024)S(1)} %pad_maximum_fusion.14), kind=kOutput, calls=%fused_computation.42 | convolution fusion | flops 3221749760 | bytes 19931140 | tf_op jit(solution)/shard_map/dot_general | solution.py:137
  185.1 1.6 collective-permute-start.10
  186.7 12.6 %collective-permute-done.10 = f32[1024,128]{0,1:T(8,128)S(1)} collective-permute-done((f32[1024,128]{0,1:T(8,128)S(1)}, f32[1024,128]{0,1:T(8,128)S(1)}, u32[]{:S(2)}, u32[]{:S(2)}) %collective-permute-start.10) | collective-permute-done | bytes 524320 | tf_op jit(solution)/shard_map/ppermute | solution.py:144
  199.4 1.3 collective-permute-done.11
  200.8 0.4 convolution_convert_fusion
  201.1 21.8 %all_to_all.25 = bf16[8,80,512]{2,1,0:T(8,128)(2,1)S(1)} all-to-all(bf16[8,80,512]{2,1,0:T(8,128)(2,1)S(1)} %bitcast.54), channel_id=1, replica_groups=mesh['tile'=8,'win'=4] {'tile'}, dimensions={0} | all-to-all | bytes 1310720 | tf_op jit(solution)/shard_map/all_to_all | solution.py:229
  223.1 0.8 copy-done.3
  (60 shorter events, 2.9 us)
Async XLA Ops:
  0.0 9.7 %copy-start.6 = (s32[256]{0:T(256)S(1)}, s32[256]{0:T(256)}, u32[]{:S(2)}) copy-start(s32[256]{0:T(256)} %param.5) | copy-start | bytes 3076
  0.0 9.7 %copy-start.5 = (s32[256]{0:T(256)S(1)}, s32[256]{0:T(256)}, u32[]{:S(2)}) copy-start(s32[256]{0:T(256)} %param.6) | copy-start | bytes 3076
  0.0 9.7 %copy-start.4 = (s32[256,1]{0,1:T(1,128)S(1)}, s32[256,1]{0,1:T(1,128)}, u32[]{:S(2)}) copy-start(s32[256,1]{0,1:T(1,128)} %param.7) | copy-start | bytes 3076
  2.4 35.7 %all-to-all-start.2 = ((bf16[8,256,256]{2,1,0:T(8,128)(2,1)}), bf16[8,256,256]{2,1,0:T(8,128)(2,1)S(1)}, u32[]{:S(2)}, u32[]{:S(2)}) async-start(bf16[8,256,256]{2,1,0:T(8,128)(2,1)} %shard_map.48), calls=%async_computation.2 | async-start | bytes 2097152 | tf_op jit(solution)/shard_map/all_to_all | solution.py:201
  9.8 27.4 %collective-permute-start = (s32[3,256]{1,0:T(4,128)S(1)}, s32[3,256]{1,0:T(4,128)S(1)}, u32[]{:S(2)}, u32[]{:S(2)}) collective-permute-start(s32[3,256]{1,0:T(4,128)S(1)} %pad_add_fusion), channel_id=1, source_target_pairs={{0,0},{4,4},{8,12},{12,20},{16,28},{20,24},{24,16},{28,8},{1,1},{5... | collective-permute-start | bytes 9224 | tf_op jit(solution)/shard_map/ppermute | solution.py:193
  38.1 34.9 %all-to-all-start.1 = ((bf16[8,256,256]{2,1,0:T(8,128)(2,1)}), bf16[8,256,256]{2,1,0:T(8,128)(2,1)S(1)}, u32[]{:S(2)}, u32[]{:S(2)}) async-start(bf16[8,256,256]{2,1,0:T(8,128)(2,1)} %shard_map.47), calls=%async_computation.1 | async-start | bytes 2097152 | tf_op jit(solution)/shard_map/all_to_all | solution.py:201
  55.2 22.1 %collective-permute-start.1 = (bf16[2048,128]{1,0:T(8,128)(2,1)S(1)}, bf16[2048,128]{1,0:T(8,128)(2,1)}, u32[]{:S(2)}, u32[]{:S(2)}) collective-permute-start(bf16[2048,128]{1,0:T(8,128)(2,1)S(1)} %get-tuple-element.34), channel_id=1, source_target_pairs={{0,4},{4,12},{12,20},{20,28},{28,24},{24,16},{16,8},{8,0},{1,5},{5... | collective-permute-start | bytes 1572872 | tf_op jit(solution)/shard_map/ppermute | solution.py:208
  57.3 20.1 %collective-permute-start.2 = (bf16[2048,128]{1,0:T(8,128)(2,1)S(1)}, bf16[2048,128]{1,0:T(8,128)(2,1)}, u32[]{:S(2)}, u32[]{:S(2)}) collective-permute-start(bf16[2048,128]{1,0:T(8,128)(2,1)S(1)} %get-tuple-element.33), channel_id=1, source_target_pairs={{0,8},{4,0},{12,4},{20,12},{28,20},{24,28},{16,24},{8,16},{1,9},{5... | collective-permute-start | bytes 1572872 | tf_op jit(solution)/shard_map/ppermute | solution.py:209
  73.1 33.9 %all-to-all-start = ((bf16[8,256,256]{2,1,0:T(8,128)(2,1)}), bf16[8,256,256]{2,1,0:T(8,128)(2,1)}, u32[]{:S(2)}, u32[]{:S(2)}) async-start(bf16[8,256,256]{2,1,0:T(8,128)(2,1)} %shard_map.46), calls=%async_computation | async-start | bytes 2097152 | tf_op jit(solution)/shard_map/all_to_all | solution.py:201
  84.9 26.3 %collective-permute-start.3 = (bf16[2048,128]{1,0:T(8,128)(2,1)}, bf16[2048,128]{1,0:T(8,128)(2,1)}, u32[]{:S(2)}, u32[]{:S(2)}) collective-permute-start(bf16[2048,128]{1,0:T(8,128)(2,1)} %get-tuple-element.32), channel_id=1, source_target_pairs={{0,4},{4,12},{12,20},{20,28},{28,24},{24,16},{16,8},{8,0},{1,5},{5... | collective-permute-start | bytes 1572872 | tf_op jit(solution)/shard_map/ppermute | solution.py:208
  86.8 24.4 %collective-permute-start.4 = (bf16[2048,128]{1,0:T(8,128)(2,1)}, bf16[2048,128]{1,0:T(8,128)(2,1)}, u32[]{:S(2)}, u32[]{:S(2)}) collective-permute-start(bf16[2048,128]{1,0:T(8,128)(2,1)} %get-tuple-element.31), channel_id=1, source_target_pairs={{0,8},{4,0},{12,4},{20,12},{28,20},{24,28},{16,24},{8,16},{1,9},{5... | collective-permute-start | bytes 1572872 | tf_op jit(solution)/shard_map/ppermute | solution.py:209
  106.9 33.8 %all-to-all-start.3 = ((bf16[8,256,256]{2,1,0:T(8,128)(2,1)}), bf16[8,256,256]{2,1,0:T(8,128)(2,1)}, u32[]{:S(2)}, u32[]{:S(2)}) async-start(bf16[8,256,256]{2,1,0:T(8,128)(2,1)} %shard_map.49), calls=%async_computation.3 | async-start | bytes 2097152 | tf_op jit(solution)/shard_map/all_to_all | solution.py:201
  119.0 25.1 %collective-permute-start.5 = (bf16[2048,128]{1,0:T(8,128)(2,1)}, bf16[2048,128]{1,0:T(8,128)(2,1)}, u32[]{:S(2)}, u32[]{:S(2)}) collective-permute-start(bf16[2048,128]{1,0:T(8,128)(2,1)} %get-tuple-element.29), channel_id=1, source_target_pairs={{0,4},{4,12},{12,20},{20,28},{28,24},{24,16},{16,8},{8,0},{1,5},{5... | collective-permute-start | bytes 1572872 | tf_op jit(solution)/shard_map/ppermute | solution.py:208
  124.1 20.0 %collective-permute-start.6 = (bf16[2048,128]{1,0:T(8,128)(2,1)}, bf16[2048,128]{1,0:T(8,128)(2,1)}, u32[]{:S(2)}, u32[]{:S(2)}) collective-permute-start(bf16[2048,128]{1,0:T(8,128)(2,1)} %get-tuple-element.30), channel_id=1, source_target_pairs={{0,8},{4,0},{12,4},{20,12},{28,20},{24,28},{16,24},{8,16},{1,9},{5... | collective-permute-start | bytes 1572872 | tf_op jit(solution)/shard_map/ppermute | solution.py:209
  150.9 16.7 %collective-permute-start.7 = (bf16[2048,128]{1,0:T(8,128)(2,1)S(1)}, bf16[2048,128]{1,0:T(8,128)(2,1)S(1)}, u32[]{:S(2)}, u32[]{:S(2)}) collective-permute-start(bf16[2048,128]{1,0:T(8,128)(2,1)S(1)} %get-tuple-element.27), channel_id=1, source_target_pairs={{0,4},{4,12},{12,20},{20,28},{28,24},{24,16},{16,8},{8,0},{1,5},{5... | collective-permute-start | bytes 1572872 | tf_op jit(solution)/shard_map/ppermute | solution.py:208
  155.8 13.6 %collective-permute-start.8 = (bf16[2048,128]{1,0:T(8,128)(2,1)S(1)}, bf16[2048,128]{1,0:T(8,128)(2,1)S(1)}, u32[]{:S(2)}, u32[]{:S(2)}) collective-permute-start(bf16[2048,128]{1,0:T(8,128)(2,1)S(1)} %get-tuple-element.28), channel_id=1, source_target_pairs={{0,8},{4,0},{12,4},{20,12},{28,20},{24,28},{16,24},{8,16},{1,9},{5... | collective-permute-start | bytes 1572872 | tf_op jit(solution)/shard_map/ppermute | solution.py:209
  170.9 1.2 copy-start
  170.9 1.5 copy-start.1
  170.9 1.8 copy-start.2
  173.4 2.9 %collective-permute-start.9 = (f32[2048,128]{1,0:T(8,128)S(1)}, f32[2048,128]{1,0:T(8,128)}, u32[]{:S(2)}, u32[]{:S(2)}) collective-permute-start(f32[2048,128]{1,0:T(8,128)S(1)} %constant_dynamic-slice_fusion.3), channel_id=1, source_target_pairs={{0,1},{1,0},{2,3},{3,2},{4,5},{5,4},{6,7},{7,6},{8,9},{9,8},{10,11... | collective-permute-start | bytes 3145736 | tf_op jit(solution)/shard_map/ppermute | solution.py:131
  185.1 14.1 %collective-permute-start.10 = (f32[1024,128]{0,1:T(8,128)S(1)}, f32[1024,128]{0,1:T(8,128)S(1)}, u32[]{:S(2)}, u32[]{:S(2)}) collective-permute-start(f32[1024,128]{0,1:T(8,128)S(1)} %constant_dynamic-slice_fusion.2), channel_id=1, source_target_pairs={{0,2},{1,3},{2,0},{3,1},{4,6},{5,7},{6,4},{7,5},{8,10},{9,11},{10,... | collective-permute-start | bytes 1572872 | tf_op jit(solution)/shard_map/ppermute | solution.py:144
  199.3 1.4 collective-permute-start.11
  223.1 0.8 copy-start.3

commit v16 on v15

--- a/solution.py
+++ b/solution.py
@@ -112,8 +112,7 @@
 
 
 def inverse_table(length, lag_start):
-    cosine, sine = phase_table(jnp.arange(length, dtype=jnp.int32) + lag_start, length // 2, length)
-    return jnp.concatenate([cosine, -sine], axis=1)
+    return phase_table(jnp.arange(length // 2 + 8, dtype=jnp.int32) + lag_start, length // 2, length)
 
 
 def sum_and_invert(cross, length, lag_count, seg_total, win_count, table):
@@ -133,8 +132,18 @@
     weights = jnp.where(jnp.arange(half_bins) == 0, 1.0, 2.0).astype(jnp.float32) * (
         1.0 / math.sqrt(half_bins * seg_total)
     )
+    cos_table, sin_table = table
     scaled = total * jnp.concatenate([weights, weights])[:, None]
-    lags = jnp.dot(table, scaled, precision=lax.Precision.HIGH)
+    even = jnp.dot(cos_table, scaled[:half_bins], precision=lax.Precision.HIGH)
+    odd = jnp.dot(sin_table, scaled[half_bins:], precision=lax.Precision.HIGH)
+    lags = jnp.concatenate(
+        [
+            even[:half_bins] - odd[:half_bins],
+            even[half_bins:half_bins + 1] - odd[half_bins:half_bins + 1],
+            jnp.flip(even[1:half_bins] + odd[1:half_bins], axis=0),
+        ],
+        axis=0,
+    )
     bit = win_count // 4
     while bit >= 1:
         rows = lags.shape[0] // 2

time: 225 us -> 232 us (1.031)
  waiting for transfers between devices: 39.6 us -> 44.5 us
  matrix products: 46.6 us -> 50.2 us
  other arithmetic: 24.8 us -> 21.7 us
    concatenate x1 -> x0, other arithmetic: 6.3 us -> none  [inverse_table(): return jnp.concatenate([cosine, -sine], axis=1)]
    all_to_all x4, waiting for transfers between devices: 11.9 us -> 17 us  [per_device(): lax.all_to_all(outgoing, 'tile', split_axis=0, concat_axis=0, tiled=True)]
    add x1 -> x3, other arithmetic: 0.01 us -> 5.07 us  [the longest x1 4.97 us: phase_table(): sine = (s_hi * c_lo + c_hi * s_lo).reshape(shape)]
    dot_general x1 -> x2, matrix products: 8.79 us -> 12.4 us  [the longest x1 6.18 us: sum_and_invert(): odd = jnp.dot(sin_table, scaled[half_bins:], precision=lax.Precision.HIGH)]
  transfers between devices with their start and end apart: 16 -> 16, of which waited for: 9 -> 9; matrix products, arithmetic and copies ran while one was open for 31% -> 28% of each run, Pallas kernels for 3% -> 3%
where the time goes in v16:
time: 232 us; the launch traced here: 231 us
  starting transfers between devices  62.7 us (27%)
  matrix products  50.2 us (22%)
  waiting for transfers between devices  44.5 us (19%)
  blocking collectives  21.9 us (9%)
  other arithmetic  21.7 us (9%)
  local copies, waits for them, and re-layouts  19.9 us (9%)
  Pallas kernels  9.32 us (4%)
    dot_general x4, matrix products, per_device(): jnp.einsum('fjm,jmc->fc', forward, received, preferred_element_type=jnp.f...  24.2 us
    all_to_all x4, starting transfers between devices, per_device(): lax.all_to_all(outgoing, 'tile', split_axis=0, concat_axis=0, tiled=True)  23.8 us
    ppermute x4, starting transfers between devices, per_device(): from_next = lax.ppermute(whitened[:, :half], 'tile', to_prev)  22.6 us
    all_to_all x1, blocking collectives, per_device(): lax.all_to_all(buckets, 'tile', split_axis=0, concat_axis=0, tiled=True)  21.9 us
    all_to_all x4, waiting for transfers between devices, per_device(): lax.all_to_all(outgoing, 'tile', split_axis=0, concat_axis=0, tiled=True)  17 us
    ppermute x4, starting transfers between devices, per_device(): from_prev = lax.ppermute(whitened[:, half:], 'tile', to_next)  13.9 us
    ppermute x1, waiting for transfers between devices, sum_and_invert(): lax.ppermute(send, 'win', [(w, w ^ 2 * bit) for w in range(win_count)])  12.5 us
    pallas_call x4, Pallas kernels, lay_out_blocks(): pl.pallas_call(kernel, out_shape=jax.ShapeDtypeStruct((parts, rows, block...  9.32 us
  transfers between devices with their start and end apart: 16, of which 9 were waited for; matrix products, arithmetic and copies ran while one was open for 28% of the time, Pallas kernels for 3%

profile of v16, /device:TPU:0, one launch (start us, length us, event | category | flops | bytes accessed | tf_op | source)
XLA Modules:
  0.0 230.7 jit_solution(11874433902605164685)
XLA Ops:
  0.0 2.4 %shard_map.48 = bf16[8,256,256]{2,1,0:T(8,128)(2,1)} custom-call(bf16[4,256,2048]{2,1,0:T(8,128)(2,1)} %src.7), custom_call_target="tpu_custom_call" | custom-call | tf_op jit(solution)/shard_map/pallas_call | solution.py:175
  2.4 7.3 %all-to-all-start.2 = ((bf16[8,256,256]{2,1,0:T(8,128)(2,1)}), bf16[8,256,256]{2,1,0:T(8,128)(2,1)S(1)}, u32[]{:S(2)}, u32[]{:S(2)}) async-start(bf16[8,256,256]{2,1,0:T(8,128)(2,1)} %shard_map.48), calls=%async_computation.2 | async-start | bytes 2097152 | tf_op jit(solution)/shard_map/all_to_all | solution.py:210
  9.8 0.7 collective-permute-start
  10.5 1.0 fusion.54
  11.5 0.6 fusion.63
  12.1 5.0 %subtract_convert_fusion = (bf16[1024,32,64]{0,2,1:T(8,128)(2,1)}, bf16[1024,32,64]{0,2,1:T(8,128)(2,1)}) fusion(f32[1024,64]{0,1:T(8,128)S(1)} %get-tuple-element.50, f32[1024,32]{0,1:T(8,128)S(1)} %get-tuple-element.49, f32[1024,64]{0,1:T(8,128)S(1)} %get-tuple-element.51, f32[1024,32]{0,1:T(8,128)S(1)} %get-tuple-element.48), kind=kLoop, calls=%fused_computation.2 | loop fusion | flops 18874368 | bytes 9175040 | tf_op jit(solution)/shard_map/convert.3
  17.1 2.3 shard_map.47
  19.4 2.3 %shard_map.46 = bf16[8,256,256]{2,1,0:T(8,128)(2,1)} custom-call(bf16[4,256,2048]{2,1,0:T(8,128)(2,1)} %src.7), custom_call_target="tpu_custom_call" | custom-call | tf_op jit(solution)/shard_map/pallas_call | solution.py:175
  21.7 2.3 shard_map.49
  24.0 6.5 %copy.5 = bf16[1024,8,256]{2,0,1:T(8,128)(2,1)} copy(bf16[1024,8,256]{0,2,1:T(8,128)(2,1)} %bitcast.50) | data formatting | bytes 8388608 | tf_op jit(solution)/shard_map/sub | solution.py:25
  30.5 6.4 %copy.6 = bf16[1024,8,256]{2,0,1:T(8,128)(2,1)} copy(bf16[1024,8,256]{0,2,1:T(8,128)(2,1)} %bitcast.49) | data formatting | bytes 8388608 | tf_op jit(solution)/shard_map/neg | solution.py:32
  37.0 0.6 reduce-window.6
  37.9 7.8 %all-to-all-start.1 = ((bf16[8,256,256]{2,1,0:T(8,128)(2,1)}), bf16[8,256,256]{2,1,0:T(8,128)(2,1)S(1)}, u32[]{:S(2)}, u32[]{:S(2)}) async-start(bf16[8,256,256]{2,1,0:T(8,128)(2,1)} %shard_map.47), calls=%async_computation.1 | async-start | bytes 2097152 | tf_op jit(solution)/shard_map/all_to_all | solution.py:210
  45.7 5.9 %convolution_bitcast_fusion.3 = f32[2048,256]{1,0:T(8,128)S(1)} fusion(bf16[8,256,256]{2,1,0:T(8,128)(2,1)S(1)} %all-to-all-done.2, bf16[1024,8,256]{2,0,1:T(8,128)(2,1)} %copy.6, bf16[1024,8,256]{2,0,1:T(8,128)(2,1)} %copy.5), kind=kOutput, calls=%fused_computation.8 | convolution fusion | flops 2164260864 | bytes 11534336 | tf_op jit(solution)/shard_map/fjm,jmc->fc/dot_general | solution.py:215
  52.4 2.1 collective-permute-start.1
  54.5 0.4 fusion.65
  54.9 1.2 fusion.50
  56.0 5.0 %multiply_add_fusion = (f32[1032,16,64]{0,2,1:T(8,128)}, f32[1032,16,64]{0,2,1:T(8,128)}) fusion(f32[1032,64]{0,1:T(8,128)S(1)} %get-tuple-element.44, f32[1032,16]{0,1:T(8,128)S(1)} %get-tuple-element.42, f32[1032,64]{0,1:T(8,128)S(1)} %get-tuple-element.43, f32[1032,16]{0,1:T(8,128)S(1)} %get-tuple-element.41), kind=kLoop, calls=%fused_computation.3 | loop fusion | flops 6340608 | bytes 9114624 | tf_op jit(solution)/shard_map/add | solution.py:26
  61.0 11.9 %all-to-all-done.1 = bf16[8,256,256]{2,1,0:T(8,128)(2,1)S(1)} async-done(((bf16[8,256,256]{2,1,0:T(8,128)(2,1)}), bf16[8,256,256]{2,1,0:T(8,128)(2,1)S(1)}, u32[]{:S(2)}, u32[]{:S(2)}) %all-to-all-start.1) | async-done | bytes 1048608 | tf_op jit(solution)/shard_map/all_to_all | solution.py:210
  72.9 4.4 %all-to-all-start = ((bf16[8,256,256]{2,1,0:T(8,128)(2,1)}), bf16[8,256,256]{2,1,0:T(8,128)(2,1)}, u32[]{:S(2)}, u32[]{:S(2)}) async-start(bf16[8,256,256]{2,1,0:T(8,128)(2,1)} %shard_map.46), calls=%async_computation | async-start | bytes 2097152 | tf_op jit(solution)/shard_map/all_to_all | solution.py:210
  77.3 5.9 %convolution_bitcast_fusion.2 = f32[2048,256]{1,0:T(8,128)S(1)} fusion(bf16[8,256,256]{2,1,0:T(8,128)(2,1)S(1)} %all-to-all-done.1, bf16[1024,8,256]{2,0,1:T(8,128)(2,1)} %copy.6, bf16[1024,8,256]{2,0,1:T(8,128)(2,1)} %copy.5), kind=kOutput, calls=%fused_computation.7 | convolution fusion | flops 2164260864 | bytes 11534336 | tf_op jit(solution)/shard_map/fjm,jmc->fc/dot_general | solution.py:215
  83.6 0.3 fusion.1
  83.9 1.0 fusion.79
  84.9 1.7 collective-permute-start.3
  86.6 12.1 %collective-permute-start.4 = (bf16[2048,128]{1,0:T(8,128)(2,1)}, bf16[2048,128]{1,0:T(8,128)(2,1)}, u32[]{:S(2)}, u32[]{:S(2)}) collective-permute-start(bf16[2048,128]{1,0:T(8,128)(2,1)} %get-tuple-element.31), channel_id=1, source_target_pairs={{0,8},{4,0},{12,4},{20,12},{28,20},{24,28},{16,24},{8,16},{1,9},{5... | collective-permute-start | bytes 1572872 | tf_op jit(solution)/shard_map/ppermute | solution.py:218
  98.8 2.0 fusion.17
  100.7 2.0 fusion.16
  102.7 1.2 multiply_add_fusion.4
  103.9 2.8 %all-to-all-done = bf16[8,256,256]{2,1,0:T(8,128)(2,1)} async-done(((bf16[8,256,256]{2,1,0:T(8,128)(2,1)}), bf16[8,256,256]{2,1,0:T(8,128)(2,1)}, u32[]{:S(2)}, u32[]{:S(2)}) %all-to-all-start) | async-done | bytes 1048608 | tf_op jit(solution)/shard_map/all_to_all | solution.py:210
  106.7 4.2 %all-to-all-start.3 = ((bf16[8,256,256]{2,1,0:T(8,128)(2,1)}), bf16[8,256,256]{2,1,0:T(8,128)(2,1)}, u32[]{:S(2)}, u32[]{:S(2)}) async-start(bf16[8,256,256]{2,1,0:T(8,128)(2,1)} %shard_map.49), calls=%async_computation.3 | async-start | bytes 2097152 | tf_op jit(solution)/shard_map/all_to_all | solution.py:210
  111.0 6.1 %convolution_bitcast_fusion.1 = f32[2048,256]{1,0:T(8,128)S(1)} fusion(bf16[8,256,256]{2,1,0:T(8,128)(2,1)} %all-to-all-done, bf16[1024,8,256]{2,0,1:T(8,128)(2,1)} %copy.6, bf16[1024,8,256]{2,0,1:T(8,128)(2,1)} %copy.5), kind=kOutput, calls=%fused_computation.6 | convolution fusion | flops 2164260864 | bytes 11534336 | tf_op jit(solution)/shard_map/fjm,jmc->fc/dot_general | solution.py:215
  117.8 1.0 fusion.78
  118.8 5.1 %collective-permute-start.5 = (bf16[2048,128]{1,0:T(8,128)(2,1)}, bf16[2048,128]{1,0:T(8,128)(2,1)}, u32[]{:S(2)}, u32[]{:S(2)}) collective-permute-start(bf16[2048,128]{1,0:T(8,128)(2,1)} %get-tuple-element.29), channel_id=1, source_target_pairs={{0,4},{4,12},{12,20},{20,28},{28,24},{24,16},{16,8},{8,0},{1,5},{5... | collective-permute-start | bytes 1572872 | tf_op jit(solution)/shard_map/ppermute | solution.py:217
  123.9 8.7 %collective-permute-start.6 = (bf16[2048,128]{1,0:T(8,128)(2,1)}, bf16[2048,128]{1,0:T(8,128)(2,1)}, u32[]{:S(2)}, u32[]{:S(2)}) collective-permute-start(bf16[2048,128]{1,0:T(8,128)(2,1)} %get-tuple-element.30), channel_id=1, source_target_pairs={{0,8},{4,0},{12,4},{20,12},{28,20},{24,28},{16,24},{8,16},{1,9},{5... | collective-permute-start | bytes 1572872 | tf_op jit(solution)/shard_map/ppermute | solution.py:218
  132.6 2.0 fusion.15
  134.6 2.0 fusion.14
  136.5 1.6 multiply_add_fusion.3
  138.2 2.3 %all-to-all-done.3 = bf16[8,256,256]{2,1,0:T(8,128)(2,1)} async-done(((bf16[8,256,256]{2,1,0:T(8,128)(2,1)}), bf16[8,256,256]{2,1,0:T(8,128)(2,1)}, u32[]{:S(2)}, u32[]{:S(2)}) %all-to-all-start.3) | async-done | bytes 1048608 | tf_op jit(solution)/shard_map/all_to_all | solution.py:210
  140.5 3.4 %collective-permute-done.5 = bf16[2048,128]{1,0:T(8,128)(2,1)} collective-permute-done((bf16[2048,128]{1,0:T(8,128)(2,1)}, bf16[2048,128]{1,0:T(8,128)(2,1)}, u32[]{:S(2)}, u32[]{:S(2)}) %collective-permute-start.5) | collective-permute-done | bytes 524320 | tf_op jit(solution)/shard_map/ppermute | solution.py:217
  143.9 6.1 %convolution_bitcast_fusion = f32[2048,256]{1,0:T(8,128)S(1)} fusion(bf16[8,256,256]{2,1,0:T(8,128)(2,1)} %all-to-all-done.3, bf16[1024,8,256]{2,0,1:T(8,128)(2,1)} %copy.6, bf16[1024,8,256]{2,0,1:T(8,128)(2,1)} %copy.5), kind=kOutput, calls=%fused_computation.5 | convolution fusion | flops 2164260864 | bytes 11534336 | tf_op jit(solution)/shard_map/fjm,jmc->fc/dot_general | solution.py:215
  150.7 5.0 %collective-permute-start.7 = (bf16[2048,128]{1,0:T(8,128)(2,1)S(1)}, bf16[2048,128]{1,0:T(8,128)(2,1)S(1)}, u32[]{:S(2)}, u32[]{:S(2)}) collective-permute-start(bf16[2048,128]{1,0:T(8,128)(2,1)S(1)} %get-tuple-element.27), channel_id=1, source_target_pairs={{0,4},{4,12},{12,20},{20,28},{28,24},{24,16},{16,8},{8,0},{1,5},{5... | collective-permute-start | bytes 1572872 | tf_op jit(solution)/shard_map/ppermute | solution.py:217
  155.7 1.7 collective-permute-start.8
  157.5 2.0 fusion.13
  159.4 2.0 fusion.12
  161.7 5.7 %collective-permute-done.7 = bf16[2048,128]{1,0:T(8,128)(2,1)S(1)} collective-permute-done((bf16[2048,128]{1,0:T(8,128)(2,1)S(1)}, bf16[2048,128]{1,0:T(8,128)(2,1)S(1)}, u32[]{:S(2)}, u32[]{:S(2)}) %collective-permute-start.7) | collective-permute-done | bytes 524320 | tf_op jit(solution)/shard_map/ppermute | solution.py:217
  167.4 1.8 collective-permute-done.8
  169.2 0.8 fusion.11
  170.0 0.8 fusion.10
  171.0 0.9 copy-done
  172.0 0.3 copy-done.1
  172.3 0.3 copy-done.2
  172.6 0.5 fusion.3
  173.4 2.7 %collective-permute-done.9 = f32[2048,128]{1,0:T(8,128)} collective-permute-done((f32[2048,128]{1,0:T(8,128)S(1)}, f32[2048,128]{1,0:T(8,128)}, u32[]{:S(2)}, u32[]{:S(2)}) %collective-permute-start.9) | collective-permute-done | bytes 1048608 | tf_op jit(solution)/shard_map/ppermute | solution.py:130
  176.1 1.6 add_multiply_fusion
  177.6 6.2 %fusion.20 = f32[1032,128]{1,0:T(8,128)S(1)} fusion(f32[1032,1024]{0,1:T(8,128)} %bitcast.48, f32[2048,128]{1,0:T(8,128)S(1)} %add_multiply_fusion), kind=kOutput, calls=%fused_computation.63 | convolution fusion | flops 811597824 | bytes 5279744 | tf_op jit(solution)/shard_map/dot_general | solution.py:137
  183.8 6.2 %fusion.18 = f32[1032,128]{1,0:T(8,128)S(1)} fusion(f32[1032,1024]{0,1:T(8,128)} %bitcast.47, f32[2048,128]{1,0:T(8,128)S(1)} %add_multiply_fusion), kind=kOutput, calls=%fused_computation.61 | convolution fusion | flops 811597824 | bytes 5279744 | tf_op jit(solution)/shard_map/dot_general | solution.py:138
  190.2 0.6 rev.4
  190.8 1.1 concatenate.67
  191.9 1.6 collective-permute-start.10
  193.5 12.5 %collective-permute-done.10 = f32[1024,128]{1,0:T(8,128)S(1)} collective-permute-done((f32[1024,128]{1,0:T(8,128)S(1)}, f32[1024,128]{1,0:T(8,128)S(1)}, u32[]{:S(2)}, u32[]{:S(2)}) %collective-permute-start.10) | collective-permute-done | bytes 524320 | tf_op jit(solution)/shard_map/ppermute | solution.py:153
  206.2 1.3 collective-permute-done.11
  207.5 0.4 convolution_convert_fusion
  207.9 21.9 %all_to_all.25 = bf16[8,80,512]{2,1,0:T(8,128)(2,1)S(1)} all-to-all(bf16[8,80,512]{2,1,0:T(8,128)(2,1)S(1)} %bitcast.55), channel_id=1, replica_groups=mesh['tile'=8,'win'=4] {'tile'}, dimensions={0} | all-to-all | bytes 1310720 | tf_op jit(solution)/shard_map/all_to_all | solution.py:238
  229.9 0.8 copy-done.3
  (66 shorter events, 3.8 us)
Async XLA Ops:
  0.0 9.7 %copy-start.6 = (s32[256]{0:T(256)S(1)}, s32[256]{0:T(256)}, u32[]{:S(2)}) copy-start(s32[256]{0:T(256)} %param.5) | copy-start | bytes 3076
  0.0 9.7 %copy-start.5 = (s32[256]{0:T(256)S(1)}, s32[256]{0:T(256)}, u32[]{:S(2)}) copy-start(s32[256]{0:T(256)} %param.6) | copy-start | bytes 3076
  0.0 9.7 %copy-start.4 = (s32[256,1]{0,1:T(1,128)S(1)}, s32[256,1]{0,1:T(1,128)}, u32[]{:S(2)}) copy-start(s32[256,1]{0,1:T(1,128)} %param.7) | copy-start | bytes 3076
  2.4 35.5 %all-to-all-start.2 = ((bf16[8,256,256]{2,1,0:T(8,128)(2,1)}), bf16[8,256,256]{2,1,0:T(8,128)(2,1)S(1)}, u32[]{:S(2)}, u32[]{:S(2)}) async-start(bf16[8,256,256]{2,1,0:T(8,128)(2,1)} %shard_map.48), calls=%async_computation.2 | async-start | bytes 2097152 | tf_op jit(solution)/shard_map/all_to_all | solution.py:210
  9.8 27.2 %collective-permute-start = (s32[3,256]{1,0:T(4,128)S(1)}, s32[3,256]{1,0:T(4,128)S(1)}, u32[]{:S(2)}, u32[]{:S(2)}) collective-permute-start(s32[3,256]{1,0:T(4,128)S(1)} %pad_add_fusion), channel_id=1, source_target_pairs={{0,0},{4,4},{8,12},{12,20},{16,28},{20,24},{24,16},{28,8},{1,1},{5... | collective-permute-start | bytes 9224 | tf_op jit(solution)/shard_map/ppermute | solution.py:202
  37.9 34.9 %all-to-all-start.1 = ((bf16[8,256,256]{2,1,0:T(8,128)(2,1)}), bf16[8,256,256]{2,1,0:T(8,128)(2,1)S(1)}, u32[]{:S(2)}, u32[]{:S(2)}) async-start(bf16[8,256,256]{2,1,0:T(8,128)(2,1)} %shard_map.47), calls=%async_computation.1 | async-start | bytes 2097152 | tf_op jit(solution)/shard_map/all_to_all | solution.py:210
  52.4 25.0 %collective-permute-start.1 = (bf16[2048,128]{1,0:T(8,128)(2,1)S(1)}, bf16[2048,128]{1,0:T(8,128)(2,1)}, u32[]{:S(2)}, u32[]{:S(2)}) collective-permute-start(bf16[2048,128]{1,0:T(8,128)(2,1)S(1)} %get-tuple-element.34), channel_id=1, source_target_pairs={{0,4},{4,12},{12,20},{20,28},{28,24},{24,16},{16,8},{8,0},{1,5},{5... | collective-permute-start | bytes 1572872 | tf_op jit(solution)/shard_map/ppermute | solution.py:217
  54.4 22.9 %collective-permute-start.2 = (bf16[2048,128]{1,0:T(8,128)(2,1)S(1)}, bf16[2048,128]{1,0:T(8,128)(2,1)}, u32[]{:S(2)}, u32[]{:S(2)}) collective-permute-start(bf16[2048,128]{1,0:T(8,128)(2,1)S(1)} %get-tuple-element.33), channel_id=1, source_target_pairs={{0,8},{4,0},{12,4},{20,12},{28,20},{24,28},{16,24},{8,16},{1,9},{5... | collective-permute-start | bytes 1572872 | tf_op jit(solution)/shard_map/ppermute | solution.py:218
  72.9 33.9 %all-to-all-start = ((bf16[8,256,256]{2,1,0:T(8,128)(2,1)}), bf16[8,256,256]{2,1,0:T(8,128)(2,1)}, u32[]{:S(2)}, u32[]{:S(2)}) async-start(bf16[8,256,256]{2,1,0:T(8,128)(2,1)} %shard_map.46), calls=%async_computation | async-start | bytes 2097152 | tf_op jit(solution)/shard_map/all_to_all | solution.py:210
  84.9 26.1 %collective-permute-start.3 = (bf16[2048,128]{1,0:T(8,128)(2,1)}, bf16[2048,128]{1,0:T(8,128)(2,1)}, u32[]{:S(2)}, u32[]{:S(2)}) collective-permute-start(bf16[2048,128]{1,0:T(8,128)(2,1)} %get-tuple-element.32), channel_id=1, source_target_pairs={{0,4},{4,12},{12,20},{20,28},{28,24},{24,16},{16,8},{8,0},{1,5},{5... | collective-permute-start | bytes 1572872 | tf_op jit(solution)/shard_map/ppermute | solution.py:217
  86.6 24.4 %collective-permute-start.4 = (bf16[2048,128]{1,0:T(8,128)(2,1)}, bf16[2048,128]{1,0:T(8,128)(2,1)}, u32[]{:S(2)}, u32[]{:S(2)}) collective-permute-start(bf16[2048,128]{1,0:T(8,128)(2,1)} %get-tuple-element.31), channel_id=1, source_target_pairs={{0,8},{4,0},{12,4},{20,12},{28,20},{24,28},{16,24},{8,16},{1,9},{5... | collective-permute-start | bytes 1572872 | tf_op jit(solution)/shard_map/ppermute | solution.py:218
  106.7 33.7 %all-to-all-start.3 = ((bf16[8,256,256]{2,1,0:T(8,128)(2,1)}), bf16[8,256,256]{2,1,0:T(8,128)(2,1)}, u32[]{:S(2)}, u32[]{:S(2)}) async-start(bf16[8,256,256]{2,1,0:T(8,128)(2,1)} %shard_map.49), calls=%async_computation.3 | async-start | bytes 2097152 | tf_op jit(solution)/shard_map/all_to_all | solution.py:210
  118.8 25.1 %collective-permute-start.5 = (bf16[2048,128]{1,0:T(8,128)(2,1)}, bf16[2048,128]{1,0:T(8,128)(2,1)}, u32[]{:S(2)}, u32[]{:S(2)}) collective-permute-start(bf16[2048,128]{1,0:T(8,128)(2,1)} %get-tuple-element.29), channel_id=1, source_target_pairs={{0,4},{4,12},{12,20},{20,28},{28,24},{24,16},{16,8},{8,0},{1,5},{5... | collective-permute-start | bytes 1572872 | tf_op jit(solution)/shard_map/ppermute | solution.py:217
  123.9 20.0 %collective-permute-start.6 = (bf16[2048,128]{1,0:T(8,128)(2,1)}, bf16[2048,128]{1,0:T(8,128)(2,1)}, u32[]{:S(2)}, u32[]{:S(2)}) collective-permute-start(bf16[2048,128]{1,0:T(8,128)(2,1)} %get-tuple-element.30), channel_id=1, source_target_pairs={{0,8},{4,0},{12,4},{20,12},{28,20},{24,28},{16,24},{8,16},{1,9},{5... | collective-permute-start | bytes 1572872 | tf_op jit(solution)/shard_map/ppermute | solution.py:218
  150.7 16.7 %collective-permute-start.7 = (bf16[2048,128]{1,0:T(8,128)(2,1)S(1)}, bf16[2048,128]{1,0:T(8,128)(2,1)S(1)}, u32[]{:S(2)}, u32[]{:S(2)}) collective-permute-start(bf16[2048,128]{1,0:T(8,128)(2,1)S(1)} %get-tuple-element.27), channel_id=1, source_target_pairs={{0,4},{4,12},{12,20},{20,28},{28,24},{24,16},{16,8},{8,0},{1,5},{5... | collective-permute-start | bytes 1572872 | tf_op jit(solution)/shard_map/ppermute | solution.py:217
  155.7 13.5 %collective-permute-start.8 = (bf16[2048,128]{1,0:T(8,128)(2,1)S(1)}, bf16[2048,128]{1,0:T(8,128)(2,1)S(1)}, u32[]{:S(2)}, u32[]{:S(2)}) collective-permute-start(bf16[2048,128]{1,0:T(8,128)(2,1)S(1)} %get-tuple-element.28), channel_id=1, source_target_pairs={{0,8},{4,0},{12,4},{20,12},{28,20},{24,28},{16,24},{8,16},{1,9},{5... | collective-permute-start | bytes 1572872 | tf_op jit(solution)/shard_map/ppermute | solution.py:218
  170.7 1.2 copy-start
  170.7 1.5 copy-start.1
  170.8 1.8 copy-start.2
  173.2 2.9 %collective-permute-start.9 = (f32[2048,128]{1,0:T(8,128)S(1)}, f32[2048,128]{1,0:T(8,128)}, u32[]{:S(2)}, u32[]{:S(2)}) collective-permute-start(f32[2048,128]{1,0:T(8,128)S(1)} %constant_dynamic-slice_fusion.3), channel_id=1, source_target_pairs={{0,1},{1,0},{2,3},{3,2},{4,5},{5,4},{6,7},{7,6},{8,9},{9,8},{10,11... | collective-permute-start | bytes 3145736 | tf_op jit(solution)/shard_map/ppermute | solution.py:130
  191.9 14.1 %collective-permute-start.10 = (f32[1024,128]{1,0:T(8,128)S(1)}, f32[1024,128]{1,0:T(8,128)S(1)}, u32[]{:S(2)}, u32[]{:S(2)}) collective-permute-start(f32[1024,128]{1,0:T(8,128)S(1)} %constant_dynamic-slice_fusion.2), channel_id=1, source_target_pairs={{0,2},{1,3},{2,0},{3,1},{4,6},{5,7},{6,4},{7,5},{8,10},{9,11},{10,... | collective-permute-start | bytes 1572872 | tf_op jit(solution)/shard_map/ppermute | solution.py:153
  206.1 1.4 collective-permute-start.11
  229.8 0.8 copy-start.3

commit v17 on v15

--- a/solution.py
+++ b/solution.py
@@ -134,7 +134,7 @@
         1.0 / math.sqrt(half_bins * seg_total)
     )
     scaled = total * jnp.concatenate([weights, weights])[:, None]
-    lags = jnp.dot(table, scaled, precision=lax.Precision.HIGH)
+    lags = jnp.dot(table, scaled, preferred_element_type=jnp.float32)
     bit = win_count // 4
     while bit >= 1:
         rows = lags.shape[0] // 2

time: 225 us -> 221 us (0.982)
  other arithmetic: 24.8 us -> 29.7 us
  waiting for transfers between devices: 39.6 us -> 35.1 us
  matrix products: 46.6 us -> 42.9 us
    all_to_all x4, waiting for transfers between devices: 11.9 us -> 7.66 us  [per_device(): lax.all_to_all(outgoing, 'tile', split_axis=0, concat_axis=0, tiled=True)]
    dot_general x1, matrix products: 8.79 us -> 5.05 us  [sum_and_invert(): lags = jnp.dot(table, scaled, preferred_element_type=jnp.float32)]
    sub x1, other arithmetic: 2.38 us -> 5.29 us  [phase_table(): cosine = (c_hi * c_lo - s_hi * s_lo).reshape(shape)]
  transfers between devices with their start and end apart: 16 -> 16, of which waited for: 9 -> 9; matrix products, arithmetic and copies ran while one was open for 31% -> 33% of each run, Pallas kernels for 3% -> 3%
where the time goes in v17:
time: 221 us; the launch traced here: 220 us
  starting transfers between devices  62.3 us (28%)
  matrix products  42.9 us (19%)
  waiting for transfers between devices  35.1 us (16%)
  other arithmetic  29.7 us (13%)
  blocking collectives  21.9 us (10%)
  local copies, waits for them, and re-layouts  18.2 us (8%)
  Pallas kernels  9.3 us (4%)
    dot_general x4, matrix products, per_device(): jnp.einsum('fjm,jmc->fc', forward, received, preferred_element_type=jnp.f...  24.2 us
    all_to_all x4, starting transfers between devices, per_device(): lax.all_to_all(outgoing, 'tile', split_axis=0, concat_axis=0, tiled=True)  23.8 us
    ppermute x4, starting transfers between devices, per_device(): from_next = lax.ppermute(whitened[:, :half], 'tile', to_prev)  22.8 us
    all_to_all x1, blocking collectives, per_device(): lax.all_to_all(buckets, 'tile', split_axis=0, concat_axis=0, tiled=True)  21.9 us
    ppermute x4, starting transfers between devices, per_device(): from_prev = lax.ppermute(whitened[:, half:], 'tile', to_next)  13.3 us
    ppermute x1, waiting for transfers between devices, sum_and_invert(): lax.ppermute(send, 'win', [(w, w ^ 2 * bit) for w in range(win_count)])  12.5 us
    pallas_call x4, Pallas kernels, lay_out_blocks(): pl.pallas_call(kernel, out_shape=jax.ShapeDtypeStruct((parts, rows, block...  9.3 us
    ppermute x4, waiting for transfers between devices, per_device(): from_prev = lax.ppermute(whitened[:, half:], 'tile', to_next)  9.07 us
  transfers between devices with their start and end apart: 16, of which 9 were waited for; matrix products, arithmetic and copies ran while one was open for 33% of the time, Pallas kernels for 3%

profile of v17, /device:TPU:0, one launch (start us, length us, event | category | flops | bytes accessed | tf_op | source)
XLA Modules:
  0.0 219.9 jit_solution(17701195816991247666)
XLA Ops:
  0.0 2.3 %shard_map.48 = bf16[8,256,256]{2,1,0:T(8,128)(2,1)} custom-call(bf16[4,256,2048]{2,1,0:T(8,128)(2,1)} %src.7), custom_call_target="tpu_custom_call" | custom-call | tf_op jit(solution)/shard_map/pallas_call | solution.py:166
  2.3 7.3 %all-to-all-start.2 = ((bf16[8,256,256]{2,1,0:T(8,128)(2,1)}), bf16[8,256,256]{2,1,0:T(8,128)(2,1)S(1)}, u32[]{:S(2)}, u32[]{:S(2)}) async-start(bf16[8,256,256]{2,1,0:T(8,128)(2,1)} %shard_map.48), calls=%async_computation.2 | async-start | bytes 2097152 | tf_op jit(solution)/shard_map/all_to_all | solution.py:201
  9.7 0.7 collective-permute-start
  10.4 1.0 fusion.58
  11.4 0.6 fusion.66
  12.0 5.0 %subtract_convert_fusion = (bf16[1024,32,64]{0,2,1:T(8,128)(2,1)}, bf16[1024,32,64]{0,2,1:T(8,128)(2,1)}) fusion(f32[1024,64]{0,1:T(8,128)S(1)} %get-tuple-element.48, f32[1024,32]{0,1:T(8,128)S(1)} %get-tuple-element.47, f32[1024,64]{0,1:T(8,128)S(1)} %get-tuple-element.49, f32[1024,32]{0,1:T(8,128)S(1)} %get-tuple-element.46), kind=kLoop, calls=%fused_computation.5 | loop fusion | flops 18874368 | bytes 9175040 | tf_op jit(solution)/shard_map/convert.3
  17.0 2.3 %shard_map.47 = bf16[8,256,256]{2,1,0:T(8,128)(2,1)} custom-call(bf16[4,256,2048]{2,1,0:T(8,128)(2,1)} %src.7), custom_call_target="tpu_custom_call" | custom-call | tf_op jit(solution)/shard_map/pallas_call | solution.py:166
  19.3 2.3 %shard_map.46 = bf16[8,256,256]{2,1,0:T(8,128)(2,1)} custom-call(bf16[4,256,2048]{2,1,0:T(8,128)(2,1)} %src.7), custom_call_target="tpu_custom_call" | custom-call | tf_op jit(solution)/shard_map/pallas_call | solution.py:166
  21.6 2.4 %shard_map.49 = bf16[8,256,256]{2,1,0:T(8,128)(2,1)} custom-call(bf16[4,256,2048]{2,1,0:T(8,128)(2,1)} %src.7), custom_call_target="tpu_custom_call" | custom-call | tf_op jit(solution)/shard_map/pallas_call | solution.py:166
  24.0 6.4 %copy.5 = bf16[1024,8,256]{2,0,1:T(8,128)(2,1)} copy(bf16[1024,8,256]{0,2,1:T(8,128)(2,1)} %bitcast.47) | data formatting | bytes 8388608 | tf_op jit(solution)/shard_map/sub | solution.py:25
  30.4 6.4 %copy.6 = bf16[1024,8,256]{2,0,1:T(8,128)(2,1)} copy(bf16[1024,8,256]{0,2,1:T(8,128)(2,1)} %bitcast.46) | data formatting | bytes 8388608 | tf_op jit(solution)/shard_map/neg | solution.py:32
  36.9 0.6 reduce-window.6
  37.9 7.8 %all-to-all-start.1 = ((bf16[8,256,256]{2,1,0:T(8,128)(2,1)}), bf16[8,256,256]{2,1,0:T(8,128)(2,1)S(1)}, u32[]{:S(2)}, u32[]{:S(2)}) async-start(bf16[8,256,256]{2,1,0:T(8,128)(2,1)} %shard_map.47), calls=%async_computation.1 | async-start | bytes 2097152 | tf_op jit(solution)/shard_map/all_to_all | solution.py:201
  45.7 5.9 %convolution_bitcast_fusion.3 = f32[2048,256]{1,0:T(8,128)S(1)} fusion(bf16[8,256,256]{2,1,0:T(8,128)(2,1)S(1)} %all-to-all-done.2, bf16[1024,8,256]{2,0,1:T(8,128)(2,1)} %copy.6, bf16[1024,8,256]{2,0,1:T(8,128)(2,1)} %copy.5), kind=kOutput, calls=%fused_computation.9 | convolution fusion | flops 2164260864 | bytes 11534336 | tf_op jit(solution)/shard_map/fjm,jmc->fc/dot_general | solution.py:206
  51.9 0.3 fusion
  52.3 2.1 collective-permute-start.1
  54.6 0.6 fusion.64
  55.2 2.0 fusion.47
  57.3 5.3 %multiply_subtract_fusion = (bf16[2048,16,64]{0,2,1:T(8,128)(2,1)}, bf16[2048,16,64]{0,2,1:T(8,128)(2,1)}) fusion(f32[2048,64]{0,1:T(8,128)S(1)} %get-tuple-element.42, f32[2048,16]{0,1:T(8,128)S(1)} %get-tuple-element.40, f32[2048,64]{0,1:T(8,128)S(1)} %get-tuple-element.41, f32[2048,16]{0,1:T(8,128)S(1)} %get-tuple-element.39), kind=kLoop, calls=%fused_computation.3 | loop fusion | flops 18874368 | bytes 9699328 | tf_op jit(solution)/shard_map/sub | solution.py:25
  62.6 8.4 %pad_maximum_fusion = bf16[2048,2048]{0,1:T(8,128)(2,1)} fusion(bf16[2048,1024]{0,1:T(8,128)(2,1)} %bitcast.49, bf16[2048,1024]{0,1:T(8,128)(2,1)} %bitcast.48), kind=kLoop, calls=%fused_computation | loop fusion | flops 16777216 | bytes 16777216 | tf_op jit(solution)/shard_map/concatenate | solution.py:116
  70.9 1.9 all-to-all-done.1
  72.8 4.2 %all-to-all-start = ((bf16[8,256,256]{2,1,0:T(8,128)(2,1)}), bf16[8,256,256]{2,1,0:T(8,128)(2,1)}, u32[]{:S(2)}, u32[]{:S(2)}) async-start(bf16[8,256,256]{2,1,0:T(8,128)(2,1)} %shard_map.46), calls=%async_computation | async-start | bytes 2097152 | tf_op jit(solution)/shard_map/all_to_all | solution.py:201
  77.1 5.9 %convolution_bitcast_fusion.2 = f32[2048,256]{1,0:T(8,128)S(1)} fusion(bf16[8,256,256]{2,1,0:T(8,128)(2,1)S(1)} %all-to-all-done.1, bf16[1024,8,256]{2,0,1:T(8,128)(2,1)} %copy.6, bf16[1024,8,256]{2,0,1:T(8,128)(2,1)} %copy.5), kind=kOutput, calls=%fused_computation.8 | convolution fusion | flops 2164260864 | bytes 11534336 | tf_op jit(solution)/shard_map/fjm,jmc->fc/dot_general | solution.py:206
  83.3 0.3 fusion.1
  83.6 1.0 fusion.81
  84.7 1.9 collective-permute-start.3
  86.5 11.5 %collective-permute-start.4 = (bf16[2048,128]{1,0:T(8,128)(2,1)}, bf16[2048,128]{1,0:T(8,128)(2,1)}, u32[]{:S(2)}, u32[]{:S(2)}) collective-permute-start(bf16[2048,128]{1,0:T(8,128)(2,1)} %get-tuple-element.31), channel_id=1, source_target_pairs={{0,8},{4,0},{12,4},{20,12},{28,20},{24,28},{16,24},{8,16},{1,9},{5... | collective-permute-start | bytes 1572872 | tf_op jit(solution)/shard_map/ppermute | solution.py:209
  98.1 2.0 fusion.21
  100.0 2.0 fusion.20
  102.0 1.2 multiply_add_fusion.3
  103.3 3.4 %all-to-all-done = bf16[8,256,256]{2,1,0:T(8,128)(2,1)} async-done(((bf16[8,256,256]{2,1,0:T(8,128)(2,1)}), bf16[8,256,256]{2,1,0:T(8,128)(2,1)}, u32[]{:S(2)}, u32[]{:S(2)}) %all-to-all-start) | async-done | bytes 1048608 | tf_op jit(solution)/shard_map/all_to_all | solution.py:201
  106.7 4.5 %all-to-all-start.3 = ((bf16[8,256,256]{2,1,0:T(8,128)(2,1)}), bf16[8,256,256]{2,1,0:T(8,128)(2,1)}, u32[]{:S(2)}, u32[]{:S(2)}) async-start(bf16[8,256,256]{2,1,0:T(8,128)(2,1)} %shard_map.49), calls=%async_computation.3 | async-start | bytes 2097152 | tf_op jit(solution)/shard_map/all_to_all | solution.py:201
  111.2 6.1 %convolution_bitcast_fusion.1 = f32[2048,256]{1,0:T(8,128)S(1)} fusion(bf16[8,256,256]{2,1,0:T(8,128)(2,1)} %all-to-all-done, bf16[1024,8,256]{2,0,1:T(8,128)(2,1)} %copy.6, bf16[1024,8,256]{2,0,1:T(8,128)(2,1)} %copy.5), kind=kOutput, calls=%fused_computation.7 | convolution fusion | flops 2164260864 | bytes 11534336 | tf_op jit(solution)/shard_map/fjm,jmc->fc/dot_general | solution.py:206
  117.6 0.3 fusion.4
  117.9 1.0 fusion.80
  119.0 4.4 %collective-permute-start.5 = (bf16[2048,128]{1,0:T(8,128)(2,1)}, bf16[2048,128]{1,0:T(8,128)(2,1)}, u32[]{:S(2)}, u32[]{:S(2)}) collective-permute-start(bf16[2048,128]{1,0:T(8,128)(2,1)} %get-tuple-element.29), channel_id=1, source_target_pairs={{0,4},{4,12},{12,20},{20,28},{28,24},{24,16},{16,8},{8,0},{1,5},{5... | collective-permute-start | bytes 1572872 | tf_op jit(solution)/shard_map/ppermute | solution.py:208
  123.3 9.2 %collective-permute-start.6 = (bf16[2048,128]{1,0:T(8,128)(2,1)}, bf16[2048,128]{1,0:T(8,128)(2,1)}, u32[]{:S(2)}, u32[]{:S(2)}) collective-permute-start(bf16[2048,128]{1,0:T(8,128)(2,1)} %get-tuple-element.30), channel_id=1, source_target_pairs={{0,8},{4,0},{12,4},{20,12},{28,20},{24,28},{16,24},{8,16},{1,9},{5... | collective-permute-start | bytes 1572872 | tf_op jit(solution)/shard_map/ppermute | solution.py:209
  132.5 2.0 fusion.19
  134.5 2.0 fusion.18
  136.5 1.6 multiply_add_fusion.2
  138.0 2.4 %all-to-all-done.3 = bf16[8,256,256]{2,1,0:T(8,128)(2,1)} async-done(((bf16[8,256,256]{2,1,0:T(8,128)(2,1)}), bf16[8,256,256]{2,1,0:T(8,128)(2,1)}, u32[]{:S(2)}, u32[]{:S(2)}) %all-to-all-start.3) | async-done | bytes 1048608 | tf_op jit(solution)/shard_map/all_to_all | solution.py:201
  140.4 3.4 %collective-permute-done.5 = bf16[2048,128]{1,0:T(8,128)(2,1)} collective-permute-done((bf16[2048,128]{1,0:T(8,128)(2,1)}, bf16[2048,128]{1,0:T(8,128)(2,1)}, u32[]{:S(2)}, u32[]{:S(2)}) %collective-permute-start.5) | collective-permute-done | bytes 524320 | tf_op jit(solution)/shard_map/ppermute | solution.py:208
  143.8 6.1 %convolution_bitcast_fusion = f32[2048,256]{1,0:T(8,128)S(1)} fusion(bf16[8,256,256]{2,1,0:T(8,128)(2,1)} %all-to-all-done.3, bf16[1024,8,256]{2,0,1:T(8,128)(2,1)} %copy.6, bf16[1024,8,256]{2,0,1:T(8,128)(2,1)} %copy.5), kind=kOutput, calls=%fused_computation.6 | convolution fusion | flops 2164260864 | bytes 11534336 | tf_op jit(solution)/shard_map/fjm,jmc->fc/dot_general | solution.py:206
  150.3 0.3 fusion.5
  150.6 5.0 %collective-permute-start.7 = (bf16[2048,128]{1,0:T(8,128)(2,1)S(1)}, bf16[2048,128]{1,0:T(8,128)(2,1)S(1)}, u32[]{:S(2)}, u32[]{:S(2)}) collective-permute-start(bf16[2048,128]{1,0:T(8,128)(2,1)S(1)} %get-tuple-element.27), channel_id=1, source_target_pairs={{0,4},{4,12},{12,20},{20,28},{28,24},{24,16},{16,8},{8,0},{1,5},{5... | collective-permute-start | bytes 1572872 | tf_op jit(solution)/shard_map/ppermute | solution.py:208
  155.6 1.8 collective-permute-start.8
  157.4 2.0 fusion.17
  159.4 2.0 fusion.16
  161.7 5.7 %collective-permute-done.7 = bf16[2048,128]{1,0:T(8,128)(2,1)S(1)} collective-permute-done((bf16[2048,128]{1,0:T(8,128)(2,1)S(1)}, bf16[2048,128]{1,0:T(8,128)(2,1)S(1)}, u32[]{:S(2)}, u32[]{:S(2)}) %collective-permute-start.7) | collective-permute-done | bytes 524320 | tf_op jit(solution)/shard_map/ppermute | solution.py:208
  167.3 1.8 collective-permute-done.8
  169.1 0.8 fusion.15
  169.9 0.8 fusion.14
  171.0 0.9 copy-done
  171.9 0.3 copy-done.1
  172.2 0.3 copy-done.2
  172.5 0.5 fusion.3
  173.3 2.7 %collective-permute-done.9 = f32[2048,128]{1,0:T(8,128)} collective-permute-done((f32[2048,128]{1,0:T(8,128)S(1)}, f32[2048,128]{1,0:T(8,128)}, u32[]{:S(2)}, u32[]{:S(2)}) %collective-permute-start.9) | collective-permute-done | bytes 1048608 | tf_op jit(solution)/shard_map/ppermute | solution.py:131
  176.0 5.0 %fusion.10 = f32[2048,128]{0,1:T(8,128)S(1)} fusion(bf16[2048,2048]{0,1:T(8,128)(2,1)} %pad_maximum_fusion, f32[2048,128]{1,0:T(8,128)} %collective-permute-done.9, f32[2048,256]{1,0:T(8,128)S(1)} %fusion.3, s32[]{:T(128)S(6)} %select_n.110, f32[2048]{0:T(1024)S(1)} %pad_maximum_fusion.14), kind=kOutput, calls=%fused_computation.42 | convolution fusion | flops 1074266112 | bytes 11542532 | tf_op jit(solution)/shard_map/dot_general | solution.py:137
  181.1 1.6 collective-permute-start.10
  182.7 12.5 %collective-permute-done.10 = f32[1024,128]{0,1:T(8,128)S(1)} collective-permute-done((f32[1024,128]{0,1:T(8,128)S(1)}, f32[1024,128]{0,1:T(8,128)S(1)}, u32[]{:S(2)}, u32[]{:S(2)}) %collective-permute-start.10) | collective-permute-done | bytes 524320 | tf_op jit(solution)/shard_map/ppermute | solution.py:144
  195.4 1.3 collective-permute-done.11
  196.7 0.4 convolution_convert_fusion
  197.1 21.9 %all_to_all.25 = bf16[8,80,512]{2,1,0:T(8,128)(2,1)S(1)} all-to-all(bf16[8,80,512]{2,1,0:T(8,128)(2,1)S(1)} %bitcast.54), channel_id=1, replica_groups=mesh['tile'=8,'win'=4] {'tile'}, dimensions={0} | all-to-all | bytes 1310720 | tf_op jit(solution)/shard_map/all_to_all | solution.py:229
  219.1 0.8 copy-done.3
  (60 shorter events, 2.9 us)
Async XLA Ops:
  0.0 9.7 %copy-start.6 = (s32[256]{0:T(256)S(1)}, s32[256]{0:T(256)}, u32[]{:S(2)}) copy-start(s32[256]{0:T(256)} %param.5) | copy-start | bytes 3076
  0.0 9.7 %copy-start.5 = (s32[256]{0:T(256)S(1)}, s32[256]{0:T(256)}, u32[]{:S(2)}) copy-start(s32[256]{0:T(256)} %param.6) | copy-start | bytes 3076
  0.0 9.7 %copy-start.4 = (s32[256,1]{0,1:T(1,128)S(1)}, s32[256,1]{0,1:T(1,128)}, u32[]{:S(2)}) copy-start(s32[256,1]{0,1:T(1,128)} %param.7) | copy-start | bytes 3076
  2.3 35.5 %all-to-all-start.2 = ((bf16[8,256,256]{2,1,0:T(8,128)(2,1)}), bf16[8,256,256]{2,1,0:T(8,128)(2,1)S(1)}, u32[]{:S(2)}, u32[]{:S(2)}) async-start(bf16[8,256,256]{2,1,0:T(8,128)(2,1)} %shard_map.48), calls=%async_computation.2 | async-start | bytes 2097152 | tf_op jit(solution)/shard_map/all_to_all | solution.py:201
  9.7 27.2 %collective-permute-start = (s32[3,256]{1,0:T(4,128)S(1)}, s32[3,256]{1,0:T(4,128)S(1)}, u32[]{:S(2)}, u32[]{:S(2)}) collective-permute-start(s32[3,256]{1,0:T(4,128)S(1)} %pad_add_fusion), channel_id=1, source_target_pairs={{0,0},{4,4},{8,12},{12,20},{16,28},{20,24},{24,16},{28,8},{1,1},{5... | collective-permute-start | bytes 9224 | tf_op jit(solution)/shard_map/ppermute | solution.py:193
  37.9 34.9 %all-to-all-start.1 = ((bf16[8,256,256]{2,1,0:T(8,128)(2,1)}), bf16[8,256,256]{2,1,0:T(8,128)(2,1)S(1)}, u32[]{:S(2)}, u32[]{:S(2)}) async-start(bf16[8,256,256]{2,1,0:T(8,128)(2,1)} %shard_map.47), calls=%async_computation.1 | async-start | bytes 2097152 | tf_op jit(solution)/shard_map/all_to_all | solution.py:201
  52.3 24.8 %collective-permute-start.1 = (bf16[2048,128]{1,0:T(8,128)(2,1)S(1)}, bf16[2048,128]{1,0:T(8,128)(2,1)}, u32[]{:S(2)}, u32[]{:S(2)}) collective-permute-start(bf16[2048,128]{1,0:T(8,128)(2,1)S(1)} %get-tuple-element.34), channel_id=1, source_target_pairs={{0,4},{4,12},{12,20},{20,28},{28,24},{24,16},{16,8},{8,0},{1,5},{5... | collective-permute-start | bytes 1572872 | tf_op jit(solution)/shard_map/ppermute | solution.py:208
  54.4 22.7 %collective-permute-start.2 = (bf16[2048,128]{1,0:T(8,128)(2,1)S(1)}, bf16[2048,128]{1,0:T(8,128)(2,1)}, u32[]{:S(2)}, u32[]{:S(2)}) collective-permute-start(bf16[2048,128]{1,0:T(8,128)(2,1)S(1)} %get-tuple-element.33), channel_id=1, source_target_pairs={{0,8},{4,0},{12,4},{20,12},{28,20},{24,28},{16,24},{8,16},{1,9},{5... | collective-permute-start | bytes 1572872 | tf_op jit(solution)/shard_map/ppermute | solution.py:209
  72.8 33.9 %all-to-all-start = ((bf16[8,256,256]{2,1,0:T(8,128)(2,1)}), bf16[8,256,256]{2,1,0:T(8,128)(2,1)}, u32[]{:S(2)}, u32[]{:S(2)}) async-start(bf16[8,256,256]{2,1,0:T(8,128)(2,1)} %shard_map.46), calls=%async_computation | async-start | bytes 2097152 | tf_op jit(solution)/shard_map/all_to_all | solution.py:201
  84.7 26.5 %collective-permute-start.3 = (bf16[2048,128]{1,0:T(8,128)(2,1)}, bf16[2048,128]{1,0:T(8,128)(2,1)}, u32[]{:S(2)}, u32[]{:S(2)}) collective-permute-start(bf16[2048,128]{1,0:T(8,128)(2,1)} %get-tuple-element.32), channel_id=1, source_target_pairs={{0,4},{4,12},{12,20},{20,28},{28,24},{24,16},{16,8},{8,0},{1,5},{5... | collective-permute-start | bytes 1572872 | tf_op jit(solution)/shard_map/ppermute | solution.py:208
  86.5 24.6 %collective-permute-start.4 = (bf16[2048,128]{1,0:T(8,128)(2,1)}, bf16[2048,128]{1,0:T(8,128)(2,1)}, u32[]{:S(2)}, u32[]{:S(2)}) collective-permute-start(bf16[2048,128]{1,0:T(8,128)(2,1)} %get-tuple-element.31), channel_id=1, source_target_pairs={{0,8},{4,0},{12,4},{20,12},{28,20},{24,28},{16,24},{8,16},{1,9},{5... | collective-permute-start | bytes 1572872 | tf_op jit(solution)/shard_map/ppermute | solution.py:209
  106.7 33.7 %all-to-all-start.3 = ((bf16[8,256,256]{2,1,0:T(8,128)(2,1)}), bf16[8,256,256]{2,1,0:T(8,128)(2,1)}, u32[]{:S(2)}, u32[]{:S(2)}) async-start(bf16[8,256,256]{2,1,0:T(8,128)(2,1)} %shard_map.49), calls=%async_computation.3 | async-start | bytes 2097152 | tf_op jit(solution)/shard_map/all_to_all | solution.py:201
  119.0 24.9 %collective-permute-start.5 = (bf16[2048,128]{1,0:T(8,128)(2,1)}, bf16[2048,128]{1,0:T(8,128)(2,1)}, u32[]{:S(2)}, u32[]{:S(2)}) collective-permute-start(bf16[2048,128]{1,0:T(8,128)(2,1)} %get-tuple-element.29), channel_id=1, source_target_pairs={{0,4},{4,12},{12,20},{20,28},{28,24},{24,16},{16,8},{8,0},{1,5},{5... | collective-permute-start | bytes 1572872 | tf_op jit(solution)/shard_map/ppermute | solution.py:208
  123.3 20.5 %collective-permute-start.6 = (bf16[2048,128]{1,0:T(8,128)(2,1)}, bf16[2048,128]{1,0:T(8,128)(2,1)}, u32[]{:S(2)}, u32[]{:S(2)}) collective-permute-start(bf16[2048,128]{1,0:T(8,128)(2,1)} %get-tuple-element.30), channel_id=1, source_target_pairs={{0,8},{4,0},{12,4},{20,12},{28,20},{24,28},{16,24},{8,16},{1,9},{5... | collective-permute-start | bytes 1572872 | tf_op jit(solution)/shard_map/ppermute | solution.py:209
  150.6 16.7 %collective-permute-start.7 = (bf16[2048,128]{1,0:T(8,128)(2,1)S(1)}, bf16[2048,128]{1,0:T(8,128)(2,1)S(1)}, u32[]{:S(2)}, u32[]{:S(2)}) collective-permute-start(bf16[2048,128]{1,0:T(8,128)(2,1)S(1)} %get-tuple-element.27), channel_id=1, source_target_pairs={{0,4},{4,12},{12,20},{20,28},{28,24},{24,16},{16,8},{8,0},{1,5},{5... | collective-permute-start | bytes 1572872 | tf_op jit(solution)/shard_map/ppermute | solution.py:208
  155.6 13.5 %collective-permute-start.8 = (bf16[2048,128]{1,0:T(8,128)(2,1)S(1)}, bf16[2048,128]{1,0:T(8,128)(2,1)S(1)}, u32[]{:S(2)}, u32[]{:S(2)}) collective-permute-start(bf16[2048,128]{1,0:T(8,128)(2,1)S(1)} %get-tuple-element.28), channel_id=1, source_target_pairs={{0,8},{4,0},{12,4},{20,12},{28,20},{24,28},{16,24},{8,16},{1,9},{5... | collective-permute-start | bytes 1572872 | tf_op jit(solution)/shard_map/ppermute | solution.py:209
  170.7 1.2 copy-start
  170.7 1.5 copy-start.1
  170.7 1.8 copy-start.2
  173.2 2.9 %collective-permute-start.9 = (f32[2048,128]{1,0:T(8,128)S(1)}, f32[2048,128]{1,0:T(8,128)}, u32[]{:S(2)}, u32[]{:S(2)}) collective-permute-start(f32[2048,128]{1,0:T(8,128)S(1)} %constant_dynamic-slice_fusion.3), channel_id=1, source_target_pairs={{0,1},{1,0},{2,3},{3,2},{4,5},{5,4},{6,7},{7,6},{8,9},{9,8},{10,11... | collective-permute-start | bytes 3145736 | tf_op jit(solution)/shard_map/ppermute | solution.py:131
  181.1 14.1 %collective-permute-start.10 = (f32[1024,128]{0,1:T(8,128)S(1)}, f32[1024,128]{0,1:T(8,128)S(1)}, u32[]{:S(2)}, u32[]{:S(2)}) collective-permute-start(f32[1024,128]{0,1:T(8,128)S(1)} %constant_dynamic-slice_fusion.2), channel_id=1, source_target_pairs={{0,2},{1,3},{2,0},{3,1},{4,6},{5,7},{6,4},{7,5},{8,10},{9,11},{10,... | collective-permute-start | bytes 1572872 | tf_op jit(solution)/shard_map/ppermute | solution.py:144
  195.3 1.4 collective-permute-start.11
  219.1 0.8 copy-start.3

commit v18 on v17

--- a/solution.py
+++ b/solution.py
@@ -189,7 +189,7 @@
         seg_total = records.shape[0] * win_count
         block = records.shape[2] // tile_count
         half = block // 2
-        forward = forward_matrix(length).reshape(length, tile_count, records.shape[1])
+        forward = forward_matrix(length)
         my_first, my_offset, my_owners = lax.ppermute(pair_data, "tile", to_owner)
         channel_ids = jnp.arange(2 * block, dtype=jnp.int32)[:, None]
         pick_first = (channel_ids == my_first[None, :]).astype(jnp.bfloat16)
@@ -203,7 +203,7 @@
                 received, _ = lax.optimization_barrier((received, arrived[-1]))
             if segment == min(2, records.shape[0] - 1):
                 received, table = lax.optimization_barrier((received, inverse_table(length, lag_start)))
-            spectra = jnp.einsum("fjm,jmc->fc", forward, received, preferred_element_type=jnp.float32)
+            spectra = jnp.dot(forward, received.reshape(length, block), preferred_element_type=jnp.float32)
             whitened = whiten(spectra, BAND)
             from_prev = lax.ppermute(whitened[:, half:], "tile", to_next)
             from_next = lax.ppermute(whitened[:, :half], "tile", to_prev)

time: 221 us -> 215 us (0.973)
  waiting for transfers between devices: 35.1 us -> 52.7 us
  local copies, waits for them, and re-layouts: 18.2 us -> 5.35 us
  starting transfers between devices: 62.3 us -> 51.6 us
    all_to_all x4, waiting for transfers between devices: 7.66 us -> 23.8 us  [per_device(): lax.all_to_all(outgoing, 'tile', split_axis=0, concat_axis=0, tiled=True)]
    neg x1 -> x0, local copies, waits for them, and re-layouts: 6.45 us -> none  [forward_matrix(): return jnp.concatenate([cosine, -sine], axis=0).astype(jnp.bfloat16)]
    sub x1 -> x0, local copies, waits for them, and re-layouts: 6.42 us -> none  [phase_table(): cosine = (c_hi * c_lo - s_hi * s_lo).reshape(shape)]
    ppermute x4, starting transfers between devices: 22.8 us -> 16.5 us  [per_device(): from_next = lax.ppermute(whitened[:, :half], 'tile', to_prev)]
    all_to_all x4, starting transfers between devices: 23.8 us -> 19.8 us  [per_device(): lax.all_to_all(outgoing, 'tile', split_axis=0, concat_axis=0, tiled=True)]
  transfers between devices with their start and end apart: 16 -> 16, of which waited for: 9 -> 10; matrix products, arithmetic and copies ran while one was open for 33% -> 28% of each run, Pallas kernels for 3% -> 3%
where the time goes in v18:
time: 215 us
  waiting for transfers between devices  52.7 us (25%)
  starting transfers between devices  51.6 us (24%)
  matrix products  43.4 us (20%)
  other arithmetic  29.6 us (14%)
  blocking collectives  22 us (10%)
  Pallas kernels  9.3 us (4%)
  local copies, waits for them, and re-layouts  5.35 us (2%)
    dot_general x4, matrix products, per_device(): jnp.dot(forward, received.reshape(length, block), preferred_element_type=...  24.7 us
    all_to_all x4, waiting for transfers between devices, per_device(): lax.all_to_all(outgoing, 'tile', split_axis=0, concat_axis=0, tiled=True)  23.8 us
    all_to_all x1, blocking collectives, per_device(): lax.all_to_all(buckets, 'tile', split_axis=0, concat_axis=0, tiled=True)  22 us
    all_to_all x4, starting transfers between devices, per_device(): lax.all_to_all(outgoing, 'tile', split_axis=0, concat_axis=0, tiled=True)  19.8 us
    ppermute x4, starting transfers between devices, per_device(): from_next = lax.ppermute(whitened[:, :half], 'tile', to_prev)  16.5 us
    ppermute x4, starting transfers between devices, per_device(): from_prev = lax.ppermute(whitened[:, half:], 'tile', to_next)  13 us
    ppermute x1, waiting for transfers between devices, sum_and_invert(): lax.ppermute(send, 'win', [(w, w ^ 2 * bit) for w in range(win_count)])  12.5 us
    ppermute x4, waiting for transfers between devices, per_device(): from_prev = lax.ppermute(whitened[:, half:], 'tile', to_next)  10.9 us
  transfers between devices with their start and end apart: 16, of which 10 were waited for; matrix products, arithmetic and copies ran while one was open for 28% of the time, Pallas kernels for 3%

profile of v18, /device:TPU:0, one launch (start us, length us, event | category | flops | bytes accessed | tf_op | source)
XLA Modules:
  0.0 214.5 jit_solution(18173294666894341493)
XLA Ops:
  0.0 2.3 %shard_map.48 = bf16[8,256,256]{2,1,0:T(8,128)(2,1)} custom-call(bf16[4,256,2048]{2,1,0:T(8,128)(2,1)} %src.7), custom_call_target="tpu_custom_call" | custom-call | tf_op jit(solution)/shard_map/pallas_call | solution.py:166
  2.3 7.3 %all-to-all-start.2 = ((bf16[8,256,256]{2,1,0:T(8,128)(2,1)}), bf16[8,256,256]{2,1,0:T(8,128)(2,1)S(1)}, u32[]{:S(2)}, u32[]{:S(2)}) async-start(bf16[8,256,256]{2,1,0:T(8,128)(2,1)} %shard_map.48), calls=%async_computation.2 | async-start | bytes 2097152 | tf_op jit(solution)/shard_map/all_to_all | solution.py:201
  9.7 0.7 collective-permute-start
  10.4 1.0 fusion.58
  11.4 0.6 fusion.66
  12.0 5.0 %subtract_convert_fusion = (bf16[1024,32,64]{0,2,1:T(8,128)(2,1)}, bf16[1024,32,64]{0,2,1:T(8,128)(2,1)}) fusion(f32[1024,64]{0,1:T(8,128)S(1)} %get-tuple-element.48, f32[1024,32]{0,1:T(8,128)S(1)} %get-tuple-element.47, f32[1024,64]{0,1:T(8,128)S(1)} %get-tuple-element.49, f32[1024,32]{0,1:T(8,128)S(1)} %get-tuple-element.46), kind=kLoop, calls=%fused_computation.5 | loop fusion | flops 18874368 | bytes 9175040 | tf_op jit(solution)/shard_map/convert.3
  17.0 2.3 %shard_map.47 = bf16[8,256,256]{2,1,0:T(8,128)(2,1)} custom-call(bf16[4,256,2048]{2,1,0:T(8,128)(2,1)} %src.7), custom_call_target="tpu_custom_call" | custom-call | tf_op jit(solution)/shard_map/pallas_call | solution.py:166
  19.3 2.3 %shard_map.46 = bf16[8,256,256]{2,1,0:T(8,128)(2,1)} custom-call(bf16[4,256,2048]{2,1,0:T(8,128)(2,1)} %src.7), custom_call_target="tpu_custom_call" | custom-call | tf_op jit(solution)/shard_map/pallas_call | solution.py:166
  21.6 2.4 %shard_map.49 = bf16[8,256,256]{2,1,0:T(8,128)(2,1)} custom-call(bf16[4,256,2048]{2,1,0:T(8,128)(2,1)} %src.7), custom_call_target="tpu_custom_call" | custom-call | tf_op jit(solution)/shard_map/pallas_call | solution.py:166
  24.0 0.6 reduce-window.6
  24.9 10.5 %all-to-all-done.2 = bf16[8,256,256]{2,1,0:T(8,128)(2,1)S(1)} async-done(((bf16[8,256,256]{2,1,0:T(8,128)(2,1)}), bf16[8,256,256]{2,1,0:T(8,128)(2,1)S(1)}, u32[]{:S(2)}, u32[]{:S(2)}) %all-to-all-start.2) | async-done | bytes 1048608 | tf_op jit(solution)/shard_map/all_to_all | solution.py:201
  35.4 3.8 %all-to-all-start.1 = ((bf16[8,256,256]{2,1,0:T(8,128)(2,1)}), bf16[8,256,256]{2,1,0:T(8,128)(2,1)S(1)}, u32[]{:S(2)}, u32[]{:S(2)}) async-start(bf16[8,256,256]{2,1,0:T(8,128)(2,1)} %shard_map.47), calls=%async_computation.1 | async-start | bytes 2097152 | tf_op jit(solution)/shard_map/all_to_all | solution.py:201
  39.2 6.1 %fusion.82 = f32[2048,256]{1,0:T(8,128)S(1)} fusion(bf16[2048,256]{1,0:T(8,128)(2,1)S(1)} %bitcast.56, bf16[1024,2048]{0,1:T(8,128)(2,1)} %bitcast.48, bf16[1024,2048]{0,1:T(8,128)(2,1)} %bitcast.44), kind=kOutput, calls=%fused_computation.165 | convolution fusion | flops 2164260864 | bytes 11534336 | tf_op jit(solution)/shard_map/dot_general | solution.py:206
  45.6 0.3 fusion
  45.9 2.1 collective-permute-start.1
  48.3 0.6 fusion.64
  48.9 2.0 fusion.47
  50.9 5.3 %multiply_subtract_fusion = (bf16[2048,16,64]{0,2,1:T(8,128)(2,1)}, bf16[2048,16,64]{0,2,1:T(8,128)(2,1)}) fusion(f32[2048,64]{0,1:T(8,128)S(1)} %get-tuple-element.42, f32[2048,16]{0,1:T(8,128)S(1)} %get-tuple-element.40, f32[2048,64]{0,1:T(8,128)S(1)} %get-tuple-element.41, f32[2048,16]{0,1:T(8,128)S(1)} %get-tuple-element.39), kind=kLoop, calls=%fused_computation.3 | loop fusion | flops 18874368 | bytes 9699328 | tf_op jit(solution)/shard_map/sub | solution.py:25
  56.2 8.4 %pad_maximum_fusion = bf16[2048,2048]{0,1:T(8,128)(2,1)} fusion(bf16[2048,1024]{0,1:T(8,128)(2,1)} %bitcast.43, bf16[2048,1024]{0,1:T(8,128)(2,1)} %bitcast.42), kind=kLoop, calls=%fused_computation | loop fusion | flops 16777216 | bytes 16777216 | tf_op jit(solution)/shard_map/concatenate | solution.py:116
  64.6 1.8 all-to-all-done.1
  66.4 4.2 %all-to-all-start = ((bf16[8,256,256]{2,1,0:T(8,128)(2,1)}), bf16[8,256,256]{2,1,0:T(8,128)(2,1)}, u32[]{:S(2)}, u32[]{:S(2)}) async-start(bf16[8,256,256]{2,1,0:T(8,128)(2,1)} %shard_map.46), calls=%async_computation | async-start | bytes 2097152 | tf_op jit(solution)/shard_map/all_to_all | solution.py:201
  70.6 6.1 %fusion.81 = f32[2048,256]{1,0:T(8,128)S(1)} fusion(bf16[2048,256]{1,0:T(8,128)(2,1)S(1)} %bitcast.57, bf16[1024,2048]{0,1:T(8,128)(2,1)} %bitcast.49, bf16[1024,2048]{0,1:T(8,128)(2,1)} %bitcast.45), kind=kOutput, calls=%fused_computation.164 | convolution fusion | flops 2164260864 | bytes 11534336 | tf_op jit(solution)/shard_map/dot_general | solution.py:206
  77.0 0.3 fusion.1
  77.3 1.0 fusion.85
  78.3 1.9 collective-permute-start.3
  80.2 7.3 %collective-permute-start.4 = (bf16[2048,128]{1,0:T(8,128)(2,1)}, bf16[2048,128]{1,0:T(8,128)(2,1)}, u32[]{:S(2)}, u32[]{:S(2)}) collective-permute-start(bf16[2048,128]{1,0:T(8,128)(2,1)} %get-tuple-element.31), channel_id=1, source_target_pairs={{0,8},{4,0},{12,4},{20,12},{28,20},{24,28},{16,24},{8,16},{1,9},{5... | collective-permute-start | bytes 1572872 | tf_op jit(solution)/shard_map/ppermute | solution.py:209
  87.5 2.0 fusion.21
  89.5 2.0 fusion.20
  91.4 1.2 multiply_add_fusion.3
  92.7 7.5 %all-to-all-done = bf16[8,256,256]{2,1,0:T(8,128)(2,1)} async-done(((bf16[8,256,256]{2,1,0:T(8,128)(2,1)}), bf16[8,256,256]{2,1,0:T(8,128)(2,1)}, u32[]{:S(2)}, u32[]{:S(2)}) %all-to-all-start) | async-done | bytes 1048608 | tf_op jit(solution)/shard_map/all_to_all | solution.py:201
  100.2 4.5 %all-to-all-start.3 = ((bf16[8,256,256]{2,1,0:T(8,128)(2,1)}), bf16[8,256,256]{2,1,0:T(8,128)(2,1)}, u32[]{:S(2)}, u32[]{:S(2)}) async-start(bf16[8,256,256]{2,1,0:T(8,128)(2,1)} %shard_map.49), calls=%async_computation.3 | async-start | bytes 2097152 | tf_op jit(solution)/shard_map/all_to_all | solution.py:201
  104.7 6.3 %fusion.80 = f32[2048,256]{1,0:T(8,128)S(1)} fusion(bf16[2048,256]{1,0:T(8,128)(2,1)} %bitcast.21, bf16[1024,2048]{0,1:T(8,128)(2,1)} %bitcast.50, bf16[1024,2048]{0,1:T(8,128)(2,1)} %bitcast.46), kind=kOutput, calls=%fused_computation.163 | convolution fusion | flops 2164260864 | bytes 11534336 | tf_op jit(solution)/shard_map/dot_general | solution.py:206
  111.3 0.3 fusion.4
  111.6 1.0 fusion.84
  112.6 5.0 %collective-permute-start.5 = (bf16[2048,128]{1,0:T(8,128)(2,1)}, bf16[2048,128]{1,0:T(8,128)(2,1)}, u32[]{:S(2)}, u32[]{:S(2)}) collective-permute-start(bf16[2048,128]{1,0:T(8,128)(2,1)} %get-tuple-element.29), channel_id=1, source_target_pairs={{0,4},{4,12},{12,20},{20,28},{28,24},{24,16},{16,8},{8,0},{1,5},{5... | collective-permute-start | bytes 1572872 | tf_op jit(solution)/shard_map/ppermute | solution.py:208
  117.6 6.8 %collective-permute-start.6 = (bf16[2048,128]{1,0:T(8,128)(2,1)}, bf16[2048,128]{1,0:T(8,128)(2,1)}, u32[]{:S(2)}, u32[]{:S(2)}) collective-permute-start(bf16[2048,128]{1,0:T(8,128)(2,1)} %get-tuple-element.30), channel_id=1, source_target_pairs={{0,8},{4,0},{12,4},{20,12},{28,20},{24,28},{16,24},{8,16},{1,9},{5... | collective-permute-start | bytes 1572872 | tf_op jit(solution)/shard_map/ppermute | solution.py:209
  124.4 2.0 fusion.19
  126.4 2.0 fusion.18
  128.4 1.6 multiply_add_fusion.2
  130.0 4.0 %all-to-all-done.3 = bf16[8,256,256]{2,1,0:T(8,128)(2,1)} async-done(((bf16[8,256,256]{2,1,0:T(8,128)(2,1)}), bf16[8,256,256]{2,1,0:T(8,128)(2,1)}, u32[]{:S(2)}, u32[]{:S(2)}) %all-to-all-start.3) | async-done | bytes 1048608 | tf_op jit(solution)/shard_map/all_to_all | solution.py:201
  134.0 4.7 %collective-permute-done.5 = bf16[2048,128]{1,0:T(8,128)(2,1)} collective-permute-done((bf16[2048,128]{1,0:T(8,128)(2,1)}, bf16[2048,128]{1,0:T(8,128)(2,1)}, u32[]{:S(2)}, u32[]{:S(2)}) %collective-permute-start.5) | collective-permute-done | bytes 524320 | tf_op jit(solution)/shard_map/ppermute | solution.py:208
  138.6 6.3 %fusion.79 = f32[2048,256]{1,0:T(8,128)S(1)} fusion(bf16[2048,256]{1,0:T(8,128)(2,1)} %bitcast.24, bf16[1024,2048]{0,1:T(8,128)(2,1)} %bitcast.51, bf16[1024,2048]{0,1:T(8,128)(2,1)} %bitcast.47), kind=kOutput, calls=%fused_computation.162 | convolution fusion | flops 2164260864 | bytes 11534336 | tf_op jit(solution)/shard_map/dot_general | solution.py:206
  145.2 0.3 fusion.5
  145.6 4.0 %collective-permute-start.7 = (bf16[2048,128]{1,0:T(8,128)(2,1)S(1)}, bf16[2048,128]{1,0:T(8,128)(2,1)S(1)}, u32[]{:S(2)}, u32[]{:S(2)}) collective-permute-start(bf16[2048,128]{1,0:T(8,128)(2,1)S(1)} %get-tuple-element.27), channel_id=1, source_target_pairs={{0,4},{4,12},{12,20},{20,28},{28,24},{24,16},{16,8},{8,0},{1,5},{5... | collective-permute-start | bytes 1572872 | tf_op jit(solution)/shard_map/ppermute | solution.py:208
  149.6 2.1 collective-permute-start.8
  151.8 2.0 fusion.17
  153.7 2.0 fusion.16
  155.7 0.3 multiply_add_fusion.1
  156.0 6.3 %collective-permute-done.7 = bf16[2048,128]{1,0:T(8,128)(2,1)S(1)} collective-permute-done((bf16[2048,128]{1,0:T(8,128)(2,1)S(1)}, bf16[2048,128]{1,0:T(8,128)(2,1)S(1)}, u32[]{:S(2)}, u32[]{:S(2)}) %collective-permute-start.7) | collective-permute-done | bytes 524320 | tf_op jit(solution)/shard_map/ppermute | solution.py:208
  162.3 1.4 collective-permute-done.8
  163.6 0.8 fusion.15
  164.4 0.8 fusion.14
  165.5 0.9 copy-done
  166.4 0.3 copy-done.1
  166.7 0.3 copy-done.2
  167.0 0.5 fusion.3
  167.8 2.7 %collective-permute-done.9 = f32[2048,128]{1,0:T(8,128)} collective-permute-done((f32[2048,128]{1,0:T(8,128)S(1)}, f32[2048,128]{1,0:T(8,128)}, u32[]{:S(2)}, u32[]{:S(2)}) %collective-permute-start.9) | collective-permute-done | bytes 1048608 | tf_op jit(solution)/shard_map/ppermute | solution.py:131
  170.5 5.0 %fusion.10 = f32[2048,128]{0,1:T(8,128)S(1)} fusion(bf16[2048,2048]{0,1:T(8,128)(2,1)} %pad_maximum_fusion, f32[2048,128]{1,0:T(8,128)} %collective-permute-done.9, f32[2048,256]{1,0:T(8,128)S(1)} %fusion.3, s32[]{:T(128)S(6)} %select_n.110, f32[2048]{0:T(1024)S(1)} %pad_maximum_fusion.14), kind=kOutput, calls=%fused_computation.38 | convolution fusion | flops 1074266112 | bytes 11542532 | tf_op jit(solution)/shard_map/dot_general | solution.py:137
  175.6 1.6 collective-permute-start.10
  177.2 12.5 %collective-permute-done.10 = f32[1024,128]{0,1:T(8,128)S(1)} collective-permute-done((f32[1024,128]{0,1:T(8,128)S(1)}, f32[1024,128]{0,1:T(8,128)S(1)}, u32[]{:S(2)}, u32[]{:S(2)}) %collective-permute-start.10) | collective-permute-done | bytes 524320 | tf_op jit(solution)/shard_map/ppermute | solution.py:144
  189.9 1.3 collective-permute-done.11
  191.2 0.4 convolution_convert_fusion
  191.6 22.0 %all_to_all.25 = bf16[8,80,512]{2,1,0:T(8,128)(2,1)S(1)} all-to-all(bf16[8,80,512]{2,1,0:T(8,128)(2,1)S(1)} %bitcast.58), channel_id=1, replica_groups=mesh['tile'=8,'win'=4] {'tile'}, dimensions={0} | all-to-all | bytes 1310720 | tf_op jit(solution)/shard_map/all_to_all | solution.py:229
  213.7 0.8 copy-done.3
  (58 shorter events, 2.6 us)
Async XLA Ops:
  0.0 9.7 %copy-start.6 = (s32[256]{0:T(256)S(1)}, s32[256]{0:T(256)}, u32[]{:S(2)}) copy-start(s32[256]{0:T(256)} %param.5) | copy-start | bytes 3076
  0.0 9.7 %copy-start.5 = (s32[256]{0:T(256)S(1)}, s32[256]{0:T(256)}, u32[]{:S(2)}) copy-start(s32[256]{0:T(256)} %param.6) | copy-start | bytes 3076
  0.0 9.7 %copy-start.4 = (s32[256,1]{0,1:T(1,128)S(1)}, s32[256,1]{0,1:T(1,128)}, u32[]{:S(2)}) copy-start(s32[256,1]{0,1:T(1,128)} %param.7) | copy-start | bytes 3076
  2.3 33.1 %all-to-all-start.2 = ((bf16[8,256,256]{2,1,0:T(8,128)(2,1)}), bf16[8,256,256]{2,1,0:T(8,128)(2,1)S(1)}, u32[]{:S(2)}, u32[]{:S(2)}) async-start(bf16[8,256,256]{2,1,0:T(8,128)(2,1)} %shard_map.48), calls=%async_computation.2 | async-start | bytes 2097152 | tf_op jit(solution)/shard_map/all_to_all | solution.py:201
  9.7 14.3 %collective-permute-start = (s32[3,256]{1,0:T(4,128)S(1)}, s32[3,256]{1,0:T(4,128)S(1)}, u32[]{:S(2)}, u32[]{:S(2)}) collective-permute-start(s32[3,256]{1,0:T(4,128)S(1)} %pad_add_fusion), channel_id=1, source_target_pairs={{0,0},{4,4},{8,12},{12,20},{16,28},{20,24},{24,16},{28,8},{1,1},{5... | collective-permute-start | bytes 9224 | tf_op jit(solution)/shard_map/ppermute | solution.py:193
  35.4 30.9 %all-to-all-start.1 = ((bf16[8,256,256]{2,1,0:T(8,128)(2,1)}), bf16[8,256,256]{2,1,0:T(8,128)(2,1)S(1)}, u32[]{:S(2)}, u32[]{:S(2)}) async-start(bf16[8,256,256]{2,1,0:T(8,128)(2,1)} %shard_map.47), calls=%async_computation.1 | async-start | bytes 2097152 | tf_op jit(solution)/shard_map/all_to_all | solution.py:201
  45.9 24.7 %collective-permute-start.1 = (bf16[2048,128]{1,0:T(8,128)(2,1)S(1)}, bf16[2048,128]{1,0:T(8,128)(2,1)}, u32[]{:S(2)}, u32[]{:S(2)}) collective-permute-start(bf16[2048,128]{1,0:T(8,128)(2,1)S(1)} %get-tuple-element.34), channel_id=1, source_target_pairs={{0,4},{4,12},{12,20},{20,28},{28,24},{24,16},{16,8},{8,0},{1,5},{5... | collective-permute-start | bytes 1572872 | tf_op jit(solution)/shard_map/ppermute | solution.py:208
  48.0 22.6 %collective-permute-start.2 = (bf16[2048,128]{1,0:T(8,128)(2,1)S(1)}, bf16[2048,128]{1,0:T(8,128)(2,1)}, u32[]{:S(2)}, u32[]{:S(2)}) collective-permute-start(bf16[2048,128]{1,0:T(8,128)(2,1)S(1)} %get-tuple-element.33), channel_id=1, source_target_pairs={{0,8},{4,0},{12,4},{20,12},{28,20},{24,28},{16,24},{8,16},{1,9},{5... | collective-permute-start | bytes 1572872 | tf_op jit(solution)/shard_map/ppermute | solution.py:209
  66.4 33.9 %all-to-all-start = ((bf16[8,256,256]{2,1,0:T(8,128)(2,1)}), bf16[8,256,256]{2,1,0:T(8,128)(2,1)}, u32[]{:S(2)}, u32[]{:S(2)}) async-start(bf16[8,256,256]{2,1,0:T(8,128)(2,1)} %shard_map.46), calls=%async_computation | async-start | bytes 2097152 | tf_op jit(solution)/shard_map/all_to_all | solution.py:201
  78.3 26.4 %collective-permute-start.3 = (bf16[2048,128]{1,0:T(8,128)(2,1)}, bf16[2048,128]{1,0:T(8,128)(2,1)}, u32[]{:S(2)}, u32[]{:S(2)}) collective-permute-start(bf16[2048,128]{1,0:T(8,128)(2,1)} %get-tuple-element.32), channel_id=1, source_target_pairs={{0,4},{4,12},{12,20},{20,28},{28,24},{24,16},{16,8},{8,0},{1,5},{5... | collective-permute-start | bytes 1572872 | tf_op jit(solution)/shard_map/ppermute | solution.py:208
  80.2 24.5 %collective-permute-start.4 = (bf16[2048,128]{1,0:T(8,128)(2,1)}, bf16[2048,128]{1,0:T(8,128)(2,1)}, u32[]{:S(2)}, u32[]{:S(2)}) collective-permute-start(bf16[2048,128]{1,0:T(8,128)(2,1)} %get-tuple-element.31), channel_id=1, source_target_pairs={{0,8},{4,0},{12,4},{20,12},{28,20},{24,28},{16,24},{8,16},{1,9},{5... | collective-permute-start | bytes 1572872 | tf_op jit(solution)/shard_map/ppermute | solution.py:209
  100.2 33.8 %all-to-all-start.3 = ((bf16[8,256,256]{2,1,0:T(8,128)(2,1)}), bf16[8,256,256]{2,1,0:T(8,128)(2,1)}, u32[]{:S(2)}, u32[]{:S(2)}) async-start(bf16[8,256,256]{2,1,0:T(8,128)(2,1)} %shard_map.49), calls=%async_computation.3 | async-start | bytes 2097152 | tf_op jit(solution)/shard_map/all_to_all | solution.py:201
  112.6 26.0 %collective-permute-start.5 = (bf16[2048,128]{1,0:T(8,128)(2,1)}, bf16[2048,128]{1,0:T(8,128)(2,1)}, u32[]{:S(2)}, u32[]{:S(2)}) collective-permute-start(bf16[2048,128]{1,0:T(8,128)(2,1)} %get-tuple-element.29), channel_id=1, source_target_pairs={{0,4},{4,12},{12,20},{20,28},{28,24},{24,16},{16,8},{8,0},{1,5},{5... | collective-permute-start | bytes 1572872 | tf_op jit(solution)/shard_map/ppermute | solution.py:208
  117.6 21.0 %collective-permute-start.6 = (bf16[2048,128]{1,0:T(8,128)(2,1)}, bf16[2048,128]{1,0:T(8,128)(2,1)}, u32[]{:S(2)}, u32[]{:S(2)}) collective-permute-start(bf16[2048,128]{1,0:T(8,128)(2,1)} %get-tuple-element.30), channel_id=1, source_target_pairs={{0,8},{4,0},{12,4},{20,12},{28,20},{24,28},{16,24},{8,16},{1,9},{5... | collective-permute-start | bytes 1572872 | tf_op jit(solution)/shard_map/ppermute | solution.py:209
  145.6 16.7 %collective-permute-start.7 = (bf16[2048,128]{1,0:T(8,128)(2,1)S(1)}, bf16[2048,128]{1,0:T(8,128)(2,1)S(1)}, u32[]{:S(2)}, u32[]{:S(2)}) collective-permute-start(bf16[2048,128]{1,0:T(8,128)(2,1)S(1)} %get-tuple-element.27), channel_id=1, source_target_pairs={{0,4},{4,12},{12,20},{20,28},{28,24},{24,16},{16,8},{8,0},{1,5},{5... | collective-permute-start | bytes 1572872 | tf_op jit(solution)/shard_map/ppermute | solution.py:208
  149.6 14.0 %collective-permute-start.8 = (bf16[2048,128]{1,0:T(8,128)(2,1)S(1)}, bf16[2048,128]{1,0:T(8,128)(2,1)S(1)}, u32[]{:S(2)}, u32[]{:S(2)}) collective-permute-start(bf16[2048,128]{1,0:T(8,128)(2,1)S(1)} %get-tuple-element.28), channel_id=1, source_target_pairs={{0,8},{4,0},{12,4},{20,12},{28,20},{24,28},{16,24},{8,16},{1,9},{5... | collective-permute-start | bytes 1572872 | tf_op jit(solution)/shard_map/ppermute | solution.py:209
  165.2 1.2 copy-start
  165.2 1.5 copy-start.1
  165.2 1.8 copy-start.2
  167.7 2.9 %collective-permute-start.9 = (f32[2048,128]{1,0:T(8,128)S(1)}, f32[2048,128]{1,0:T(8,128)}, u32[]{:S(2)}, u32[]{:S(2)}) collective-permute-start(f32[2048,128]{1,0:T(8,128)S(1)} %constant_dynamic-slice_fusion.3), channel_id=1, source_target_pairs={{0,1},{1,0},{2,3},{3,2},{4,5},{5,4},{6,7},{7,6},{8,9},{9,8},{10,11... | collective-permute-start | bytes 3145736 | tf_op jit(solution)/shard_map/ppermute | solution.py:131
  175.6 14.1 %collective-permute-start.10 = (f32[1024,128]{0,1:T(8,128)S(1)}, f32[1024,128]{0,1:T(8,128)S(1)}, u32[]{:S(2)}, u32[]{:S(2)}) collective-permute-start(f32[1024,128]{0,1:T(8,128)S(1)} %constant_dynamic-slice_fusion.2), channel_id=1, source_target_pairs={{0,2},{1,3},{2,0},{3,1},{4,6},{5,7},{6,4},{7,5},{8,10},{9,11},{10,... | collective-permute-start | bytes 1572872 | tf_op jit(solution)/shard_map/ppermute | solution.py:144
  189.8 1.4 collective-permute-start.11
  213.7 0.8 copy-start.3

commit v19 on v18

--- a/solution.py
+++ b/solution.py
@@ -134,7 +134,7 @@
         1.0 / math.sqrt(half_bins * seg_total)
     )
     scaled = total * jnp.concatenate([weights, weights])[:, None]
-    lags = jnp.dot(table, scaled, preferred_element_type=jnp.float32)
+    lags = jnp.dot(table, scaled, precision=lax.Precision.HIGH)
     bit = win_count // 4
     while bit >= 1:
         rows = lags.shape[0] // 2

time: 215 us -> 219 us (1.019)
  other arithmetic: 29.6 us -> 24.9 us
  matrix products: 43.4 us -> 47.1 us
  starting transfers between devices: 51.6 us -> 54.5 us
    dot_general x1, matrix products: 5.05 us -> 8.79 us  [sum_and_invert(): lags = jnp.dot(table, scaled, precision=lax.Precision.HIGH)]
    ppermute x4, starting transfers between devices: 16.5 us -> 19.4 us  [per_device(): from_next = lax.ppermute(whitened[:, :half], 'tile', to_prev)]
    sub x1, other arithmetic: 5.29 us -> 2.38 us  [phase_table(): cosine = (c_hi * c_lo - s_hi * s_lo).reshape(shape)]
  transfers between devices with their start and end apart: 16 -> 16, of which waited for: 10 -> 11; matrix products, arithmetic and copies ran while one was open for 28% -> 26% of each run, Pallas kernels for 3% -> 3%
where the time goes in v19:
time: 219 us; the launch traced here: 218 us
  waiting for transfers between devices  54.6 us (25%)
  starting transfers between devices  54.5 us (25%)
  matrix products  47.1 us (22%)
  other arithmetic  24.9 us (11%)
  blocking collectives  21.9 us (10%)
  Pallas kernels  9.3 us (4%)
  local copies, waits for them, and re-layouts  5.35 us (2%)
    all_to_all x4, waiting for transfers between devices, per_device(): lax.all_to_all(outgoing, 'tile', split_axis=0, concat_axis=0, tiled=True)  25.3 us
    dot_general x4, matrix products, per_device(): jnp.dot(forward, received.reshape(length, block), preferred_element_type=...  24.7 us
    all_to_all x1, blocking collectives, per_device(): lax.all_to_all(buckets, 'tile', split_axis=0, concat_axis=0, tiled=True)  21.9 us
    all_to_all x4, starting transfers between devices, per_device(): lax.all_to_all(outgoing, 'tile', split_axis=0, concat_axis=0, tiled=True)  19.6 us
    ppermute x4, starting transfers between devices, per_device(): from_next = lax.ppermute(whitened[:, :half], 'tile', to_prev)  19.4 us
    ppermute x4, starting transfers between devices, per_device(): from_prev = lax.ppermute(whitened[:, half:], 'tile', to_next)  13.2 us
    ppermute x1, waiting for transfers between devices, sum_and_invert(): lax.ppermute(send, 'win', [(w, w ^ 2 * bit) for w in range(win_count)])  12.6 us
    ppermute x4, waiting for transfers between devices, per_device(): from_prev = lax.ppermute(whitened[:, half:], 'tile', to_next)  11.3 us
  transfers between devices with their start and end apart: 16, of which 11 were waited for; matrix products, arithmetic and copies ran while one was open for 26% of the time, Pallas kernels for 3%

profile of v19, /device:TPU:0, one launch (start us, length us, event | category | flops | bytes accessed | tf_op | source)
XLA Modules:
  0.0 218.2 jit_solution(3103568148455550007)
XLA Ops:
  0.0 2.3 %shard_map.48 = bf16[8,256,256]{2,1,0:T(8,128)(2,1)} custom-call(bf16[4,256,2048]{2,1,0:T(8,128)(2,1)} %src.7), custom_call_target="tpu_custom_call" | custom-call | tf_op jit(solution)/shard_map/pallas_call | solution.py:166
  2.3 7.3 %all-to-all-start.2 = ((bf16[8,256,256]{2,1,0:T(8,128)(2,1)}), bf16[8,256,256]{2,1,0:T(8,128)(2,1)S(1)}, u32[]{:S(2)}, u32[]{:S(2)}) async-start(bf16[8,256,256]{2,1,0:T(8,128)(2,1)} %shard_map.48), calls=%async_computation.2 | async-start | bytes 2097152 | tf_op jit(solution)/shard_map/all_to_all | solution.py:201
  9.7 0.7 collective-permute-start
  10.4 1.0 fusion.58
  11.4 0.6 fusion.66
  12.0 5.1 %subtract_convert_fusion = (bf16[1024,32,64]{0,2,1:T(8,128)(2,1)}, bf16[1024,32,64]{0,2,1:T(8,128)(2,1)}) fusion(f32[1024,64]{0,1:T(8,128)S(1)} %get-tuple-element.48, f32[1024,32]{0,1:T(8,128)S(1)} %get-tuple-element.47, f32[1024,64]{0,1:T(8,128)S(1)} %get-tuple-element.49, f32[1024,32]{0,1:T(8,128)S(1)} %get-tuple-element.46), kind=kLoop, calls=%fused_computation.5 | loop fusion | flops 18874368 | bytes 9175040 | tf_op jit(solution)/shard_map/convert.3
  17.1 2.3 %shard_map.47 = bf16[8,256,256]{2,1,0:T(8,128)(2,1)} custom-call(bf16[4,256,2048]{2,1,0:T(8,128)(2,1)} %src.7), custom_call_target="tpu_custom_call" | custom-call | tf_op jit(solution)/shard_map/pallas_call | solution.py:166
  19.4 2.3 %shard_map.46 = bf16[8,256,256]{2,1,0:T(8,128)(2,1)} custom-call(bf16[4,256,2048]{2,1,0:T(8,128)(2,1)} %src.7), custom_call_target="tpu_custom_call" | custom-call | tf_op jit(solution)/shard_map/pallas_call | solution.py:166
  21.7 2.4 %shard_map.49 = bf16[8,256,256]{2,1,0:T(8,128)(2,1)} custom-call(bf16[4,256,2048]{2,1,0:T(8,128)(2,1)} %src.7), custom_call_target="tpu_custom_call" | custom-call | tf_op jit(solution)/shard_map/pallas_call | solution.py:166
  24.1 0.6 reduce-window.6
  25.0 10.4 %all-to-all-done.2 = bf16[8,256,256]{2,1,0:T(8,128)(2,1)S(1)} async-done(((bf16[8,256,256]{2,1,0:T(8,128)(2,1)}), bf16[8,256,256]{2,1,0:T(8,128)(2,1)S(1)}, u32[]{:S(2)}, u32[]{:S(2)}) %all-to-all-start.2) | async-done | bytes 1048608 | tf_op jit(solution)/shard_map/all_to_all | solution.py:201
  35.4 3.8 %all-to-all-start.1 = ((bf16[8,256,256]{2,1,0:T(8,128)(2,1)}), bf16[8,256,256]{2,1,0:T(8,128)(2,1)S(1)}, u32[]{:S(2)}, u32[]{:S(2)}) async-start(bf16[8,256,256]{2,1,0:T(8,128)(2,1)} %shard_map.47), calls=%async_computation.1 | async-start | bytes 2097152 | tf_op jit(solution)/shard_map/all_to_all | solution.py:201
  39.2 6.1 %fusion.82 = f32[2048,256]{1,0:T(8,128)S(1)} fusion(bf16[2048,256]{1,0:T(8,128)(2,1)S(1)} %bitcast.56, bf16[1024,2048]{0,1:T(8,128)(2,1)} %bitcast.48, bf16[1024,2048]{0,1:T(8,128)(2,1)} %bitcast.44), kind=kOutput, calls=%fused_computation.165 | convolution fusion | flops 2164260864 | bytes 11534336 | tf_op jit(solution)/shard_map/dot_general | solution.py:206
  45.6 0.3 fusion
  45.9 2.0 fusion.47
  48.0 0.6 fusion.64
  48.6 2.1 collective-permute-start.1
  50.9 2.4 %multiply_subtract_fusion = (f32[2048,16,64]{0,2,1:T(8,128)S(1)}, f32[2048,16,64]{0,2,1:T(8,128)S(1)}) fusion(f32[2048,64]{0,1:T(8,128)S(1)} %get-tuple-element.42, f32[2048,16]{0,1:T(8,128)S(1)} %get-tuple-element.40, f32[2048,64]{0,1:T(8,128)S(1)} %get-tuple-element.41, f32[2048,16]{0,1:T(8,128)S(1)} %get-tuple-element.39), kind=kLoop, calls=%fused_computation.3 | loop fusion | flops 14680064 | bytes 18087936 | tf_op jit(solution)/shard_map/sub | solution.py:25
  53.3 6.3 %pad_maximum_fusion = f32[2048,2048]{0,1:T(8,128)} fusion(f32[2048,1024]{0,1:T(8,128)S(1)} %bitcast.43, f32[2048,1024]{0,1:T(8,128)S(1)} %bitcast.42), kind=kLoop, calls=%fused_computation | loop fusion | flops 4194304 | bytes 33554432 | tf_op jit(solution)/shard_map/concatenate | solution.py:116
  59.6 6.8 %all-to-all-done.1 = bf16[8,256,256]{2,1,0:T(8,128)(2,1)S(1)} async-done(((bf16[8,256,256]{2,1,0:T(8,128)(2,1)}), bf16[8,256,256]{2,1,0:T(8,128)(2,1)S(1)}, u32[]{:S(2)}, u32[]{:S(2)}) %all-to-all-start.1) | async-done | bytes 1048608 | tf_op jit(solution)/shard_map/all_to_all | solution.py:201
  66.4 4.2 %all-to-all-start = ((bf16[8,256,256]{2,1,0:T(8,128)(2,1)}), bf16[8,256,256]{2,1,0:T(8,128)(2,1)}, u32[]{:S(2)}, u32[]{:S(2)}) async-start(bf16[8,256,256]{2,1,0:T(8,128)(2,1)} %shard_map.46), calls=%async_computation | async-start | bytes 2097152 | tf_op jit(solution)/shard_map/all_to_all | solution.py:201
  70.6 6.1 %fusion.81 = f32[2048,256]{1,0:T(8,128)S(1)} fusion(bf16[2048,256]{1,0:T(8,128)(2,1)S(1)} %bitcast.57, bf16[1024,2048]{0,1:T(8,128)(2,1)} %bitcast.49, bf16[1024,2048]{0,1:T(8,128)(2,1)} %bitcast.45), kind=kOutput, calls=%fused_computation.164 | convolution fusion | flops 2164260864 | bytes 11534336 | tf_op jit(solution)/shard_map/dot_general | solution.py:206
  77.0 0.3 fusion.1
  77.3 1.0 fusion.85
  78.4 1.9 collective-permute-start.3
  80.2 10.4 %collective-permute-start.4 = (bf16[2048,128]{1,0:T(8,128)(2,1)}, bf16[2048,128]{1,0:T(8,128)(2,1)}, u32[]{:S(2)}, u32[]{:S(2)}) collective-permute-start(bf16[2048,128]{1,0:T(8,128)(2,1)} %get-tuple-element.31), channel_id=1, source_target_pairs={{0,8},{4,0},{12,4},{20,12},{28,20},{24,28},{16,24},{8,16},{1,9},{5... | collective-permute-start | bytes 1572872 | tf_op jit(solution)/shard_map/ppermute | solution.py:209
  90.7 2.0 fusion.20
  92.6 2.0 fusion.21
  94.6 1.3 multiply_add_fusion.3
  95.9 4.4 %all-to-all-done = bf16[8,256,256]{2,1,0:T(8,128)(2,1)} async-done(((bf16[8,256,256]{2,1,0:T(8,128)(2,1)}), bf16[8,256,256]{2,1,0:T(8,128)(2,1)}, u32[]{:S(2)}, u32[]{:S(2)}) %all-to-all-start) | async-done | bytes 1048608 | tf_op jit(solution)/shard_map/all_to_all | solution.py:201
  100.2 4.2 %all-to-all-start.3 = ((bf16[8,256,256]{2,1,0:T(8,128)(2,1)}), bf16[8,256,256]{2,1,0:T(8,128)(2,1)}, u32[]{:S(2)}, u32[]{:S(2)}) async-start(bf16[8,256,256]{2,1,0:T(8,128)(2,1)} %shard_map.49), calls=%async_computation.3 | async-start | bytes 2097152 | tf_op jit(solution)/shard_map/all_to_all | solution.py:201
  104.6 6.3 %fusion.80 = f32[2048,256]{1,0:T(8,128)S(1)} fusion(bf16[2048,256]{1,0:T(8,128)(2,1)} %bitcast.21, bf16[1024,2048]{0,1:T(8,128)(2,1)} %bitcast.50, bf16[1024,2048]{0,1:T(8,128)(2,1)} %bitcast.46), kind=kOutput, calls=%fused_computation.163 | convolution fusion | flops 2164260864 | bytes 11534336 | tf_op jit(solution)/shard_map/dot_general | solution.py:206
  111.2 0.3 fusion.4
  111.5 1.0 fusion.84
  112.5 5.2 %collective-permute-start.5 = (bf16[2048,128]{1,0:T(8,128)(2,1)}, bf16[2048,128]{1,0:T(8,128)(2,1)}, u32[]{:S(2)}, u32[]{:S(2)}) collective-permute-start(bf16[2048,128]{1,0:T(8,128)(2,1)} %get-tuple-element.29), channel_id=1, source_target_pairs={{0,4},{4,12},{12,20},{20,28},{28,24},{24,16},{16,8},{8,0},{1,5},{5... | collective-permute-start | bytes 1572872 | tf_op jit(solution)/shard_map/ppermute | solution.py:208
  117.7 6.8 %collective-permute-start.6 = (bf16[2048,128]{1,0:T(8,128)(2,1)}, bf16[2048,128]{1,0:T(8,128)(2,1)}, u32[]{:S(2)}, u32[]{:S(2)}) collective-permute-start(bf16[2048,128]{1,0:T(8,128)(2,1)} %get-tuple-element.30), channel_id=1, source_target_pairs={{0,8},{4,0},{12,4},{20,12},{28,20},{24,28},{16,24},{8,16},{1,9},{5... | collective-permute-start | bytes 1572872 | tf_op jit(solution)/shard_map/ppermute | solution.py:209
  124.5 2.0 fusion.19
  126.5 2.0 fusion.18
  128.5 1.7 multiply_add_fusion.2
  130.2 3.8 %all-to-all-done.3 = bf16[8,256,256]{2,1,0:T(8,128)(2,1)} async-done(((bf16[8,256,256]{2,1,0:T(8,128)(2,1)}), bf16[8,256,256]{2,1,0:T(8,128)(2,1)}, u32[]{:S(2)}, u32[]{:S(2)}) %all-to-all-start.3) | async-done | bytes 1048608 | tf_op jit(solution)/shard_map/all_to_all | solution.py:201
  134.0 4.7 %collective-permute-done.5 = bf16[2048,128]{1,0:T(8,128)(2,1)} collective-permute-done((bf16[2048,128]{1,0:T(8,128)(2,1)}, bf16[2048,128]{1,0:T(8,128)(2,1)}, u32[]{:S(2)}, u32[]{:S(2)}) %collective-permute-start.5) | collective-permute-done | bytes 524320 | tf_op jit(solution)/shard_map/ppermute | solution.py:208
  138.6 6.3 %fusion.79 = f32[2048,256]{1,0:T(8,128)S(1)} fusion(bf16[2048,256]{1,0:T(8,128)(2,1)} %bitcast.24, bf16[1024,2048]{0,1:T(8,128)(2,1)} %bitcast.51, bf16[1024,2048]{0,1:T(8,128)(2,1)} %bitcast.47), kind=kOutput, calls=%fused_computation.162 | convolution fusion | flops 2164260864 | bytes 11534336 | tf_op jit(solution)/shard_map/dot_general | solution.py:206
  145.2 0.3 fusion.5
  145.6 4.0 %collective-permute-start.7 = (bf16[2048,128]{1,0:T(8,128)(2,1)S(1)}, bf16[2048,128]{1,0:T(8,128)(2,1)S(1)}, u32[]{:S(2)}, u32[]{:S(2)}) collective-permute-start(bf16[2048,128]{1,0:T(8,128)(2,1)S(1)} %get-tuple-element.27), channel_id=1, source_target_pairs={{0,4},{4,12},{12,20},{20,28},{28,24},{24,16},{16,8},{8,0},{1,5},{5... | collective-permute-start | bytes 1572872 | tf_op jit(solution)/shard_map/ppermute | solution.py:208
  149.6 1.9 collective-permute-start.8
  151.5 2.0 fusion.17
  153.5 2.0 fusion.16
  155.4 0.3 multiply_add_fusion.1
  155.7 6.6 %collective-permute-done.7 = bf16[2048,128]{1,0:T(8,128)(2,1)S(1)} collective-permute-done((bf16[2048,128]{1,0:T(8,128)(2,1)S(1)}, bf16[2048,128]{1,0:T(8,128)(2,1)S(1)}, u32[]{:S(2)}, u32[]{:S(2)}) %collective-permute-start.7) | collective-permute-done | bytes 524320 | tf_op jit(solution)/shard_map/ppermute | solution.py:208
  162.3 1.4 collective-permute-done.8
  163.6 0.8 fusion.15
  164.4 0.8 fusion.14
  165.5 0.9 copy-done
  166.4 0.3 copy-done.1
  166.7 0.3 copy-done.2
  167.0 0.5 fusion.3
  167.8 2.7 %collective-permute-done.9 = f32[2048,128]{1,0:T(8,128)} collective-permute-done((f32[2048,128]{1,0:T(8,128)S(1)}, f32[2048,128]{1,0:T(8,128)}, u32[]{:S(2)}, u32[]{:S(2)}) %collective-permute-start.9) | collective-permute-done | bytes 1048608 | tf_op jit(solution)/shard_map/ppermute | solution.py:131
  170.5 8.8 %fusion.10 = f32[2048,128]{0,1:T(8,128)S(1)} fusion(f32[2048,2048]{0,1:T(8,128)} %pad_maximum_fusion, f32[2048,128]{1,0:T(8,128)} %collective-permute-done.9, f32[2048,256]{1,0:T(8,128)S(1)} %fusion.3, s32[]{:T(128)S(6)} %select_n.110, f32[2048]{0:T(1024)S(1)} %pad_maximum_fusion.14), kind=kOutput, calls=%fused_computation.38 | convolution fusion | flops 3221749760 | bytes 19931140 | tf_op jit(solution)/shard_map/dot_general | solution.py:137
  179.4 1.6 collective-permute-start.10
  180.9 12.6 %collective-permute-done.10 = f32[1024,128]{0,1:T(8,128)S(1)} collective-permute-done((f32[1024,128]{0,1:T(8,128)S(1)}, f32[1024,128]{0,1:T(8,128)S(1)}, u32[]{:S(2)}, u32[]{:S(2)}) %collective-permute-start.10) | collective-permute-done | bytes 524320 | tf_op jit(solution)/shard_map/ppermute | solution.py:144
  193.7 1.3 collective-permute-done.11
  195.0 0.4 convolution_convert_fusion
  195.4 21.9 %all_to_all.25 = bf16[8,80,512]{2,1,0:T(8,128)(2,1)S(1)} all-to-all(bf16[8,80,512]{2,1,0:T(8,128)(2,1)S(1)} %bitcast.58), channel_id=1, replica_groups=mesh['tile'=8,'win'=4] {'tile'}, dimensions={0} | all-to-all | bytes 1310720 | tf_op jit(solution)/shard_map/all_to_all | solution.py:229
  217.4 0.8 copy-done.3
  (58 shorter events, 2.7 us)
Async XLA Ops:
  0.0 9.7 %copy-start.6 = (s32[256]{0:T(256)S(1)}, s32[256]{0:T(256)}, u32[]{:S(2)}) copy-start(s32[256]{0:T(256)} %param.5) | copy-start | bytes 3076
  0.0 9.7 %copy-start.5 = (s32[256]{0:T(256)S(1)}, s32[256]{0:T(256)}, u32[]{:S(2)}) copy-start(s32[256]{0:T(256)} %param.6) | copy-start | bytes 3076
  0.0 9.7 %copy-start.4 = (s32[256,1]{0,1:T(1,128)S(1)}, s32[256,1]{0,1:T(1,128)}, u32[]{:S(2)}) copy-start(s32[256,1]{0,1:T(1,128)} %param.7) | copy-start | bytes 3076
  2.3 33.1 %all-to-all-start.2 = ((bf16[8,256,256]{2,1,0:T(8,128)(2,1)}), bf16[8,256,256]{2,1,0:T(8,128)(2,1)S(1)}, u32[]{:S(2)}, u32[]{:S(2)}) async-start(bf16[8,256,256]{2,1,0:T(8,128)(2,1)} %shard_map.48), calls=%async_computation.2 | async-start | bytes 2097152 | tf_op jit(solution)/shard_map/all_to_all | solution.py:201
  9.7 14.4 %collective-permute-start = (s32[3,256]{1,0:T(4,128)S(1)}, s32[3,256]{1,0:T(4,128)S(1)}, u32[]{:S(2)}, u32[]{:S(2)}) collective-permute-start(s32[3,256]{1,0:T(4,128)S(1)} %pad_add_fusion), channel_id=1, source_target_pairs={{0,0},{4,4},{8,12},{12,20},{16,28},{20,24},{24,16},{28,8},{1,1},{5... | collective-permute-start | bytes 9224 | tf_op jit(solution)/shard_map/ppermute | solution.py:193
  35.4 30.9 %all-to-all-start.1 = ((bf16[8,256,256]{2,1,0:T(8,128)(2,1)}), bf16[8,256,256]{2,1,0:T(8,128)(2,1)S(1)}, u32[]{:S(2)}, u32[]{:S(2)}) async-start(bf16[8,256,256]{2,1,0:T(8,128)(2,1)} %shard_map.47), calls=%async_computation.1 | async-start | bytes 2097152 | tf_op jit(solution)/shard_map/all_to_all | solution.py:201
  48.6 22.0 %collective-permute-start.1 = (bf16[2048,128]{1,0:T(8,128)(2,1)S(1)}, bf16[2048,128]{1,0:T(8,128)(2,1)}, u32[]{:S(2)}, u32[]{:S(2)}) collective-permute-start(bf16[2048,128]{1,0:T(8,128)(2,1)S(1)} %get-tuple-element.34), channel_id=1, source_target_pairs={{0,4},{4,12},{12,20},{20,28},{28,24},{24,16},{16,8},{8,0},{1,5},{5... | collective-permute-start | bytes 1572872 | tf_op jit(solution)/shard_map/ppermute | solution.py:208
  50.7 20.0 %collective-permute-start.2 = (bf16[2048,128]{1,0:T(8,128)(2,1)S(1)}, bf16[2048,128]{1,0:T(8,128)(2,1)}, u32[]{:S(2)}, u32[]{:S(2)}) collective-permute-start(bf16[2048,128]{1,0:T(8,128)(2,1)S(1)} %get-tuple-element.33), channel_id=1, source_target_pairs={{0,8},{4,0},{12,4},{20,12},{28,20},{24,28},{16,24},{8,16},{1,9},{5... | collective-permute-start | bytes 1572872 | tf_op jit(solution)/shard_map/ppermute | solution.py:209
  66.4 33.9 %all-to-all-start = ((bf16[8,256,256]{2,1,0:T(8,128)(2,1)}), bf16[8,256,256]{2,1,0:T(8,128)(2,1)}, u32[]{:S(2)}, u32[]{:S(2)}) async-start(bf16[8,256,256]{2,1,0:T(8,128)(2,1)} %shard_map.46), calls=%async_computation | async-start | bytes 2097152 | tf_op jit(solution)/shard_map/all_to_all | solution.py:201
  78.4 26.2 %collective-permute-start.3 = (bf16[2048,128]{1,0:T(8,128)(2,1)}, bf16[2048,128]{1,0:T(8,128)(2,1)}, u32[]{:S(2)}, u32[]{:S(2)}) collective-permute-start(bf16[2048,128]{1,0:T(8,128)(2,1)} %get-tuple-element.32), channel_id=1, source_target_pairs={{0,4},{4,12},{12,20},{20,28},{28,24},{24,16},{16,8},{8,0},{1,5},{5... | collective-permute-start | bytes 1572872 | tf_op jit(solution)/shard_map/ppermute | solution.py:208
  80.2 24.3 %collective-permute-start.4 = (bf16[2048,128]{1,0:T(8,128)(2,1)}, bf16[2048,128]{1,0:T(8,128)(2,1)}, u32[]{:S(2)}, u32[]{:S(2)}) collective-permute-start(bf16[2048,128]{1,0:T(8,128)(2,1)} %get-tuple-element.31), channel_id=1, source_target_pairs={{0,8},{4,0},{12,4},{20,12},{28,20},{24,28},{16,24},{8,16},{1,9},{5... | collective-permute-start | bytes 1572872 | tf_op jit(solution)/shard_map/ppermute | solution.py:209
  100.2 33.8 %all-to-all-start.3 = ((bf16[8,256,256]{2,1,0:T(8,128)(2,1)}), bf16[8,256,256]{2,1,0:T(8,128)(2,1)}, u32[]{:S(2)}, u32[]{:S(2)}) async-start(bf16[8,256,256]{2,1,0:T(8,128)(2,1)} %shard_map.49), calls=%async_computation.3 | async-start | bytes 2097152 | tf_op jit(solution)/shard_map/all_to_all | solution.py:201
  112.5 26.1 %collective-permute-start.5 = (bf16[2048,128]{1,0:T(8,128)(2,1)}, bf16[2048,128]{1,0:T(8,128)(2,1)}, u32[]{:S(2)}, u32[]{:S(2)}) collective-permute-start(bf16[2048,128]{1,0:T(8,128)(2,1)} %get-tuple-element.29), channel_id=1, source_target_pairs={{0,4},{4,12},{12,20},{20,28},{28,24},{24,16},{16,8},{8,0},{1,5},{5... | collective-permute-start | bytes 1572872 | tf_op jit(solution)/shard_map/ppermute | solution.py:208
  117.7 20.9 %collective-permute-start.6 = (bf16[2048,128]{1,0:T(8,128)(2,1)}, bf16[2048,128]{1,0:T(8,128)(2,1)}, u32[]{:S(2)}, u32[]{:S(2)}) collective-permute-start(bf16[2048,128]{1,0:T(8,128)(2,1)} %get-tuple-element.30), channel_id=1, source_target_pairs={{0,8},{4,0},{12,4},{20,12},{28,20},{24,28},{16,24},{8,16},{1,9},{5... | collective-permute-start | bytes 1572872 | tf_op jit(solution)/shard_map/ppermute | solution.py:209
  145.6 16.7 %collective-permute-start.7 = (bf16[2048,128]{1,0:T(8,128)(2,1)S(1)}, bf16[2048,128]{1,0:T(8,128)(2,1)S(1)}, u32[]{:S(2)}, u32[]{:S(2)}) collective-permute-start(bf16[2048,128]{1,0:T(8,128)(2,1)S(1)} %get-tuple-element.27), channel_id=1, source_target_pairs={{0,4},{4,12},{12,20},{20,28},{28,24},{24,16},{16,8},{8,0},{1,5},{5... | collective-permute-start | bytes 1572872 | tf_op jit(solution)/shard_map/ppermute | solution.py:208
  149.6 14.0 %collective-permute-start.8 = (bf16[2048,128]{1,0:T(8,128)(2,1)S(1)}, bf16[2048,128]{1,0:T(8,128)(2,1)S(1)}, u32[]{:S(2)}, u32[]{:S(2)}) collective-permute-start(bf16[2048,128]{1,0:T(8,128)(2,1)S(1)} %get-tuple-element.28), channel_id=1, source_target_pairs={{0,8},{4,0},{12,4},{20,12},{28,20},{24,28},{16,24},{8,16},{1,9},{5... | collective-permute-start | bytes 1572872 | tf_op jit(solution)/shard_map/ppermute | solution.py:209
  165.2 1.2 copy-start
  165.2 1.5 copy-start.1
  165.2 1.8 copy-start.2
  167.7 2.9 %collective-permute-start.9 = (f32[2048,128]{1,0:T(8,128)S(1)}, f32[2048,128]{1,0:T(8,128)}, u32[]{:S(2)}, u32[]{:S(2)}) collective-permute-start(f32[2048,128]{1,0:T(8,128)S(1)} %constant_dynamic-slice_fusion.3), channel_id=1, source_target_pairs={{0,1},{1,0},{2,3},{3,2},{4,5},{5,4},{6,7},{7,6},{8,9},{9,8},{10,11... | collective-permute-start | bytes 3145736 | tf_op jit(solution)/shard_map/ppermute | solution.py:131
  179.4 14.1 %collective-permute-start.10 = (f32[1024,128]{0,1:T(8,128)S(1)}, f32[1024,128]{0,1:T(8,128)S(1)}, u32[]{:S(2)}, u32[]{:S(2)}) collective-permute-start(f32[1024,128]{0,1:T(8,128)S(1)} %constant_dynamic-slice_fusion.2), channel_id=1, source_target_pairs={{0,2},{1,3},{2,0},{3,1},{4,6},{5,7},{6,4},{7,5},{8,10},{9,11},{10,... | collective-permute-start | bytes 1572872 | tf_op jit(solution)/shard_map/ppermute | solution.py:144
  193.6 1.4 collective-permute-start.11
  217.4 0.8 copy-start.3

commit v20 on v18

--- a/solution.py
+++ b/solution.py
@@ -67,12 +67,12 @@
     return jnp.concatenate([real_sum, imag_sum], axis=-2)
 
 
-def bucket_select(owner_ids, owner_count, capacity):
+def bucket_select(owner_ids, owner_count, capacity, order=lambda v: v):
     onehot = (owner_ids[:, None] == jnp.arange(owner_count, dtype=jnp.int32)[None, :]).astype(
         jnp.int32
     )
     slot_rank = jnp.sum((jnp.cumsum(onehot, axis=0, dtype=jnp.int32) - 1) * onehot, axis=1)
-    slot_id = owner_ids * capacity + slot_rank
+    slot_id = order(owner_ids * capacity + slot_rank)
     return (
         slot_id[None, :] == jnp.arange(owner_count * capacity, dtype=jnp.int32)[:, None]
     ).astype(jnp.bfloat16)
@@ -125,8 +125,8 @@
     core = win % 2
     chip = win // 2
     half = cross.shape[1] // 2
-    mine = lax.dynamic_slice_in_dim(cross, core * half, half, axis=1)
-    other = lax.dynamic_slice_in_dim(cross, (1 - core) * half, half, axis=1)
+    mine = cross[:, :half]
+    other = cross[:, half:]
     partner = [(w, w ^ 1) for w in range(win_count)]
     total = mine + lax.ppermute(other, "win", partner)
     half_bins = length // 2
@@ -147,7 +147,7 @@
     kept = lax.dynamic_slice_in_dim(both, core * lag_count, lag_count, axis=0)
     given = lax.dynamic_slice_in_dim(both, (1 - core) * lag_count, lag_count, axis=0)
     got = lax.ppermute(given, "win", partner)
-    return jnp.where(core == 0, jnp.concatenate([kept, got], axis=1), jnp.concatenate([got, kept], axis=1))
+    return jnp.concatenate([kept, got], axis=1)
 
 
 def lay_out_blocks(records, segment, block_of, block, half):
@@ -191,6 +191,11 @@
         half = block // 2
         forward = forward_matrix(length)
         my_first, my_offset, my_owners = lax.ppermute(pair_data, "tile", to_owner)
+        order = lambda v: v
+        if win_count % 2 == 0 and not win_count & (win_count - 1):
+            core = lax.axis_index("win") % 2
+            order = lambda v: jnp.where(core == 0, v, jnp.roll(v, -(v.shape[0] // 2)))
+        my_first, my_offset = order(my_first), order(my_offset)
         channel_ids = jnp.arange(2 * block, dtype=jnp.int32)[:, None]
         pick_first = (channel_ids == my_first[None, :]).astype(jnp.bfloat16)
         pick_second = (channel_ids == (my_first + my_offset)[None, :]).astype(jnp.bfloat16)
@@ -218,7 +223,7 @@
         lag_count = length // win_count
         correlation = sum_and_invert(cross, length, lag_count, seg_total, win_count, table)
         capacity = 5 * pair_first.shape[0] // (2 * tile_count)
-        chooser = bucket_select(my_owners, tile_count, capacity)
+        chooser = bucket_select(my_owners, tile_count, capacity, order)
         picked = lax.dot_general(
             chooser,
             correlation,

time: 215 us -> 215 us (level)
  starting transfers between devices: 51.6 us -> 47.9 us
  waiting for transfers between devices: 52.7 us -> 56.3 us
    all_to_all x4, waiting for transfers between devices: 23.8 us -> 27.8 us  [per_device(): lax.all_to_all(outgoing, 'tile', split_axis=0, concat_axis=0, tiled=True)]
    ppermute x4, starting transfers between devices: 16.5 us -> 13.3 us  [per_device(): from_next = lax.ppermute(whitened[:, :half], 'tile', to_prev)]
    another operation x4 -> x3, other arithmetic: 5.61 us -> 5.61 us
  transfers between devices with their start and end apart: 16 -> 16, of which waited for: 10 -> 11; matrix products, arithmetic and copies ran while one was open for 28% -> 28% of each run, Pallas kernels for 3% -> 3%
where the time goes in v20:
time: 215 us; the launch traced here: 214 us
  waiting for transfers between devices  56.3 us (26%)
  starting transfers between devices  47.9 us (22%)
  matrix products  43.3 us (20%)
  other arithmetic  29.6 us (14%)
  blocking collectives  22 us (10%)
  Pallas kernels  9.33 us (4%)
  local copies, waits for them, and re-layouts  5.34 us (2%)
    all_to_all x4, waiting for transfers between devices, per_device(): lax.all_to_all(outgoing, 'tile', split_axis=0, concat_axis=0, tiled=True)  27.8 us
    dot_general x4, matrix products, per_device(): jnp.dot(forward, received.reshape(length, block), preferred_element_type=...  24.7 us
    all_to_all x1, blocking collectives, per_device(): lax.all_to_all(buckets, 'tile', split_axis=0, concat_axis=0, tiled=True)  22 us
    all_to_all x4, starting transfers between devices, per_device(): lax.all_to_all(outgoing, 'tile', split_axis=0, concat_axis=0, tiled=True)  19.6 us
    ppermute x4, starting transfers between devices, per_device(): from_next = lax.ppermute(whitened[:, :half], 'tile', to_prev)  13.3 us
    ppermute x4, starting transfers between devices, per_device(): from_prev = lax.ppermute(whitened[:, half:], 'tile', to_next)  12.6 us
    ppermute x1, waiting for transfers between devices, sum_and_invert(): lax.ppermute(send, 'win', [(w, w ^ 2 * bit) for w in range(win_count)])  12.4 us
    ppermute x4, waiting for transfers between devices, per_device(): from_prev = lax.ppermute(whitened[:, half:], 'tile', to_next)  11.7 us
  transfers between devices with their start and end apart: 16, of which 11 were waited for; matrix products, arithmetic and copies ran while one was open for 28% of the time, Pallas kernels for 3%

profile of v20, /device:TPU:0, one launch (start us, length us, event | category | flops | bytes accessed | tf_op | source)
XLA Modules:
  0.0 214.4 jit_solution(7879987802900375697)
XLA Ops:
  0.0 2.3 %shard_map.48 = bf16[8,256,256]{2,1,0:T(8,128)(2,1)} custom-call(bf16[4,256,2048]{2,1,0:T(8,128)(2,1)} %src.7), custom_call_target="tpu_custom_call" | custom-call | tf_op jit(solution)/shard_map/pallas_call | solution.py:166
  2.4 7.3 %all-to-all-start.2 = ((bf16[8,256,256]{2,1,0:T(8,128)(2,1)}), bf16[8,256,256]{2,1,0:T(8,128)(2,1)S(1)}, u32[]{:S(2)}, u32[]{:S(2)}) async-start(bf16[8,256,256]{2,1,0:T(8,128)(2,1)} %shard_map.48), calls=%async_computation.2 | async-start | bytes 2097152 | tf_op jit(solution)/shard_map/all_to_all | solution.py:206
  9.7 0.7 collective-permute-start
  10.4 1.0 fusion.54
  11.4 0.6 fusion.62
  12.0 5.0 %subtract_convert_fusion = (bf16[1024,32,64]{0,2,1:T(8,128)(2,1)}, bf16[1024,32,64]{0,2,1:T(8,128)(2,1)}) fusion(f32[1024,64]{0,1:T(8,128)S(1)} %get-tuple-element.54, f32[1024,32]{0,1:T(8,128)S(1)} %get-tuple-element.53, f32[1024,64]{0,1:T(8,128)S(1)} %get-tuple-element.55, f32[1024,32]{0,1:T(8,128)S(1)} %get-tuple-element.52), kind=kLoop, calls=%fused_computation.5 | loop fusion | flops 18874368 | bytes 9175040 | tf_op jit(solution)/shard_map/convert.3
  17.0 2.3 %shard_map.47 = bf16[8,256,256]{2,1,0:T(8,128)(2,1)} custom-call(bf16[4,256,2048]{2,1,0:T(8,128)(2,1)} %src.7), custom_call_target="tpu_custom_call" | custom-call | tf_op jit(solution)/shard_map/pallas_call | solution.py:166
  19.3 2.3 %shard_map.46 = bf16[8,256,256]{2,1,0:T(8,128)(2,1)} custom-call(bf16[4,256,2048]{2,1,0:T(8,128)(2,1)} %src.7), custom_call_target="tpu_custom_call" | custom-call | tf_op jit(solution)/shard_map/pallas_call | solution.py:166
  21.6 2.4 %shard_map.49 = bf16[8,256,256]{2,1,0:T(8,128)(2,1)} custom-call(bf16[4,256,2048]{2,1,0:T(8,128)(2,1)} %src.7), custom_call_target="tpu_custom_call" | custom-call | tf_op jit(solution)/shard_map/pallas_call | solution.py:166
  24.0 11.4 %all-to-all-done.2 = bf16[8,256,256]{2,1,0:T(8,128)(2,1)S(1)} async-done(((bf16[8,256,256]{2,1,0:T(8,128)(2,1)}), bf16[8,256,256]{2,1,0:T(8,128)(2,1)S(1)}, u32[]{:S(2)}, u32[]{:S(2)}) %all-to-all-start.2) | async-done | bytes 1048608 | tf_op jit(solution)/shard_map/all_to_all | solution.py:206
  35.4 3.6 %all-to-all-start.1 = ((bf16[8,256,256]{2,1,0:T(8,128)(2,1)}), bf16[8,256,256]{2,1,0:T(8,128)(2,1)S(1)}, u32[]{:S(2)}, u32[]{:S(2)}) async-start(bf16[8,256,256]{2,1,0:T(8,128)(2,1)} %shard_map.47), calls=%async_computation.1 | async-start | bytes 2097152 | tf_op jit(solution)/shard_map/all_to_all | solution.py:206
  39.1 6.1 %fusion.78 = f32[2048,256]{1,0:T(8,128)S(1)} fusion(bf16[2048,256]{1,0:T(8,128)(2,1)S(1)} %bitcast.60, bf16[1024,2048]{0,1:T(8,128)(2,1)} %bitcast.52, bf16[1024,2048]{0,1:T(8,128)(2,1)} %bitcast.48), kind=kOutput, calls=%fused_computation.163 | convolution fusion | flops 2164260864 | bytes 11534336 | tf_op jit(solution)/shard_map/dot_general | solution.py:211
  45.4 0.3 fusion
  45.8 2.1 collective-permute-start.1
  48.1 0.6 fusion.60
  48.7 2.0 fusion.44
  50.8 5.3 %multiply_subtract_fusion = (bf16[2048,16,64]{0,2,1:T(8,128)(2,1)}, bf16[2048,16,64]{0,2,1:T(8,128)(2,1)}) fusion(f32[2048,64]{0,1:T(8,128)S(1)} %get-tuple-element.44, f32[2048,16]{0,1:T(8,128)S(1)} %get-tuple-element.42, f32[2048,64]{0,1:T(8,128)S(1)} %get-tuple-element.43, f32[2048,16]{0,1:T(8,128)S(1)} %get-tuple-element.41), kind=kLoop, calls=%fused_computation.3 | loop fusion | flops 18874368 | bytes 9699328 | tf_op jit(solution)/shard_map/sub | solution.py:25
  56.1 8.4 %pad_maximum_fusion = bf16[2048,2048]{0,1:T(8,128)(2,1)} fusion(bf16[2048,1024]{0,1:T(8,128)(2,1)} %bitcast.47, bf16[2048,1024]{0,1:T(8,128)(2,1)} %bitcast.46), kind=kLoop, calls=%fused_computation | loop fusion | flops 16777216 | bytes 16777216 | tf_op jit(solution)/shard_map/concatenate | solution.py:116
  64.5 1.8 all-to-all-done.1
  66.2 4.2 %all-to-all-start = ((bf16[8,256,256]{2,1,0:T(8,128)(2,1)}), bf16[8,256,256]{2,1,0:T(8,128)(2,1)}, u32[]{:S(2)}, u32[]{:S(2)}) async-start(bf16[8,256,256]{2,1,0:T(8,128)(2,1)} %shard_map.46), calls=%async_computation | async-start | bytes 2097152 | tf_op jit(solution)/shard_map/all_to_all | solution.py:206
  70.5 6.1 %fusion.77 = f32[2048,256]{1,0:T(8,128)S(1)} fusion(bf16[2048,256]{1,0:T(8,128)(2,1)S(1)} %bitcast.61, bf16[1024,2048]{0,1:T(8,128)(2,1)} %bitcast.53, bf16[1024,2048]{0,1:T(8,128)(2,1)} %bitcast.49), kind=kOutput, calls=%fused_computation.162 | convolution fusion | flops 2164260864 | bytes 11534336 | tf_op jit(solution)/shard_map/dot_general | solution.py:211
  76.9 0.3 fusion.1
  77.2 1.0 fusion.81
  78.2 1.9 collective-permute-start.3
  80.1 7.3 %collective-permute-start.4 = (bf16[2048,128]{1,0:T(8,128)(2,1)}, bf16[2048,128]{1,0:T(8,128)(2,1)}, u32[]{:S(2)}, u32[]{:S(2)}) collective-permute-start(bf16[2048,128]{1,0:T(8,128)(2,1)} %get-tuple-element.33), channel_id=1, source_target_pairs={{0,8},{4,0},{12,4},{20,12},{28,20},{24,28},{16,24},{8,16},{1,9},{5... | collective-permute-start | bytes 1572872 | tf_op jit(solution)/shard_map/ppermute | solution.py:214
  87.4 2.0 fusion.20
  89.3 2.0 fusion.19
  91.3 1.3 multiply_add_fusion.3
  92.6 7.5 %all-to-all-done = bf16[8,256,256]{2,1,0:T(8,128)(2,1)} async-done(((bf16[8,256,256]{2,1,0:T(8,128)(2,1)}), bf16[8,256,256]{2,1,0:T(8,128)(2,1)}, u32[]{:S(2)}, u32[]{:S(2)}) %all-to-all-start) | async-done | bytes 1048608 | tf_op jit(solution)/shard_map/all_to_all | solution.py:206
  100.1 4.5 %all-to-all-start.3 = ((bf16[8,256,256]{2,1,0:T(8,128)(2,1)}), bf16[8,256,256]{2,1,0:T(8,128)(2,1)}, u32[]{:S(2)}, u32[]{:S(2)}) async-start(bf16[8,256,256]{2,1,0:T(8,128)(2,1)} %shard_map.49), calls=%async_computation.3 | async-start | bytes 2097152 | tf_op jit(solution)/shard_map/all_to_all | solution.py:206
  104.8 6.3 %fusion.76 = f32[2048,256]{1,0:T(8,128)S(1)} fusion(bf16[2048,256]{1,0:T(8,128)(2,1)} %bitcast.23, bf16[1024,2048]{0,1:T(8,128)(2,1)} %bitcast.54, bf16[1024,2048]{0,1:T(8,128)(2,1)} %bitcast.50), kind=kOutput, calls=%fused_computation.161 | convolution fusion | flops 2164260864 | bytes 11534336 | tf_op jit(solution)/shard_map/dot_general | solution.py:211
  111.4 0.3 fusion.4
  111.7 1.0 fusion.80
  112.8 4.9 %collective-permute-start.5 = (bf16[2048,128]{1,0:T(8,128)(2,1)}, bf16[2048,128]{1,0:T(8,128)(2,1)}, u32[]{:S(2)}, u32[]{:S(2)}) collective-permute-start(bf16[2048,128]{1,0:T(8,128)(2,1)} %get-tuple-element.31), channel_id=1, source_target_pairs={{0,4},{4,12},{12,20},{20,28},{28,24},{24,16},{16,8},{8,0},{1,5},{5... | collective-permute-start | bytes 1572872 | tf_op jit(solution)/shard_map/ppermute | solution.py:213
  117.6 3.7 %collective-permute-start.6 = (bf16[2048,128]{1,0:T(8,128)(2,1)}, bf16[2048,128]{1,0:T(8,128)(2,1)}, u32[]{:S(2)}, u32[]{:S(2)}) collective-permute-start(bf16[2048,128]{1,0:T(8,128)(2,1)} %get-tuple-element.32), channel_id=1, source_target_pairs={{0,8},{4,0},{12,4},{20,12},{28,20},{24,28},{16,24},{8,16},{1,9},{5... | collective-permute-start | bytes 1572872 | tf_op jit(solution)/shard_map/ppermute | solution.py:214
  121.3 2.0 fusion.18
  123.2 2.0 fusion.17
  125.2 1.6 multiply_add_fusion.2
  126.8 7.1 %all-to-all-done.3 = bf16[8,256,256]{2,1,0:T(8,128)(2,1)} async-done(((bf16[8,256,256]{2,1,0:T(8,128)(2,1)}), bf16[8,256,256]{2,1,0:T(8,128)(2,1)}, u32[]{:S(2)}, u32[]{:S(2)}) %all-to-all-start.3) | async-done | bytes 1048608 | tf_op jit(solution)/shard_map/all_to_all | solution.py:206
  133.9 5.1 %collective-permute-done.5 = bf16[2048,128]{1,0:T(8,128)(2,1)} collective-permute-done((bf16[2048,128]{1,0:T(8,128)(2,1)}, bf16[2048,128]{1,0:T(8,128)(2,1)}, u32[]{:S(2)}, u32[]{:S(2)}) %collective-permute-start.5) | collective-permute-done | bytes 524320 | tf_op jit(solution)/shard_map/ppermute | solution.py:213
  138.9 6.3 %fusion.75 = f32[2048,256]{1,0:T(8,128)S(1)} fusion(bf16[2048,256]{1,0:T(8,128)(2,1)} %bitcast.26, bf16[1024,2048]{0,1:T(8,128)(2,1)} %bitcast.55, bf16[1024,2048]{0,1:T(8,128)(2,1)} %bitcast.51), kind=kOutput, calls=%fused_computation.160 | convolution fusion | flops 2164260864 | bytes 11534336 | tf_op jit(solution)/shard_map/dot_general | solution.py:211
  145.5 0.3 fusion.5
  145.9 3.8 %collective-permute-start.7 = (bf16[2048,128]{1,0:T(8,128)(2,1)S(1)}, bf16[2048,128]{1,0:T(8,128)(2,1)S(1)}, u32[]{:S(2)}, u32[]{:S(2)}) collective-permute-start(bf16[2048,128]{1,0:T(8,128)(2,1)S(1)} %get-tuple-element.29), channel_id=1, source_target_pairs={{0,4},{4,12},{12,20},{20,28},{28,24},{24,16},{16,8},{8,0},{1,5},{5... | collective-permute-start | bytes 1572872 | tf_op jit(solution)/shard_map/ppermute | solution.py:213
  149.6 2.1 collective-permute-start.8
  151.8 2.0 fusion.16
  153.7 2.0 fusion.15
  155.7 0.3 multiply_add_fusion.1
  156.0 6.4 %collective-permute-done.7 = bf16[2048,128]{1,0:T(8,128)(2,1)S(1)} collective-permute-done((bf16[2048,128]{1,0:T(8,128)(2,1)S(1)}, bf16[2048,128]{1,0:T(8,128)(2,1)S(1)}, u32[]{:S(2)}, u32[]{:S(2)}) %collective-permute-start.7) | collective-permute-done | bytes 524320 | tf_op jit(solution)/shard_map/ppermute | solution.py:213
  162.4 1.2 collective-permute-done.8
  163.6 0.8 fusion.14
  164.4 0.8 fusion.13
  165.5 0.9 copy-done
  166.4 0.3 copy-done.1
  166.7 0.3 copy-done.2
  167.0 0.5 fusion.3
  167.8 0.6 reduce-window.6
  168.7 1.8 collective-permute-done.9
  170.5 5.0 %fusion.7 = f32[2048,128]{0,1:T(8,128)S(1)} fusion(bf16[2048,2048]{0,1:T(8,128)(2,1)} %pad_maximum_fusion, f32[2048,128]{1,0:T(8,128)} %collective-permute-done.9, f32[2048,256]{1,0:T(8,128)S(1)} %fusion.3, f32[2048]{0:T(1024)S(1)} %pad_maximum_fusion.14), kind=kOutput, calls=%fused_computation.24 | convolution fusion | flops 1074266112 | bytes 11542528 | tf_op jit(solution)/shard_map/dot_general | solution.py:137
  175.6 1.6 collective-permute-start.10
  177.3 12.4 %collective-permute-done.10 = f32[1024,128]{0,1:T(8,128)S(1)} collective-permute-done((f32[1024,128]{0,1:T(8,128)S(1)}, f32[1024,128]{0,1:T(8,128)S(1)}, u32[]{:S(2)}, u32[]{:S(2)}) %collective-permute-start.10) | collective-permute-done | bytes 524320 | tf_op jit(solution)/shard_map/ppermute | solution.py:144
  189.8 1.3 collective-permute-done.11
  191.2 0.3 convolution_convert_fusion
  191.5 22.0 %all_to_all.25 = bf16[8,80,512]{2,1,0:T(8,128)(2,1)S(1)} all-to-all(bf16[8,80,512]{2,1,0:T(8,128)(2,1)S(1)} %bitcast.62), channel_id=1, replica_groups=mesh['tile'=8,'win'=4] {'tile'}, dimensions={0} | all-to-all | bytes 1310720 | tf_op jit(solution)/shard_map/all_to_all | solution.py:234
  213.6 0.8 copy-done.3
  (61 shorter events, 2.8 us)
Async XLA Ops:
  0.0 9.7 %copy-start.6 = (s32[256]{0:T(256)S(1)}, s32[256]{0:T(256)}, u32[]{:S(2)}) copy-start(s32[256]{0:T(256)} %param.5) | copy-start | bytes 3076
  0.0 9.7 %copy-start.5 = (s32[256]{0:T(256)S(1)}, s32[256]{0:T(256)}, u32[]{:S(2)}) copy-start(s32[256]{0:T(256)} %param.6) | copy-start | bytes 3076
  0.0 9.7 %copy-start.4 = (s32[256,1]{0,1:T(1,128)S(1)}, s32[256,1]{0,1:T(1,128)}, u32[]{:S(2)}) copy-start(s32[256,1]{0,1:T(1,128)} %param.7) | copy-start | bytes 3076
  2.4 33.1 %all-to-all-start.2 = ((bf16[8,256,256]{2,1,0:T(8,128)(2,1)}), bf16[8,256,256]{2,1,0:T(8,128)(2,1)S(1)}, u32[]{:S(2)}, u32[]{:S(2)}) async-start(bf16[8,256,256]{2,1,0:T(8,128)(2,1)} %shard_map.48), calls=%async_computation.2 | async-start | bytes 2097152 | tf_op jit(solution)/shard_map/all_to_all | solution.py:206
  9.7 14.3 %collective-permute-start = (s32[3,256]{1,0:T(4,128)S(1)}, s32[3,256]{1,0:T(4,128)S(1)}, u32[]{:S(2)}, u32[]{:S(2)}) collective-permute-start(s32[3,256]{1,0:T(4,128)S(1)} %pad_add_fusion), channel_id=1, source_target_pairs={{0,0},{4,4},{8,12},{12,20},{16,28},{20,24},{24,16},{28,8},{1,1},{5... | collective-permute-start | bytes 9224 | tf_op jit(solution)/shard_map/ppermute | solution.py:193
  35.4 30.8 %all-to-all-start.1 = ((bf16[8,256,256]{2,1,0:T(8,128)(2,1)}), bf16[8,256,256]{2,1,0:T(8,128)(2,1)S(1)}, u32[]{:S(2)}, u32[]{:S(2)}) async-start(bf16[8,256,256]{2,1,0:T(8,128)(2,1)} %shard_map.47), calls=%async_computation.1 | async-start | bytes 2097152 | tf_op jit(solution)/shard_map/all_to_all | solution.py:206
  45.8 24.7 %collective-permute-start.1 = (bf16[2048,128]{1,0:T(8,128)(2,1)S(1)}, bf16[2048,128]{1,0:T(8,128)(2,1)}, u32[]{:S(2)}, u32[]{:S(2)}) collective-permute-start(bf16[2048,128]{1,0:T(8,128)(2,1)S(1)} %get-tuple-element.36), channel_id=1, source_target_pairs={{0,4},{4,12},{12,20},{20,28},{28,24},{24,16},{16,8},{8,0},{1,5},{5... | collective-permute-start | bytes 1572872 | tf_op jit(solution)/shard_map/ppermute | solution.py:213
  47.9 22.6 %collective-permute-start.2 = (bf16[2048,128]{1,0:T(8,128)(2,1)S(1)}, bf16[2048,128]{1,0:T(8,128)(2,1)}, u32[]{:S(2)}, u32[]{:S(2)}) collective-permute-start(bf16[2048,128]{1,0:T(8,128)(2,1)S(1)} %get-tuple-element.35), channel_id=1, source_target_pairs={{0,8},{4,0},{12,4},{20,12},{28,20},{24,28},{16,24},{8,16},{1,9},{5... | collective-permute-start | bytes 1572872 | tf_op jit(solution)/shard_map/ppermute | solution.py:214
  66.2 33.9 %all-to-all-start = ((bf16[8,256,256]{2,1,0:T(8,128)(2,1)}), bf16[8,256,256]{2,1,0:T(8,128)(2,1)}, u32[]{:S(2)}, u32[]{:S(2)}) async-start(bf16[8,256,256]{2,1,0:T(8,128)(2,1)} %shard_map.46), calls=%async_computation | async-start | bytes 2097152 | tf_op jit(solution)/shard_map/all_to_all | solution.py:206
  78.2 26.6 %collective-permute-start.3 = (bf16[2048,128]{1,0:T(8,128)(2,1)}, bf16[2048,128]{1,0:T(8,128)(2,1)}, u32[]{:S(2)}, u32[]{:S(2)}) collective-permute-start(bf16[2048,128]{1,0:T(8,128)(2,1)} %get-tuple-element.34), channel_id=1, source_target_pairs={{0,4},{4,12},{12,20},{20,28},{28,24},{24,16},{16,8},{8,0},{1,5},{5... | collective-permute-start | bytes 1572872 | tf_op jit(solution)/shard_map/ppermute | solution.py:213
  80.1 24.7 %collective-permute-start.4 = (bf16[2048,128]{1,0:T(8,128)(2,1)}, bf16[2048,128]{1,0:T(8,128)(2,1)}, u32[]{:S(2)}, u32[]{:S(2)}) collective-permute-start(bf16[2048,128]{1,0:T(8,128)(2,1)} %get-tuple-element.33), channel_id=1, source_target_pairs={{0,8},{4,0},{12,4},{20,12},{28,20},{24,28},{16,24},{8,16},{1,9},{5... | collective-permute-start | bytes 1572872 | tf_op jit(solution)/shard_map/ppermute | solution.py:214
  100.1 33.8 %all-to-all-start.3 = ((bf16[8,256,256]{2,1,0:T(8,128)(2,1)}), bf16[8,256,256]{2,1,0:T(8,128)(2,1)}, u32[]{:S(2)}, u32[]{:S(2)}) async-start(bf16[8,256,256]{2,1,0:T(8,128)(2,1)} %shard_map.49), calls=%async_computation.3 | async-start | bytes 2097152 | tf_op jit(solution)/shard_map/all_to_all | solution.py:206
  112.8 26.2 %collective-permute-start.5 = (bf16[2048,128]{1,0:T(8,128)(2,1)}, bf16[2048,128]{1,0:T(8,128)(2,1)}, u32[]{:S(2)}, u32[]{:S(2)}) collective-permute-start(bf16[2048,128]{1,0:T(8,128)(2,1)} %get-tuple-element.31), channel_id=1, source_target_pairs={{0,4},{4,12},{12,20},{20,28},{28,24},{24,16},{16,8},{8,0},{1,5},{5... | collective-permute-start | bytes 1572872 | tf_op jit(solution)/shard_map/ppermute | solution.py:213
  117.6 21.3 %collective-permute-start.6 = (bf16[2048,128]{1,0:T(8,128)(2,1)}, bf16[2048,128]{1,0:T(8,128)(2,1)}, u32[]{:S(2)}, u32[]{:S(2)}) collective-permute-start(bf16[2048,128]{1,0:T(8,128)(2,1)} %get-tuple-element.32), channel_id=1, source_target_pairs={{0,8},{4,0},{12,4},{20,12},{28,20},{24,28},{16,24},{8,16},{1,9},{5... | collective-permute-start | bytes 1572872 | tf_op jit(solution)/shard_map/ppermute | solution.py:214
  145.9 16.5 %collective-permute-start.7 = (bf16[2048,128]{1,0:T(8,128)(2,1)S(1)}, bf16[2048,128]{1,0:T(8,128)(2,1)S(1)}, u32[]{:S(2)}, u32[]{:S(2)}) collective-permute-start(bf16[2048,128]{1,0:T(8,128)(2,1)S(1)} %get-tuple-element.29), channel_id=1, source_target_pairs={{0,4},{4,12},{12,20},{20,28},{28,24},{24,16},{16,8},{8,0},{1,5},{5... | collective-permute-start | bytes 1572872 | tf_op jit(solution)/shard_map/ppermute | solution.py:213
  149.6 14.0 %collective-permute-start.8 = (bf16[2048,128]{1,0:T(8,128)(2,1)S(1)}, bf16[2048,128]{1,0:T(8,128)(2,1)S(1)}, u32[]{:S(2)}, u32[]{:S(2)}) collective-permute-start(bf16[2048,128]{1,0:T(8,128)(2,1)S(1)} %get-tuple-element.30), channel_id=1, source_target_pairs={{0,8},{4,0},{12,4},{20,12},{28,20},{24,28},{16,24},{8,16},{1,9},{5... | collective-permute-start | bytes 1572872 | tf_op jit(solution)/shard_map/ppermute | solution.py:214
  165.2 1.2 copy-start
  165.2 1.5 copy-start.1
  165.2 1.8 copy-start.2
  167.7 2.9 %collective-permute-start.9 = (f32[2048,128]{1,0:T(8,128)S(1)}, f32[2048,128]{1,0:T(8,128)}, u32[]{:S(2)}, u32[]{:S(2)}) collective-permute-start(f32[2048,128]{1,0:T(8,128)S(1)} %slice.246), channel_id=1, source_target_pairs={{0,1},{1,0},{2,3},{3,2},{4,5},{5,4},{6,7},{7,6},{8,9},{9,8},{10,11... | collective-permute-start | bytes 3145736 | tf_op jit(solution)/shard_map/ppermute | solution.py:131
  175.6 14.0 %collective-permute-start.10 = (f32[1024,128]{0,1:T(8,128)S(1)}, f32[1024,128]{0,1:T(8,128)S(1)}, u32[]{:S(2)}, u32[]{:S(2)}) collective-permute-start(f32[1024,128]{0,1:T(8,128)S(1)} %constant_dynamic-slice_fusion.2), channel_id=1, source_target_pairs={{0,2},{1,3},{2,0},{3,1},{4,6},{5,7},{6,4},{7,5},{8,10},{9,11},{10,... | collective-permute-start | bytes 1572872 | tf_op jit(solution)/shard_map/ppermute | solution.py:144
  189.7 1.4 collective-permute-start.11
  213.6 0.8 copy-start.3

commit v21 on v20

--- a/solution.py
+++ b/solution.py
@@ -209,9 +209,11 @@
             if segment == min(2, records.shape[0] - 1):
                 received, table = lax.optimization_barrier((received, inverse_table(length, lag_start)))
             spectra = jnp.dot(forward, received.reshape(length, block), preferred_element_type=jnp.float32)
-            whitened = whiten(spectra, BAND)
-            from_prev = lax.ppermute(whitened[:, half:], "tile", to_next)
-            from_next = lax.ppermute(whitened[:, :half], "tile", to_prev)
+            lower = whiten(spectra[:, :half], BAND)
+            upper = whiten(spectra[:, half:], BAND)
+            from_prev = lax.ppermute(upper, "tile", to_next)
+            from_next = lax.ppermute(lower, "tile", to_prev)
+            whitened = jnp.concatenate([lower, upper], axis=1)
             if segment == 0:
                 lag_start, _ = lax.optimization_barrier((jnp.int32(0), whitened))
             arrived.append((from_prev, from_next))

time: 215 us -> 218 us (1.014)
  waiting for transfers between devices: 56.3 us -> 59.2 us
  local copies, waits for them, and re-layouts: 5.34 us -> 3.1 us
    ppermute x8, waiting for transfers between devices: 13 us -> 19.6 us  [the longest x4 18.4 us: per_device(): from_prev = lax.ppermute(upper, 'tile', to_next)]
    all_to_all x4, waiting for transfers between devices: 27.8 us -> 24.1 us  [per_device(): lax.all_to_all(outgoing, 'tile', split_axis=0, concat_axis=0, tiled=True)]
    slice x4 -> x0, local copies, waits for them, and re-layouts: 2.21 us -> none  [the longest x2 1.11 us: per_device(): from_prev = lax.ppermute(whitened[:, half:], 'tile', to_next)]
  transfers between devices with their start and end apart: 16 -> 16, of which waited for: 11 -> 11; matrix products, arithmetic and copies ran while one was open for 28% -> 28% of each run, Pallas kernels for 3% -> 4%
where the time goes in v21:
time: 218 us; the launch traced here: 217 us
  waiting for transfers between devices  59.2 us (27%)
  starting transfers between devices  48.1 us (22%)
  matrix products  43.6 us (20%)
  other arithmetic  31.1 us (14%)
  blocking collectives  21.9 us (10%)
  Pallas kernels  9.3 us (4%)
  local copies, waits for them, and re-layouts  3.1 us (1%)
    dot_general x4, matrix products, per_device(): jnp.dot(forward, received.reshape(length, block), preferred_element_type=...  24.3 us
    all_to_all x4, waiting for transfers between devices, per_device(): lax.all_to_all(outgoing, 'tile', split_axis=0, concat_axis=0, tiled=True)  24.1 us
    ppermute x4, starting transfers between devices, per_device(): from_next = lax.ppermute(lower, 'tile', to_prev)  22 us
    all_to_all x1, blocking collectives, per_device(): lax.all_to_all(buckets, 'tile', split_axis=0, concat_axis=0, tiled=True)  21.9 us
    all_to_all x4, starting transfers between devices, per_device(): lax.all_to_all(outgoing, 'tile', split_axis=0, concat_axis=0, tiled=True)  19.8 us
    ppermute x4, waiting for transfers between devices, per_device(): from_prev = lax.ppermute(upper, 'tile', to_next)  18.4 us
    ppermute x1, waiting for transfers between devices, sum_and_invert(): lax.ppermute(send, 'win', [(w, w ^ 2 * bit) for w in range(win_count)])  12.4 us
    pallas_call x4, Pallas kernels, lay_out_blocks(): pl.pallas_call(kernel, out_shape=jax.ShapeDtypeStruct((parts, rows, block...  9.3 us
  transfers between devices with their start and end apart: 16, of which 11 were waited for; matrix products, arithmetic and copies ran while one was open for 28% of the time, Pallas kernels for 4%

profile of v21, /device:TPU:0, one launch (start us, length us, event | category | flops | bytes accessed | tf_op | source)
XLA Modules:
  0.0 216.9 jit_solution(10054740336510731471)
XLA Ops:
  0.0 0.7 pad_add_fusion
  0.7 0.6 collective-permute-start
  1.4 2.3 %shard_map.48 = bf16[8,256,256]{2,1,0:T(8,128)(2,1)} custom-call(bf16[4,256,2048]{2,1,0:T(8,128)(2,1)} %src.7), custom_call_target="tpu_custom_call" | custom-call | tf_op jit(solution)/shard_map/pallas_call | solution.py:166
  3.7 9.1 %all-to-all-start.2 = ((bf16[8,256,256]{2,1,0:T(8,128)(2,1)}), bf16[8,256,256]{2,1,0:T(8,128)(2,1)S(1)}, u32[]{:S(2)}, u32[]{:S(2)}) async-start(bf16[8,256,256]{2,1,0:T(8,128)(2,1)} %shard_map.48), calls=%async_computation.2 | async-start | bytes 2097152 | tf_op jit(solution)/shard_map/all_to_all | solution.py:206
  12.8 0.6 fusion.68
  13.4 0.6 fusion.70
  14.0 2.4 %shard_map.47 = bf16[8,256,256]{2,1,0:T(8,128)(2,1)} custom-call(bf16[4,256,2048]{2,1,0:T(8,128)(2,1)} %src.7), custom_call_target="tpu_custom_call" | custom-call | tf_op jit(solution)/shard_map/pallas_call | solution.py:166
  16.4 1.0 fusion.62
  17.4 2.0 fusion.52
  19.5 4.9 %subtract_convert_fusion = (bf16[1024,32,64]{0,2,1:T(8,128)(2,1)}, bf16[1024,32,64]{0,2,1:T(8,128)(2,1)}) fusion(f32[1024,64]{0,1:T(8,128)S(1)} %get-tuple-element.60, f32[1024,32]{0,1:T(8,128)S(1)} %get-tuple-element.59, f32[1024,64]{0,1:T(8,128)S(1)} %get-tuple-element.61, f32[1024,32]{0,1:T(8,128)S(1)} %get-tuple-element.58), kind=kLoop, calls=%fused_computation.5 | loop fusion | flops 18874368 | bytes 9175040 | tf_op jit(solution)/shard_map/convert.3
  24.4 5.1 %multiply_subtract_fusion = (bf16[2048,16,64]{0,2,1:T(8,128)(2,1)}, bf16[2048,16,64]{0,2,1:T(8,128)(2,1)}) fusion(f32[2048,64]{0,1:T(8,128)S(1)} %get-tuple-element.50, f32[2048,16]{0,1:T(8,128)S(1)} %get-tuple-element.48, f32[2048,64]{0,1:T(8,128)S(1)} %get-tuple-element.49, f32[2048,16]{0,1:T(8,128)S(1)} %get-tuple-element.47), kind=kLoop, calls=%fused_computation.3 | loop fusion | flops 18874368 | bytes 9699328 | tf_op jit(solution)/shard_map/sub | solution.py:25
  29.5 8.9 %all-to-all-done.2 = bf16[8,256,256]{2,1,0:T(8,128)(2,1)S(1)} async-done(((bf16[8,256,256]{2,1,0:T(8,128)(2,1)}), bf16[8,256,256]{2,1,0:T(8,128)(2,1)S(1)}, u32[]{:S(2)}, u32[]{:S(2)}) %all-to-all-start.2) | async-done | bytes 1048608 | tf_op jit(solution)/shard_map/all_to_all | solution.py:206
  38.4 3.6 %all-to-all-start.1 = ((bf16[8,256,256]{2,1,0:T(8,128)(2,1)}), bf16[8,256,256]{2,1,0:T(8,128)(2,1)S(1)}, u32[]{:S(2)}, u32[]{:S(2)}) async-start(bf16[8,256,256]{2,1,0:T(8,128)(2,1)} %shard_map.47), calls=%async_computation.1 | async-start | bytes 2097152 | tf_op jit(solution)/shard_map/all_to_all | solution.py:206
  42.0 6.1 %fusion.86 = f32[2048,256]{1,0:T(8,128)S(1)} fusion(bf16[2048,256]{1,0:T(8,128)(2,1)S(1)} %bitcast.79, bf16[1024,2048]{0,1:T(8,128)(2,1)} %bitcast.64, bf16[1024,2048]{0,1:T(8,128)(2,1)} %bitcast.60), kind=kOutput, calls=%fused_computation.191 | convolution fusion | flops 2164260864 | bytes 11534336 | tf_op jit(solution)/shard_map/dot_general | solution.py:211
  48.3 0.3 fusion.11
  48.6 2.0 collective-permute-start.2
  50.6 0.2 collective-permute-start.1
  50.9 8.4 %pad_maximum_fusion = bf16[2048,2048]{0,1:T(8,128)(2,1)} fusion(bf16[2048,1024]{0,1:T(8,128)(2,1)} %bitcast.59, bf16[2048,1024]{0,1:T(8,128)(2,1)} %bitcast.58), kind=kLoop, calls=%fused_computation | loop fusion | flops 16777216 | bytes 16777216 | tf_op jit(solution)/shard_map/concatenate | solution.py:116
  59.2 2.3 %shard_map.46 = bf16[8,256,256]{2,1,0:T(8,128)(2,1)} custom-call(bf16[4,256,2048]{2,1,0:T(8,128)(2,1)} %src.7), custom_call_target="tpu_custom_call" | custom-call | tf_op jit(solution)/shard_map/pallas_call | solution.py:166
  61.5 2.3 %shard_map.49 = bf16[8,256,256]{2,1,0:T(8,128)(2,1)} custom-call(bf16[4,256,2048]{2,1,0:T(8,128)(2,1)} %src.7), custom_call_target="tpu_custom_call" | custom-call | tf_op jit(solution)/shard_map/pallas_call | solution.py:166
  63.8 5.2 %all-to-all-done.1 = bf16[8,256,256]{2,1,0:T(8,128)(2,1)S(1)} async-done(((bf16[8,256,256]{2,1,0:T(8,128)(2,1)}), bf16[8,256,256]{2,1,0:T(8,128)(2,1)S(1)}, u32[]{:S(2)}, u32[]{:S(2)}) %all-to-all-start.1) | async-done | bytes 1048608 | tf_op jit(solution)/shard_map/all_to_all | solution.py:206
  69.1 3.6 %all-to-all-start = ((bf16[8,256,256]{2,1,0:T(8,128)(2,1)}), bf16[8,256,256]{2,1,0:T(8,128)(2,1)S(1)}, u32[]{:S(2)}, u32[]{:S(2)}) async-start(bf16[8,256,256]{2,1,0:T(8,128)(2,1)} %shard_map.46), calls=%async_computation | async-start | bytes 2097152 | tf_op jit(solution)/shard_map/all_to_all | solution.py:206
  72.7 6.1 %fusion.85 = f32[2048,256]{1,0:T(8,128)S(1)} fusion(bf16[2048,256]{1,0:T(8,128)(2,1)S(1)} %bitcast.76, bf16[1024,2048]{0,1:T(8,128)(2,1)} %bitcast.65, bf16[1024,2048]{0,1:T(8,128)(2,1)} %bitcast.61), kind=kOutput, calls=%fused_computation.190 | convolution fusion | flops 2164260864 | bytes 11534336 | tf_op jit(solution)/shard_map/dot_general | solution.py:211
  79.0 1.3 fusion.9
  80.3 12.1 %collective-permute-start.4 = (bf16[2048,128]{1,0:T(8,128)(2,1)}, bf16[2048,128]{1,0:T(8,128)(2,1)}, u32[]{:S(2)}, u32[]{:S(2)}) collective-permute-start(bf16[2048,128]{1,0:T(8,128)(2,1)} %get-tuple-element.37), channel_id=1, source_target_pairs={{0,8},{4,0},{12,4},{20,12},{28,20},{24,28},{16,24},{8,16},{1,9},{5... | collective-permute-start | bytes 1572872 | tf_op jit(solution)/shard_map/ppermute | solution.py:215
  92.4 2.0 fusion.32
  94.4 2.0 fusion.28
  96.4 1.3 multiply_add_fusion.3
  97.6 5.2 %all-to-all-done = bf16[8,256,256]{2,1,0:T(8,128)(2,1)S(1)} async-done(((bf16[8,256,256]{2,1,0:T(8,128)(2,1)}), bf16[8,256,256]{2,1,0:T(8,128)(2,1)S(1)}, u32[]{:S(2)}, u32[]{:S(2)}) %all-to-all-start) | async-done | bytes 1048608 | tf_op jit(solution)/shard_map/all_to_all | solution.py:206
  102.8 3.6 %all-to-all-start.3 = ((bf16[8,256,256]{2,1,0:T(8,128)(2,1)}), bf16[8,256,256]{2,1,0:T(8,128)(2,1)S(1)}, u32[]{:S(2)}, u32[]{:S(2)}) async-start(bf16[8,256,256]{2,1,0:T(8,128)(2,1)} %shard_map.49), calls=%async_computation.3 | async-start | bytes 2097152 | tf_op jit(solution)/shard_map/all_to_all | solution.py:206
  106.4 7.5 %collective-permute-done.3 = bf16[2048,128]{1,0:T(8,128)(2,1)} collective-permute-done((bf16[2048,128]{1,0:T(8,128)(2,1)}, bf16[2048,128]{1,0:T(8,128)(2,1)}, u32[]{:S(2)}, u32[]{:S(2)}) %collective-permute-start.3) | collective-permute-done | bytes 524320 | tf_op jit(solution)/shard_map/ppermute | solution.py:214
  113.9 6.1 %fusion.84 = f32[2048,256]{1,0:T(8,128)S(1)} fusion(bf16[2048,256]{1,0:T(8,128)(2,1)S(1)} %bitcast.77, bf16[1024,2048]{0,1:T(8,128)(2,1)} %bitcast.66, bf16[1024,2048]{0,1:T(8,128)(2,1)} %bitcast.62), kind=kOutput, calls=%fused_computation.189 | convolution fusion | flops 2164260864 | bytes 11534336 | tf_op jit(solution)/shard_map/dot_general | solution.py:211
  120.2 0.3 fusion.8
  120.6 4.9 %collective-permute-start.6 = (bf16[2048,128]{1,0:T(8,128)(2,1)S(1)}, bf16[2048,128]{1,0:T(8,128)(2,1)}, u32[]{:S(2)}, u32[]{:S(2)}) collective-permute-start(bf16[2048,128]{1,0:T(8,128)(2,1)S(1)} %get-tuple-element.36), channel_id=1, source_target_pairs={{0,8},{4,0},{12,4},{20,12},{28,20},{24,28},{16,24},{8,16},{1,9},{5... | collective-permute-start | bytes 1572872 | tf_op jit(solution)/shard_map/ppermute | solution.py:215
  125.5 2.3 %fusion.27 = f32[2048,256]{1,0:T(8,128)S(1)} fusion(bf16[2048,128]{1,0:T(8,128)(2,1)} %collective-permute-done.4, bf16[2048,128]{1,0:T(8,128)(2,1)} %get-tuple-element.38, bf16[2048,128]{1,0:T(8,128)(2,1)} %get-tuple-element.37, bf16[2048,128]{1,0:T(8,128)(2,1)} %collective-permute-done.3, s32[256]{0:T(256)S(1)} %bitcast.93), kind=kOutput, calls=%fused_computation.85 | convolution fusion | flops 545390592 | bytes 4195328 | tf_op jit(solution)/shard_map/dot_general | solution.py:222
  127.8 2.3 %fusion.31 = f32[2048,256]{1,0:T(8,128)S(1)} fusion(bf16[2048,128]{1,0:T(8,128)(2,1)} %collective-permute-done.4, bf16[2048,128]{1,0:T(8,128)(2,1)} %get-tuple-element.38, bf16[2048,128]{1,0:T(8,128)(2,1)} %get-tuple-element.37, bf16[2048,128]{1,0:T(8,128)(2,1)} %collective-permute-done.3, s32[256]{0:T(256)S(1)} %bitcast.89), kind=kOutput, calls=%fused_computation.90 | convolution fusion | flops 545390592 | bytes 4195328 | tf_op jit(solution)/shard_map/dot_general | solution.py:221
  130.1 1.6 multiply_add_fusion.2
  131.7 4.9 %all-to-all-done.3 = bf16[8,256,256]{2,1,0:T(8,128)(2,1)S(1)} async-done(((bf16[8,256,256]{2,1,0:T(8,128)(2,1)}), bf16[8,256,256]{2,1,0:T(8,128)(2,1)S(1)}, u32[]{:S(2)}, u32[]{:S(2)}) %all-to-all-start.3) | async-done | bytes 1048608 | tf_op jit(solution)/shard_map/all_to_all | solution.py:206
  136.6 4.2 %collective-permute-done.5 = bf16[2048,128]{1,0:T(8,128)(2,1)} collective-permute-done((bf16[2048,128]{1,0:T(8,128)(2,1)S(1)}, bf16[2048,128]{1,0:T(8,128)(2,1)}, u32[]{:S(2)}, u32[]{:S(2)}) %collective-permute-start.5) | collective-permute-done | bytes 524320 | tf_op jit(solution)/shard_map/ppermute | solution.py:214
  140.8 6.1 %fusion.83 = f32[2048,256]{1,0:T(8,128)S(1)} fusion(bf16[2048,256]{1,0:T(8,128)(2,1)S(1)} %bitcast.78, bf16[1024,2048]{0,1:T(8,128)(2,1)} %bitcast.67, bf16[1024,2048]{0,1:T(8,128)(2,1)} %bitcast.63), kind=kOutput, calls=%fused_computation.188 | convolution fusion | flops 2164260864 | bytes 11534336 | tf_op jit(solution)/shard_map/dot_general | solution.py:211
  147.1 0.3 fusion.6
  147.5 3.7 %collective-permute-start.7 = (bf16[2048,128]{1,0:T(8,128)(2,1)S(1)}, bf16[2048,128]{1,0:T(8,128)(2,1)S(1)}, u32[]{:S(2)}, u32[]{:S(2)}) collective-permute-start(bf16[2048,128]{1,0:T(8,128)(2,1)S(1)} %get-tuple-element.33), channel_id=1, source_target_pairs={{0,4},{4,12},{12,20},{20,28},{28,24},{24,16},{16,8},{8,0},{1,5},{5... | collective-permute-start | bytes 1572872 | tf_op jit(solution)/shard_map/ppermute | solution.py:214
  151.2 2.9 %collective-permute-start.8 = (bf16[2048,128]{1,0:T(8,128)(2,1)S(1)}, bf16[2048,128]{1,0:T(8,128)(2,1)S(1)}, u32[]{:S(2)}, u32[]{:S(2)}) collective-permute-start(bf16[2048,128]{1,0:T(8,128)(2,1)S(1)} %get-tuple-element.34), channel_id=1, source_target_pairs={{0,8},{4,0},{12,4},{20,12},{28,20},{24,28},{16,24},{8,16},{1,9},{5... | collective-permute-start | bytes 1572872 | tf_op jit(solution)/shard_map/ppermute | solution.py:215
  154.1 2.0 fusion.26
  156.0 2.0 fusion.30
  158.0 0.3 multiply_add_fusion.1
  158.3 6.7 %collective-permute-done.7 = bf16[2048,128]{1,0:T(8,128)(2,1)S(1)} collective-permute-done((bf16[2048,128]{1,0:T(8,128)(2,1)S(1)}, bf16[2048,128]{1,0:T(8,128)(2,1)S(1)}, u32[]{:S(2)}, u32[]{:S(2)}) %collective-permute-start.7) | collective-permute-done | bytes 524320 | tf_op jit(solution)/shard_map/ppermute | solution.py:214
  165.0 1.2 collective-permute-done.8
  166.2 0.8 fusion.25
  167.0 0.8 fusion.29
  167.8 0.3 multiply_add_fusion
  168.0 0.9 copy-done
  169.0 0.3 copy-done.1
  169.3 0.3 copy-done.2
  169.6 0.5 fusion.1
  170.4 0.6 reduce-window.6
  171.2 1.8 collective-permute-done.9
  173.1 5.0 %fusion.3 = f32[2048,128]{0,1:T(8,128)S(1)} fusion(bf16[2048,2048]{0,1:T(8,128)(2,1)} %pad_maximum_fusion, f32[2048,128]{1,0:T(8,128)} %collective-permute-done.9, f32[2048,256]{1,0:T(8,128)S(1)} %fusion.1, f32[2048]{0:T(1024)S(1)} %pad_maximum_fusion.14), kind=kOutput, calls=%fused_computation.16 | convolution fusion | flops 1074266112 | bytes 11542528 | tf_op jit(solution)/shard_map/dot_general | solution.py:137
  178.2 1.6 collective-permute-start.10
  179.8 12.4 %collective-permute-done.10 = f32[1024,128]{0,1:T(8,128)S(1)} collective-permute-done((f32[1024,128]{0,1:T(8,128)S(1)}, f32[1024,128]{0,1:T(8,128)S(1)}, u32[]{:S(2)}, u32[]{:S(2)}) %collective-permute-start.10) | collective-permute-done | bytes 524320 | tf_op jit(solution)/shard_map/ppermute | solution.py:144
  192.4 1.3 collective-permute-done.11
  193.7 0.3 convolution_convert_fusion
  194.1 21.9 %all_to_all.25 = bf16[8,80,512]{2,1,0:T(8,128)(2,1)S(1)} all-to-all(bf16[8,80,512]{2,1,0:T(8,128)(2,1)S(1)} %bitcast.80), channel_id=1, replica_groups=mesh['tile'=8,'win'=4] {'tile'}, dimensions={0} | all-to-all | bytes 1310720 | tf_op jit(solution)/shard_map/all_to_all | solution.py:236
  216.1 0.8 copy-done.3
  (59 shorter events, 1.9 us)
Async XLA Ops:
  0.7 63.1 %collective-permute-start = (s32[3,256]{1,0:T(4,128)S(1)}, s32[3,256]{1,0:T(4,128)S(1)}, u32[]{:S(2)}, u32[]{:S(2)}) collective-permute-start(s32[3,256]{1,0:T(4,128)S(1)} %pad_add_fusion), channel_id=1, source_target_pairs={{0,0},{4,4},{8,12},{12,20},{16,28},{20,24},{24,16},{28,8},{1,1},{5... | collective-permute-start | bytes 9224 | tf_op jit(solution)/shard_map/ppermute | solution.py:193
  3.7 34.7 %all-to-all-start.2 = ((bf16[8,256,256]{2,1,0:T(8,128)(2,1)}), bf16[8,256,256]{2,1,0:T(8,128)(2,1)S(1)}, u32[]{:S(2)}, u32[]{:S(2)}) async-start(bf16[8,256,256]{2,1,0:T(8,128)(2,1)} %shard_map.48), calls=%async_computation.2 | async-start | bytes 2097152 | tf_op jit(solution)/shard_map/all_to_all | solution.py:206
  38.4 30.7 %all-to-all-start.1 = ((bf16[8,256,256]{2,1,0:T(8,128)(2,1)}), bf16[8,256,256]{2,1,0:T(8,128)(2,1)S(1)}, u32[]{:S(2)}, u32[]{:S(2)}) async-start(bf16[8,256,256]{2,1,0:T(8,128)(2,1)} %shard_map.47), calls=%async_computation.1 | async-start | bytes 2097152 | tf_op jit(solution)/shard_map/all_to_all | solution.py:206
  48.6 24.0 %collective-permute-start.2 = (bf16[2048,128]{1,0:T(8,128)(2,1)S(1)}, bf16[2048,128]{1,0:T(8,128)(2,1)}, u32[]{:S(2)}, u32[]{:S(2)}) collective-permute-start(bf16[2048,128]{1,0:T(8,128)(2,1)S(1)} %get-tuple-element.39), channel_id=1, source_target_pairs={{0,8},{4,0},{12,4},{20,12},{28,20},{24,28},{16,24},{8,16},{1,9},{5... | collective-permute-start | bytes 1572872 | tf_op jit(solution)/shard_map/ppermute | solution.py:215
  50.6 22.0 %collective-permute-start.1 = (bf16[2048,128]{1,0:T(8,128)(2,1)S(1)}, bf16[2048,128]{1,0:T(8,128)(2,1)}, u32[]{:S(2)}, u32[]{:S(2)}) collective-permute-start(bf16[2048,128]{1,0:T(8,128)(2,1)S(1)} %get-tuple-element.40), channel_id=1, source_target_pairs={{0,4},{4,12},{12,20},{20,28},{28,24},{24,16},{16,8},{8,0},{1,5},{5... | collective-permute-start | bytes 1572872 | tf_op jit(solution)/shard_map/ppermute | solution.py:214
  69.1 33.8 %all-to-all-start = ((bf16[8,256,256]{2,1,0:T(8,128)(2,1)}), bf16[8,256,256]{2,1,0:T(8,128)(2,1)S(1)}, u32[]{:S(2)}, u32[]{:S(2)}) async-start(bf16[8,256,256]{2,1,0:T(8,128)(2,1)} %shard_map.46), calls=%async_computation | async-start | bytes 2097152 | tf_op jit(solution)/shard_map/all_to_all | solution.py:206
  80.3 26.1 %collective-permute-start.4 = (bf16[2048,128]{1,0:T(8,128)(2,1)}, bf16[2048,128]{1,0:T(8,128)(2,1)}, u32[]{:S(2)}, u32[]{:S(2)}) collective-permute-start(bf16[2048,128]{1,0:T(8,128)(2,1)} %get-tuple-element.37), channel_id=1, source_target_pairs={{0,8},{4,0},{12,4},{20,12},{28,20},{24,28},{16,24},{8,16},{1,9},{5... | collective-permute-start | bytes 1572872 | tf_op jit(solution)/shard_map/ppermute | solution.py:215
  92.4 21.4 %collective-permute-start.3 = (bf16[2048,128]{1,0:T(8,128)(2,1)}, bf16[2048,128]{1,0:T(8,128)(2,1)}, u32[]{:S(2)}, u32[]{:S(2)}) collective-permute-start(bf16[2048,128]{1,0:T(8,128)(2,1)} %get-tuple-element.38), channel_id=1, source_target_pairs={{0,4},{4,12},{12,20},{20,28},{28,24},{24,16},{16,8},{8,0},{1,5},{5... | collective-permute-start | bytes 1572872 | tf_op jit(solution)/shard_map/ppermute | solution.py:214
  102.8 33.8 %all-to-all-start.3 = ((bf16[8,256,256]{2,1,0:T(8,128)(2,1)}), bf16[8,256,256]{2,1,0:T(8,128)(2,1)S(1)}, u32[]{:S(2)}, u32[]{:S(2)}) async-start(bf16[8,256,256]{2,1,0:T(8,128)(2,1)} %shard_map.49), calls=%async_computation.3 | async-start | bytes 2097152 | tf_op jit(solution)/shard_map/all_to_all | solution.py:206
  120.5 20.2 %collective-permute-start.5 = (bf16[2048,128]{1,0:T(8,128)(2,1)S(1)}, bf16[2048,128]{1,0:T(8,128)(2,1)}, u32[]{:S(2)}, u32[]{:S(2)}) collective-permute-start(bf16[2048,128]{1,0:T(8,128)(2,1)S(1)} %get-tuple-element.35), channel_id=1, source_target_pairs={{0,4},{4,12},{12,20},{20,28},{28,24},{24,16},{16,8},{8,0},{1,5},{5... | collective-permute-start | bytes 1572872 | tf_op jit(solution)/shard_map/ppermute | solution.py:214
  120.6 20.2 %collective-permute-start.6 = (bf16[2048,128]{1,0:T(8,128)(2,1)S(1)}, bf16[2048,128]{1,0:T(8,128)(2,1)}, u32[]{:S(2)}, u32[]{:S(2)}) collective-permute-start(bf16[2048,128]{1,0:T(8,128)(2,1)S(1)} %get-tuple-element.36), channel_id=1, source_target_pairs={{0,8},{4,0},{12,4},{20,12},{28,20},{24,28},{16,24},{8,16},{1,9},{5... | collective-permute-start | bytes 1572872 | tf_op jit(solution)/shard_map/ppermute | solution.py:215
  147.5 17.6 %collective-permute-start.7 = (bf16[2048,128]{1,0:T(8,128)(2,1)S(1)}, bf16[2048,128]{1,0:T(8,128)(2,1)S(1)}, u32[]{:S(2)}, u32[]{:S(2)}) collective-permute-start(bf16[2048,128]{1,0:T(8,128)(2,1)S(1)} %get-tuple-element.33), channel_id=1, source_target_pairs={{0,4},{4,12},{12,20},{20,28},{28,24},{24,16},{16,8},{8,0},{1,5},{5... | collective-permute-start | bytes 1572872 | tf_op jit(solution)/shard_map/ppermute | solution.py:214
  151.2 15.0 %collective-permute-start.8 = (bf16[2048,128]{1,0:T(8,128)(2,1)S(1)}, bf16[2048,128]{1,0:T(8,128)(2,1)S(1)}, u32[]{:S(2)}, u32[]{:S(2)}) collective-permute-start(bf16[2048,128]{1,0:T(8,128)(2,1)S(1)} %get-tuple-element.34), channel_id=1, source_target_pairs={{0,8},{4,0},{12,4},{20,12},{28,20},{24,28},{16,24},{8,16},{1,9},{5... | collective-permute-start | bytes 1572872 | tf_op jit(solution)/shard_map/ppermute | solution.py:215
  167.7 1.2 copy-start
  167.7 1.5 copy-start.1
  167.8 1.8 copy-start.2
  170.2 2.9 %collective-permute-start.9 = (f32[2048,128]{1,0:T(8,128)S(1)}, f32[2048,128]{1,0:T(8,128)}, u32[]{:S(2)}, u32[]{:S(2)}) collective-permute-start(f32[2048,128]{1,0:T(8,128)S(1)} %slice.302), channel_id=1, source_target_pairs={{0,1},{1,0},{2,3},{3,2},{4,5},{5,4},{6,7},{7,6},{8,9},{9,8},{10,11... | collective-permute-start | bytes 3145736 | tf_op jit(solution)/shard_map/ppermute | solution.py:131
  178.2 14.0 %collective-permute-start.10 = (f32[1024,128]{0,1:T(8,128)S(1)}, f32[1024,128]{0,1:T(8,128)S(1)}, u32[]{:S(2)}, u32[]{:S(2)}) collective-permute-start(f32[1024,128]{0,1:T(8,128)S(1)} %constant_dynamic-slice_fusion.2), channel_id=1, source_target_pairs={{0,2},{1,3},{2,0},{3,1},{4,6},{5,7},{6,4},{7,5},{8,10},{9,11},{10,... | collective-permute-start | bytes 1572872 | tf_op jit(solution)/shard_map/ppermute | solution.py:144
  192.3 1.4 collective-permute-start.11
  216.1 0.8 copy-start.3
